TPU v7x, 128 devices: a whole 4x4x4 slice. The times are simulated.
128 devices in a mesh: tm: 8 (over z_lo, x), row: 16 (over z_hi, y, core).
Axes of the slice: x: 4, y: 4, z: 4 (z_hi: 2, z_lo: 2; z = z_hi * 2 + z_lo), core: 2. Of those that a mesh axis runs over, the one named last changes fastest.
Arguments:
- video_clip: bfloat16 [128, 128, 64, 128], P('tm', 'row'), may hold values from -6 to 6
- spatial_one: bfloat16 [3, 3, 144, 64], replicated, may hold values from -0.25 to 0.25
- temporal_one: bfloat16 [3, 64, 144], replicated, may hold values from -0.3125 to 0.3125
- down_weight: bfloat16 [3, 3, 128, 64], replicated, may hold values from -0.25 to 0.25
- spatial_two: bfloat16 [3, 3, 288, 128], replicated, may hold values from -0.1875 to 0.1875
- temporal_two: bfloat16 [3, 128, 288], replicated, may hold values from -0.21875 to 0.21875
Outputs:
- encoded: bfloat16 [128, 64, 64, 128], P('tm', 'row')
All inputs are finite; a program needn't handle non-finite values.
Results may differ from a plain program's by a relative error of at most 0.0061.
Values may be sent and summed in bfloat16 or wider, within the bound.
No kernel may reach another device: no remote copies, remote signals or barrier semaphores. Data moves between devices by JAX's collectives and lax.ppermute only.
A program may use at most 64 MiB of HBM per device.

v0:
```python
import jax
import jax.numpy as jnp
from jax import lax
from jax.sharding import PartitionSpec as P


def padded_2(block, sides, width):
    for axis, dim in sides:
        count = lax.axis_size(axis)
        forward = [(i, i + 1) for i in range(count - 1)]
        backward = [(target, source) for source, target in forward]
        low = lax.ppermute(
            lax.slice_in_dim(block, block.shape[dim] - width, None, axis=dim), axis, forward
        )
        high = lax.ppermute(lax.slice_in_dim(block, 0, width, axis=dim), axis, backward)
        block = jnp.concatenate([low, block, high], axis=dim)
    return block


def from_behind(array, axis, by):
    devices = lax.axis_size(axis)
    pairs = [(i, i + by) for i in range(devices) if 0 <= i + by < devices]
    return lax.ppermute(array, axis, pairs)


def spatial(source, kernel, layout):
    return lax.conv_general_dilated(
        source,
        kernel,
        (1, 1),
        ((0, 0), (1, 1)),
        dimension_numbers=(layout, "HWOI", layout),
        preferred_element_type=jnp.float32,
    )


def temporal(source, kernel, layout):
    return lax.conv_general_dilated(
        source,
        kernel[:, None],
        (1, 1),
        ((0, 0), (0, 0)),
        dimension_numbers=(layout, "HWOI", layout),
        preferred_element_type=jnp.float32,
    )


def residual_block(source, spatial_kernel, temporal_kernel, space_layout, time_layout):
    padded = padded_2(source, (("tm", 0), ("row", 1)), 1)
    framed = jax.nn.relu(spatial(padded, spatial_kernel, space_layout)).astype(jnp.bfloat16)
    summed = source.astype(jnp.float32) + temporal(framed, temporal_kernel, time_layout)
    return jax.nn.relu(summed).astype(jnp.bfloat16)


def on_device(video_clip, spatial_one, temporal_one, down_weight, spatial_two, temporal_two):
    section_one = residual_block(video_clip, spatial_one, temporal_one, "NHCW", "HWCN")
    upper_row = from_behind(section_one[:, -1:], "row", 1)
    joined = jnp.concatenate([upper_row, section_one], axis=1)
    reduced = lax.conv_general_dilated(
        joined,
        down_weight,
        (2, 2),
        ((0, 0), (1, 1)),
        dimension_numbers=("NHCW", "HWOI", "NHWC"),
        preferred_element_type=jnp.float32,
    )
    reduced = jax.nn.relu(reduced).astype(jnp.bfloat16)
    return residual_block(reduced, spatial_two, temporal_two, "NHWC", "HWNC")


def solution(mesh):
    placed = (P("tm", "row", None, None), P(), P(), P(), P(), P())
    return jax.shard_map(
        on_device, mesh=mesh, in_specs=placed, out_specs=P("tm", "row", None, None), check_vma=False
    )
```

profile of v0, /device:TPU:31, one launch (start us, length us, event | category | flops | bytes accessed | tf_op | source)
XLA Modules:
  0.0 124.8 jit_solution(8221863039376968058)
XLA Ops:
  0.0 0.0 copy-start
  0.0 1.1 fusion.21
  1.1 3.5 %collective-permute-start = (bf16[1,8,64,128]{3,2,1,0:T(8,128)(2,1)S(1)}, bf16[1,8,64,128]{3,2,1,0:T(8,128)(2,1)S(1)}, u32[]{:S(2)}, u32[]{:S(2)}) collective-permute-start(bf16[1,8,64,128]{3,2,1,0:T(8,128)(2,1)S(1)} %get-tuple-element.8), channel_id=1, source_target_pairs={{0,16},{16,32},{32,48},{48,64},{64,80},{80,96},{96,112},{1,17},{17... | collective-permute-start | bytes 393224 | tf_op jit(solution)/shard_map/ppermute | solution.py:12
  4.5 1.9 %collective-permute-start.1 = (bf16[1,8,64,128]{3,2,1,0:T(8,128)(2,1)S(1)}, bf16[1,8,64,128]{3,2,1,0:T(8,128)(2,1)S(1)}, u32[]{:S(2)}, u32[]{:S(2)}) collective-permute-start(bf16[1,8,64,128]{3,2,1,0:T(8,128)(2,1)S(1)} %get-tuple-element.7), channel_id=1, source_target_pairs={{16,0},{32,16},{48,32},{64,48},{80,64},{96,80},{112,96},{17,1},{33... | collective-permute-start | bytes 393224 | tf_op jit(solution)/shard_map/ppermute | solution.py:15
  6.5 0.9 collective-permute-done
  7.3 1.9 %constant_dynamic-update-slice_fusion.1 = bf16[18,8,64,128]{3,2,1,0:T(8,128)(2,1)S(1)} fusion(bf16[18,8,64,128]{3,2,1,0:T(8,128)(2,1)S(1)} %constant_dynamic-update-slice_fusion.2, bf16[16,8,64,128]{3,2,1,0:T(8,128)(2,1)} %param.6), kind=kLoop, calls=%fused_computation.28 | loop fusion | bytes 4194304
  9.3 3.0 %collective-permute-done.1 = bf16[1,8,64,128]{3,2,1,0:T(8,128)(2,1)S(1)} collective-permute-done((bf16[1,8,64,128]{3,2,1,0:T(8,128)(2,1)S(1)}, bf16[1,8,64,128]{3,2,1,0:T(8,128)(2,1)S(1)}, u32[]{:S(2)}, u32[]{:S(2)}) %collective-permute-start.1) | collective-permute-done | bytes 131104 | tf_op jit(solution)/shard_map/ppermute | solution.py:15
  12.4 6.9 %collective-permute-start.2 = (bf16[18,1,64,128]{3,2,1,0:T(8,128)(2,1)S(1)}, bf16[18,1,64,128]{3,2,1,0:T(8,128)(2,1)S(1)}, u32[]{:S(2)}, u32[]{:S(2)}) collective-permute-start(bf16[18,1,64,128]{3,2,1,0:T(8,128)(2,1)S(1)} %get-tuple-element.5), channel_id=1, source_target_pairs={{0,1},{1,2},{2,3},{3,4},{4,5},{5,6},{6,7},{7,8},{8,9},{9,10},{10,1... | collective-permute-start | bytes 884744 | tf_op jit(solution)/shard_map/ppermute | solution.py:12
  19.3 1.9 %collective-permute-start.3 = (bf16[18,1,64,128]{3,2,1,0:T(8,128)(2,1)S(1)}, bf16[18,1,64,128]{3,2,1,0:T(8,128)(2,1)S(1)}, u32[]{:S(2)}, u32[]{:S(2)}) collective-permute-start(bf16[18,1,64,128]{3,2,1,0:T(8,128)(2,1)S(1)} %get-tuple-element.6), channel_id=1, source_target_pairs={{1,0},{2,1},{3,2},{4,3},{5,4},{6,5},{7,6},{8,7},{9,8},{10,9},{11,1... | collective-permute-start | bytes 884744 | tf_op jit(solution)/shard_map/ppermute | solution.py:15
  21.2 1.7 %collective-permute-done.2 = bf16[18,1,64,128]{3,2,1,0:T(8,128)(2,1)S(1)} collective-permute-done((bf16[18,1,64,128]{3,2,1,0:T(8,128)(2,1)S(1)}, bf16[18,1,64,128]{3,2,1,0:T(8,128)(2,1)S(1)}, u32[]{:S(2)}, u32[]{:S(2)}) %collective-permute-start.2) | collective-permute-done | bytes 294944 | tf_op jit(solution)/shard_map/ppermute | solution.py:12
  22.9 8.0 %collective-permute-done.3 = bf16[18,1,64,128]{3,2,1,0:T(8,128)(2,1)S(1)} collective-permute-done((bf16[18,1,64,128]{3,2,1,0:T(8,128)(2,1)S(1)}, bf16[18,1,64,128]{3,2,1,0:T(8,128)(2,1)S(1)}, u32[]{:S(2)}, u32[]{:S(2)}) %collective-permute-start.3) | collective-permute-done | bytes 294944 | tf_op jit(solution)/shard_map/ppermute | solution.py:15
  30.9 2.1 %pad_maximum_fusion = bf16[18,10,64,128]{3,2,1,0:T(8,128)(2,1)} fusion(bf16[18,1,64,128]{3,2,1,0:T(8,128)(2,1)S(1)} %collective-permute-done.3, bf16[18,8,64,128]{3,2,1,0:T(8,128)(2,1)S(1)} %constant_dynamic-update-slice_fusion, bf16[18,1,64,128]{3,2,1,0:T(8,128)(2,1)S(1)} %collective-permute-done.2), kind=kLoop, calls=%fused_computation.7 | loop fusion | flops 2949120 | bytes 5898240 | tf_op jit(solution)/shard_map/concatenate | solution.py:16
  33.0 0.0 copy-start.2
  33.0 9.1 %copy.17 = bf16[18,10,64,128]{2,0,3,1:T(8,128)(2,1)} copy(bf16[18,10,64,128]{3,2,1,0:T(8,128)(2,1)} %pad_maximum_fusion) | data formatting | bytes 5898240 | tf_op jit(solution)/shard_map/concatenate | solution.py:16
  42.1 0.0 copy-done.2
  42.1 0.0 copy-start.1
  42.1 0.0 copy-start.5
  42.1 13.8 %maximum_convert_fusion = bf16[18,8,144,128]{2,0,3,1:T(8,128)(2,1)S(1)} fusion(bf16[18,10,64,128]{2,0,3,1:T(8,128)(2,1)} %copy.17, bf16[3,3,144,64]{2,3,1,0:T(8,128)(2,1)S(1)} %copy-done.2), kind=kOutput, calls=%fused_computation | convolution fusion | flops 3047030784 | bytes 8423424 | tf_op jit(solution)/shard_map/conv_general_dilated | solution.py:27
  56.0 0.0 copy-done.1
  56.0 0.0 copy-done.5
  56.0 7.9 %maximum_convert_fusion.2 = bf16[16,8,64,128]{3,2,1,0:T(8,128)(2,1)S(1)} fusion(bf16[16,8,64,128]{3,2,1,0:T(8,128)(2,1)S(1)} %copy-done.1, bf16[18,8,144,128]{2,0,3,1:T(8,128)(2,1)S(1)} %maximum_convert_fusion, bf16[3,64,144]{2,1,0:T(8,128)(2,1)S(1)} %copy-done.5), kind=kOutput, calls=%fused_computation.4 | convolution fusion | flops 910163968 | bytes 9558016 | tf_op jit(solution)/shard_map/conv_general_dilated | solution.py:38
  63.9 2.1 %collective-permute-start.4 = (bf16[16,1,64,128]{3,2,1,0:T(8,128)(2,1)S(1)}, bf16[16,1,64,128]{3,2,1,0:T(8,128)(2,1)S(1)}, u32[]{:S(2)}, u32[]{:S(2)}) collective-permute-start(bf16[16,1,64,128]{3,2,1,0:T(8,128)(2,1)S(1)} %slice.38), channel_id=1, source_target_pairs={{0,1},{1,2},{2,3},{3,4},{4,5},{5,6},{6,7},{7,8},{8,9},{9,10},{10,1... | collective-permute-start | bytes 786440 | tf_op jit(solution)/shard_map/ppermute | solution.py:23
  66.0 3.1 %collective-permute-done.4 = bf16[16,1,64,128]{3,2,1,0:T(8,128)(2,1)S(1)} collective-permute-done((bf16[16,1,64,128]{3,2,1,0:T(8,128)(2,1)S(1)}, bf16[16,1,64,128]{3,2,1,0:T(8,128)(2,1)S(1)}, u32[]{:S(2)}, u32[]{:S(2)}) %collective-permute-start.4) | collective-permute-done | bytes 262176 | tf_op jit(solution)/shard_map/ppermute | solution.py:23
  69.1 0.2 pad_maximum_fusion.1
  69.3 0.0 copy-start.4
  69.3 5.3 %copy.20 = bf16[16,9,64,128]{2,0,3,1:T(8,128)(2,1)} copy(bf16[16,9,64,128]{3,2,1,0:T(8,128)(2,1)S(1)} %pad_maximum_fusion.1) | data formatting | bytes 4718592 | tf_op jit(solution)/shard_map/concatenate | solution.py:58
  74.6 0.0 copy-done.4
  74.6 3.9 %maximum_convert_fusion.3 = bf16[16,4,64,128]{3,0,2,1:T(8,128)(2,1)S(1)} fusion(bf16[16,9,64,128]{2,0,3,1:T(8,128)(2,1)} %copy.20, bf16[3,3,128,64]{2,3,1,0:T(8,128)(2,1)S(1)} %copy-done.4), kind=kOutput, calls=%fused_computation.21 | convolution fusion | flops 601882624 | bytes 3555328 | tf_op jit(solution)/shard_map/conv_general_dilated | solution.py:59
  78.5 0.2 fusion.22
  78.8 1.9 %collective-permute-start.5 = (bf16[1,4,64,128]{3,0,2,1:T(2,128)(2,1)S(1)}, bf16[1,4,64,128]{3,0,2,1:T(2,128)(2,1)S(1)}, u32[]{:S(2)}, u32[]{:S(2)}) collective-permute-start(bf16[1,4,64,128]{3,0,2,1:T(2,128)(2,1)S(1)} %get-tuple-element.11), channel_id=1, source_target_pairs={{0,16},{16,32},{32,48},{48,64},{64,80},{80,96},{96,112},{1,17},{17... | collective-permute-start | bytes 196616 | tf_op jit(solution)/shard_map/ppermute | solution.py:12
  80.7 3.4 %collective-permute-start.6 = (bf16[1,4,64,128]{3,0,2,1:T(2,128)(2,1)S(1)}, bf16[1,4,64,128]{3,0,2,1:T(2,128)(2,1)S(1)}, u32[]{:S(2)}, u32[]{:S(2)}) collective-permute-start(bf16[1,4,64,128]{3,0,2,1:T(2,128)(2,1)S(1)} %get-tuple-element.12), channel_id=1, source_target_pairs={{16,0},{32,16},{48,32},{64,48},{80,64},{96,80},{112,96},{17,1},{33... | collective-permute-start | bytes 196616 | tf_op jit(solution)/shard_map/ppermute | solution.py:15
  84.1 0.6 collective-permute-done.5
  84.7 4.0 %collective-permute-done.6 = bf16[1,4,64,128]{3,0,2,1:T(2,128)(2,1)S(1)} collective-permute-done((bf16[1,4,64,128]{3,0,2,1:T(2,128)(2,1)S(1)}, bf16[1,4,64,128]{3,0,2,1:T(2,128)(2,1)S(1)}, u32[]{:S(2)}, u32[]{:S(2)}) %collective-permute-start.6) | collective-permute-done | bytes 65568 | tf_op jit(solution)/shard_map/ppermute | solution.py:15
  88.7 0.4 pad_maximum_fusion.4
  89.2 9.3 %collective-permute-start.7 = (bf16[18,1,64,128]{3,0,2,1:T(8,128)(2,1)S(1)}, bf16[18,1,64,128]{3,0,2,1:T(8,128)(2,1)S(1)}, u32[]{:S(2)}, u32[]{:S(2)}) collective-permute-start(bf16[18,1,64,128]{3,0,2,1:T(8,128)(2,1)S(1)} %get-tuple-element.9), channel_id=1, source_target_pairs={{0,1},{1,2},{2,3},{3,4},{4,5},{5,6},{6,7},{7,8},{8,9},{9,10},{10,1... | collective-permute-start | bytes 884744 | tf_op jit(solution)/shard_map/ppermute | solution.py:12
  98.4 0.0 copy-start.3
  98.4 2.1 %collective-permute-start.8 = (bf16[18,1,64,128]{3,0,2,1:T(8,128)(2,1)S(1)}, bf16[18,1,64,128]{3,0,2,1:T(8,128)(2,1)S(1)}, u32[]{:S(2)}, u32[]{:S(2)}) collective-permute-start(bf16[18,1,64,128]{3,0,2,1:T(8,128)(2,1)S(1)} %get-tuple-element.10), channel_id=1, source_target_pairs={{1,0},{2,1},{3,2},{4,3},{5,4},{6,5},{7,6},{8,7},{9,8},{10,9},{11,1... | collective-permute-start | bytes 884744 | tf_op jit(solution)/shard_map/ppermute | solution.py:15
  100.5 2.6 %collective-permute-done.7 = bf16[18,1,64,128]{3,0,2,1:T(8,128)(2,1)S(1)} collective-permute-done((bf16[18,1,64,128]{3,0,2,1:T(8,128)(2,1)S(1)}, bf16[18,1,64,128]{3,0,2,1:T(8,128)(2,1)S(1)}, u32[]{:S(2)}, u32[]{:S(2)}) %collective-permute-start.7) | collective-permute-done | bytes 294944 | tf_op jit(solution)/shard_map/ppermute | solution.py:12
  103.1 8.2 %collective-permute-done.8 = bf16[18,1,64,128]{3,0,2,1:T(8,128)(2,1)S(1)} collective-permute-done((bf16[18,1,64,128]{3,0,2,1:T(8,128)(2,1)S(1)}, bf16[18,1,64,128]{3,0,2,1:T(8,128)(2,1)S(1)}, u32[]{:S(2)}, u32[]{:S(2)}) %collective-permute-start.8) | collective-permute-done | bytes 294944 | tf_op jit(solution)/shard_map/ppermute | solution.py:15
  111.3 0.0 copy-done
  111.3 8.6 %maximum_convert_fusion.1 = bf16[18,4,64,288]{3,0,2,1:T(8,128)(2,1)S(1)} fusion(bf16[3,3,288,128]{3,2,1,0:T(8,128)(2,1)S(1)} %copy-done, bf16[18,1,64,128]{3,0,2,1:T(8,128)(2,1)S(1)} %collective-permute-done.8, bf16[1,4,64,128]{3,0,2,1:T(2,128)(2,1)S(1)} %collective-permute-done.6, bf16[16,4,64,128]{3,0,2,1:T(8,128)(2,1)S(1)} %maximum_convert_fusion.3, ...), kind=kOutput, calls=%fused_computation.3 | convolution fusion | flops 3037298688 | bytes 5087232 | tf_op jit(solution)/shard_map/conv_general_dilated | solution.py:27
  119.9 0.0 copy-done.3
  119.9 2.2 %fusion.2 = f32[16,4,64,128]{3,2,1,0:T(8,128)S(1)} fusion(bf16[18,4,64,288]{3,0,2,1:T(8,128)(2,1)S(1)} %maximum_convert_fusion.1, bf16[3,128,288]{1,2,0:T(8,128)(2,1)S(1)} %copy-done.3), kind=kOutput, calls=%fused_computation.5 | convolution fusion | flops 905969664 | bytes 4972544 | tf_op jit(solution)/shard_map/conv_general_dilated | solution.py:38
  122.1 1.4 %fusion.14 = bf16[16,4,64,128]{3,0,2,1:T(8,128)(2,1)S(1)} fusion(f32[16,4,64,128]{3,2,1,0:T(8,128)S(1)} %fusion.2, bf16[16,4,64,128]{3,0,2,1:T(8,128)(2,1)S(1)} %maximum_convert_fusion.3), kind=kLoop, calls=%fused_computation.20 | loop fusion | flops 2097152 | bytes 4194304 | tf_op jit(solution)/shard_map/convert_element_type | solution.py:52
  123.5 1.2 copy.24
  (4 shorter events, 0.1 us)
Async XLA Ops:
  0.0 111.3 %copy-start = (bf16[3,3,288,128]{3,2,1,0:T(8,128)(2,1)S(1)}, bf16[3,3,288,128]{3,2,1,0:T(8,128)(2,1)}, u32[]{:S(2)}) copy-start(bf16[3,3,288,128]{3,2,1,0:T(8,128)(2,1)} %param.10) | copy-start | bytes 1990660
  1.1 6.3 %collective-permute-start = (bf16[1,8,64,128]{3,2,1,0:T(8,128)(2,1)S(1)}, bf16[1,8,64,128]{3,2,1,0:T(8,128)(2,1)S(1)}, u32[]{:S(2)}, u32[]{:S(2)}) collective-permute-start(bf16[1,8,64,128]{3,2,1,0:T(8,128)(2,1)S(1)} %get-tuple-element.8), channel_id=1, source_target_pairs={{0,16},{16,32},{32,48},{48,64},{64,80},{80,96},{96,112},{1,17},{17... | collective-permute-start | bytes 393224 | tf_op jit(solution)/shard_map/ppermute | solution.py:12
  4.5 7.8 %collective-permute-start.1 = (bf16[1,8,64,128]{3,2,1,0:T(8,128)(2,1)S(1)}, bf16[1,8,64,128]{3,2,1,0:T(8,128)(2,1)S(1)}, u32[]{:S(2)}, u32[]{:S(2)}) collective-permute-start(bf16[1,8,64,128]{3,2,1,0:T(8,128)(2,1)S(1)} %get-tuple-element.7), channel_id=1, source_target_pairs={{16,0},{32,16},{48,32},{64,48},{80,64},{96,80},{112,96},{17,1},{33... | collective-permute-start | bytes 393224 | tf_op jit(solution)/shard_map/ppermute | solution.py:15
  12.4 10.5 %collective-permute-start.2 = (bf16[18,1,64,128]{3,2,1,0:T(8,128)(2,1)S(1)}, bf16[18,1,64,128]{3,2,1,0:T(8,128)(2,1)S(1)}, u32[]{:S(2)}, u32[]{:S(2)}) collective-permute-start(bf16[18,1,64,128]{3,2,1,0:T(8,128)(2,1)S(1)} %get-tuple-element.5), channel_id=1, source_target_pairs={{0,1},{1,2},{2,3},{3,4},{4,5},{5,6},{6,7},{7,8},{8,9},{9,10},{10,1... | collective-permute-start | bytes 884744 | tf_op jit(solution)/shard_map/ppermute | solution.py:12
  19.3 11.7 %collective-permute-start.3 = (bf16[18,1,64,128]{3,2,1,0:T(8,128)(2,1)S(1)}, bf16[18,1,64,128]{3,2,1,0:T(8,128)(2,1)S(1)}, u32[]{:S(2)}, u32[]{:S(2)}) collective-permute-start(bf16[18,1,64,128]{3,2,1,0:T(8,128)(2,1)S(1)} %get-tuple-element.6), channel_id=1, source_target_pairs={{1,0},{2,1},{3,2},{4,3},{5,4},{6,5},{7,6},{8,7},{9,8},{10,9},{11,1... | collective-permute-start | bytes 884744 | tf_op jit(solution)/shard_map/ppermute | solution.py:15
  33.0 9.1 %copy-start.2 = (bf16[3,3,144,64]{2,3,1,0:T(8,128)(2,1)S(1)}, bf16[3,3,144,64]{2,3,1,0:T(8,128)(2,1)}, u32[]{:S(2)}) copy-start(bf16[3,3,144,64]{2,3,1,0:T(8,128)(2,1)} %param.7) | copy-start | bytes 497668
  42.1 13.9 %copy-start.1 = (bf16[16,8,64,128]{3,2,1,0:T(8,128)(2,1)S(1)}, bf16[16,8,64,128]{3,2,1,0:T(8,128)(2,1)}, u32[]{:S(2)}) copy-start(bf16[16,8,64,128]{3,2,1,0:T(8,128)(2,1)} %param.6) | copy-start | bytes 6291460
  42.1 13.9 %copy-start.5 = (bf16[3,64,144]{2,1,0:T(8,128)(2,1)S(1)}, bf16[3,64,144]{2,1,0:T(8,128)(2,1)}, u32[]{:S(2)}) copy-start(bf16[3,64,144]{2,1,0:T(8,128)(2,1)} %param.8) | copy-start | bytes 165892
  63.9 5.2 %collective-permute-start.4 = (bf16[16,1,64,128]{3,2,1,0:T(8,128)(2,1)S(1)}, bf16[16,1,64,128]{3,2,1,0:T(8,128)(2,1)S(1)}, u32[]{:S(2)}, u32[]{:S(2)}) collective-permute-start(bf16[16,1,64,128]{3,2,1,0:T(8,128)(2,1)S(1)} %slice.38), channel_id=1, source_target_pairs={{0,1},{1,2},{2,3},{3,4},{4,5},{5,6},{6,7},{7,8},{8,9},{9,10},{10,1... | collective-permute-start | bytes 786440 | tf_op jit(solution)/shard_map/ppermute | solution.py:23
  69.3 5.3 %copy-start.4 = (bf16[3,3,128,64]{2,3,1,0:T(8,128)(2,1)S(1)}, bf16[3,3,128,64]{2,3,1,0:T(8,128)(2,1)}, u32[]{:S(2)}) copy-start(bf16[3,3,128,64]{2,3,1,0:T(8,128)(2,1)} %param.9) | copy-start | bytes 442372
  78.8 5.9 %collective-permute-start.5 = (bf16[1,4,64,128]{3,0,2,1:T(2,128)(2,1)S(1)}, bf16[1,4,64,128]{3,0,2,1:T(2,128)(2,1)S(1)}, u32[]{:S(2)}, u32[]{:S(2)}) collective-permute-start(bf16[1,4,64,128]{3,0,2,1:T(2,128)(2,1)S(1)} %get-tuple-element.11), channel_id=1, source_target_pairs={{0,16},{16,32},{32,48},{48,64},{64,80},{80,96},{96,112},{1,17},{17... | collective-permute-start | bytes 196616 | tf_op jit(solution)/shard_map/ppermute | solution.py:12
  80.7 8.0 %collective-permute-start.6 = (bf16[1,4,64,128]{3,0,2,1:T(2,128)(2,1)S(1)}, bf16[1,4,64,128]{3,0,2,1:T(2,128)(2,1)S(1)}, u32[]{:S(2)}, u32[]{:S(2)}) collective-permute-start(bf16[1,4,64,128]{3,0,2,1:T(2,128)(2,1)S(1)} %get-tuple-element.12), channel_id=1, source_target_pairs={{16,0},{32,16},{48,32},{64,48},{80,64},{96,80},{112,96},{17,1},{33... | collective-permute-start | bytes 196616 | tf_op jit(solution)/shard_map/ppermute | solution.py:15
  89.2 14.0 %collective-permute-start.7 = (bf16[18,1,64,128]{3,0,2,1:T(8,128)(2,1)S(1)}, bf16[18,1,64,128]{3,0,2,1:T(8,128)(2,1)S(1)}, u32[]{:S(2)}, u32[]{:S(2)}) collective-permute-start(bf16[18,1,64,128]{3,0,2,1:T(8,128)(2,1)S(1)} %get-tuple-element.9), channel_id=1, source_target_pairs={{0,1},{1,2},{2,3},{3,4},{4,5},{5,6},{6,7},{7,8},{8,9},{9,10},{10,1... | collective-permute-start | bytes 884744 | tf_op jit(solution)/shard_map/ppermute | solution.py:12
  98.4 21.5 %copy-start.3 = (bf16[3,128,288]{1,2,0:T(8,128)(2,1)S(1)}, bf16[3,128,288]{1,2,0:T(8,128)(2,1)}, u32[]{:S(2)}) copy-start(bf16[3,128,288]{1,2,0:T(8,128)(2,1)} %param.11) | copy-start | bytes 663556
  98.4 12.8 %collective-permute-start.8 = (bf16[18,1,64,128]{3,0,2,1:T(8,128)(2,1)S(1)}, bf16[18,1,64,128]{3,0,2,1:T(8,128)(2,1)S(1)}, u32[]{:S(2)}, u32[]{:S(2)}) collective-permute-start(bf16[18,1,64,128]{3,0,2,1:T(8,128)(2,1)S(1)} %get-tuple-element.10), channel_id=1, source_target_pairs={{1,0},{2,1},{3,2},{4,3},{5,4},{6,5},{7,6},{8,7},{9,8},{10,9},{11,1... | collective-permute-start | bytes 884744 | tf_op jit(solution)/shard_map/ppermute | solution.py:15
where the time goes:
time: 125 us
  matrix products  36.5 us (29%)
  starting transfers between devices  32.9 us (26%)
  waiting for transfers between devices  32.2 us (26%)
  local copies, waits for them, and re-layouts  18.9 us (15%)
  other arithmetic  4.13 us (3%)
    ppermute x4, waiting for transfers between devices, padded_2(): lax.ppermute(lax.slice_in_dim(block, 0, width, axis=dim), axis, backward)  23.2 us
    conv_general_dilated x2, matrix products, spatial(): lax.conv_general_dilated(source, kernel, (1, 1), ((0, 0), (1, 1)), dimens...  22.5 us
    ppermute x4, starting transfers between devices, padded_2(): lax.ppermute(lax.slice_in_dim(block, block.shape[dim] - width, None, axis...  21.5 us
    conv_general_dilated x2, matrix products, temporal(): lax.conv_general_dilated(source, kernel[:, None], (1, 1), ((0, 0), (0, 0)...  10 us
    ppermute x4, starting transfers between devices, padded_2(): lax.ppermute(lax.slice_in_dim(block, 0, width, axis=dim), axis, backward)  9.26 us
    concatenate x2, local copies, waits for them, and re-layouts, padded_2(): block = jnp.concatenate([low, block, high], axis=dim)  9.1 us
    ppermute x4, waiting for transfers between devices, padded_2(): lax.ppermute(lax.slice_in_dim(block, block.shape[dim] - width, None, axis...  5.85 us
    concatenate x1, local copies, waits for them, and re-layouts, on_device(): joined = jnp.concatenate([upper_row, section_one], axis=1)  5.25 us
  transfers between devices with their start and end apart: 9, of which 9 were waited for; matrix products, arithmetic and copies ran while one was open for 2% of the time, Pallas kernels for 0%

commit v1 on v0

v1 whole, which is shorter than its diff:
```python
import jax
import jax.numpy as jnp
from jax import lax
from jax.sharding import PartitionSpec as P


def from_offset(block, dt, dr):
    nt, nr = lax.axis_size("tm"), lax.axis_size("row")
    pairs = []
    for t in range(nt):
        for r in range(nr):
            if 0 <= t + dt < nt and 0 <= r + dr < nr:
                pairs.append(((t + dt) * nr + r + dr, t * nr + r))
    return lax.ppermute(block, ("tm", "row"), pairs)


def with_halo(block, top, bottom):
    frames, rows = block.shape[0], block.shape[1]
    frame_part = {-1: slice(frames - 1, frames), 0: slice(None), 1: slice(0, 1)}
    row_part = {-1: slice(rows - top, rows), 0: slice(None), 1: slice(0, bottom)}
    slabs = []
    for dt in (-1, 0, 1):
        pieces = []
        for dr in (-1, 0, 1):
            if dt == 0 and dr == 0:
                pieces.append(block)
            else:
                pieces.append(from_offset(block[frame_part[dt]][:, row_part[dr]], dt, dr))
        slabs.append(jnp.concatenate(pieces, axis=1))
    return jnp.concatenate(slabs, axis=0)


def spatial(source, kernel, layout):
    return lax.conv_general_dilated(
        source,
        kernel,
        (1, 1),
        ((0, 0), (1, 1)),
        dimension_numbers=(layout, "HWOI", layout),
        preferred_element_type=jnp.float32,
    )


def temporal(source, kernel, layout):
    return lax.conv_general_dilated(
        source,
        kernel[:, None],
        (1, 1),
        ((0, 0), (0, 0)),
        dimension_numbers=(layout, "HWOI", layout),
        preferred_element_type=jnp.float32,
    )


def residual_block(padded, top, spatial_kernel, temporal_kernel, space_layout, time_layout):
    framed = jax.nn.relu(spatial(padded, spatial_kernel, space_layout)).astype(jnp.bfloat16)
    inner = padded[1:-1, 1:-1]
    summed = inner.astype(jnp.float32) + temporal(framed, temporal_kernel, time_layout)
    return jax.nn.relu(summed).astype(jnp.bfloat16)


def on_device(video_clip, spatial_one, temporal_one, down_weight, spatial_two, temporal_two):
    padded = with_halo(video_clip, 2, 1)
    section_one = residual_block(padded, 2, spatial_one, temporal_one, "NHCW", "HWCN")
    first_device = lax.axis_index("row") == 0
    keep = jnp.logical_or(jnp.arange(section_one.shape[1]) > 0, jnp.logical_not(first_device))
    section_one = jnp.where(keep[None, :, None, None], section_one, jnp.zeros_like(section_one))
    reduced = lax.conv_general_dilated(
        section_one,
        down_weight,
        (2, 2),
        ((0, 0), (1, 1)),
        dimension_numbers=("NHCW", "HWOI", "NHWC"),
        preferred_element_type=jnp.float32,
    )
    reduced = jax.nn.relu(reduced).astype(jnp.bfloat16)
    padded_two = with_halo(reduced, 1, 1)
    return residual_block(padded_two, 1, spatial_two, temporal_two, "NHWC", "HWNC")


def solution(mesh):
    placed = (P("tm", "row", None, None), P(), P(), P(), P(), P())
    return jax.shard_map(
        on_device, mesh=mesh, in_specs=placed, out_specs=P("tm", "row", None, None), check_vma=False
    )
```

time: 125 us -> 151 us (1.21)
  the two profiles are of different devices: /device:TPU:31 before, /device:TPU:70 now
where the time goes in v1:
time: 151 us; the launch traced here: 150 us
  starting transfers between devices  51.2 us (34%)
  matrix products  40.8 us (27%)
  waiting for transfers between devices  28.5 us (19%)
  local copies, waits for them, and re-layouts  25.1 us (17%)
  other arithmetic  4.25 us (3%)
    ppermute x16, starting transfers between devices, from_offset(): return lax.ppermute(block, ('tm', 'row'), pairs)  51.2 us
    ppermute x16, waiting for transfers between devices, from_offset(): return lax.ppermute(block, ('tm', 'row'), pairs)  28.5 us
    conv_general_dilated x2, matrix products, spatial(): lax.conv_general_dilated(source, kernel, (1, 1), ((0, 0), (1, 1)), dimens...  23.9 us
    conv_general_dilated x2, matrix products, temporal(): lax.conv_general_dilated(source, kernel[:, None], (1, 1), ((0, 0), (0, 0)...  12.9 us
    concatenate x1, local copies, waits for them, and re-layouts, with_halo(): return jnp.concatenate(slabs, axis=0)  9.31 us
    slice x8, local copies, waits for them, and re-layouts, with_halo(): pieces.append(from_offset(block[frame_part[dt]][:, row_part[dr]], dt, dr))  7.91 us
    select_n x1, local copies, waits for them, and re-layouts, on_device(): jnp.where(keep[None, :, None, None], section_one, jnp.zeros_like(section_...  6.64 us
    conv_general_dilated x1, matrix products, on_device(): lax.conv_general_dilated(section_one, down_weight, (2, 2), ((0, 0), (1, 1...  3.95 us
  transfers between devices with their start and end apart: 16, of which 4 were waited for; matrix products, arithmetic and copies ran while one was open for 4% of the time, Pallas kernels for 0%

profile of v1, /device:TPU:70, one launch (start us, length us, event | category | flops | bytes accessed | tf_op | source)
XLA Modules:
  0.0 150.2 jit_solution(18187845159669862827)
XLA Ops:
  0.0 0.0 copy-start
  0.0 0.0 copy-start.1
  0.0 2.0 %slice.68 = bf16[16,2,64,128]{3,2,1,0:T(8,128)(2,1)} slice(bf16[16,8,64,128]{3,2,1,0:T(8,128)(2,1)} %param.6), slice={[0:16], [6:8], [0:64], [0:128]} | slice | bytes 1048576 | tf_op jit(solution)/shard_map/slice | solution.py:28
  2.0 1.9 %collective-permute-start = (bf16[16,2,64,128]{3,2,1,0:T(8,128)(2,1)}, bf16[16,2,64,128]{3,2,1,0:T(8,128)(2,1)S(1)}, u32[]{:S(2)}, u32[]{:S(2)}) collective-permute-start(bf16[16,2,64,128]{3,2,1,0:T(8,128)(2,1)} %slice.68), channel_id=1, source_target_pairs={{0,1},{1,2},{2,3},{3,4},{4,5},{5,6},{6,7},{7,8},{8,9},{9,10},{10,1... | collective-permute-start | bytes 1572872 | tf_op jit(solution)/shard_map/ppermute | solution.py:14
  4.0 1.4 fusion.31
  5.4 4.7 %collective-permute-start.1 = (bf16[1,2,64,128]{3,2,1,0:T(8,128)(2,1)}, bf16[1,2,64,128]{3,2,1,0:T(8,128)(2,1)}, u32[]{:S(2)}, u32[]{:S(2)}) collective-permute-start(bf16[1,2,64,128]{3,2,1,0:T(8,128)(2,1)} %get-tuple-element.5), channel_id=1, source_target_pairs={{0,17},{1,18},{2,19},{3,20},{4,21},{5,22},{6,23},{7,24},{8,25},{9,... | collective-permute-start | bytes 98312 | tf_op jit(solution)/shard_map/ppermute | solution.py:14
  10.1 0.7 fusion.33
  10.8 4.8 %collective-permute-start.3 = (bf16[1,1,64,128]{3,2,1,0:T(8,128)(2,1)S(1)}, bf16[1,1,64,128]{3,2,1,0:T(8,128)(2,1)}, u32[]{:S(2)}, u32[]{:S(2)}) collective-permute-start(bf16[1,1,64,128]{3,2,1,0:T(8,128)(2,1)S(1)} %get-tuple-element.9), channel_id=1, source_target_pairs={{1,16},{2,17},{3,18},{4,19},{5,20},{6,21},{7,22},{8,23},{9,24},{10... | collective-permute-start | bytes 49160 | tf_op jit(solution)/shard_map/ppermute | solution.py:14
  15.7 3.6 %collective-permute-start.7 = (bf16[1,1,64,128]{3,2,1,0:T(8,128)(2,1)S(1)}, bf16[1,1,64,128]{3,2,1,0:T(8,128)(2,1)}, u32[]{:S(2)}, u32[]{:S(2)}) collective-permute-start(bf16[1,1,64,128]{3,2,1,0:T(8,128)(2,1)S(1)} %get-tuple-element.10), channel_id=1, source_target_pairs={{17,0},{18,1},{19,2},{20,3},{21,4},{22,5},{23,6},{24,7},{25,8},{26... | collective-permute-start | bytes 49160 | tf_op jit(solution)/shard_map/ppermute | solution.py:14
  19.3 1.7 %slice.73 = bf16[16,1,64,128]{3,2,1,0:T(8,128)(2,1)} slice(bf16[16,8,64,128]{3,2,1,0:T(8,128)(2,1)} %param.6), slice={[0:16], [0:1], [0:64], [0:128]} | slice | bytes 524288 | tf_op jit(solution)/shard_map/slice | solution.py:28
  21.0 1.9 %collective-permute-start.4 = (bf16[16,1,64,128]{3,2,1,0:T(8,128)(2,1)}, bf16[16,1,64,128]{3,2,1,0:T(8,128)(2,1)S(1)}, u32[]{:S(2)}, u32[]{:S(2)}) collective-permute-start(bf16[16,1,64,128]{3,2,1,0:T(8,128)(2,1)} %slice.73), channel_id=1, source_target_pairs={{1,0},{2,1},{3,2},{4,3},{5,4},{6,5},{7,6},{8,7},{9,8},{10,9},{11,1... | collective-permute-start | bytes 786440 | tf_op jit(solution)/shard_map/ppermute | solution.py:14
  22.9 1.7 %fusion.32 = (bf16[1,8,64,128]{3,2,1,0:T(8,128)(2,1)}, bf16[1,8,64,128]{3,2,1,0:T(8,128)(2,1)}) fusion(bf16[16,8,64,128]{3,2,1,0:T(8,128)(2,1)} %param.6), kind=kLoop, calls=%fused_computation.36 | loop fusion | bytes 524288 | tf_op jit(solution)/shard_map/slice | solution.py:28
  24.6 0.0 collective-permute-done.3
  24.6 5.2 %collective-permute-start.2 = (bf16[1,8,64,128]{3,2,1,0:T(8,128)(2,1)}, bf16[1,8,64,128]{3,2,1,0:T(8,128)(2,1)}, u32[]{:S(2)}, u32[]{:S(2)}) collective-permute-start(bf16[1,8,64,128]{3,2,1,0:T(8,128)(2,1)} %get-tuple-element.7), channel_id=1, source_target_pairs={{0,16},{1,17},{2,18},{3,19},{4,20},{5,21},{6,22},{7,23},{8,24},{9,... | collective-permute-start | bytes 393224 | tf_op jit(solution)/shard_map/ppermute | solution.py:14
  29.8 0.0 collective-permute-done.7
  29.8 1.9 %collective-permute-start.6 = (bf16[1,8,64,128]{3,2,1,0:T(8,128)(2,1)}, bf16[1,8,64,128]{3,2,1,0:T(8,128)(2,1)}, u32[]{:S(2)}, u32[]{:S(2)}) collective-permute-start(bf16[1,8,64,128]{3,2,1,0:T(8,128)(2,1)} %get-tuple-element.8), channel_id=1, source_target_pairs={{16,0},{17,1},{18,2},{19,3},{20,4},{21,5},{22,6},{23,7},{24,8},{25... | collective-permute-start | bytes 393224 | tf_op jit(solution)/shard_map/ppermute | solution.py:14
  31.7 0.0 collective-permute-done.1
  31.8 1.9 %collective-permute-start.5 = (bf16[1,2,64,128]{3,2,1,0:T(8,128)(2,1)}, bf16[1,2,64,128]{3,2,1,0:T(8,128)(2,1)S(1)}, u32[]{:S(2)}, u32[]{:S(2)}) collective-permute-start(bf16[1,2,64,128]{3,2,1,0:T(8,128)(2,1)} %get-tuple-element.6), channel_id=1, source_target_pairs={{16,1},{17,2},{18,3},{19,4},{20,5},{21,6},{22,7},{23,8},{24,9},{25... | collective-permute-start | bytes 98312 | tf_op jit(solution)/shard_map/ppermute | solution.py:14
  33.7 7.7 %collective-permute-done.5 = bf16[1,2,64,128]{3,2,1,0:T(8,128)(2,1)S(1)} collective-permute-done((bf16[1,2,64,128]{3,2,1,0:T(8,128)(2,1)}, bf16[1,2,64,128]{3,2,1,0:T(8,128)(2,1)S(1)}, u32[]{:S(2)}, u32[]{:S(2)}) %collective-permute-start.5) | collective-permute-done | bytes 32800 | tf_op jit(solution)/shard_map/ppermute | solution.py:14
  41.4 0.0 collective-permute-done.2
  41.4 0.0 collective-permute-done.6
  41.4 0.0 collective-permute-done.4
  41.4 0.0 collective-permute-done
  41.4 0.0 copy-done.1
  41.4 2.8 %maximum_maximum_fusion = bf16[18,11,64,128]{3,2,1,0:T(8,128)(2,1)} fusion(bf16[1,1,64,128]{3,2,1,0:T(8,128)(2,1)} %collective-permute-done.7, bf16[1,8,64,128]{3,2,1,0:T(8,128)(2,1)} %collective-permute-done.6, bf16[1,2,64,128]{3,2,1,0:T(8,128)(2,1)S(1)} %collective-permute-done.5, bf16[16,1,64,128]{3,2,1,0:T(8,128)(2,1)S(1)} %collective-permute-done.4, ...), kind=kLoop, calls=%fused_computation.7 | loop fusion | flops 12976128 | bytes 6488064 | tf_op jit(solution)/shard_map/concatenate | solution.py:30
  44.3 9.3 %copy.24 = bf16[18,11,64,128]{2,0,3,1:T(8,128)(2,1)} copy(bf16[18,11,64,128]{3,2,1,0:T(8,128)(2,1)} %maximum_maximum_fusion) | data formatting | bytes 6488064 | tf_op jit(solution)/shard_map/concatenate | solution.py:30
  53.6 0.0 copy-start.4
  53.6 15.3 %maximum_convert_fusion = bf16[18,9,144,128]{2,0,3,1:T(8,128)(2,1)S(1)} fusion(bf16[18,11,64,128]{2,0,3,1:T(8,128)(2,1)} %copy.24, bf16[3,3,144,64]{2,3,1,0:T(8,128)(2,1)} %param.7), kind=kOutput, calls=%fused_computation | convolution fusion | flops 3427909632 | bytes 9381888 | tf_op jit(solution)/shard_map/conv_general_dilated | solution.py:34
  68.9 0.0 copy-done.4
  68.9 10.7 %fusion.4 = bf16[16,9,64,128]{3,2,1,0:T(8,128)(2,1)} fusion(bf16[16,8,64,128]{3,2,1,0:T(8,128)(2,1)S(1)} %copy-done.1, bf16[16,2,64,128]{3,2,1,0:T(8,128)(2,1)S(1)} %collective-permute-done, pred[9]{0:T(512)(128)(4,1)S(1)} %compare_or_fusion, bf16[3,64,144]{2,1,0:T(8,128)(2,1)S(1)} %copy-done.4, bf16[18,9,144,128]{2,0,3,1:T(8,128)(2,1)S(1)} %maximum_convert_fusion), kind=kOutput, calls=%fused_computation.8 | convolution fusion | flops 1026293760 | bytes 11008009 | tf_op jit(solution)/shard_map/conv_general_dilated | solution.py:45
  79.7 0.0 copy-start.3
  79.7 6.6 %copy.27 = bf16[16,9,64,128]{2,0,3,1:T(8,128)(2,1)} copy(bf16[16,9,64,128]{3,2,1,0:T(8,128)(2,1)} %fusion.4) | data formatting | bytes 4718592 | tf_op jit(solution)/shard_map/jit(_where)/select_n | solution.py:67
  86.3 0.0 copy-done.3
  86.3 3.9 %maximum_convert_fusion.3 = bf16[16,4,64,128]{3,0,2,1:T(8,128)(2,1)S(1)} fusion(bf16[16,9,64,128]{2,0,3,1:T(8,128)(2,1)} %copy.27, bf16[3,3,128,64]{2,3,1,0:T(8,128)(2,1)S(1)} %copy-done.3), kind=kOutput, calls=%fused_computation.30 | convolution fusion | flops 601882624 | bytes 3555328 | tf_op jit(solution)/shard_map/conv_general_dilated | solution.py:68
  90.2 0.1 fusion.34
  90.4 1.9 %collective-permute-start.10 = (bf16[1,1,64,128]{3,0,2,1:T(2,128)(2,1)S(1)}, bf16[1,1,64,128]{3,0,2,1:T(2,128)(2,1)S(1)}, u32[]{:S(2)}, u32[]{:S(2)}) collective-permute-start(bf16[1,1,64,128]{3,0,2,1:T(2,128)(2,1)S(1)} %get-tuple-element.14), channel_id=1, source_target_pairs={{1,16},{2,17},{3,18},{4,19},{5,20},{6,21},{7,22},{8,23},{9,24},{10... | collective-permute-start | bytes 49160 | tf_op jit(solution)/shard_map/ppermute | solution.py:14
  92.3 6.4 %collective-permute-start.11 = (bf16[16,1,64,128]{3,0,2,1:T(8,128)(2,1)S(1)}, bf16[16,1,64,128]{3,0,2,1:T(8,128)(2,1)S(1)}, u32[]{:S(2)}, u32[]{:S(2)}) collective-permute-start(bf16[16,1,64,128]{3,0,2,1:T(8,128)(2,1)S(1)} %get-tuple-element.17), channel_id=1, source_target_pairs={{0,1},{1,2},{2,3},{3,4},{4,5},{5,6},{6,7},{7,8},{8,9},{9,10},{10,1... | collective-permute-start | bytes 786440 | tf_op jit(solution)/shard_map/ppermute | solution.py:14
  98.8 2.7 %collective-permute-start.12 = (bf16[16,1,64,128]{3,0,2,1:T(8,128)(2,1)S(1)}, bf16[16,1,64,128]{3,0,2,1:T(8,128)(2,1)S(1)}, u32[]{:S(2)}, u32[]{:S(2)}) collective-permute-start(bf16[16,1,64,128]{3,0,2,1:T(8,128)(2,1)S(1)} %get-tuple-element.18), channel_id=1, source_target_pairs={{1,0},{2,1},{3,2},{4,3},{5,4},{6,5},{7,6},{8,7},{9,8},{10,9},{11,1... | collective-permute-start | bytes 786440 | tf_op jit(solution)/shard_map/ppermute | solution.py:14
  101.5 0.2 fusion.35
  101.8 2.0 %collective-permute-start.14 = (bf16[1,4,64,128]{3,0,2,1:T(2,128)(2,1)S(1)}, bf16[1,4,64,128]{3,0,2,1:T(2,128)(2,1)S(1)}, u32[]{:S(2)}, u32[]{:S(2)}) collective-permute-start(bf16[1,4,64,128]{3,0,2,1:T(2,128)(2,1)S(1)} %get-tuple-element.16), channel_id=1, source_target_pairs={{16,0},{17,1},{18,2},{19,3},{20,4},{21,5},{22,6},{23,7},{24,8},{25... | collective-permute-start | bytes 196616 | tf_op jit(solution)/shard_map/ppermute | solution.py:14
  103.8 6.2 %collective-permute-start.9 = (bf16[1,4,64,128]{3,0,2,1:T(2,128)(2,1)S(1)}, bf16[1,4,64,128]{3,0,2,1:T(2,128)(2,1)S(1)}, u32[]{:S(2)}, u32[]{:S(2)}) collective-permute-start(bf16[1,4,64,128]{3,0,2,1:T(2,128)(2,1)S(1)} %get-tuple-element.15), channel_id=1, source_target_pairs={{0,16},{1,17},{2,18},{3,19},{4,20},{5,21},{6,22},{7,23},{8,24},{9,... | collective-permute-start | bytes 196616 | tf_op jit(solution)/shard_map/ppermute | solution.py:14
  110.0 0.0 collective-permute-done.10
  110.0 1.9 %collective-permute-start.13 = (bf16[1,1,64,128]{3,0,2,1:T(2,128)(2,1)S(1)}, bf16[1,1,64,128]{3,0,2,1:T(2,128)(2,1)S(1)}, u32[]{:S(2)}, u32[]{:S(2)}) collective-permute-start(bf16[1,1,64,128]{3,0,2,1:T(2,128)(2,1)S(1)} %get-tuple-element.13), channel_id=1, source_target_pairs={{16,1},{17,2},{18,3},{19,4},{20,5},{21,6},{22,7},{23,8},{24,9},{25... | collective-permute-start | bytes 49160 | tf_op jit(solution)/shard_map/ppermute | solution.py:14
  112.0 7.5 %collective-permute-done.13 = bf16[1,1,64,128]{3,0,2,1:T(2,128)(2,1)S(1)} collective-permute-done((bf16[1,1,64,128]{3,0,2,1:T(2,128)(2,1)S(1)}, bf16[1,1,64,128]{3,0,2,1:T(2,128)(2,1)S(1)}, u32[]{:S(2)}, u32[]{:S(2)}) %collective-permute-start.13) | collective-permute-done | bytes 16416 | tf_op jit(solution)/shard_map/ppermute | solution.py:14
  119.5 1.9 %collective-permute-start.15 = (bf16[1,1,64,128]{3,0,2,1:T(2,128)(2,1)S(1)}, bf16[1,1,64,128]{3,0,2,1:T(2,128)(2,1)S(1)}, u32[]{:S(2)}, u32[]{:S(2)}) collective-permute-start(bf16[1,1,64,128]{3,0,2,1:T(2,128)(2,1)S(1)} %get-tuple-element.12), channel_id=1, source_target_pairs={{17,0},{18,1},{19,2},{20,3},{21,4},{22,5},{23,6},{24,7},{25,8},{26... | collective-permute-start | bytes 49160 | tf_op jit(solution)/shard_map/ppermute | solution.py:14
  121.4 5.4 %collective-permute-done.15 = bf16[1,1,64,128]{3,0,2,1:T(2,128)(2,1)S(1)} collective-permute-done((bf16[1,1,64,128]{3,0,2,1:T(2,128)(2,1)S(1)}, bf16[1,1,64,128]{3,0,2,1:T(2,128)(2,1)S(1)}, u32[]{:S(2)}, u32[]{:S(2)}) %collective-permute-start.15) | collective-permute-done | bytes 16416 | tf_op jit(solution)/shard_map/ppermute | solution.py:14
  126.8 0.0 copy-start.2
  126.8 2.0 %collective-permute-start.8 = (bf16[1,1,64,128]{3,0,2,1:T(2,128)(2,1)S(1)}, bf16[1,1,64,128]{3,0,2,1:T(2,128)(2,1)S(1)}, u32[]{:S(2)}, u32[]{:S(2)}) collective-permute-start(bf16[1,1,64,128]{3,0,2,1:T(2,128)(2,1)S(1)} %get-tuple-element.11), channel_id=1, source_target_pairs={{0,17},{1,18},{2,19},{3,20},{4,21},{5,22},{6,23},{7,24},{8,25},{9,... | collective-permute-start | bytes 49160 | tf_op jit(solution)/shard_map/ppermute | solution.py:14
  128.9 7.8 %collective-permute-done.8 = bf16[1,1,64,128]{3,0,2,1:T(2,128)(2,1)S(1)} collective-permute-done((bf16[1,1,64,128]{3,0,2,1:T(2,128)(2,1)S(1)}, bf16[1,1,64,128]{3,0,2,1:T(2,128)(2,1)S(1)}, u32[]{:S(2)}, u32[]{:S(2)}) %collective-permute-start.8) | collective-permute-done | bytes 16416 | tf_op jit(solution)/shard_map/ppermute | solution.py:14
  136.7 0.0 collective-permute-done.14
  136.7 0.0 collective-permute-done.9
  136.7 0.0 collective-permute-done.11
  136.7 0.0 collective-permute-done.12
  136.7 0.0 copy-done
  136.7 8.6 %maximum_convert_fusion.1 = bf16[18,4,64,288]{3,0,2,1:T(8,128)(2,1)S(1)} fusion(bf16[3,3,288,128]{3,2,1,0:T(8,128)(2,1)S(1)} %copy-done, bf16[1,1,64,128]{3,0,2,1:T(2,128)(2,1)S(1)} %collective-permute-done.15, bf16[1,4,64,128]{3,0,2,1:T(2,128)(2,1)S(1)} %collective-permute-done.14, bf16[1,1,64,128]{3,0,2,1:T(2,128)(2,1)S(1)} %collective-permute-done.13, ...), kind=kOutput, calls=%fused_computation.3 | convolution fusion | flops 3044376576 | bytes 5087232 | tf_op jit(solution)/shard_map/conv_general_dilated | solution.py:34
  145.4 0.0 copy-done.2
  145.4 2.2 %fusion.2 = f32[16,4,64,128]{3,2,1,0:T(8,128)S(1)} fusion(bf16[18,4,64,288]{3,0,2,1:T(8,128)(2,1)S(1)} %maximum_convert_fusion.1, bf16[3,128,288]{1,2,0:T(8,128)(2,1)S(1)} %copy-done.2), kind=kOutput, calls=%fused_computation.5 | convolution fusion | flops 905969664 | bytes 4972544 | tf_op jit(solution)/shard_map/conv_general_dilated | solution.py:45
  147.6 1.4 fusion.23
  149.0 1.2 copy.31
  (2 shorter events, 0.0 us)
Async XLA Ops:
  0.0 136.7 %copy-start = (bf16[3,3,288,128]{3,2,1,0:T(8,128)(2,1)S(1)}, bf16[3,3,288,128]{3,2,1,0:T(8,128)(2,1)}, u32[]{:S(2)}) copy-start(bf16[3,3,288,128]{3,2,1,0:T(8,128)(2,1)} %param.10) | copy-start | bytes 1990660
  0.0 41.4 %copy-start.1 = (bf16[16,8,64,128]{3,2,1,0:T(8,128)(2,1)S(1)}, bf16[16,8,64,128]{3,2,1,0:T(8,128)(2,1)}, u32[]{:S(2)}) copy-start(bf16[16,8,64,128]{3,2,1,0:T(8,128)(2,1)} %param.6) | copy-start | bytes 6291460
  2.0 39.4 %collective-permute-start = (bf16[16,2,64,128]{3,2,1,0:T(8,128)(2,1)}, bf16[16,2,64,128]{3,2,1,0:T(8,128)(2,1)S(1)}, u32[]{:S(2)}, u32[]{:S(2)}) collective-permute-start(bf16[16,2,64,128]{3,2,1,0:T(8,128)(2,1)} %slice.68), channel_id=1, source_target_pairs={{0,1},{1,2},{2,3},{3,4},{4,5},{5,6},{6,7},{7,8},{8,9},{9,10},{10,1... | collective-permute-start | bytes 1572872 | tf_op jit(solution)/shard_map/ppermute | solution.py:14
  5.4 26.4 %collective-permute-start.1 = (bf16[1,2,64,128]{3,2,1,0:T(8,128)(2,1)}, bf16[1,2,64,128]{3,2,1,0:T(8,128)(2,1)}, u32[]{:S(2)}, u32[]{:S(2)}) collective-permute-start(bf16[1,2,64,128]{3,2,1,0:T(8,128)(2,1)} %get-tuple-element.5), channel_id=1, source_target_pairs={{0,17},{1,18},{2,19},{3,20},{4,21},{5,22},{6,23},{7,24},{8,25},{9,... | collective-permute-start | bytes 98312 | tf_op jit(solution)/shard_map/ppermute | solution.py:14
  10.8 13.8 %collective-permute-start.3 = (bf16[1,1,64,128]{3,2,1,0:T(8,128)(2,1)S(1)}, bf16[1,1,64,128]{3,2,1,0:T(8,128)(2,1)}, u32[]{:S(2)}, u32[]{:S(2)}) collective-permute-start(bf16[1,1,64,128]{3,2,1,0:T(8,128)(2,1)S(1)} %get-tuple-element.9), channel_id=1, source_target_pairs={{1,16},{2,17},{3,18},{4,19},{5,20},{6,21},{7,22},{8,23},{9,24},{10... | collective-permute-start | bytes 49160 | tf_op jit(solution)/shard_map/ppermute | solution.py:14
  15.7 14.1 %collective-permute-start.7 = (bf16[1,1,64,128]{3,2,1,0:T(8,128)(2,1)S(1)}, bf16[1,1,64,128]{3,2,1,0:T(8,128)(2,1)}, u32[]{:S(2)}, u32[]{:S(2)}) collective-permute-start(bf16[1,1,64,128]{3,2,1,0:T(8,128)(2,1)S(1)} %get-tuple-element.10), channel_id=1, source_target_pairs={{17,0},{18,1},{19,2},{20,3},{21,4},{22,5},{23,6},{24,7},{25,8},{26... | collective-permute-start | bytes 49160 | tf_op jit(solution)/shard_map/ppermute | solution.py:14
  21.0 20.4 %collective-permute-start.4 = (bf16[16,1,64,128]{3,2,1,0:T(8,128)(2,1)}, bf16[16,1,64,128]{3,2,1,0:T(8,128)(2,1)S(1)}, u32[]{:S(2)}, u32[]{:S(2)}) collective-permute-start(bf16[16,1,64,128]{3,2,1,0:T(8,128)(2,1)} %slice.73), channel_id=1, source_target_pairs={{1,0},{2,1},{3,2},{4,3},{5,4},{6,5},{7,6},{8,7},{9,8},{10,9},{11,1... | collective-permute-start | bytes 786440 | tf_op jit(solution)/shard_map/ppermute | solution.py:14
  24.6 16.8 %collective-permute-start.2 = (bf16[1,8,64,128]{3,2,1,0:T(8,128)(2,1)}, bf16[1,8,64,128]{3,2,1,0:T(8,128)(2,1)}, u32[]{:S(2)}, u32[]{:S(2)}) collective-permute-start(bf16[1,8,64,128]{3,2,1,0:T(8,128)(2,1)} %get-tuple-element.7), channel_id=1, source_target_pairs={{0,16},{1,17},{2,18},{3,19},{4,20},{5,21},{6,22},{7,23},{8,24},{9,... | collective-permute-start | bytes 393224 | tf_op jit(solution)/shard_map/ppermute | solution.py:14
  29.8 11.6 %collective-permute-start.6 = (bf16[1,8,64,128]{3,2,1,0:T(8,128)(2,1)}, bf16[1,8,64,128]{3,2,1,0:T(8,128)(2,1)}, u32[]{:S(2)}, u32[]{:S(2)}) collective-permute-start(bf16[1,8,64,128]{3,2,1,0:T(8,128)(2,1)} %get-tuple-element.8), channel_id=1, source_target_pairs={{16,0},{17,1},{18,2},{19,3},{20,4},{21,5},{22,6},{23,7},{24,8},{25... | collective-permute-start | bytes 393224 | tf_op jit(solution)/shard_map/ppermute | solution.py:14
  31.8 9.7 %collective-permute-start.5 = (bf16[1,2,64,128]{3,2,1,0:T(8,128)(2,1)}, bf16[1,2,64,128]{3,2,1,0:T(8,128)(2,1)S(1)}, u32[]{:S(2)}, u32[]{:S(2)}) collective-permute-start(bf16[1,2,64,128]{3,2,1,0:T(8,128)(2,1)} %get-tuple-element.6), channel_id=1, source_target_pairs={{16,1},{17,2},{18,3},{19,4},{20,5},{21,6},{22,7},{23,8},{24,9},{25... | collective-permute-start | bytes 98312 | tf_op jit(solution)/shard_map/ppermute | solution.py:14
  53.6 15.3 %copy-start.4 = (bf16[3,64,144]{2,1,0:T(8,128)(2,1)S(1)}, bf16[3,64,144]{2,1,0:T(8,128)(2,1)}, u32[]{:S(2)}) copy-start(bf16[3,64,144]{2,1,0:T(8,128)(2,1)} %param.8) | copy-start | bytes 165892
  79.7 6.6 %copy-start.3 = (bf16[3,3,128,64]{2,3,1,0:T(8,128)(2,1)S(1)}, bf16[3,3,128,64]{2,3,1,0:T(8,128)(2,1)}, u32[]{:S(2)}) copy-start(bf16[3,3,128,64]{2,3,1,0:T(8,128)(2,1)} %param.9) | copy-start | bytes 442372
  90.4 19.6 %collective-permute-start.10 = (bf16[1,1,64,128]{3,0,2,1:T(2,128)(2,1)S(1)}, bf16[1,1,64,128]{3,0,2,1:T(2,128)(2,1)S(1)}, u32[]{:S(2)}, u32[]{:S(2)}) collective-permute-start(bf16[1,1,64,128]{3,0,2,1:T(2,128)(2,1)S(1)} %get-tuple-element.14), channel_id=1, source_target_pairs={{1,16},{2,17},{3,18},{4,19},{5,20},{6,21},{7,22},{8,23},{9,24},{10... | collective-permute-start | bytes 49160 | tf_op jit(solution)/shard_map/ppermute | solution.py:14
  92.3 44.4 %collective-permute-start.11 = (bf16[16,1,64,128]{3,0,2,1:T(8,128)(2,1)S(1)}, bf16[16,1,64,128]{3,0,2,1:T(8,128)(2,1)S(1)}, u32[]{:S(2)}, u32[]{:S(2)}) collective-permute-start(bf16[16,1,64,128]{3,0,2,1:T(8,128)(2,1)S(1)} %get-tuple-element.17), channel_id=1, source_target_pairs={{0,1},{1,2},{2,3},{3,4},{4,5},{5,6},{6,7},{7,8},{8,9},{9,10},{10,1... | collective-permute-start | bytes 786440 | tf_op jit(solution)/shard_map/ppermute | solution.py:14
  98.8 37.9 %collective-permute-start.12 = (bf16[16,1,64,128]{3,0,2,1:T(8,128)(2,1)S(1)}, bf16[16,1,64,128]{3,0,2,1:T(8,128)(2,1)S(1)}, u32[]{:S(2)}, u32[]{:S(2)}) collective-permute-start(bf16[16,1,64,128]{3,0,2,1:T(8,128)(2,1)S(1)} %get-tuple-element.18), channel_id=1, source_target_pairs={{1,0},{2,1},{3,2},{4,3},{5,4},{6,5},{7,6},{8,7},{9,8},{10,9},{11,1... | collective-permute-start | bytes 786440 | tf_op jit(solution)/shard_map/ppermute | solution.py:14
  101.8 34.9 %collective-permute-start.14 = (bf16[1,4,64,128]{3,0,2,1:T(2,128)(2,1)S(1)}, bf16[1,4,64,128]{3,0,2,1:T(2,128)(2,1)S(1)}, u32[]{:S(2)}, u32[]{:S(2)}) collective-permute-start(bf16[1,4,64,128]{3,0,2,1:T(2,128)(2,1)S(1)} %get-tuple-element.16), channel_id=1, source_target_pairs={{16,0},{17,1},{18,2},{19,3},{20,4},{21,5},{22,6},{23,7},{24,8},{25... | collective-permute-start | bytes 196616 | tf_op jit(solution)/shard_map/ppermute | solution.py:14
  103.8 32.9 %collective-permute-start.9 = (bf16[1,4,64,128]{3,0,2,1:T(2,128)(2,1)S(1)}, bf16[1,4,64,128]{3,0,2,1:T(2,128)(2,1)S(1)}, u32[]{:S(2)}, u32[]{:S(2)}) collective-permute-start(bf16[1,4,64,128]{3,0,2,1:T(2,128)(2,1)S(1)} %get-tuple-element.15), channel_id=1, source_target_pairs={{0,16},{1,17},{2,18},{3,19},{4,20},{5,21},{6,22},{7,23},{8,24},{9,... | collective-permute-start | bytes 196616 | tf_op jit(solution)/shard_map/ppermute | solution.py:14
  110.0 9.5 %collective-permute-start.13 = (bf16[1,1,64,128]{3,0,2,1:T(2,128)(2,1)S(1)}, bf16[1,1,64,128]{3,0,2,1:T(2,128)(2,1)S(1)}, u32[]{:S(2)}, u32[]{:S(2)}) collective-permute-start(bf16[1,1,64,128]{3,0,2,1:T(2,128)(2,1)S(1)} %get-tuple-element.13), channel_id=1, source_target_pairs={{16,1},{17,2},{18,3},{19,4},{20,5},{21,6},{22,7},{23,8},{24,9},{25... | collective-permute-start | bytes 49160 | tf_op jit(solution)/shard_map/ppermute | solution.py:14
  119.5 7.3 %collective-permute-start.15 = (bf16[1,1,64,128]{3,0,2,1:T(2,128)(2,1)S(1)}, bf16[1,1,64,128]{3,0,2,1:T(2,128)(2,1)S(1)}, u32[]{:S(2)}, u32[]{:S(2)}) collective-permute-start(bf16[1,1,64,128]{3,0,2,1:T(2,128)(2,1)S(1)} %get-tuple-element.12), channel_id=1, source_target_pairs={{17,0},{18,1},{19,2},{20,3},{21,4},{22,5},{23,6},{24,7},{25,8},{26... | collective-permute-start | bytes 49160 | tf_op jit(solution)/shard_map/ppermute | solution.py:14
  126.8 18.5 %copy-start.2 = (bf16[3,128,288]{1,2,0:T(8,128)(2,1)S(1)}, bf16[3,128,288]{1,2,0:T(8,128)(2,1)}, u32[]{:S(2)}) copy-start(bf16[3,128,288]{1,2,0:T(8,128)(2,1)} %param.11) | copy-start | bytes 663556
  126.8 9.9 %collective-permute-start.8 = (bf16[1,1,64,128]{3,0,2,1:T(2,128)(2,1)S(1)}, bf16[1,1,64,128]{3,0,2,1:T(2,128)(2,1)S(1)}, u32[]{:S(2)}, u32[]{:S(2)}) collective-permute-start(bf16[1,1,64,128]{3,0,2,1:T(2,128)(2,1)S(1)} %get-tuple-element.11), channel_id=1, source_target_pairs={{0,17},{1,18},{2,19},{3,20},{4,21},{5,22},{6,23},{7,24},{8,25},{9,... | collective-permute-start | bytes 49160 | tf_op jit(solution)/shard_map/ppermute | solution.py:14

commit v2 on v0

v2 whole, which is shorter than its diff:
```python
import jax
import jax.numpy as jnp
from jax import lax
from jax.sharding import PartitionSpec as P


def from_neighbour(block, axis, by):
    n = lax.axis_size(axis)
    pairs = [(i + by, i) for i in range(n) if 0 <= i + by < n]
    return lax.ppermute(block, axis, pairs)


def spatial(source, kernel, layout):
    return lax.conv_general_dilated(
        source,
        kernel,
        (1, 1),
        ((0, 0), (1, 1)),
        dimension_numbers=(layout, "HWOI", layout),
        preferred_element_type=jnp.float32,
    )


def temporal(source, kernel, layout):
    return lax.conv_general_dilated(
        source,
        kernel[:, None],
        (1, 1),
        ((0, 0), (0, 0)),
        dimension_numbers=(layout, "HWOI", layout),
        preferred_element_type=jnp.float32,
    )


def residual_block(rowed, spatial_kernel, temporal_kernel, space_layout, time_layout):
    middle = jax.nn.relu(spatial(rowed, spatial_kernel, space_layout)).astype(jnp.bfloat16)
    frames = middle.shape[0]
    before = from_neighbour(middle[frames - 1 :], "tm", -1)
    after = from_neighbour(middle[:1], "tm", 1)
    inner = temporal(middle, temporal_kernel, time_layout)
    first = temporal(jnp.concatenate([before, middle[:2]], axis=0), temporal_kernel, time_layout)
    last = temporal(jnp.concatenate([middle[frames - 2 :], after], axis=0), temporal_kernel, time_layout)
    mixed = jnp.concatenate([first, inner, last], axis=0)
    summed = rowed[:, 1:-1].astype(jnp.float32) + mixed
    return jax.nn.relu(summed).astype(jnp.bfloat16)


def with_rows(block, top, bottom):
    rows = block.shape[1]
    above = from_neighbour(block[:, rows - top :], "row", -1)
    below = from_neighbour(block[:, :bottom], "row", 1)
    return jnp.concatenate([above, block, below], axis=1)


def on_device(video_clip, spatial_one, temporal_one, down_weight, spatial_two, temporal_two):
    section_one = residual_block(with_rows(video_clip, 2, 1), spatial_one, temporal_one, "NHCW", "HWCN")
    first_device = lax.axis_index("row") == 0
    keep = jnp.logical_or(jnp.arange(section_one.shape[1]) > 0, jnp.logical_not(first_device))
    section_one = jnp.where(keep[None, :, None, None], section_one, jnp.zeros_like(section_one))
    reduced = lax.conv_general_dilated(
        section_one,
        down_weight,
        (2, 2),
        ((0, 0), (1, 1)),
        dimension_numbers=("NHCW", "HWOI", "NHWC"),
        preferred_element_type=jnp.float32,
    )
    reduced = jax.nn.relu(reduced).astype(jnp.bfloat16)
    return residual_block(with_rows(reduced, 1, 1), spatial_two, temporal_two, "NHWC", "HWNC")


def solution(mesh):
    placed = (P("tm", "row", None, None), P(), P(), P(), P(), P())
    return jax.shard_map(
        on_device, mesh=mesh, in_specs=placed, out_specs=P("tm", "row", None, None), check_vma=False
    )
```

time: 125 us -> 139 us (1.11)
  the two profiles are of different devices: /device:TPU:31 before, /device:TPU:57 now
where the time goes in v2:
time: 139 us; the launch traced here: 136 us
  local copies, waits for them, and re-layouts  44.4 us (32%)
  matrix products  37.6 us (27%)
  starting transfers between devices  26.4 us (19%)
  waiting for transfers between devices  21.1 us (15%)
  other arithmetic  6.28 us (5%)
    ppermute x8, starting transfers between devices, from_neighbour(): return lax.ppermute(block, axis, pairs)  26.4 us
    ppermute x8, waiting for transfers between devices, from_neighbour(): return lax.ppermute(block, axis, pairs)  21.1 us
    conv_general_dilated x6, matrix products, temporal(): lax.conv_general_dilated(source, kernel[:, None], (1, 1), ((0, 0), (0, 0)...  18.6 us
    conv_general_dilated x2, matrix products, spatial(): lax.conv_general_dilated(source, kernel, (1, 1), ((0, 0), (1, 1)), dimens...  15.1 us
    slice x3, local copies, waits for them, and re-layouts, residual_block(): middle[:2]  10.5 us
    unnamed x13, local copies, waits for them, and re-layouts  9.35 us
    select_n x1, local copies, waits for them, and re-layouts, on_device(): jnp.where(keep[None, :, None, None], section_one, jnp.zeros_like(section_...  6.63 us
    slice x3, local copies, waits for them, and re-layouts, residual_block(): before = from_neighbour(middle[frames - 1:], 'tm', -1)  5.65 us
  transfers between devices with their start and end apart: 8, of which 4 were waited for; matrix products, arithmetic and copies ran while one was open for 31% of the time, Pallas kernels for 0%

profile of v2, /device:TPU:57, one launch (start us, length us, event | category | flops | bytes accessed | tf_op | source)
XLA Modules:
  0.0 136.0 jit_solution(235254294457298115)
XLA Ops:
  0.0 0.0 copy-start
  0.0 1.1 slice.40
  1.2 4.8 %collective-permute-start = (bf16[16,2,64,128]{3,2,1,0:T(8,128)(2,1)S(1)}, bf16[16,2,64,128]{3,2,1,0:T(8,128)(2,1)S(1)}, u32[]{:S(2)}, u32[]{:S(2)}) collective-permute-start(bf16[16,2,64,128]{3,2,1,0:T(8,128)(2,1)S(1)} %slice.40), channel_id=1, source_target_pairs={{0,1},{1,2},{2,3},{3,4},{4,5},{5,6},{6,7},{7,8},{8,9},{9,10},{10,1... | collective-permute-start | bytes 1572872 | tf_op jit(solution)/shard_map/ppermute | solution.py:10
  6.0 5.7 %copy.30 = bf16[16,8,64,128]{2,0,3,1:T(8,128)(2,1)} copy(bf16[16,8,64,128]{3,2,1,0:T(8,128)(2,1)} %param.6) | data formatting | bytes 4194304 | tf_op args[0]
  11.7 1.1 slice.53
  12.7 1.9 %collective-permute-start.1 = (bf16[16,1,64,128]{2,0,3,1:T(8,128)(2,1)S(1)}, bf16[16,1,64,128]{2,0,3,1:T(8,128)(2,1)S(1)}, u32[]{:S(2)}, u32[]{:S(2)}) collective-permute-start(bf16[16,1,64,128]{2,0,3,1:T(8,128)(2,1)S(1)} %slice.53), channel_id=1, source_target_pairs={{1,0},{2,1},{3,2},{4,3},{5,4},{6,5},{7,6},{8,7},{9,8},{10,9},{11,1... | collective-permute-start | bytes 786440 | tf_op jit(solution)/shard_map/ppermute | solution.py:10
  14.7 0.0 collective-permute-done
  14.7 0.8 copy.29
  15.5 11.3 %collective-permute-done.1 = bf16[16,1,64,128]{2,0,3,1:T(8,128)(2,1)S(1)} collective-permute-done((bf16[16,1,64,128]{2,0,3,1:T(8,128)(2,1)S(1)}, bf16[16,1,64,128]{2,0,3,1:T(8,128)(2,1)S(1)}, u32[]{:S(2)}, u32[]{:S(2)}) %collective-permute-start.1) | collective-permute-done | bytes 262176 | tf_op jit(solution)/shard_map/ppermute | solution.py:10
  26.9 9.5 %maximum_convert_fusion = bf16[16,9,144,128]{2,0,3,1:T(8,128)(2,1)S(1)} fusion(bf16[3,3,144,64]{2,3,1,0:T(8,128)(2,1)} %param.7, bf16[16,1,64,128]{2,0,3,1:T(8,128)(2,1)S(1)} %collective-permute-done.1, bf16[16,8,64,128]{2,0,3,1:T(8,128)(2,1)} %copy.30, bf16[16,2,64,128]{2,0,3,1:T(8,128)(2,1)S(1)} %copy.29), kind=kOutput, calls=%fused_computation | convolution fusion | flops 3055681536 | bytes 8357888 | tf_op jit(solution)/shard_map/conv_general_dilated | solution.py:14
  36.3 0.0 copy-start.2
  36.3 3.6 %copy-done.2 = bf16[16,9,144,128]{2,0,3,1:T(8,128)(2,1)} copy-done((bf16[16,9,144,128]{2,0,3,1:T(8,128)(2,1)}, bf16[16,9,144,128]{2,0,3,1:T(8,128)(2,1)S(1)}, u32[]{:S(2)}) %copy-start.2) | copy-done | bytes 5308440
  40.0 2.4 %fusion.41 = (bf16[1,9,144,128]{2,0,3,1:T(2,128)(2,1)S(1)}, bf16[1,9,144,128]{2,0,3,1:T(2,128)(2,1)S(1)}) fusion(bf16[16,9,144,128]{2,0,3,1:T(8,128)(2,1)S(1)} %maximum_convert_fusion), kind=kLoop, calls=%fused_computation.50 | loop fusion | bytes 1327104 | tf_op jit(solution)/shard_map/slice | solution.py:38
  42.4 2.6 %copy.31 = bf16[1,9,144,128]{3,2,1,0:T(8,128)(2,1)} copy(bf16[1,9,144,128]{2,0,3,1:T(2,128)(2,1)S(1)} %get-tuple-element.5) | data formatting | bytes 663552 | tf_op jit(solution)/shard_map/slice | solution.py:38
  45.0 3.1 %collective-permute-start.2 = (bf16[1,9,144,128]{3,2,1,0:T(8,128)(2,1)}, bf16[1,9,144,128]{3,2,1,0:T(8,128)(2,1)}, u32[]{:S(2)}, u32[]{:S(2)}) collective-permute-start(bf16[1,9,144,128]{3,2,1,0:T(8,128)(2,1)} %copy.31), channel_id=1, source_target_pairs={{0,16},{16,32},{32,48},{48,64},{64,80},{80,96},{96,112},{1,17},{17... | collective-permute-start | bytes 995336 | tf_op jit(solution)/shard_map/ppermute | solution.py:10
  48.1 2.6 %copy.36 = bf16[1,9,144,128]{3,2,1,0:T(8,128)(2,1)} copy(bf16[1,9,144,128]{2,0,3,1:T(2,128)(2,1)S(1)} %get-tuple-element.6) | data formatting | bytes 663552 | tf_op jit(solution)/shard_map/slice | solution.py:39
  50.8 4.4 %collective-permute-start.3 = (bf16[1,9,144,128]{3,2,1,0:T(8,128)(2,1)}, bf16[1,9,144,128]{3,2,1,0:T(8,128)(2,1)}, u32[]{:S(2)}, u32[]{:S(2)}) collective-permute-start(bf16[1,9,144,128]{3,2,1,0:T(8,128)(2,1)} %copy.36), channel_id=1, source_target_pairs={{16,0},{32,16},{48,32},{64,48},{80,64},{96,80},{112,96},{17,1},{33... | collective-permute-start | bytes 995336 | tf_op jit(solution)/shard_map/ppermute | solution.py:10
  55.2 12.6 %fusion = f32[14,9,64,128]{3,2,1,0:T(8,128)} fusion(bf16[16,9,144,128]{2,0,3,1:T(8,128)(2,1)} %copy-done.2, bf16[3,64,144]{2,1,0:T(8,128)(2,1)} %param.8), kind=kOutput, calls=%fused_computation.1 | convolution fusion | flops 891813888 | bytes 9492480 | tf_op jit(solution)/shard_map/conv_general_dilated | solution.py:25
  67.9 0.0 copy-start.5
  67.9 7.2 %fusion.42 = (bf16[2,9,144,128]{2,0,3,1:T(2,128)(2,1)S(1)}, bf16[2,9,144,128]{2,0,3,1:T(2,128)(2,1)}) fusion(bf16[16,9,144,128]{2,0,3,1:T(8,128)(2,1)} %copy-done.2), kind=kLoop, calls=%fused_computation.51 | loop fusion | bytes 2654208 | tf_op jit(solution)/shard_map/slice | solution.py:41
  75.0 2.8 %copy.32 = bf16[2,9,144,128]{3,2,1,0:T(8,128)(2,1)} copy(bf16[2,9,144,128]{2,0,3,1:T(2,128)(2,1)S(1)} %get-tuple-element.7) | data formatting | bytes 1327104 | tf_op jit(solution)/shard_map/slice | solution.py:41
  77.8 0.0 copy-start.1
  77.8 4.2 %copy.37 = bf16[2,9,144,128]{3,2,1,0:T(8,128)(2,1)} copy(bf16[2,9,144,128]{2,0,3,1:T(2,128)(2,1)} %get-tuple-element.8) | data formatting | bytes 1327104 | tf_op jit(solution)/shard_map/slice | solution.py:42
  82.0 0.0 collective-permute-done.2
  82.0 0.0 copy-done.5
  82.0 1.5 %fusion.19 = f32[1,9,64,128]{3,2,1,0:T(8,128)S(1)} fusion(bf16[2,9,144,128]{3,2,1,0:T(8,128)(2,1)} %copy.32, bf16[1,9,144,128]{3,2,1,0:T(8,128)(2,1)} %collective-permute-done.2, bf16[3,64,144]{2,1,0:T(8,128)(2,1)S(1)} %copy-done.5), kind=kOutput, calls=%fused_computation.25 | convolution fusion | flops 65691648 | bytes 1345536 | tf_op jit(solution)/shard_map/conv_general_dilated | solution.py:25
  83.5 0.0 collective-permute-done.3
  83.6 1.5 %fusion.23 = f32[1,9,64,128]{3,2,1,0:T(8,128)S(1)} fusion(bf16[1,9,144,128]{3,2,1,0:T(8,128)(2,1)} %collective-permute-done.3, bf16[2,9,144,128]{3,2,1,0:T(8,128)(2,1)} %copy.37, bf16[3,64,144]{2,1,0:T(8,128)(2,1)S(1)} %copy-done.5), kind=kOutput, calls=%fused_computation.29 | convolution fusion | flops 65691648 | bytes 1345536 | tf_op jit(solution)/shard_map/conv_general_dilated | solution.py:25
  85.1 0.0 copy-done.1
  85.1 3.9 %fusion.11 = bf16[16,9,64,128]{3,2,1,0:T(8,128)(2,1)} fusion(f32[1,9,64,128]{3,2,1,0:T(8,128)S(1)} %fusion.23, f32[14,9,64,128]{3,2,1,0:T(8,128)} %fusion, f32[1,9,64,128]{3,2,1,0:T(8,128)S(1)} %fusion.19, bf16[16,8,64,128]{3,2,1,0:T(8,128)(2,1)S(1)} %copy-done.1, bf16[16,2,64,128]{3,2,1,0:T(8,128)(2,1)S(1)} %collective-permute-done, ...), kind=kLoop, calls=%fused_computation.14 | loop fusion | flops 9437184 | bytes 9699337 | tf_op jit(solution)/shard_map/jit(_where)/select_n | solution.py:59
  89.0 0.0 copy-start.4
  89.0 6.6 %copy.39 = bf16[16,9,64,128]{2,0,3,1:T(8,128)(2,1)} copy(bf16[16,9,64,128]{3,2,1,0:T(8,128)(2,1)} %fusion.11) | data formatting | bytes 4718592 | tf_op jit(solution)/shard_map/jit(_where)/select_n | solution.py:59
  95.6 0.0 copy-done.4
  95.6 3.9 %maximum_convert_fusion.2 = bf16[16,4,64,128]{3,0,2,1:T(8,128)(2,1)S(1)} fusion(bf16[16,9,64,128]{2,0,3,1:T(8,128)(2,1)} %copy.39, bf16[3,3,128,64]{2,3,1,0:T(8,128)(2,1)S(1)} %copy-done.4), kind=kOutput, calls=%fused_computation.19 | convolution fusion | flops 601882624 | bytes 3555328 | tf_op jit(solution)/shard_map/conv_general_dilated | solution.py:60
  99.6 2.3 %collective-permute-start.4 = (bf16[16,1,64,128]{3,0,2,1:T(8,128)(2,1)S(1)}, bf16[16,1,64,128]{3,0,2,1:T(8,128)(2,1)S(1)}, u32[]{:S(2)}, u32[]{:S(2)}) collective-permute-start(bf16[16,1,64,128]{3,0,2,1:T(8,128)(2,1)S(1)} %get-tuple-element.13), channel_id=1, source_target_pairs={{0,1},{1,2},{2,3},{3,4},{4,5},{5,6},{6,7},{7,8},{8,9},{9,10},{10,1... | collective-permute-start | bytes 786440 | tf_op jit(solution)/shard_map/ppermute | solution.py:10
  101.9 0.0 copy-start.3
  101.9 2.4 %collective-permute-start.5 = (bf16[16,1,64,128]{3,0,2,1:T(8,128)(2,1)S(1)}, bf16[16,1,64,128]{3,0,2,1:T(8,128)(2,1)S(1)}, u32[]{:S(2)}, u32[]{:S(2)}) collective-permute-start(bf16[16,1,64,128]{3,0,2,1:T(8,128)(2,1)S(1)} %get-tuple-element.14), channel_id=1, source_target_pairs={{1,0},{2,1},{3,2},{4,3},{5,4},{6,5},{7,6},{8,7},{9,8},{10,9},{11,1... | collective-permute-start | bytes 786440 | tf_op jit(solution)/shard_map/ppermute | solution.py:10
  104.3 0.9 collective-permute-done.4
  105.2 8.2 %collective-permute-done.5 = bf16[16,1,64,128]{3,0,2,1:T(8,128)(2,1)S(1)} collective-permute-done((bf16[16,1,64,128]{3,0,2,1:T(8,128)(2,1)S(1)}, bf16[16,1,64,128]{3,0,2,1:T(8,128)(2,1)S(1)}, u32[]{:S(2)}, u32[]{:S(2)}) %collective-permute-start.5) | collective-permute-done | bytes 262176 | tf_op jit(solution)/shard_map/ppermute | solution.py:10
  113.4 0.0 copy-done
  113.4 5.6 %maximum_convert_fusion.1 = bf16[16,4,64,288]{3,0,2,1:T(8,128)(2,1)S(1)} fusion(bf16[3,3,288,128]{3,2,1,0:T(8,128)(2,1)S(1)} %copy-done, bf16[16,1,64,128]{3,0,2,1:T(8,128)(2,1)S(1)} %collective-permute-done.5, bf16[16,4,64,128]{3,0,2,1:T(8,128)(2,1)S(1)} %maximum_convert_fusion.2, bf16[16,1,64,128]{3,0,2,1:T(8,128)(2,1)S(1)} %collective-permute-done.4), kind=kOutput, calls=%fused_computation.3 | convolution fusion | flops 2696675328 | bytes 4595712 | tf_op jit(solution)/shard_map/conv_general_dilated | solution.py:14
  119.0 0.6 fusion.43
  119.6 1.9 %collective-permute-start.6 = (bf16[1,4,64,288]{3,0,2,1:T(2,128)(2,1)S(1)}, bf16[1,4,64,288]{3,0,2,1:T(2,128)(2,1)S(1)}, u32[]{:S(2)}, u32[]{:S(2)}) collective-permute-start(bf16[1,4,64,288]{3,0,2,1:T(2,128)(2,1)S(1)} %get-tuple-element.9), channel_id=1, source_target_pairs={{0,16},{16,32},{32,48},{48,64},{64,80},{80,96},{96,112},{1,17},{17... | collective-permute-start | bytes 442376 | tf_op jit(solution)/shard_map/ppermute | solution.py:10
  121.5 5.5 %collective-permute-start.7 = (bf16[1,4,64,288]{3,0,2,1:T(2,128)(2,1)S(1)}, bf16[1,4,64,288]{3,0,2,1:T(2,128)(2,1)S(1)}, u32[]{:S(2)}, u32[]{:S(2)}) collective-permute-start(bf16[1,4,64,288]{3,0,2,1:T(2,128)(2,1)S(1)} %get-tuple-element.10), channel_id=1, source_target_pairs={{16,0},{32,16},{48,32},{64,48},{80,64},{96,80},{112,96},{17,1},{33... | collective-permute-start | bytes 442376 | tf_op jit(solution)/shard_map/ppermute | solution.py:10
  127.0 0.0 copy-done.3
  127.0 2.3 %fusion.9 = f32[14,4,64,128]{3,2,1,0:T(8,128)S(1)} fusion(bf16[16,4,64,288]{3,0,2,1:T(8,128)(2,1)S(1)} %maximum_convert_fusion.1, bf16[3,128,288]{1,2,0:T(8,128)(2,1)S(1)} %copy-done.3), kind=kOutput, calls=%fused_computation.12 | convolution fusion | flops 792723456 | bytes 4415488 | tf_op jit(solution)/shard_map/conv_general_dilated | solution.py:25
  129.3 0.6 fusion.44
  129.9 1.1 copy.47
  131.0 0.0 collective-permute-done.6
  131.0 0.7 collective-permute-done.7
  131.7 1.8 %pad_maximum_fusion.1 = (bf16[3,4,64,288]{3,0,2,1:T(4,128)(2,1)S(1)}, bf16[3,4,64,288]{3,0,2,1:T(4,128)(2,1)S(1)}) fusion(bf16[2,4,64,288]{3,0,2,1:T(2,128)(2,1)S(1)} %get-tuple-element.11, bf16[1,4,64,288]{3,0,2,1:T(2,128)(2,1)S(1)} %collective-permute-done.6, bf16[1,4,64,288]{3,0,2,1:T(2,128)(2,1)S(1)} %collective-permute-done.7, ...), kind=kLoop, calls=%fused_computation.33 | loop fusion | flops 1769472 | bytes 1769472 | tf_op jit(solution)/shard_map/concatenate | solution.py:41
  133.5 0.3 fusion.29
  133.8 0.3 fusion.27
  134.1 0.6 fusion.13
  134.7 1.2 copy.49
  (2 shorter events, 0.0 us)
Async XLA Ops:
  0.0 113.4 %copy-start = (bf16[3,3,288,128]{3,2,1,0:T(8,128)(2,1)S(1)}, bf16[3,3,288,128]{3,2,1,0:T(8,128)(2,1)}, u32[]{:S(2)}) copy-start(bf16[3,3,288,128]{3,2,1,0:T(8,128)(2,1)} %param.10) | copy-start | bytes 1990660
  1.2 13.5 %collective-permute-start = (bf16[16,2,64,128]{3,2,1,0:T(8,128)(2,1)S(1)}, bf16[16,2,64,128]{3,2,1,0:T(8,128)(2,1)S(1)}, u32[]{:S(2)}, u32[]{:S(2)}) collective-permute-start(bf16[16,2,64,128]{3,2,1,0:T(8,128)(2,1)S(1)} %slice.40), channel_id=1, source_target_pairs={{0,1},{1,2},{2,3},{3,4},{4,5},{5,6},{6,7},{7,8},{8,9},{9,10},{10,1... | collective-permute-start | bytes 1572872 | tf_op jit(solution)/shard_map/ppermute | solution.py:10
  12.7 14.1 %collective-permute-start.1 = (bf16[16,1,64,128]{2,0,3,1:T(8,128)(2,1)S(1)}, bf16[16,1,64,128]{2,0,3,1:T(8,128)(2,1)S(1)}, u32[]{:S(2)}, u32[]{:S(2)}) collective-permute-start(bf16[16,1,64,128]{2,0,3,1:T(8,128)(2,1)S(1)} %slice.53), channel_id=1, source_target_pairs={{1,0},{2,1},{3,2},{4,3},{5,4},{6,5},{7,6},{8,7},{9,8},{10,9},{11,1... | collective-permute-start | bytes 786440 | tf_op jit(solution)/shard_map/ppermute | solution.py:10
  36.3 3.7 %copy-start.2 = (bf16[16,9,144,128]{2,0,3,1:T(8,128)(2,1)}, bf16[16,9,144,128]{2,0,3,1:T(8,128)(2,1)S(1)}, u32[]{:S(2)}) copy-start(bf16[16,9,144,128]{2,0,3,1:T(8,128)(2,1)S(1)} %maximum_convert_fusion) | copy-start | bytes 15925252
  45.0 37.0 %collective-permute-start.2 = (bf16[1,9,144,128]{3,2,1,0:T(8,128)(2,1)}, bf16[1,9,144,128]{3,2,1,0:T(8,128)(2,1)}, u32[]{:S(2)}, u32[]{:S(2)}) collective-permute-start(bf16[1,9,144,128]{3,2,1,0:T(8,128)(2,1)} %copy.31), channel_id=1, source_target_pairs={{0,16},{16,32},{32,48},{48,64},{64,80},{80,96},{96,112},{1,17},{17... | collective-permute-start | bytes 995336 | tf_op jit(solution)/shard_map/ppermute | solution.py:10
  50.8 32.8 %collective-permute-start.3 = (bf16[1,9,144,128]{3,2,1,0:T(8,128)(2,1)}, bf16[1,9,144,128]{3,2,1,0:T(8,128)(2,1)}, u32[]{:S(2)}, u32[]{:S(2)}) collective-permute-start(bf16[1,9,144,128]{3,2,1,0:T(8,128)(2,1)} %copy.36), channel_id=1, source_target_pairs={{16,0},{32,16},{48,32},{64,48},{80,64},{96,80},{112,96},{17,1},{33... | collective-permute-start | bytes 995336 | tf_op jit(solution)/shard_map/ppermute | solution.py:10
  67.9 14.2 %copy-start.5 = (bf16[3,64,144]{2,1,0:T(8,128)(2,1)S(1)}, bf16[3,64,144]{2,1,0:T(8,128)(2,1)}, u32[]{:S(2)}) copy-start(bf16[3,64,144]{2,1,0:T(8,128)(2,1)} %param.8) | copy-start | bytes 165892
  77.8 7.3 %copy-start.1 = (bf16[16,8,64,128]{3,2,1,0:T(8,128)(2,1)S(1)}, bf16[16,8,64,128]{3,2,1,0:T(8,128)(2,1)}, u32[]{:S(2)}) copy-start(bf16[16,8,64,128]{3,2,1,0:T(8,128)(2,1)} %param.6) | copy-start | bytes 6291460
  89.0 6.6 %copy-start.4 = (bf16[3,3,128,64]{2,3,1,0:T(8,128)(2,1)S(1)}, bf16[3,3,128,64]{2,3,1,0:T(8,128)(2,1)}, u32[]{:S(2)}) copy-start(bf16[3,3,128,64]{2,3,1,0:T(8,128)(2,1)} %param.9) | copy-start | bytes 442372
  99.6 5.6 %collective-permute-start.4 = (bf16[16,1,64,128]{3,0,2,1:T(8,128)(2,1)S(1)}, bf16[16,1,64,128]{3,0,2,1:T(8,128)(2,1)S(1)}, u32[]{:S(2)}, u32[]{:S(2)}) collective-permute-start(bf16[16,1,64,128]{3,0,2,1:T(8,128)(2,1)S(1)} %get-tuple-element.13), channel_id=1, source_target_pairs={{0,1},{1,2},{2,3},{3,4},{4,5},{5,6},{6,7},{7,8},{8,9},{9,10},{10,1... | collective-permute-start | bytes 786440 | tf_op jit(solution)/shard_map/ppermute | solution.py:10
  101.9 25.1 %copy-start.3 = (bf16[3,128,288]{1,2,0:T(8,128)(2,1)S(1)}, bf16[3,128,288]{1,2,0:T(8,128)(2,1)}, u32[]{:S(2)}) copy-start(bf16[3,128,288]{1,2,0:T(8,128)(2,1)} %param.11) | copy-start | bytes 663556
  101.9 11.4 %collective-permute-start.5 = (bf16[16,1,64,128]{3,0,2,1:T(8,128)(2,1)S(1)}, bf16[16,1,64,128]{3,0,2,1:T(8,128)(2,1)S(1)}, u32[]{:S(2)}, u32[]{:S(2)}) collective-permute-start(bf16[16,1,64,128]{3,0,2,1:T(8,128)(2,1)S(1)} %get-tuple-element.14), channel_id=1, source_target_pairs={{1,0},{2,1},{3,2},{4,3},{5,4},{6,5},{7,6},{8,7},{9,8},{10,9},{11,1... | collective-permute-start | bytes 786440 | tf_op jit(solution)/shard_map/ppermute | solution.py:10
  119.6 11.4 %collective-permute-start.6 = (bf16[1,4,64,288]{3,0,2,1:T(2,128)(2,1)S(1)}, bf16[1,4,64,288]{3,0,2,1:T(2,128)(2,1)S(1)}, u32[]{:S(2)}, u32[]{:S(2)}) collective-permute-start(bf16[1,4,64,288]{3,0,2,1:T(2,128)(2,1)S(1)} %get-tuple-element.9), channel_id=1, source_target_pairs={{0,16},{16,32},{32,48},{48,64},{64,80},{80,96},{96,112},{1,17},{17... | collective-permute-start | bytes 442376 | tf_op jit(solution)/shard_map/ppermute | solution.py:10
  121.5 10.2 %collective-permute-start.7 = (bf16[1,4,64,288]{3,0,2,1:T(2,128)(2,1)S(1)}, bf16[1,4,64,288]{3,0,2,1:T(2,128)(2,1)S(1)}, u32[]{:S(2)}, u32[]{:S(2)}) collective-permute-start(bf16[1,4,64,288]{3,0,2,1:T(2,128)(2,1)S(1)} %get-tuple-element.10), channel_id=1, source_target_pairs={{16,0},{32,16},{48,32},{64,48},{80,64},{96,80},{112,96},{17,1},{33... | collective-permute-start | bytes 442376 | tf_op jit(solution)/shard_map/ppermute | solution.py:10

commit v3 on v0

--- a/solution.py
+++ b/solution.py
@@ -1,6 +1,10 @@
+import functools
+
 import jax
 import jax.numpy as jnp
 from jax import lax
+from jax.experimental import pallas as pl
+from jax.experimental.pallas import tpu as pltpu
 from jax.sharding import PartitionSpec as P
 
 
@@ -52,8 +56,70 @@
     return jax.nn.relu(summed).astype(jnp.bfloat16)
 
 
+def _lane_shift(x, by):
+    width = x.shape[-1]
+    rolled = pltpu.roll(x, (-by) % width, x.ndim - 1)
+    lane = lax.broadcasted_iota(jnp.int32, x.shape, x.ndim - 1)
+    inside = jnp.logical_and(lane + by >= 0, lane + by < width)
+    return jnp.where(inside, rolled, jnp.zeros_like(rolled))
+
+
+def _block_one_kernel(xp_ref, w9_ref, t3_ref, out_ref, mid_ref):
+    frames_p, rows_p = xp_ref.shape[0], xp_ref.shape[1]
+    rows = rows_p - 2
+    frames = frames_p - 2
+
+    def middle(f, carry):
+        slab = xp_ref[f].astype(jnp.float32)
+        shifted = [_lane_shift(slab, b - 1).astype(jnp.bfloat16) for b in range(3)]
+        parts = []
+        for a in range(3):
+            for b in range(3):
+                parts.append(jnp.concatenate([shifted[b][h + a] for h in range(rows)], axis=1))
+        stacked = jnp.concatenate(parts, axis=0)
+        m = jnp.dot(w9_ref[...], stacked, preferred_element_type=jnp.float32)
+        m = jnp.maximum(m, 0.0).astype(jnp.bfloat16)
+        width = out_ref.shape[-1]
+        for h in range(rows):
+            mid_ref[f, h] = m[:, h * width : (h + 1) * width]
+        return carry
+
+    lax.fori_loop(0, frames_p, middle, 0)
+
+    def section(t, carry):
+        width = out_ref.shape[-1]
+        parts = []
+        for k in range(3):
+            parts.append(jnp.concatenate([mid_ref[t + k, h] for h in range(rows)], axis=1))
+        stacked = jnp.concatenate(parts, axis=0)
+        s = jnp.dot(t3_ref[...], stacked, preferred_element_type=jnp.float32)
+        for h in range(rows):
+            v = s[:, h * width : (h + 1) * width] + xp_ref[t + 1, h + 1].astype(jnp.float32)
+            out_ref[t, h] = jnp.maximum(v, 0.0).astype(out_ref.dtype)
+        return carry
+
+    lax.fori_loop(0, frames, section, 0)
+
+
+def block_one(padded, spatial_kernel, temporal_kernel):
+    frames_p, rows_p, channels, width = padded.shape
+    mids = spatial_kernel.shape[2]
+    w9 = jnp.transpose(spatial_kernel, (2, 0, 1, 3)).reshape(mids, 9 * channels)
+    t3 = jnp.transpose(temporal_kernel, (1, 0, 2)).reshape(channels, 3 * mids)
+    vmem = pltpu.MemorySpace.VMEM if hasattr(pltpu, "MemorySpace") else pltpu.VMEM
+    return pl.pallas_call(
+        _block_one_kernel,
+        out_shape=jax.ShapeDtypeStruct((frames_p - 2, rows_p - 2, channels, width), padded.dtype),
+        in_specs=[pl.BlockSpec(memory_space=vmem)] * 3,
+        out_specs=pl.BlockSpec(memory_space=vmem),
+        scratch_shapes=[pltpu.VMEM((frames_p, rows_p - 2, mids, width), jnp.bfloat16)],
+        compiler_params=pltpu.CompilerParams(vmem_limit_bytes=48 * 1024 * 1024),
+    )(padded, w9, t3)
+
+
 def on_device(video_clip, spatial_one, temporal_one, down_weight, spatial_two, temporal_two):
-    section_one = residual_block(video_clip, spatial_one, temporal_one, "NHCW", "HWCN")
+    padded = padded_2(video_clip, (("tm", 0), ("row", 1)), 1)
+    section_one = block_one(padded, spatial_one, temporal_one)
     upper_row = from_behind(section_one[:, -1:], "row", 1)
     joined = jnp.concatenate([upper_row, section_one], axis=1)
     reduced = lax.conv_general_dilated(

time: 125 us -> 108 us (0.86)
  matrix products: 36.5 us -> 14.8 us
  Pallas kernels: 0 us -> 13.1 us
  local copies, waits for them, and re-layouts: 18.9 us -> 12 us
    conv_general_dilated x2 -> x1, matrix products: 22.5 us -> 8.63 us  [spatial(): lax.conv_general_dilated(source, kernel, (1, 1), ((0, 0), (1, 1)), dimens...]
    pallas_call x0 -> x1, Pallas kernels: none -> 13.1 us  [block_one(): pl.pallas_call(_block_one_kernel, out_shape=jax.ShapeDtypeStruct((frames_...]
    concatenate x2 -> x1, local copies, waits for them, and re-layouts: 9.1 us -> 0.02 us  [padded_2(): block = jnp.concatenate([low, block, high], axis=dim)]
    conv_general_dilated x2 -> x1, matrix products: 10 us -> 2.19 us  [temporal(): lax.conv_general_dilated(source, kernel[:, None], (1, 1), ((0, 0), (0, 0)...]
  transfers between devices with their start and end apart: 9 -> 9, of which waited for: 9 -> 9; matrix products, arithmetic and copies ran while one was open for 2% -> 3% of each run, Pallas kernels for 0% -> 0%
where the time goes in v3:
time: 108 us
  starting transfers between devices  32.9 us (30%)
  waiting for transfers between devices  31.1 us (29%)
  matrix products  14.8 us (14%)
  Pallas kernels  13.1 us (12%)
  local copies, waits for them, and re-layouts  12 us (11%)
  other arithmetic  3.46 us (3%)
    ppermute x4, waiting for transfers between devices, padded_2(): lax.ppermute(lax.slice_in_dim(block, 0, width, axis=dim), axis, backward)  23.2 us
    ppermute x4, starting transfers between devices, padded_2(): lax.ppermute(lax.slice_in_dim(block, block.shape[dim] - width, None, axis...  21.5 us
    pallas_call x1, Pallas kernels, block_one(): pl.pallas_call(_block_one_kernel, out_shape=jax.ShapeDtypeStruct((frames_...  13.1 us
    ppermute x4, starting transfers between devices, padded_2(): lax.ppermute(lax.slice_in_dim(block, 0, width, axis=dim), axis, backward)  9.44 us
    conv_general_dilated x1, matrix products, spatial(): lax.conv_general_dilated(source, kernel, (1, 1), ((0, 0), (1, 1)), dimens...  8.63 us
    concatenate x1, local copies, waits for them, and re-layouts, on_device(): joined = jnp.concatenate([upper_row, section_one], axis=1)  5.24 us
    ppermute x4, waiting for transfers between devices, padded_2(): lax.ppermute(lax.slice_in_dim(block, block.shape[dim] - width, None, axis...  4.62 us
    conv_general_dilated x1, matrix products, on_device(): lax.conv_general_dilated(joined, down_weight, (2, 2), ((0, 0), (1, 1)), d...  3.94 us
  transfers between devices with their start and end apart: 9, of which 9 were waited for; matrix products, arithmetic and copies ran while one was open for 3% of the time, Pallas kernels for 0%

profile of v3, /device:TPU:31, one launch (start us, length us, event | category | flops | bytes accessed | tf_op | source)
XLA Modules:
  0.0 107.5 jit_solution(2421889808322535910)
XLA Ops:
  0.0 0.0 copy-start
  0.0 1.1 fusion.16
  1.1 3.5 %collective-permute-start = (bf16[1,8,64,128]{3,2,1,0:T(8,128)(2,1)S(1)}, bf16[1,8,64,128]{3,2,1,0:T(8,128)(2,1)S(1)}, u32[]{:S(2)}, u32[]{:S(2)}) collective-permute-start(bf16[1,8,64,128]{3,2,1,0:T(8,128)(2,1)S(1)} %get-tuple-element.8), channel_id=1, source_target_pairs={{0,16},{16,32},{32,48},{48,64},{64,80},{80,96},{96,112},{1,17},{17... | collective-permute-start | bytes 393224 | tf_op jit(solution)/shard_map/ppermute | solution.py:16
  4.5 1.9 %collective-permute-start.1 = (bf16[1,8,64,128]{3,2,1,0:T(8,128)(2,1)S(1)}, bf16[1,8,64,128]{3,2,1,0:T(8,128)(2,1)S(1)}, u32[]{:S(2)}, u32[]{:S(2)}) collective-permute-start(bf16[1,8,64,128]{3,2,1,0:T(8,128)(2,1)S(1)} %get-tuple-element.7), channel_id=1, source_target_pairs={{16,0},{32,16},{48,32},{64,48},{80,64},{96,80},{112,96},{17,1},{33... | collective-permute-start | bytes 393224 | tf_op jit(solution)/shard_map/ppermute | solution.py:19
  6.5 0.9 collective-permute-done
  7.3 0.0 copy-start.1
  7.4 2.0 %constant_dynamic-update-slice_fusion.1 = bf16[18,8,64,128]{3,2,1,0:T(8,128)(2,1)S(1)} fusion(bf16[18,8,64,128]{3,2,1,0:T(8,128)(2,1)S(1)} %constant_dynamic-update-slice_fusion.2, bf16[16,8,64,128]{3,2,1,0:T(8,128)(2,1)} %param.6), kind=kLoop, calls=%fused_computation.23 | loop fusion | bytes 4194304
  9.3 3.0 %collective-permute-done.1 = bf16[1,8,64,128]{3,2,1,0:T(8,128)(2,1)S(1)} collective-permute-done((bf16[1,8,64,128]{3,2,1,0:T(8,128)(2,1)S(1)}, bf16[1,8,64,128]{3,2,1,0:T(8,128)(2,1)S(1)}, u32[]{:S(2)}, u32[]{:S(2)}) %collective-permute-start.1) | collective-permute-done | bytes 131104 | tf_op jit(solution)/shard_map/ppermute | solution.py:19
  12.4 0.9 fusion.15
  13.2 6.8 %collective-permute-start.2 = (bf16[18,1,64,128]{3,2,1,0:T(8,128)(2,1)}, bf16[18,1,64,128]{3,2,1,0:T(8,128)(2,1)}, u32[]{:S(2)}, u32[]{:S(2)}) collective-permute-start(bf16[18,1,64,128]{3,2,1,0:T(8,128)(2,1)} %get-tuple-element.5), channel_id=1, source_target_pairs={{0,1},{1,2},{2,3},{3,4},{4,5},{5,6},{6,7},{7,8},{8,9},{9,10},{10,1... | collective-permute-start | bytes 884744 | tf_op jit(solution)/shard_map/ppermute | solution.py:16
  20.1 1.9 %collective-permute-start.3 = (bf16[18,1,64,128]{3,2,1,0:T(8,128)(2,1)}, bf16[18,1,64,128]{3,2,1,0:T(8,128)(2,1)}, u32[]{:S(2)}, u32[]{:S(2)}) collective-permute-start(bf16[18,1,64,128]{3,2,1,0:T(8,128)(2,1)} %get-tuple-element.6), channel_id=1, source_target_pairs={{1,0},{2,1},{3,2},{4,3},{5,4},{6,5},{7,6},{8,7},{9,8},{10,9},{11,1... | collective-permute-start | bytes 884744 | tf_op jit(solution)/shard_map/ppermute | solution.py:19
  22.0 0.0 copy-done.1
  22.0 0.1 copy.14
  22.1 0.1 reshape.7.t3_ref
  22.2 1.1 %copy.15.w9_ref = bf16[144,576]{1,0:T(8,128)(2,1)S(1)} copy(bf16[144,576]{0,1:T(8,128)(2,1)} %bitcast.12) | data formatting | bytes 331776 | tf_op jit(solution)/shard_map/reshape | solution.py:107
  23.4 0.7 collective-permute-done.2
  24.0 8.0 %collective-permute-done.3 = bf16[18,1,64,128]{3,2,1,0:T(8,128)(2,1)} collective-permute-done((bf16[18,1,64,128]{3,2,1,0:T(8,128)(2,1)}, bf16[18,1,64,128]{3,2,1,0:T(8,128)(2,1)}, u32[]{:S(2)}, u32[]{:S(2)}) %collective-permute-start.3) | collective-permute-done | bytes 294944 | tf_op jit(solution)/shard_map/ppermute | solution.py:19
  32.1 1.4 %pad_maximum_fusion.xp_ref = bf16[18,10,64,128]{3,2,1,0:T(8,128)(2,1)S(1)} fusion(bf16[18,1,64,128]{3,2,1,0:T(8,128)(2,1)} %collective-permute-done.3, bf16[18,8,64,128]{3,2,1,0:T(8,128)(2,1)S(1)} %constant_dynamic-update-slice_fusion, bf16[18,1,64,128]{3,2,1,0:T(8,128)(2,1)} %collective-permute-done.2), kind=kLoop, calls=%fused_computation.3 | loop fusion | flops 2949120 | bytes 5898240 | tf_op jit(solution)/shard_map/concatenate | solution.py:20
  33.5 13.1 %shard_map.64 = bf16[16,8,64,128]{3,2,1,0:T(8,128)(2,1)S(1)} custom-call(bf16[18,10,64,128]{3,2,1,0:T(8,128)(2,1)S(1)} %pad_maximum_fusion.xp_ref, bf16[144,576]{1,0:T(8,128)(2,1)S(1)} %copy.15.w9_ref, bf16[64,432]{1,0:T(8,128)(2,1)S(1)} %reshape.7.t3_ref), custom_call_target="tpu_custom_call" | custom-call | tf_op jit(solution)/shard_map/pallas_call | solution.py:110
  46.6 1.9 %collective-permute-start.4 = (bf16[16,1,64,128]{3,2,1,0:T(8,128)(2,1)S(1)}, bf16[16,1,64,128]{3,2,1,0:T(8,128)(2,1)S(1)}, u32[]{:S(2)}, u32[]{:S(2)}) collective-permute-start(bf16[16,1,64,128]{3,2,1,0:T(8,128)(2,1)S(1)} %slice.38), channel_id=1, source_target_pairs={{0,1},{1,2},{2,3},{3,4},{4,5},{5,6},{6,7},{7,8},{8,9},{9,10},{10,1... | collective-permute-start | bytes 786440 | tf_op jit(solution)/shard_map/ppermute | solution.py:27
  48.5 3.3 %collective-permute-done.4 = bf16[16,1,64,128]{3,2,1,0:T(8,128)(2,1)S(1)} collective-permute-done((bf16[16,1,64,128]{3,2,1,0:T(8,128)(2,1)S(1)}, bf16[16,1,64,128]{3,2,1,0:T(8,128)(2,1)S(1)}, u32[]{:S(2)}, u32[]{:S(2)}) %collective-permute-start.4) | collective-permute-done | bytes 262176 | tf_op jit(solution)/shard_map/ppermute | solution.py:27
  51.8 0.2 pad_maximum_fusion.1
  52.0 0.0 copy-start.3
  52.1 5.2 %copy.16 = bf16[16,9,64,128]{2,0,3,1:T(8,128)(2,1)} copy(bf16[16,9,64,128]{3,2,1,0:T(8,128)(2,1)S(1)} %pad_maximum_fusion.1) | data formatting | bytes 4718592 | tf_op jit(solution)/shard_map/concatenate | solution.py:124
  57.3 0.0 copy-done.3
  57.3 3.9 %maximum_convert_fusion.1 = bf16[16,4,64,128]{3,0,2,1:T(8,128)(2,1)S(1)} fusion(bf16[16,9,64,128]{2,0,3,1:T(8,128)(2,1)} %copy.16, bf16[3,3,128,64]{2,3,1,0:T(8,128)(2,1)S(1)} %copy-done.3), kind=kOutput, calls=%fused_computation.17 | convolution fusion | flops 601882624 | bytes 3555328 | tf_op jit(solution)/shard_map/conv_general_dilated | solution.py:125
  61.3 0.2 fusion.17
  61.5 1.9 %collective-permute-start.5 = (bf16[1,4,64,128]{3,0,2,1:T(2,128)(2,1)S(1)}, bf16[1,4,64,128]{3,0,2,1:T(2,128)(2,1)S(1)}, u32[]{:S(2)}, u32[]{:S(2)}) collective-permute-start(bf16[1,4,64,128]{3,0,2,1:T(2,128)(2,1)S(1)} %get-tuple-element.11), channel_id=1, source_target_pairs={{0,16},{16,32},{32,48},{48,64},{64,80},{80,96},{96,112},{1,17},{17... | collective-permute-start | bytes 196616 | tf_op jit(solution)/shard_map/ppermute | solution.py:16
  63.4 3.4 %collective-permute-start.6 = (bf16[1,4,64,128]{3,0,2,1:T(2,128)(2,1)S(1)}, bf16[1,4,64,128]{3,0,2,1:T(2,128)(2,1)S(1)}, u32[]{:S(2)}, u32[]{:S(2)}) collective-permute-start(bf16[1,4,64,128]{3,0,2,1:T(2,128)(2,1)S(1)} %get-tuple-element.12), channel_id=1, source_target_pairs={{16,0},{32,16},{48,32},{64,48},{80,64},{96,80},{112,96},{17,1},{33... | collective-permute-start | bytes 196616 | tf_op jit(solution)/shard_map/ppermute | solution.py:19
  66.8 0.6 collective-permute-done.5
  67.4 4.0 %collective-permute-done.6 = bf16[1,4,64,128]{3,0,2,1:T(2,128)(2,1)S(1)} collective-permute-done((bf16[1,4,64,128]{3,0,2,1:T(2,128)(2,1)S(1)}, bf16[1,4,64,128]{3,0,2,1:T(2,128)(2,1)S(1)}, u32[]{:S(2)}, u32[]{:S(2)}) %collective-permute-start.6) | collective-permute-done | bytes 65568 | tf_op jit(solution)/shard_map/ppermute | solution.py:19
  71.4 0.4 pad_maximum_fusion.4
  71.9 9.3 %collective-permute-start.7 = (bf16[18,1,64,128]{3,0,2,1:T(8,128)(2,1)S(1)}, bf16[18,1,64,128]{3,0,2,1:T(8,128)(2,1)S(1)}, u32[]{:S(2)}, u32[]{:S(2)}) collective-permute-start(bf16[18,1,64,128]{3,0,2,1:T(8,128)(2,1)S(1)} %get-tuple-element.9), channel_id=1, source_target_pairs={{0,1},{1,2},{2,3},{3,4},{4,5},{5,6},{6,7},{7,8},{8,9},{9,10},{10,1... | collective-permute-start | bytes 884744 | tf_op jit(solution)/shard_map/ppermute | solution.py:16
  81.2 0.0 copy-start.2
  81.2 2.2 %collective-permute-start.8 = (bf16[18,1,64,128]{3,0,2,1:T(8,128)(2,1)S(1)}, bf16[18,1,64,128]{3,0,2,1:T(8,128)(2,1)S(1)}, u32[]{:S(2)}, u32[]{:S(2)}) collective-permute-start(bf16[18,1,64,128]{3,0,2,1:T(8,128)(2,1)S(1)} %get-tuple-element.10), channel_id=1, source_target_pairs={{1,0},{2,1},{3,2},{4,3},{5,4},{6,5},{7,6},{8,7},{9,8},{10,9},{11,1... | collective-permute-start | bytes 884744 | tf_op jit(solution)/shard_map/ppermute | solution.py:19
  83.4 2.4 %collective-permute-done.7 = bf16[18,1,64,128]{3,0,2,1:T(8,128)(2,1)S(1)} collective-permute-done((bf16[18,1,64,128]{3,0,2,1:T(8,128)(2,1)S(1)}, bf16[18,1,64,128]{3,0,2,1:T(8,128)(2,1)S(1)}, u32[]{:S(2)}, u32[]{:S(2)}) %collective-permute-start.7) | collective-permute-done | bytes 294944 | tf_op jit(solution)/shard_map/ppermute | solution.py:16
  85.9 8.2 %collective-permute-done.8 = bf16[18,1,64,128]{3,0,2,1:T(8,128)(2,1)S(1)} collective-permute-done((bf16[18,1,64,128]{3,0,2,1:T(8,128)(2,1)S(1)}, bf16[18,1,64,128]{3,0,2,1:T(8,128)(2,1)S(1)}, u32[]{:S(2)}, u32[]{:S(2)}) %collective-permute-start.8) | collective-permute-done | bytes 294944 | tf_op jit(solution)/shard_map/ppermute | solution.py:19
  94.0 0.0 copy-done
  94.0 8.6 %maximum_convert_fusion = bf16[18,4,64,288]{3,0,2,1:T(8,128)(2,1)S(1)} fusion(bf16[3,3,288,128]{3,2,1,0:T(8,128)(2,1)S(1)} %copy-done, bf16[18,1,64,128]{3,0,2,1:T(8,128)(2,1)S(1)} %collective-permute-done.8, bf16[1,4,64,128]{3,0,2,1:T(2,128)(2,1)S(1)} %collective-permute-done.6, bf16[16,4,64,128]{3,0,2,1:T(8,128)(2,1)S(1)} %maximum_convert_fusion.1, ...), kind=kOutput, calls=%fused_computation | convolution fusion | flops 3037298688 | bytes 5087232 | tf_op jit(solution)/shard_map/conv_general_dilated | solution.py:31
  102.7 0.0 copy-done.2
  102.7 2.2 %fusion = f32[16,4,64,128]{3,2,1,0:T(8,128)S(1)} fusion(bf16[18,4,64,288]{3,0,2,1:T(8,128)(2,1)S(1)} %maximum_convert_fusion, bf16[3,128,288]{1,2,0:T(8,128)(2,1)S(1)} %copy-done.2), kind=kOutput, calls=%fused_computation.1 | convolution fusion | flops 905969664 | bytes 4972544 | tf_op jit(solution)/shard_map/conv_general_dilated | solution.py:42
  104.9 1.4 %fusion.12 = bf16[16,4,64,128]{3,0,2,1:T(8,128)(2,1)S(1)} fusion(f32[16,4,64,128]{3,2,1,0:T(8,128)S(1)} %fusion, bf16[16,4,64,128]{3,0,2,1:T(8,128)(2,1)S(1)} %maximum_convert_fusion.1), kind=kLoop, calls=%fused_computation.16 | loop fusion | flops 2097152 | bytes 4194304 | tf_op jit(solution)/shard_map/convert_element_type | solution.py:56
  106.3 1.2 %copy.20 = bf16[16,4,64,128]{3,2,1,0:T(8,128)(2,1)} copy(bf16[16,4,64,128]{3,0,2,1:T(8,128)(2,1)S(1)} %fusion.12) | data formatting | bytes 2097152 | tf_op jit(solution)/shard_map/convert_element_type | solution.py:56
  (3 shorter events, 0.0 us)
Async XLA Ops:
  0.0 94.0 %copy-start = (bf16[3,3,288,128]{3,2,1,0:T(8,128)(2,1)S(1)}, bf16[3,3,288,128]{3,2,1,0:T(8,128)(2,1)}, u32[]{:S(2)}) copy-start(bf16[3,3,288,128]{3,2,1,0:T(8,128)(2,1)} %param.10) | copy-start | bytes 1990660
  1.1 6.3 %collective-permute-start = (bf16[1,8,64,128]{3,2,1,0:T(8,128)(2,1)S(1)}, bf16[1,8,64,128]{3,2,1,0:T(8,128)(2,1)S(1)}, u32[]{:S(2)}, u32[]{:S(2)}) collective-permute-start(bf16[1,8,64,128]{3,2,1,0:T(8,128)(2,1)S(1)} %get-tuple-element.8), channel_id=1, source_target_pairs={{0,16},{16,32},{32,48},{48,64},{64,80},{80,96},{96,112},{1,17},{17... | collective-permute-start | bytes 393224 | tf_op jit(solution)/shard_map/ppermute | solution.py:16
  4.5 7.8 %collective-permute-start.1 = (bf16[1,8,64,128]{3,2,1,0:T(8,128)(2,1)S(1)}, bf16[1,8,64,128]{3,2,1,0:T(8,128)(2,1)S(1)}, u32[]{:S(2)}, u32[]{:S(2)}) collective-permute-start(bf16[1,8,64,128]{3,2,1,0:T(8,128)(2,1)S(1)} %get-tuple-element.7), channel_id=1, source_target_pairs={{16,0},{32,16},{48,32},{64,48},{80,64},{96,80},{112,96},{17,1},{33... | collective-permute-start | bytes 393224 | tf_op jit(solution)/shard_map/ppermute | solution.py:19
  7.3 14.7 %copy-start.1 = (bf16[3,64,144]{2,1,0:T(8,128)(2,1)S(1)}, bf16[3,64,144]{2,1,0:T(8,128)(2,1)}, u32[]{:S(2)}) copy-start(bf16[3,64,144]{2,1,0:T(8,128)(2,1)} %param.8) | copy-start | bytes 165892
  13.2 10.8 %collective-permute-start.2 = (bf16[18,1,64,128]{3,2,1,0:T(8,128)(2,1)}, bf16[18,1,64,128]{3,2,1,0:T(8,128)(2,1)}, u32[]{:S(2)}, u32[]{:S(2)}) collective-permute-start(bf16[18,1,64,128]{3,2,1,0:T(8,128)(2,1)} %get-tuple-element.5), channel_id=1, source_target_pairs={{0,1},{1,2},{2,3},{3,4},{4,5},{5,6},{6,7},{7,8},{8,9},{9,10},{10,1... | collective-permute-start | bytes 884744 | tf_op jit(solution)/shard_map/ppermute | solution.py:16
  20.1 12.0 %collective-permute-start.3 = (bf16[18,1,64,128]{3,2,1,0:T(8,128)(2,1)}, bf16[18,1,64,128]{3,2,1,0:T(8,128)(2,1)}, u32[]{:S(2)}, u32[]{:S(2)}) collective-permute-start(bf16[18,1,64,128]{3,2,1,0:T(8,128)(2,1)} %get-tuple-element.6), channel_id=1, source_target_pairs={{1,0},{2,1},{3,2},{4,3},{5,4},{6,5},{7,6},{8,7},{9,8},{10,9},{11,1... | collective-permute-start | bytes 884744 | tf_op jit(solution)/shard_map/ppermute | solution.py:19
  46.6 5.2 %collective-permute-start.4 = (bf16[16,1,64,128]{3,2,1,0:T(8,128)(2,1)S(1)}, bf16[16,1,64,128]{3,2,1,0:T(8,128)(2,1)S(1)}, u32[]{:S(2)}, u32[]{:S(2)}) collective-permute-start(bf16[16,1,64,128]{3,2,1,0:T(8,128)(2,1)S(1)} %slice.38), channel_id=1, source_target_pairs={{0,1},{1,2},{2,3},{3,4},{4,5},{5,6},{6,7},{7,8},{8,9},{9,10},{10,1... | collective-permute-start | bytes 786440 | tf_op jit(solution)/shard_map/ppermute | solution.py:27
  52.0 5.3 %copy-start.3 = (bf16[3,3,128,64]{2,3,1,0:T(8,128)(2,1)S(1)}, bf16[3,3,128,64]{2,3,1,0:T(8,128)(2,1)}, u32[]{:S(2)}) copy-start(bf16[3,3,128,64]{2,3,1,0:T(8,128)(2,1)} %param.9) | copy-start | bytes 442372
  61.5 5.9 %collective-permute-start.5 = (bf16[1,4,64,128]{3,0,2,1:T(2,128)(2,1)S(1)}, bf16[1,4,64,128]{3,0,2,1:T(2,128)(2,1)S(1)}, u32[]{:S(2)}, u32[]{:S(2)}) collective-permute-start(bf16[1,4,64,128]{3,0,2,1:T(2,128)(2,1)S(1)} %get-tuple-element.11), channel_id=1, source_target_pairs={{0,16},{16,32},{32,48},{48,64},{64,80},{80,96},{96,112},{1,17},{17... | collective-permute-start | bytes 196616 | tf_op jit(solution)/shard_map/ppermute | solution.py:16
  63.4 8.0 %collective-permute-start.6 = (bf16[1,4,64,128]{3,0,2,1:T(2,128)(2,1)S(1)}, bf16[1,4,64,128]{3,0,2,1:T(2,128)(2,1)S(1)}, u32[]{:S(2)}, u32[]{:S(2)}) collective-permute-start(bf16[1,4,64,128]{3,0,2,1:T(2,128)(2,1)S(1)} %get-tuple-element.12), channel_id=1, source_target_pairs={{16,0},{32,16},{48,32},{64,48},{80,64},{96,80},{112,96},{17,1},{33... | collective-permute-start | bytes 196616 | tf_op jit(solution)/shard_map/ppermute | solution.py:19
  71.9 14.0 %collective-permute-start.7 = (bf16[18,1,64,128]{3,0,2,1:T(8,128)(2,1)S(1)}, bf16[18,1,64,128]{3,0,2,1:T(8,128)(2,1)S(1)}, u32[]{:S(2)}, u32[]{:S(2)}) collective-permute-start(bf16[18,1,64,128]{3,0,2,1:T(8,128)(2,1)S(1)} %get-tuple-element.9), channel_id=1, source_target_pairs={{0,1},{1,2},{2,3},{3,4},{4,5},{5,6},{6,7},{7,8},{8,9},{9,10},{10,1... | collective-permute-start | bytes 884744 | tf_op jit(solution)/shard_map/ppermute | solution.py:16
  81.2 21.5 %copy-start.2 = (bf16[3,128,288]{1,2,0:T(8,128)(2,1)S(1)}, bf16[3,128,288]{1,2,0:T(8,128)(2,1)}, u32[]{:S(2)}) copy-start(bf16[3,128,288]{1,2,0:T(8,128)(2,1)} %param.11) | copy-start | bytes 663556
  81.2 12.8 %collective-permute-start.8 = (bf16[18,1,64,128]{3,0,2,1:T(8,128)(2,1)S(1)}, bf16[18,1,64,128]{3,0,2,1:T(8,128)(2,1)S(1)}, u32[]{:S(2)}, u32[]{:S(2)}) collective-permute-start(bf16[18,1,64,128]{3,0,2,1:T(8,128)(2,1)S(1)} %get-tuple-element.10), channel_id=1, source_target_pairs={{1,0},{2,1},{3,2},{4,3},{5,4},{6,5},{7,6},{8,7},{9,8},{10,9},{11,1... | collective-permute-start | bytes 884744 | tf_op jit(solution)/shard_map/ppermute | solution.py:19

commit v4 on v3

--- a/solution.py
+++ b/solution.py
@@ -117,6 +117,63 @@
     )(padded, w9, t3)
 
 
+def _sublane_shift(x, by, axis):
+    size = x.shape[axis]
+    rolled = pltpu.roll(x, (-by) % size, axis)
+    index = lax.broadcasted_iota(jnp.int32, x.shape, axis)
+    inside = jnp.logical_and(index + by >= 0, index + by < size)
+    return jnp.where(inside, rolled, jnp.zeros_like(rolled))
+
+
+def _block_two_kernel(xp_ref, w9_ref, t3_ref, out_ref, mid_ref):
+    frames_p, rows_p, width, channels = xp_ref.shape
+    rows = rows_p - 2
+    frames = frames_p - 2
+
+    def middle(f, carry):
+        slab = xp_ref[f].astype(jnp.float32)
+        shifted = [_sublane_shift(slab, b - 1, 1).astype(jnp.bfloat16) for b in range(3)]
+        stacked = jnp.concatenate(
+            [
+                jnp.concatenate([shifted[b][i + a] for a in range(3) for b in range(3)], axis=1)
+                for i in range(rows)
+            ],
+            axis=0,
+        )
+        m = jnp.dot(stacked, w9_ref[...], preferred_element_type=jnp.float32)
+        mid_ref[f] = jnp.maximum(m, 0.0).astype(jnp.bfloat16)
+        return carry
+
+    lax.fori_loop(0, frames_p, middle, 0)
+
+    def section(t, carry):
+        s = jnp.dot(mid_ref[t], t3_ref[0], preferred_element_type=jnp.float32)
+        s = s + jnp.dot(mid_ref[t + 1], t3_ref[1], preferred_element_type=jnp.float32)
+        s = s + jnp.dot(mid_ref[t + 2], t3_ref[2], preferred_element_type=jnp.float32)
+        for i in range(rows):
+            v = s[i * width : (i + 1) * width] + xp_ref[t + 1, i + 1].astype(jnp.float32)
+            out_ref[t, i] = jnp.maximum(v, 0.0).astype(out_ref.dtype)
+        return carry
+
+    lax.fori_loop(0, frames, section, 0)
+
+
+def block_two(padded, spatial_kernel, temporal_kernel):
+    frames_p, rows_p, width, channels = padded.shape
+    mids = spatial_kernel.shape[2]
+    w9 = jnp.transpose(spatial_kernel, (0, 1, 3, 2)).reshape(9 * channels, mids)
+    t3 = jnp.transpose(temporal_kernel, (0, 2, 1))
+    vmem = pltpu.MemorySpace.VMEM if hasattr(pltpu, "MemorySpace") else pltpu.VMEM
+    return pl.pallas_call(
+        _block_two_kernel,
+        out_shape=jax.ShapeDtypeStruct((frames_p - 2, rows_p - 2, width, channels), padded.dtype),
+        in_specs=[pl.BlockSpec(memory_space=vmem)] * 3,
+        out_specs=pl.BlockSpec(memory_space=vmem),
+        scratch_shapes=[pltpu.VMEM((frames_p, (rows_p - 2) * width, mids), jnp.bfloat16)],
+        compiler_params=pltpu.CompilerParams(vmem_limit_bytes=48 * 1024 * 1024),
+    )(padded, w9, t3)
+
+
 def on_device(video_clip, spatial_one, temporal_one, down_weight, spatial_two, temporal_two):
     padded = padded_2(video_clip, (("tm", 0), ("row", 1)), 1)
     section_one = block_one(padded, spatial_one, temporal_one)
@@ -131,7 +188,8 @@
         preferred_element_type=jnp.float32,
     )
     reduced = jax.nn.relu(reduced).astype(jnp.bfloat16)
-    return residual_block(reduced, spatial_two, temporal_two, "NHWC", "HWNC")
+    padded_two = padded_2(reduced, (("tm", 0), ("row", 1)), 1)
+    return block_two(padded_two, spatial_two, temporal_two)
 
 
 def solution(mesh):

time: 108 us -> 108 us (level)
  Pallas kernels: 13.1 us -> 27.4 us
  matrix products: 14.8 us -> 3.94 us
  waiting for transfers between devices: 31.1 us -> 29 us
  local copies, waits for them, and re-layouts: 12 us -> 10.9 us
    pallas_call x0 -> x1, Pallas kernels: none -> 14.3 us  [block_two(): pl.pallas_call(_block_two_kernel, out_shape=jax.ShapeDtypeStruct((frames_...]
    conv_general_dilated x2 -> x0, matrix products: 10.8 us -> none  [the longest x1 8.63 us: spatial(): lax.conv_general_dilated(source, kernel, (1, 1), ((0, 0), (1, 1)), dimens...]
    ppermute x4, waiting for transfers between devices: 4.62 us -> 3.14 us  [padded_2(): lax.ppermute(lax.slice_in_dim(block, block.shape[dim] - width, None, axis...]
    convert_element_type x1 -> x0, local copies, waits for them, and re-layouts: 1.24 us -> none  [residual_block(): return jax.nn.relu(summed).astype(jnp.bfloat16)]
  transfers between devices with their start and end apart: 9 -> 9, of which waited for: 9 -> 8; matrix products, arithmetic and copies ran while one was open for 3% -> 3% of each run, Pallas kernels for 0% -> 0%
where the time goes in v4:
time: 108 us; the launch traced here: 107 us
  starting transfers between devices  32.8 us (30%)
  waiting for transfers between devices  29 us (27%)
  Pallas kernels  27.4 us (25%)
  local copies, waits for them, and re-layouts  10.9 us (10%)
  matrix products  3.94 us (4%)
  other arithmetic  2.96 us (3%)
    ppermute x4, waiting for transfers between devices, padded_2(): lax.ppermute(lax.slice_in_dim(block, 0, width, axis=dim), axis, backward)  22.5 us
    ppermute x4, starting transfers between devices, padded_2(): lax.ppermute(lax.slice_in_dim(block, block.shape[dim] - width, None, axis...  21.8 us
    pallas_call x1, Pallas kernels, block_two(): pl.pallas_call(_block_two_kernel, out_shape=jax.ShapeDtypeStruct((frames_...  14.3 us
    pallas_call x1, Pallas kernels, block_one(): pl.pallas_call(_block_one_kernel, out_shape=jax.ShapeDtypeStruct((frames_...  13.1 us
    ppermute x4, starting transfers between devices, padded_2(): lax.ppermute(lax.slice_in_dim(block, 0, width, axis=dim), axis, backward)  9.12 us
    concatenate x1, local copies, waits for them, and re-layouts, on_device(): joined = jnp.concatenate([upper_row, section_one], axis=1)  5.25 us
    conv_general_dilated x1, matrix products, on_device(): lax.conv_general_dilated(joined, down_weight, (2, 2), ((0, 0), (1, 1)), d...  3.94 us
    ppermute x1, waiting for transfers between devices, from_behind(): return lax.ppermute(array, axis, pairs)  3.29 us
  transfers between devices with their start and end apart: 9, of which 8 were waited for; matrix products, arithmetic and copies ran while one was open for 3% of the time, Pallas kernels for 0%

profile of v4, /device:TPU:31, one launch (start us, length us, event | category | flops | bytes accessed | tf_op | source)
XLA Modules:
  0.0 107.3 jit_solution(7714593016176854649)
XLA Ops:
  0.0 0.0 copy-start
  0.0 1.0 fusion.2
  1.0 3.5 %collective-permute-start = (bf16[1,8,64,128]{3,2,1,0:T(8,128)(2,1)S(1)}, bf16[1,8,64,128]{3,2,1,0:T(8,128)(2,1)S(1)}, u32[]{:S(2)}, u32[]{:S(2)}) collective-permute-start(bf16[1,8,64,128]{3,2,1,0:T(8,128)(2,1)S(1)} %get-tuple-element.8), channel_id=1, source_target_pairs={{0,16},{16,32},{32,48},{48,64},{64,80},{80,96},{96,112},{1,17},{17... | collective-permute-start | bytes 393224 | tf_op jit(solution)/shard_map/ppermute | solution.py:16
  4.5 1.9 %collective-permute-start.1 = (bf16[1,8,64,128]{3,2,1,0:T(8,128)(2,1)S(1)}, bf16[1,8,64,128]{3,2,1,0:T(8,128)(2,1)S(1)}, u32[]{:S(2)}, u32[]{:S(2)}) collective-permute-start(bf16[1,8,64,128]{3,2,1,0:T(8,128)(2,1)S(1)} %get-tuple-element.7), channel_id=1, source_target_pairs={{16,0},{32,16},{48,32},{64,48},{80,64},{96,80},{112,96},{17,1},{33... | collective-permute-start | bytes 393224 | tf_op jit(solution)/shard_map/ppermute | solution.py:19
  6.4 0.9 collective-permute-done
  7.3 0.0 copy-start.5
  7.3 2.0 %constant_dynamic-update-slice_fusion.1 = bf16[18,8,64,128]{3,2,1,0:T(8,128)(2,1)S(1)} fusion(bf16[18,8,64,128]{3,2,1,0:T(8,128)(2,1)S(1)} %constant_dynamic-update-slice_fusion.2, bf16[16,8,64,128]{3,2,1,0:T(8,128)(2,1)} %param.6), kind=kLoop, calls=%fused_computation.9 | loop fusion | bytes 4194304
  9.3 3.0 %collective-permute-done.1 = bf16[1,8,64,128]{3,2,1,0:T(8,128)(2,1)S(1)} collective-permute-done((bf16[1,8,64,128]{3,2,1,0:T(8,128)(2,1)S(1)}, bf16[1,8,64,128]{3,2,1,0:T(8,128)(2,1)S(1)}, u32[]{:S(2)}, u32[]{:S(2)}) %collective-permute-start.1) | collective-permute-done | bytes 131104 | tf_op jit(solution)/shard_map/ppermute | solution.py:19
  12.3 0.9 fusion.1
  13.2 6.8 %collective-permute-start.2 = (bf16[18,1,64,128]{3,2,1,0:T(8,128)(2,1)}, bf16[18,1,64,128]{3,2,1,0:T(8,128)(2,1)S(1)}, u32[]{:S(2)}, u32[]{:S(2)}) collective-permute-start(bf16[18,1,64,128]{3,2,1,0:T(8,128)(2,1)} %get-tuple-element.5), channel_id=1, source_target_pairs={{0,1},{1,2},{2,3},{3,4},{4,5},{5,6},{6,7},{7,8},{8,9},{9,10},{10,1... | collective-permute-start | bytes 884744 | tf_op jit(solution)/shard_map/ppermute | solution.py:16
  20.0 1.9 %collective-permute-start.3 = (bf16[18,1,64,128]{3,2,1,0:T(8,128)(2,1)}, bf16[18,1,64,128]{3,2,1,0:T(8,128)(2,1)S(1)}, u32[]{:S(2)}, u32[]{:S(2)}) collective-permute-start(bf16[18,1,64,128]{3,2,1,0:T(8,128)(2,1)} %get-tuple-element.6), channel_id=1, source_target_pairs={{1,0},{2,1},{3,2},{4,3},{5,4},{6,5},{7,6},{8,7},{9,8},{10,9},{11,1... | collective-permute-start | bytes 884744 | tf_op jit(solution)/shard_map/ppermute | solution.py:19
  22.0 0.0 copy-done.5
  22.0 0.1 copy.12
  22.1 0.1 reshape.10.t3_ref
  22.2 1.1 %copy.13.w9_ref = bf16[144,576]{1,0:T(8,128)(2,1)S(1)} copy(bf16[144,576]{0,1:T(8,128)(2,1)} %bitcast.12) | data formatting | bytes 331776 | tf_op jit(solution)/shard_map/reshape | solution.py:107
  23.3 0.7 collective-permute-done.2
  24.0 7.9 %collective-permute-done.3 = bf16[18,1,64,128]{3,2,1,0:T(8,128)(2,1)S(1)} collective-permute-done((bf16[18,1,64,128]{3,2,1,0:T(8,128)(2,1)}, bf16[18,1,64,128]{3,2,1,0:T(8,128)(2,1)S(1)}, u32[]{:S(2)}, u32[]{:S(2)}) %collective-permute-start.3) | collective-permute-done | bytes 294944 | tf_op jit(solution)/shard_map/ppermute | solution.py:19
  31.9 0.4 pad_maximum_fusion.xp_ref
  32.3 13.1 %shard_map.64 = bf16[16,8,64,128]{3,2,1,0:T(8,128)(2,1)S(1)} custom-call(bf16[18,10,64,128]{3,2,1,0:T(8,128)(2,1)S(1)} %pad_maximum_fusion.xp_ref, bf16[144,576]{1,0:T(8,128)(2,1)S(1)} %copy.13.w9_ref, bf16[64,432]{1,0:T(8,128)(2,1)S(1)} %reshape.10.t3_ref), custom_call_target="tpu_custom_call" | custom-call | tf_op jit(solution)/shard_map/pallas_call | solution.py:110
  45.4 1.9 %collective-permute-start.4 = (bf16[16,1,64,128]{3,2,1,0:T(8,128)(2,1)S(1)}, bf16[16,1,64,128]{3,2,1,0:T(8,128)(2,1)S(1)}, u32[]{:S(2)}, u32[]{:S(2)}) collective-permute-start(bf16[16,1,64,128]{3,2,1,0:T(8,128)(2,1)S(1)} %slice.38), channel_id=1, source_target_pairs={{0,1},{1,2},{2,3},{3,4},{4,5},{5,6},{6,7},{7,8},{8,9},{9,10},{10,1... | collective-permute-start | bytes 786440 | tf_op jit(solution)/shard_map/ppermute | solution.py:27
  47.4 3.3 %collective-permute-done.4 = bf16[16,1,64,128]{3,2,1,0:T(8,128)(2,1)S(1)} collective-permute-done((bf16[16,1,64,128]{3,2,1,0:T(8,128)(2,1)S(1)}, bf16[16,1,64,128]{3,2,1,0:T(8,128)(2,1)S(1)}, u32[]{:S(2)}, u32[]{:S(2)}) %collective-permute-start.4) | collective-permute-done | bytes 262176 | tf_op jit(solution)/shard_map/ppermute | solution.py:27
  50.6 0.2 pad_maximum_fusion.1
  50.9 5.3 %copy.14 = bf16[16,9,64,128]{2,0,3,1:T(8,128)(2,1)} copy(bf16[16,9,64,128]{3,2,1,0:T(8,128)(2,1)S(1)} %pad_maximum_fusion.1) | data formatting | bytes 4718592 | tf_op jit(solution)/shard_map/concatenate | solution.py:181
  56.1 0.0 copy-done
  56.1 3.9 %fusion.4 = bf16[16,4,64,128]{3,0,2,1:T(8,128)(2,1)S(1)} fusion(bf16[16,9,64,128]{2,0,3,1:T(8,128)(2,1)} %copy.14, bf16[3,3,128,64]{2,3,1,0:T(8,128)(2,1)S(1)} %copy-done), kind=kOutput, calls=%fused_computation.14 | convolution fusion | flops 600834048 | bytes 3555328 | tf_op jit(solution)/shard_map/conv_general_dilated | solution.py:182
  60.1 0.0 copy-start.2
  60.1 0.3 fusion
  60.4 1.9 %collective-permute-start.5 = (bf16[1,4,64,128]{3,2,1,0:T(8,128)(2,1)S(1)}, bf16[1,4,64,128]{3,2,1,0:T(8,128)(2,1)S(1)}, u32[]{:S(2)}, u32[]{:S(2)}) collective-permute-start(bf16[1,4,64,128]{3,2,1,0:T(8,128)(2,1)S(1)} %get-tuple-element.11), channel_id=1, source_target_pairs={{0,16},{16,32},{32,48},{48,64},{64,80},{80,96},{96,112},{1,17},{17... | collective-permute-start | bytes 196616 | tf_op jit(solution)/shard_map/ppermute | solution.py:16
  62.4 3.4 %collective-permute-start.6 = (bf16[1,4,64,128]{3,2,1,0:T(8,128)(2,1)S(1)}, bf16[1,4,64,128]{3,2,1,0:T(8,128)(2,1)S(1)}, u32[]{:S(2)}, u32[]{:S(2)}) collective-permute-start(bf16[1,4,64,128]{3,2,1,0:T(8,128)(2,1)S(1)} %get-tuple-element.12), channel_id=1, source_target_pairs={{16,0},{32,16},{48,32},{64,48},{80,64},{96,80},{112,96},{17,1},{33... | collective-permute-start | bytes 196616 | tf_op jit(solution)/shard_map/ppermute | solution.py:19
  65.7 0.0 collective-permute-done.5
  65.7 0.0 copy-start.3
  65.8 3.7 %collective-permute-done.6 = bf16[1,4,64,128]{3,2,1,0:T(8,128)(2,1)S(1)} collective-permute-done((bf16[1,4,64,128]{3,2,1,0:T(8,128)(2,1)S(1)}, bf16[1,4,64,128]{3,2,1,0:T(8,128)(2,1)S(1)}, u32[]{:S(2)}, u32[]{:S(2)}) %collective-permute-start.6) | collective-permute-done | bytes 65568 | tf_op jit(solution)/shard_map/ppermute | solution.py:19
  69.5 0.0 copy-start.4
  69.5 0.9 pad_maximum_fusion.5
  70.4 9.5 %collective-permute-start.7 = (bf16[18,1,64,128]{3,2,1,0:T(8,128)(2,1)}, bf16[18,1,64,128]{3,2,1,0:T(8,128)(2,1)S(1)}, u32[]{:S(2)}, u32[]{:S(2)}) collective-permute-start(bf16[18,1,64,128]{3,2,1,0:T(8,128)(2,1)} %get-tuple-element.9), channel_id=1, source_target_pairs={{0,1},{1,2},{2,3},{3,4},{4,5},{5,6},{6,7},{7,8},{8,9},{9,10},{10,1... | collective-permute-start | bytes 884744 | tf_op jit(solution)/shard_map/ppermute | solution.py:16
  79.9 1.9 %collective-permute-start.8 = (bf16[18,1,64,128]{3,2,1,0:T(8,128)(2,1)}, bf16[18,1,64,128]{3,2,1,0:T(8,128)(2,1)S(1)}, u32[]{:S(2)}, u32[]{:S(2)}) collective-permute-start(bf16[18,1,64,128]{3,2,1,0:T(8,128)(2,1)} %get-tuple-element.10), channel_id=1, source_target_pairs={{1,0},{2,1},{3,2},{4,3},{5,4},{6,5},{7,6},{8,7},{9,8},{10,9},{11,1... | collective-permute-start | bytes 884744 | tf_op jit(solution)/shard_map/ppermute | solution.py:19
  81.9 0.0 copy-done.3
  81.9 0.0 copy-done.4
  81.9 0.0 copy-done.2
  81.9 0.0 copy-start.1
  81.9 0.4 copy.16
  82.3 1.6 %collective-permute-done.7 = bf16[18,1,64,128]{3,2,1,0:T(8,128)(2,1)S(1)} collective-permute-done((bf16[18,1,64,128]{3,2,1,0:T(8,128)(2,1)}, bf16[18,1,64,128]{3,2,1,0:T(8,128)(2,1)S(1)}, u32[]{:S(2)}, u32[]{:S(2)}) %collective-permute-start.7) | collective-permute-done | bytes 294944 | tf_op jit(solution)/shard_map/ppermute | solution.py:16
  83.9 7.9 %collective-permute-done.8 = bf16[18,1,64,128]{3,2,1,0:T(8,128)(2,1)S(1)} collective-permute-done((bf16[18,1,64,128]{3,2,1,0:T(8,128)(2,1)}, bf16[18,1,64,128]{3,2,1,0:T(8,128)(2,1)S(1)}, u32[]{:S(2)}, u32[]{:S(2)}) %collective-permute-start.8) | collective-permute-done | bytes 294944 | tf_op jit(solution)/shard_map/ppermute | solution.py:19
  91.8 1.2 %pad_maximum_fusion.2.xp_ref = bf16[18,6,64,128]{3,2,1,0:T(8,128)(2,1)S(1)} fusion(bf16[18,1,64,128]{3,2,1,0:T(8,128)(2,1)S(1)} %collective-permute-done.8, bf16[1,4,64,128]{3,2,1,0:T(8,128)(2,1)} %copy-done.4, bf16[16,4,64,128]{3,2,1,0:T(8,128)(2,1)S(1)} %fusion, bf16[1,4,64,128]{3,2,1,0:T(8,128)(2,1)} %copy-done.3, ...), kind=kLoop, calls=%fused_computation.4 | loop fusion | flops 3538944 | bytes 3538944 | tf_op jit(solution)/shard_map/concatenate | solution.py:20
  93.0 0.0 copy-done.1
  93.0 14.3 %shard_map.65 = bf16[16,4,64,128]{3,2,1,0:T(8,128)(2,1)} custom-call(bf16[18,6,64,128]{3,2,1,0:T(8,128)(2,1)S(1)} %pad_maximum_fusion.2.xp_ref, bf16[1152,288]{1,0:T(8,128)(2,1)S(1)} %bitcast.9, bf16[3,288,128]{2,1,0:T(8,128)(2,1)S(1)} %bitcast.10), custom_call_target="tpu_custom_call" | custom-call | tf_op jit(solution)/shard_map/pallas_call | solution.py:167
  (4 shorter events, 0.1 us)
Async XLA Ops:
  0.0 56.1 %copy-start = (bf16[3,3,128,64]{2,3,1,0:T(8,128)(2,1)S(1)}, bf16[3,3,128,64]{2,3,1,0:T(8,128)(2,1)}, u32[]{:S(2)}) copy-start(bf16[3,3,128,64]{2,3,1,0:T(8,128)(2,1)} %param.9) | copy-start | bytes 442372
  1.0 6.3 %collective-permute-start = (bf16[1,8,64,128]{3,2,1,0:T(8,128)(2,1)S(1)}, bf16[1,8,64,128]{3,2,1,0:T(8,128)(2,1)S(1)}, u32[]{:S(2)}, u32[]{:S(2)}) collective-permute-start(bf16[1,8,64,128]{3,2,1,0:T(8,128)(2,1)S(1)} %get-tuple-element.8), channel_id=1, source_target_pairs={{0,16},{16,32},{32,48},{48,64},{64,80},{80,96},{96,112},{1,17},{17... | collective-permute-start | bytes 393224 | tf_op jit(solution)/shard_map/ppermute | solution.py:16
  4.5 7.8 %collective-permute-start.1 = (bf16[1,8,64,128]{3,2,1,0:T(8,128)(2,1)S(1)}, bf16[1,8,64,128]{3,2,1,0:T(8,128)(2,1)S(1)}, u32[]{:S(2)}, u32[]{:S(2)}) collective-permute-start(bf16[1,8,64,128]{3,2,1,0:T(8,128)(2,1)S(1)} %get-tuple-element.7), channel_id=1, source_target_pairs={{16,0},{32,16},{48,32},{64,48},{80,64},{96,80},{112,96},{17,1},{33... | collective-permute-start | bytes 393224 | tf_op jit(solution)/shard_map/ppermute | solution.py:19
  7.3 14.7 %copy-start.5 = (bf16[3,64,144]{2,1,0:T(8,128)(2,1)S(1)}, bf16[3,64,144]{2,1,0:T(8,128)(2,1)}, u32[]{:S(2)}) copy-start(bf16[3,64,144]{2,1,0:T(8,128)(2,1)} %param.8) | copy-start | bytes 165892
  13.2 10.8 %collective-permute-start.2 = (bf16[18,1,64,128]{3,2,1,0:T(8,128)(2,1)}, bf16[18,1,64,128]{3,2,1,0:T(8,128)(2,1)S(1)}, u32[]{:S(2)}, u32[]{:S(2)}) collective-permute-start(bf16[18,1,64,128]{3,2,1,0:T(8,128)(2,1)} %get-tuple-element.5), channel_id=1, source_target_pairs={{0,1},{1,2},{2,3},{3,4},{4,5},{5,6},{6,7},{7,8},{8,9},{9,10},{10,1... | collective-permute-start | bytes 884744 | tf_op jit(solution)/shard_map/ppermute | solution.py:16
  20.0 11.9 %collective-permute-start.3 = (bf16[18,1,64,128]{3,2,1,0:T(8,128)(2,1)}, bf16[18,1,64,128]{3,2,1,0:T(8,128)(2,1)S(1)}, u32[]{:S(2)}, u32[]{:S(2)}) collective-permute-start(bf16[18,1,64,128]{3,2,1,0:T(8,128)(2,1)} %get-tuple-element.6), channel_id=1, source_target_pairs={{1,0},{2,1},{3,2},{4,3},{5,4},{6,5},{7,6},{8,7},{9,8},{10,9},{11,1... | collective-permute-start | bytes 884744 | tf_op jit(solution)/shard_map/ppermute | solution.py:19
  45.4 5.2 %collective-permute-start.4 = (bf16[16,1,64,128]{3,2,1,0:T(8,128)(2,1)S(1)}, bf16[16,1,64,128]{3,2,1,0:T(8,128)(2,1)S(1)}, u32[]{:S(2)}, u32[]{:S(2)}) collective-permute-start(bf16[16,1,64,128]{3,2,1,0:T(8,128)(2,1)S(1)} %slice.38), channel_id=1, source_target_pairs={{0,1},{1,2},{2,3},{3,4},{4,5},{5,6},{6,7},{7,8},{8,9},{9,10},{10,1... | collective-permute-start | bytes 786440 | tf_op jit(solution)/shard_map/ppermute | solution.py:27
  60.1 21.8 %copy-start.2 = (bf16[3,3,288,128]{3,2,1,0:T(8,128)(2,1)S(1)}, bf16[3,3,288,128]{3,2,1,0:T(8,128)(2,1)}, u32[]{:S(2)}) copy-start(bf16[3,3,288,128]{3,2,1,0:T(8,128)(2,1)} %param.10) | copy-start | bytes 1990660
  60.4 5.3 %collective-permute-start.5 = (bf16[1,4,64,128]{3,2,1,0:T(8,128)(2,1)S(1)}, bf16[1,4,64,128]{3,2,1,0:T(8,128)(2,1)S(1)}, u32[]{:S(2)}, u32[]{:S(2)}) collective-permute-start(bf16[1,4,64,128]{3,2,1,0:T(8,128)(2,1)S(1)} %get-tuple-element.11), channel_id=1, source_target_pairs={{0,16},{16,32},{32,48},{48,64},{64,80},{80,96},{96,112},{1,17},{17... | collective-permute-start | bytes 196616 | tf_op jit(solution)/shard_map/ppermute | solution.py:16
  62.4 7.1 %collective-permute-start.6 = (bf16[1,4,64,128]{3,2,1,0:T(8,128)(2,1)S(1)}, bf16[1,4,64,128]{3,2,1,0:T(8,128)(2,1)S(1)}, u32[]{:S(2)}, u32[]{:S(2)}) collective-permute-start(bf16[1,4,64,128]{3,2,1,0:T(8,128)(2,1)S(1)} %get-tuple-element.12), channel_id=1, source_target_pairs={{16,0},{32,16},{48,32},{64,48},{80,64},{96,80},{112,96},{17,1},{33... | collective-permute-start | bytes 196616 | tf_op jit(solution)/shard_map/ppermute | solution.py:19
  65.7 16.1 %copy-start.3 = (bf16[1,4,64,128]{3,2,1,0:T(8,128)(2,1)}, bf16[1,4,64,128]{3,2,1,0:T(8,128)(2,1)S(1)}, u32[]{:S(2)}) copy-start(bf16[1,4,64,128]{3,2,1,0:T(8,128)(2,1)S(1)} %collective-permute-done.5) | copy-start | bytes 196612
  69.5 12.4 %copy-start.4 = (bf16[1,4,64,128]{3,2,1,0:T(8,128)(2,1)}, bf16[1,4,64,128]{3,2,1,0:T(8,128)(2,1)S(1)}, u32[]{:S(2)}) copy-start(bf16[1,4,64,128]{3,2,1,0:T(8,128)(2,1)S(1)} %collective-permute-done.6) | copy-start | bytes 196612
  70.4 13.5 %collective-permute-start.7 = (bf16[18,1,64,128]{3,2,1,0:T(8,128)(2,1)}, bf16[18,1,64,128]{3,2,1,0:T(8,128)(2,1)S(1)}, u32[]{:S(2)}, u32[]{:S(2)}) collective-permute-start(bf16[18,1,64,128]{3,2,1,0:T(8,128)(2,1)} %get-tuple-element.9), channel_id=1, source_target_pairs={{0,1},{1,2},{2,3},{3,4},{4,5},{5,6},{6,7},{7,8},{8,9},{9,10},{10,1... | collective-permute-start | bytes 884744 | tf_op jit(solution)/shard_map/ppermute | solution.py:16
  79.9 11.9 %collective-permute-start.8 = (bf16[18,1,64,128]{3,2,1,0:T(8,128)(2,1)}, bf16[18,1,64,128]{3,2,1,0:T(8,128)(2,1)S(1)}, u32[]{:S(2)}, u32[]{:S(2)}) collective-permute-start(bf16[18,1,64,128]{3,2,1,0:T(8,128)(2,1)} %get-tuple-element.10), channel_id=1, source_target_pairs={{1,0},{2,1},{3,2},{4,3},{5,4},{6,5},{7,6},{8,7},{9,8},{10,9},{11,1... | collective-permute-start | bytes 884744 | tf_op jit(solution)/shard_map/ppermute | solution.py:19
  81.9 11.1 %copy-start.1 = (bf16[3,128,288]{1,2,0:T(8,128)(2,1)S(1)}, bf16[3,128,288]{1,2,0:T(8,128)(2,1)}, u32[]{:S(2)}) copy-start(bf16[3,128,288]{1,2,0:T(8,128)(2,1)} %param.11) | copy-start | bytes 663556

commit v5 on v4

--- a/solution.py
+++ b/solution.py
@@ -64,10 +64,11 @@
     return jnp.where(inside, rolled, jnp.zeros_like(rolled))
 
 
-def _block_one_kernel(xp_ref, w9_ref, t3_ref, out_ref, mid_ref):
-    frames_p, rows_p = xp_ref.shape[0], xp_ref.shape[1]
+def _block_one_kernel(keep_ref, xp_ref, w9_ref, t3_ref, wd_ref, out_ref, mid_ref):
+    frames_p, rows_p, channels, width = xp_ref.shape
     rows = rows_p - 2
     frames = frames_p - 2
+    reduced_rows = (rows - 1) // 2
 
     def middle(f, carry):
         slab = xp_ref[f].astype(jnp.float32)
@@ -79,42 +80,81 @@
         stacked = jnp.concatenate(parts, axis=0)
         m = jnp.dot(w9_ref[...], stacked, preferred_element_type=jnp.float32)
         m = jnp.maximum(m, 0.0).astype(jnp.bfloat16)
-        width = out_ref.shape[-1]
         for h in range(rows):
             mid_ref[f, h] = m[:, h * width : (h + 1) * width]
         return carry
 
     lax.fori_loop(0, frames_p, middle, 0)
 
+    lane = lax.broadcasted_iota(jnp.int32, (width // 2, width), 1)
+    column = lax.broadcasted_iota(jnp.int32, (width // 2, width), 0)
+    pick = (lane == 2 * column).astype(jnp.bfloat16)
+    keep_first = keep_ref[0].astype(jnp.float32)
+
     def section(t, carry):
-        width = out_ref.shape[-1]
         parts = []
         for k in range(3):
             parts.append(jnp.concatenate([mid_ref[t + k, h] for h in range(rows)], axis=1))
         stacked = jnp.concatenate(parts, axis=0)
         s = jnp.dot(t3_ref[...], stacked, preferred_element_type=jnp.float32)
+        sec = []
         for h in range(rows):
             v = s[:, h * width : (h + 1) * width] + xp_ref[t + 1, h + 1].astype(jnp.float32)
-            out_ref[t, h] = jnp.maximum(v, 0.0).astype(out_ref.dtype)
+            v = jnp.maximum(v, 0.0)
+            if h == 0:
+                v = v * keep_first
+            sec.append(v.astype(jnp.bfloat16).astype(jnp.float32))
+        shifted = [[_lane_shift(r, b - 1).astype(jnp.bfloat16) for b in range(3)] for r in sec]
+        parts = []
+        for a in range(3):
+            for b in range(3):
+                parts.append(
+                    jnp.concatenate([shifted[2 * i + a][b] for i in range(reduced_rows)], axis=1)
+                )
+        stacked = jnp.concatenate(parts, axis=0)
+        full = jnp.dot(wd_ref[...], stacked, preferred_element_type=jnp.float32)
+        full = jnp.maximum(full, 0.0).astype(jnp.bfloat16)
+        for i in range(reduced_rows):
+            r = lax.dot_general(
+                pick,
+                full[:, i * width : (i + 1) * width],
+                (((1,), (1,)), ((), ())),
+                preferred_element_type=jnp.float32,
+            )
+            out_ref[t, i] = r.astype(out_ref.dtype)
         return carry
 
     lax.fori_loop(0, frames, section, 0)
 
 
-def block_one(padded, spatial_kernel, temporal_kernel):
+def block_one(padded, keep_first, spatial_kernel, temporal_kernel, down_kernel):
     frames_p, rows_p, channels, width = padded.shape
     mids = spatial_kernel.shape[2]
+    outs = down_kernel.shape[2]
     w9 = jnp.transpose(spatial_kernel, (2, 0, 1, 3)).reshape(mids, 9 * channels)
     t3 = jnp.transpose(temporal_kernel, (1, 0, 2)).reshape(channels, 3 * mids)
+    wd = jnp.transpose(down_kernel, (2, 0, 1, 3)).reshape(outs, 9 * channels)
     vmem = pltpu.MemorySpace.VMEM if hasattr(pltpu, "MemorySpace") else pltpu.VMEM
+    smem = pltpu.MemorySpace.SMEM if hasattr(pltpu, "MemorySpace") else pltpu.SMEM
+    reduced_rows = (rows_p - 3) // 2
     return pl.pallas_call(
         _block_one_kernel,
-        out_shape=jax.ShapeDtypeStruct((frames_p - 2, rows_p - 2, channels, width), padded.dtype),
-        in_specs=[pl.BlockSpec(memory_space=vmem)] * 3,
+        out_shape=jax.ShapeDtypeStruct((frames_p - 2, reduced_rows, width // 2, outs), padded.dtype),
+        in_specs=[pl.BlockSpec(memory_space=smem)] + [pl.BlockSpec(memory_space=vmem)] * 4,
         out_specs=pl.BlockSpec(memory_space=vmem),
         scratch_shapes=[pltpu.VMEM((frames_p, rows_p - 2, mids, width), jnp.bfloat16)],
         compiler_params=pltpu.CompilerParams(vmem_limit_bytes=48 * 1024 * 1024),
-    )(padded, w9, t3)
+    )(keep_first, padded, w9, t3, wd)
+
+
+def with_halo_one(block):
+    frames, rows = block.shape[0], block.shape[1]
+    before = from_behind(block[frames - 1 :], "tm", 1)
+    after = from_behind(block[:1], "tm", -1)
+    block = jnp.concatenate([before, block, after], axis=0)
+    above = from_behind(block[:, rows - 2 :], "row", 1)
+    below = from_behind(block[:, :1], "row", -1)
+    return jnp.concatenate([above, block, below], axis=1)
 
 
 def _sublane_shift(x, by, axis):
@@ -175,19 +215,9 @@
 
 
 def on_device(video_clip, spatial_one, temporal_one, down_weight, spatial_two, temporal_two):
-    padded = padded_2(video_clip, (("tm", 0), ("row", 1)), 1)
-    section_one = block_one(padded, spatial_one, temporal_one)
-    upper_row = from_behind(section_one[:, -1:], "row", 1)
-    joined = jnp.concatenate([upper_row, section_one], axis=1)
-    reduced = lax.conv_general_dilated(
-        joined,
-        down_weight,
-        (2, 2),
-        ((0, 0), (1, 1)),
-        dimension_numbers=("NHCW", "HWOI", "NHWC"),
-        preferred_element_type=jnp.float32,
-    )
-    reduced = jax.nn.relu(reduced).astype(jnp.bfloat16)
+    padded = with_halo_one(video_clip)
+    keep_first = (lax.axis_index("row") > 0).astype(jnp.int32).reshape(1)
+    reduced = block_one(padded, keep_first, spatial_one, temporal_one, down_weight)
     padded_two = padded_2(reduced, (("tm", 0), ("row", 1)), 1)
     return block_two(padded_two, spatial_two, temporal_two)
 

time: 108 us -> 95.8 us (0.89)
  Pallas kernels: 27.4 us -> 35.6 us
  local copies, waits for them, and re-layouts: 10.9 us -> 4.09 us
  starting transfers between devices: 32.8 us -> 26.1 us
  matrix products: 3.94 us -> 0 us
  waiting for transfers between devices: 29 us -> 26.2 us
    ppermute x4 -> x2, starting transfers between devices: 21.8 us -> 6.61 us  [padded_2(): lax.ppermute(lax.slice_in_dim(block, block.shape[dim] - width, None, axis...]
    ppermute x1 -> x4, starting transfers between devices: 1.92 us -> 14.2 us  [from_behind(): return lax.ppermute(array, axis, pairs)]
    ppermute x4 -> x2, waiting for transfers between devices: 22.5 us -> 11.6 us  [padded_2(): lax.ppermute(lax.slice_in_dim(block, 0, width, axis=dim), axis, backward)]
    ppermute x1 -> x4, waiting for transfers between devices: 3.29 us -> 13 us  [from_behind(): return lax.ppermute(array, axis, pairs)]
    pallas_call x1, Pallas kernels: 13.1 us -> 21.4 us  [block_one(): pl.pallas_call(_block_one_kernel, out_shape=jax.ShapeDtypeStruct((frames_...]
    concatenate x2 -> x1, local copies, waits for them, and re-layouts: 5.27 us -> 0.02 us  [with_halo_one(): block = jnp.concatenate([before, block, after], axis=0)]
    conv_general_dilated x1 -> x0, matrix products: 3.94 us -> none  [on_device(): lax.conv_general_dilated(joined, down_weight, (2, 2), ((0, 0), (1, 1)), d...]
    ppermute x4 -> x2, starting transfers between devices: 9.12 us -> 5.28 us  [padded_2(): lax.ppermute(lax.slice_in_dim(block, 0, width, axis=dim), axis, backward)]
  transfers between devices with their start and end apart: 9 -> 8, of which waited for: 8 -> 6; matrix products, arithmetic and copies ran while one was open for 3% -> 3% of each run, Pallas kernels for 0% -> 0%
where the time goes in v5:
time: 95.8 us; the launch traced here: 95.5 us
  Pallas kernels  35.6 us (37%)
  waiting for transfers between devices  26.2 us (27%)
  starting transfers between devices  26.1 us (27%)
  local copies, waits for them, and re-layouts  4.09 us (4%)
  other arithmetic  3.24 us (3%)
    pallas_call x1, Pallas kernels, block_one(): pl.pallas_call(_block_one_kernel, out_shape=jax.ShapeDtypeStruct((frames_...  21.4 us
    pallas_call x1, Pallas kernels, block_two(): pl.pallas_call(_block_two_kernel, out_shape=jax.ShapeDtypeStruct((frames_...  14.3 us
    ppermute x4, starting transfers between devices, from_behind(): return lax.ppermute(array, axis, pairs)  14.2 us
    ppermute x4, waiting for transfers between devices, from_behind(): return lax.ppermute(array, axis, pairs)  13 us
    ppermute x2, waiting for transfers between devices, padded_2(): lax.ppermute(lax.slice_in_dim(block, 0, width, axis=dim), axis, backward)  11.6 us
    ppermute x2, starting transfers between devices, padded_2(): lax.ppermute(lax.slice_in_dim(block, block.shape[dim] - width, None, axis...  6.61 us
    ppermute x2, starting transfers between devices, padded_2(): lax.ppermute(lax.slice_in_dim(block, 0, width, axis=dim), axis, backward)  5.28 us
    concatenate x1, other arithmetic, with_halo_one(): return jnp.concatenate([above, block, below], axis=1)  2.07 us
  transfers between devices with their start and end apart: 8, of which 6 were waited for; matrix products, arithmetic and copies ran while one was open for 3% of the time, Pallas kernels for 0%

profile of v5, /device:TPU:31, one launch (start us, length us, event | category | flops | bytes accessed | tf_op | source)
XLA Modules:
  0.0 95.5 jit_solution(7016544054749995025)
XLA Ops:
  0.0 1.0 %fusion = (bf16[1,8,64,128]{3,2,1,0:T(8,128)(2,1)S(1)}, bf16[1,8,64,128]{3,2,1,0:T(8,128)(2,1)S(1)}) fusion(bf16[16,8,64,128]{3,2,1,0:T(8,128)(2,1)} %param.6), kind=kLoop, calls=%fused_computation.8 | loop fusion | bytes 524288 | tf_op jit(solution)/shard_map/slice | solution.py:153
  1.0 3.5 %collective-permute-start = (bf16[1,8,64,128]{3,2,1,0:T(8,128)(2,1)S(1)}, bf16[1,8,64,128]{3,2,1,0:T(8,128)(2,1)S(1)}, u32[]{:S(2)}, u32[]{:S(2)}) collective-permute-start(bf16[1,8,64,128]{3,2,1,0:T(8,128)(2,1)S(1)} %get-tuple-element.6), channel_id=1, source_target_pairs={{0,16},{16,32},{32,48},{48,64},{64,80},{80,96},{96,112},{1,17},{17... | collective-permute-start | bytes 393224 | tf_op jit(solution)/shard_map/ppermute | solution.py:27
  4.5 1.9 %collective-permute-start.1 = (bf16[1,8,64,128]{3,2,1,0:T(8,128)(2,1)S(1)}, bf16[1,8,64,128]{3,2,1,0:T(8,128)(2,1)S(1)}, u32[]{:S(2)}, u32[]{:S(2)}) collective-permute-start(bf16[1,8,64,128]{3,2,1,0:T(8,128)(2,1)S(1)} %get-tuple-element.5), channel_id=1, source_target_pairs={{16,0},{32,16},{48,32},{64,48},{80,64},{96,80},{112,96},{17,1},{33... | collective-permute-start | bytes 393224 | tf_op jit(solution)/shard_map/ppermute | solution.py:27
  6.4 0.9 collective-permute-done
  7.3 0.0 copy-start.5
  7.3 0.0 copy-start.3
  7.3 2.0 %constant_dynamic-update-slice_fusion.1 = bf16[18,8,64,128]{3,2,1,0:T(8,128)(2,1)S(1)} fusion(bf16[18,8,64,128]{3,2,1,0:T(8,128)(2,1)S(1)} %constant_dynamic-update-slice_fusion.2, bf16[16,8,64,128]{3,2,1,0:T(8,128)(2,1)} %param.6), kind=kLoop, calls=%fused_computation.6 | loop fusion | bytes 4194304
  9.3 0.0 copy-start.4
  9.3 3.0 %collective-permute-done.1 = bf16[1,8,64,128]{3,2,1,0:T(8,128)(2,1)S(1)} collective-permute-done((bf16[1,8,64,128]{3,2,1,0:T(8,128)(2,1)S(1)}, bf16[1,8,64,128]{3,2,1,0:T(8,128)(2,1)S(1)}, u32[]{:S(2)}, u32[]{:S(2)}) %collective-permute-start.1) | collective-permute-done | bytes 131104 | tf_op jit(solution)/shard_map/ppermute | solution.py:27
  12.3 0.0 copy-start.1
  12.4 6.9 %collective-permute-start.2 = (bf16[18,2,64,128]{3,2,1,0:T(8,128)(2,1)S(1)}, bf16[18,2,64,128]{3,2,1,0:T(8,128)(2,1)S(1)}, u32[]{:S(2)}, u32[]{:S(2)}) collective-permute-start(bf16[18,2,64,128]{3,2,1,0:T(8,128)(2,1)S(1)} %slice.32), channel_id=1, source_target_pairs={{0,1},{1,2},{2,3},{3,4},{4,5},{5,6},{6,7},{7,8},{8,9},{9,10},{10,1... | collective-permute-start | bytes 1769480 | tf_op jit(solution)/shard_map/ppermute | solution.py:27
  19.3 1.9 %collective-permute-start.3 = (bf16[18,1,64,128]{3,2,1,0:T(8,128)(2,1)S(1)}, bf16[18,1,64,128]{3,2,1,0:T(8,128)(2,1)S(1)}, u32[]{:S(2)}, u32[]{:S(2)}) collective-permute-start(bf16[18,1,64,128]{3,2,1,0:T(8,128)(2,1)S(1)} %slice.33), channel_id=1, source_target_pairs={{1,0},{2,1},{3,2},{4,3},{5,4},{6,5},{7,6},{8,7},{9,8},{10,9},{11,1... | collective-permute-start | bytes 884744 | tf_op jit(solution)/shard_map/ppermute | solution.py:27
  21.2 0.0 copy-done.1
  21.2 0.0 copy-done.5
  21.2 0.1 copy.11
  21.3 0.1 reshape.20.t3_ref
  21.4 0.0 copy-done.3
  21.4 0.2 copy.12.w9_ref
  21.6 0.0 copy-done.4
  21.6 0.2 copy.13.wd_ref
  21.8 9.1 %collective-permute-done.3 = bf16[18,1,64,128]{3,2,1,0:T(8,128)(2,1)S(1)} collective-permute-done((bf16[18,1,64,128]{3,2,1,0:T(8,128)(2,1)S(1)}, bf16[18,1,64,128]{3,2,1,0:T(8,128)(2,1)S(1)}, u32[]{:S(2)}, u32[]{:S(2)}) %collective-permute-start.3) | collective-permute-done | bytes 294944 | tf_op jit(solution)/shard_map/ppermute | solution.py:27
  30.9 0.0 collective-permute-done.2
  30.9 2.1 %pad_maximum_fusion.xp_ref = bf16[18,11,64,128]{3,2,1,0:T(8,128)(2,1)S(1)} fusion(bf16[18,1,64,128]{3,2,1,0:T(8,128)(2,1)S(1)} %collective-permute-done.3, bf16[18,8,64,128]{3,2,1,0:T(8,128)(2,1)} %copy-done.1, bf16[18,2,64,128]{3,2,1,0:T(8,128)(2,1)S(1)} %collective-permute-done.2), kind=kLoop, calls=%fused_computation | loop fusion | flops 3244032 | bytes 6488064 | tf_op jit(solution)/shard_map/concatenate | solution.py:157
  33.0 0.0 copy-start.2
  33.0 21.4 %shard_map.64 = bf16[16,4,64,128]{3,2,1,0:T(8,128)(2,1)S(1)} custom-call(s32[1]{0:T(128)} %bitcast.keep_ref, bf16[18,11,64,128]{3,2,1,0:T(8,128)(2,1)S(1)} %pad_maximum_fusion.xp_ref, bf16[144,576]{1,0:T(8,128)(2,1)S(1)} %copy.12.w9_ref, bf16[64,432]{1,0:T(8,128)(2,1)S(1)} %reshape.20.t3_ref, bf16[128,576]{1,0:T(8,128)(2,1)S(1)} %copy.13.wd_ref), custom_call_target="tpu_custom_call" | custom-call | tf_op jit(solution)/shard_map/pallas_call | solution.py:140
  54.4 1.9 %collective-permute-start.4 = (bf16[1,4,64,128]{3,2,1,0:T(8,128)(2,1)S(1)}, bf16[1,4,64,128]{3,2,1,0:T(8,128)(2,1)S(1)}, u32[]{:S(2)}, u32[]{:S(2)}) collective-permute-start(bf16[1,4,64,128]{3,2,1,0:T(8,128)(2,1)S(1)} %get-tuple-element.9), channel_id=1, source_target_pairs={{0,16},{16,32},{32,48},{48,64},{64,80},{80,96},{96,112},{1,17},{17... | collective-permute-start | bytes 196616 | tf_op jit(solution)/shard_map/ppermute | solution.py:16
  56.3 3.4 %collective-permute-start.5 = (bf16[1,4,64,128]{3,2,1,0:T(8,128)(2,1)S(1)}, bf16[1,4,64,128]{3,2,1,0:T(8,128)(2,1)S(1)}, u32[]{:S(2)}, u32[]{:S(2)}) collective-permute-start(bf16[1,4,64,128]{3,2,1,0:T(8,128)(2,1)S(1)} %get-tuple-element.10), channel_id=1, source_target_pairs={{16,0},{32,16},{48,32},{64,48},{80,64},{96,80},{112,96},{17,1},{33... | collective-permute-start | bytes 196616 | tf_op jit(solution)/shard_map/ppermute | solution.py:19
  59.7 0.0 collective-permute-done.4
  59.7 3.7 %collective-permute-done.5 = bf16[1,4,64,128]{3,2,1,0:T(8,128)(2,1)S(1)} collective-permute-done((bf16[1,4,64,128]{3,2,1,0:T(8,128)(2,1)S(1)}, bf16[1,4,64,128]{3,2,1,0:T(8,128)(2,1)S(1)}, u32[]{:S(2)}, u32[]{:S(2)}) %collective-permute-start.5) | collective-permute-done | bytes 65568 | tf_op jit(solution)/shard_map/ppermute | solution.py:19
  63.4 0.9 pad_maximum_fusion.4
  64.3 4.7 %collective-permute-start.6 = (bf16[18,1,64,128]{3,2,1,0:T(8,128)(2,1)}, bf16[18,1,64,128]{3,2,1,0:T(8,128)(2,1)S(1)}, u32[]{:S(2)}, u32[]{:S(2)}) collective-permute-start(bf16[18,1,64,128]{3,2,1,0:T(8,128)(2,1)} %get-tuple-element.7), channel_id=1, source_target_pairs={{0,1},{1,2},{2,3},{3,4},{4,5},{5,6},{6,7},{7,8},{8,9},{9,10},{10,1... | collective-permute-start | bytes 884744 | tf_op jit(solution)/shard_map/ppermute | solution.py:16
  69.0 1.9 %collective-permute-start.7 = (bf16[18,1,64,128]{3,2,1,0:T(8,128)(2,1)}, bf16[18,1,64,128]{3,2,1,0:T(8,128)(2,1)S(1)}, u32[]{:S(2)}, u32[]{:S(2)}) collective-permute-start(bf16[18,1,64,128]{3,2,1,0:T(8,128)(2,1)} %get-tuple-element.8), channel_id=1, source_target_pairs={{1,0},{2,1},{3,2},{4,3},{5,4},{6,5},{7,6},{8,7},{9,8},{10,9},{11,1... | collective-permute-start | bytes 884744 | tf_op jit(solution)/shard_map/ppermute | solution.py:19
  71.0 0.0 copy-done.2
  71.0 0.0 copy-start
  71.0 0.4 copy.14
  71.4 1.6 %collective-permute-done.6 = bf16[18,1,64,128]{3,2,1,0:T(8,128)(2,1)S(1)} collective-permute-done((bf16[18,1,64,128]{3,2,1,0:T(8,128)(2,1)}, bf16[18,1,64,128]{3,2,1,0:T(8,128)(2,1)S(1)}, u32[]{:S(2)}, u32[]{:S(2)}) %collective-permute-start.6) | collective-permute-done | bytes 294944 | tf_op jit(solution)/shard_map/ppermute | solution.py:16
  73.0 7.9 %collective-permute-done.7 = bf16[18,1,64,128]{3,2,1,0:T(8,128)(2,1)S(1)} collective-permute-done((bf16[18,1,64,128]{3,2,1,0:T(8,128)(2,1)}, bf16[18,1,64,128]{3,2,1,0:T(8,128)(2,1)S(1)}, u32[]{:S(2)}, u32[]{:S(2)}) %collective-permute-start.7) | collective-permute-done | bytes 294944 | tf_op jit(solution)/shard_map/ppermute | solution.py:19
  80.9 0.3 pad_maximum_fusion.1.xp_ref
  81.2 0.0 copy-done
  81.2 14.3 %shard_map.65 = bf16[16,4,64,128]{3,2,1,0:T(8,128)(2,1)} custom-call(bf16[18,6,64,128]{3,2,1,0:T(8,128)(2,1)S(1)} %pad_maximum_fusion.1.xp_ref, bf16[1152,288]{1,0:T(8,128)(2,1)S(1)} %bitcast.11, bf16[3,288,128]{2,1,0:T(8,128)(2,1)S(1)} %bitcast.12), custom_call_target="tpu_custom_call" | custom-call | tf_op jit(solution)/shard_map/pallas_call | solution.py:207
  (5 shorter events, 0.1 us)
Async XLA Ops:
  1.0 6.3 %collective-permute-start = (bf16[1,8,64,128]{3,2,1,0:T(8,128)(2,1)S(1)}, bf16[1,8,64,128]{3,2,1,0:T(8,128)(2,1)S(1)}, u32[]{:S(2)}, u32[]{:S(2)}) collective-permute-start(bf16[1,8,64,128]{3,2,1,0:T(8,128)(2,1)S(1)} %get-tuple-element.6), channel_id=1, source_target_pairs={{0,16},{16,32},{32,48},{48,64},{64,80},{80,96},{96,112},{1,17},{17... | collective-permute-start | bytes 393224 | tf_op jit(solution)/shard_map/ppermute | solution.py:27
  4.5 7.8 %collective-permute-start.1 = (bf16[1,8,64,128]{3,2,1,0:T(8,128)(2,1)S(1)}, bf16[1,8,64,128]{3,2,1,0:T(8,128)(2,1)S(1)}, u32[]{:S(2)}, u32[]{:S(2)}) collective-permute-start(bf16[1,8,64,128]{3,2,1,0:T(8,128)(2,1)S(1)} %get-tuple-element.5), channel_id=1, source_target_pairs={{16,0},{32,16},{48,32},{64,48},{80,64},{96,80},{112,96},{17,1},{33... | collective-permute-start | bytes 393224 | tf_op jit(solution)/shard_map/ppermute | solution.py:27
  7.3 13.9 %copy-start.5 = (bf16[3,64,144]{2,1,0:T(8,128)(2,1)S(1)}, bf16[3,64,144]{2,1,0:T(8,128)(2,1)}, u32[]{:S(2)}) copy-start(bf16[3,64,144]{2,1,0:T(8,128)(2,1)} %param.8) | copy-start | bytes 165892
  7.3 14.1 %copy-start.3 = (bf16[3,3,144,64]{2,3,1,0:T(8,128)(2,1)S(1)}, bf16[3,3,144,64]{2,3,1,0:T(8,128)(2,1)}, u32[]{:S(2)}) copy-start(bf16[3,3,144,64]{2,3,1,0:T(8,128)(2,1)} %param.7) | copy-start | bytes 497668
  9.3 12.3 %copy-start.4 = (bf16[3,3,128,64]{2,3,1,0:T(8,128)(2,1)S(1)}, bf16[3,3,128,64]{2,3,1,0:T(8,128)(2,1)}, u32[]{:S(2)}) copy-start(bf16[3,3,128,64]{2,3,1,0:T(8,128)(2,1)} %param.9) | copy-start | bytes 442372
  12.3 8.9 %copy-start.1 = (bf16[18,8,64,128]{3,2,1,0:T(8,128)(2,1)}, bf16[18,8,64,128]{3,2,1,0:T(8,128)(2,1)S(1)}, u32[]{:S(2)}) copy-start(bf16[18,8,64,128]{3,2,1,0:T(8,128)(2,1)S(1)} %constant_dynamic-update-slice_fusion) | copy-start | bytes 7077892
  12.4 18.6 %collective-permute-start.2 = (bf16[18,2,64,128]{3,2,1,0:T(8,128)(2,1)S(1)}, bf16[18,2,64,128]{3,2,1,0:T(8,128)(2,1)S(1)}, u32[]{:S(2)}, u32[]{:S(2)}) collective-permute-start(bf16[18,2,64,128]{3,2,1,0:T(8,128)(2,1)S(1)} %slice.32), channel_id=1, source_target_pairs={{0,1},{1,2},{2,3},{3,4},{4,5},{5,6},{6,7},{7,8},{8,9},{9,10},{10,1... | collective-permute-start | bytes 1769480 | tf_op jit(solution)/shard_map/ppermute | solution.py:27
  19.3 11.7 %collective-permute-start.3 = (bf16[18,1,64,128]{3,2,1,0:T(8,128)(2,1)S(1)}, bf16[18,1,64,128]{3,2,1,0:T(8,128)(2,1)S(1)}, u32[]{:S(2)}, u32[]{:S(2)}) collective-permute-start(bf16[18,1,64,128]{3,2,1,0:T(8,128)(2,1)S(1)} %slice.33), channel_id=1, source_target_pairs={{1,0},{2,1},{3,2},{4,3},{5,4},{6,5},{7,6},{8,7},{9,8},{10,9},{11,1... | collective-permute-start | bytes 884744 | tf_op jit(solution)/shard_map/ppermute | solution.py:27
  33.0 38.0 %copy-start.2 = (bf16[3,3,288,128]{3,2,1,0:T(8,128)(2,1)S(1)}, bf16[3,3,288,128]{3,2,1,0:T(8,128)(2,1)}, u32[]{:S(2)}) copy-start(bf16[3,3,288,128]{3,2,1,0:T(8,128)(2,1)} %param.10) | copy-start | bytes 1990660
  54.4 5.3 %collective-permute-start.4 = (bf16[1,4,64,128]{3,2,1,0:T(8,128)(2,1)S(1)}, bf16[1,4,64,128]{3,2,1,0:T(8,128)(2,1)S(1)}, u32[]{:S(2)}, u32[]{:S(2)}) collective-permute-start(bf16[1,4,64,128]{3,2,1,0:T(8,128)(2,1)S(1)} %get-tuple-element.9), channel_id=1, source_target_pairs={{0,16},{16,32},{32,48},{48,64},{64,80},{80,96},{96,112},{1,17},{17... | collective-permute-start | bytes 196616 | tf_op jit(solution)/shard_map/ppermute | solution.py:16
  56.3 7.1 %collective-permute-start.5 = (bf16[1,4,64,128]{3,2,1,0:T(8,128)(2,1)S(1)}, bf16[1,4,64,128]{3,2,1,0:T(8,128)(2,1)S(1)}, u32[]{:S(2)}, u32[]{:S(2)}) collective-permute-start(bf16[1,4,64,128]{3,2,1,0:T(8,128)(2,1)S(1)} %get-tuple-element.10), channel_id=1, source_target_pairs={{16,0},{32,16},{48,32},{64,48},{80,64},{96,80},{112,96},{17,1},{33... | collective-permute-start | bytes 196616 | tf_op jit(solution)/shard_map/ppermute | solution.py:19
  64.3 8.7 %collective-permute-start.6 = (bf16[18,1,64,128]{3,2,1,0:T(8,128)(2,1)}, bf16[18,1,64,128]{3,2,1,0:T(8,128)(2,1)S(1)}, u32[]{:S(2)}, u32[]{:S(2)}) collective-permute-start(bf16[18,1,64,128]{3,2,1,0:T(8,128)(2,1)} %get-tuple-element.7), channel_id=1, source_target_pairs={{0,1},{1,2},{2,3},{3,4},{4,5},{5,6},{6,7},{7,8},{8,9},{9,10},{10,1... | collective-permute-start | bytes 884744 | tf_op jit(solution)/shard_map/ppermute | solution.py:16
  69.0 11.9 %collective-permute-start.7 = (bf16[18,1,64,128]{3,2,1,0:T(8,128)(2,1)}, bf16[18,1,64,128]{3,2,1,0:T(8,128)(2,1)S(1)}, u32[]{:S(2)}, u32[]{:S(2)}) collective-permute-start(bf16[18,1,64,128]{3,2,1,0:T(8,128)(2,1)} %get-tuple-element.8), channel_id=1, source_target_pairs={{1,0},{2,1},{3,2},{4,3},{5,4},{6,5},{7,6},{8,7},{9,8},{10,9},{11,1... | collective-permute-start | bytes 884744 | tf_op jit(solution)/shard_map/ppermute | solution.py:19
  71.0 10.2 %copy-start = (bf16[3,128,288]{1,2,0:T(8,128)(2,1)S(1)}, bf16[3,128,288]{1,2,0:T(8,128)(2,1)}, u32[]{:S(2)}) copy-start(bf16[3,128,288]{1,2,0:T(8,128)(2,1)} %param.11) | copy-start | bytes 663556

commit v6 on v5

--- a/solution.py
+++ b/solution.py
@@ -165,61 +165,123 @@
     return jnp.where(inside, rolled, jnp.zeros_like(rolled))
 
 
-def _block_two_kernel(xp_ref, w9_ref, t3_ref, out_ref, mid_ref):
-    frames_p, rows_p, width, channels = xp_ref.shape
+def _middle_two(xp_ref, f, w9_ref):
+    rows = xp_ref.shape[1] - 2
+    slab = xp_ref[f].astype(jnp.float32)
+    shifted = [_sublane_shift(slab, b - 1, 1).astype(jnp.bfloat16) for b in range(3)]
+    stacked = jnp.concatenate(
+        [
+            jnp.concatenate([shifted[b][i + a] for a in range(3) for b in range(3)], axis=1)
+            for i in range(rows)
+        ],
+        axis=0,
+    )
+    m = jnp.dot(stacked, w9_ref[...], preferred_element_type=jnp.float32)
+    return jnp.maximum(m, 0.0).astype(jnp.bfloat16)
+
+
+def _edges_two_kernel(xp_ref, w9_ref, edge_ref):
+    frames = xp_ref.shape[0]
+    edge_ref[0] = _middle_two(xp_ref, 0, w9_ref)
+    edge_ref[1] = _middle_two(xp_ref, frames - 1, w9_ref)
+
+
+def _finish(s, xp_ref, t, out_ref, slot):
+    rows, width = xp_ref.shape[1] - 2, xp_ref.shape[2]
+    for i in range(rows):
+        v = s[i * width : (i + 1) * width] + xp_ref[t, i + 1].astype(jnp.float32)
+        out_ref[slot, i] = jnp.maximum(v, 0.0).astype(out_ref.dtype)
+
+
+def _inner_two_kernel(xp_ref, w9_ref, t3_ref, out_ref, side_ref, mid_ref):
+    frames = xp_ref.shape[0]
+
+    def middle(f, carry):
+        mid_ref[f] = _middle_two(xp_ref, f, w9_ref)
+        return carry
+
+    lax.fori_loop(0, frames, middle, 0)
+    side_ref[0] = mid_ref[1]
+    side_ref[1] = mid_ref[frames - 2]
+
+    def section(t, carry):
+        s = jnp.dot(mid_ref[t - 1], t3_ref[0], preferred_element_type=jnp.float32)
+        s = s + jnp.dot(mid_ref[t], t3_ref[1], preferred_element_type=jnp.float32)
+        s = s + jnp.dot(mid_ref[t + 1], t3_ref[2], preferred_element_type=jnp.float32)
+        _finish(s, xp_ref, t, out_ref, t - 1)
+        return carry
+
+    lax.fori_loop(1, frames - 1, section, 0)
+
+
+def _outer_two_kernel(xp_ref, t3_ref, before_ref, after_ref, edge_ref, side_ref, out_ref):
+    frames = xp_ref.shape[0]
+    s = jnp.dot(before_ref[0], t3_ref[0], preferred_element_type=jnp.float32)
+    s = s + jnp.dot(edge_ref[0], t3_ref[1], preferred_element_type=jnp.float32)
+    s = s + jnp.dot(side_ref[0], t3_ref[2], preferred_element_type=jnp.float32)
+    _finish(s, xp_ref, 0, out_ref, 0)
+    s = jnp.dot(side_ref[1], t3_ref[0], preferred_element_type=jnp.float32)
+    s = s + jnp.dot(edge_ref[1], t3_ref[1], preferred_element_type=jnp.float32)
+    s = s + jnp.dot(after_ref[0], t3_ref[2], preferred_element_type=jnp.float32)
+    _finish(s, xp_ref, frames - 1, out_ref, 1)
+
+
+def block_two(rowed, spatial_kernel, temporal_kernel):
+    frames, rows_p, width, channels = rowed.shape
     rows = rows_p - 2
-    frames = frames_p - 2
-
-    def middle(f, carry):
-        slab = xp_ref[f].astype(jnp.float32)
-        shifted = [_sublane_shift(slab, b - 1, 1).astype(jnp.bfloat16) for b in range(3)]
-        stacked = jnp.concatenate(
-            [
-                jnp.concatenate([shifted[b][i + a] for a in range(3) for b in range(3)], axis=1)
-                for i in range(rows)
-            ],
-            axis=0,
-        )
-        m = jnp.dot(stacked, w9_ref[...], preferred_element_type=jnp.float32)
-        mid_ref[f] = jnp.maximum(m, 0.0).astype(jnp.bfloat16)
-        return carry
-
-    lax.fori_loop(0, frames_p, middle, 0)
-
-    def section(t, carry):
-        s = jnp.dot(mid_ref[t], t3_ref[0], preferred_element_type=jnp.float32)
-        s = s + jnp.dot(mid_ref[t + 1], t3_ref[1], preferred_element_type=jnp.float32)
-        s = s + jnp.dot(mid_ref[t + 2], t3_ref[2], preferred_element_type=jnp.float32)
-        for i in range(rows):
-            v = s[i * width : (i + 1) * width] + xp_ref[t + 1, i + 1].astype(jnp.float32)
-            out_ref[t, i] = jnp.maximum(v, 0.0).astype(out_ref.dtype)
-        return carry
-
-    lax.fori_loop(0, frames, section, 0)
-
-
-def block_two(padded, spatial_kernel, temporal_kernel):
-    frames_p, rows_p, width, channels = padded.shape
     mids = spatial_kernel.shape[2]
     w9 = jnp.transpose(spatial_kernel, (0, 1, 3, 2)).reshape(9 * channels, mids)
     t3 = jnp.transpose(temporal_kernel, (0, 2, 1))
     vmem = pltpu.MemorySpace.VMEM if hasattr(pltpu, "MemorySpace") else pltpu.VMEM
-    return pl.pallas_call(
-        _block_two_kernel,
-        out_shape=jax.ShapeDtypeStruct((frames_p - 2, rows_p - 2, width, channels), padded.dtype),
-        in_specs=[pl.BlockSpec(memory_space=vmem)] * 3,
-        out_specs=pl.BlockSpec(memory_space=vmem),
-        scratch_shapes=[pltpu.VMEM((frames_p, (rows_p - 2) * width, mids), jnp.bfloat16)],
-        compiler_params=pltpu.CompilerParams(vmem_limit_bytes=48 * 1024 * 1024),
-    )(padded, w9, t3)
+    params = pltpu.CompilerParams(vmem_limit_bytes=48 * 1024 * 1024)
+    spec = pl.BlockSpec(memory_space=vmem)
+    plane = (rows * width, mids)
+    edges = pl.pallas_call(
+        _edges_two_kernel,
+        out_shape=jax.ShapeDtypeStruct((2,) + plane, rowed.dtype),
+        in_specs=[spec] * 2,
+        out_specs=spec,
+        compiler_params=params,
+        cost_estimate=pl.CostEstimate(
+            flops=2 * 2 * rows * width * 9 * channels * mids, bytes_accessed=2 * rowed.size, transcendentals=0
+        ),
+    )(rowed, w9)
+    before = from_behind(edges[1:], "tm", 1)
+    after = from_behind(edges[:1], "tm", -1)
+    inner, side = pl.pallas_call(
+        _inner_two_kernel,
+        out_shape=(
+            jax.ShapeDtypeStruct((frames - 2, rows, width, channels), rowed.dtype),
+            jax.ShapeDtypeStruct((2,) + plane, rowed.dtype),
+        ),
+        in_specs=[spec] * 3,
+        out_specs=(spec, spec),
+        scratch_shapes=[pltpu.VMEM((frames,) + plane, jnp.bfloat16)],
+        compiler_params=params,
+        cost_estimate=pl.CostEstimate(
+            flops=2 * frames * rows * width * (9 * channels * mids + 3 * mids * channels),
+            bytes_accessed=4 * rowed.size,
+            transcendentals=0,
+        ),
+    )(rowed, w9, t3)
+    outer = pl.pallas_call(
+        _outer_two_kernel,
+        out_shape=jax.ShapeDtypeStruct((2, rows, width, channels), rowed.dtype),
+        in_specs=[spec] * 6,
+        out_specs=spec,
+        compiler_params=params,
+    )(rowed, t3, before, after, edges, side)
+    return jnp.concatenate([outer[:1], inner, outer[1:]], axis=0)
 
 
 def on_device(video_clip, spatial_one, temporal_one, down_weight, spatial_two, temporal_two):
     padded = with_halo_one(video_clip)
     keep_first = (lax.axis_index("row") > 0).astype(jnp.int32).reshape(1)
     reduced = block_one(padded, keep_first, spatial_one, temporal_one, down_weight)
-    padded_two = padded_2(reduced, (("tm", 0), ("row", 1)), 1)
-    return block_two(padded_two, spatial_two, temporal_two)
+    rows = reduced.shape[1]
+    above = from_behind(reduced[:, rows - 1 :], "row", 1)
+    below = from_behind(reduced[:, :1], "row", -1)
+    return block_two(jnp.concatenate([above, reduced, below], axis=1), spatial_two, temporal_two)
 
 
 def solution(mesh):

time: 95.8 us -> 90.6 us (0.946)
  the two profiles are of different devices: /device:TPU:31 before, /device:TPU:57 now
where the time goes in v6:
time: 90.6 us; the launch traced here: 90.2 us
  Pallas kernels  34.4 us (38%)
  starting transfers between devices  27.2 us (30%)
  waiting for transfers between devices  18.4 us (20%)
  local copies, waits for them, and re-layouts  7.28 us (8%)
  other arithmetic  2.65 us (3%)
    ppermute x8, starting transfers between devices, from_behind(): return lax.ppermute(array, axis, pairs)  27.2 us
    pallas_call x1, Pallas kernels, block_one(): pl.pallas_call(_block_one_kernel, out_shape=jax.ShapeDtypeStruct((frames_...  21.4 us
    ppermute x8, waiting for transfers between devices, from_behind(): return lax.ppermute(array, axis, pairs)  18.4 us
    pallas_call x1, Pallas kernels, block_two(): pl.pallas_call(_inner_two_kernel, out_shape=(jax.ShapeDtypeStruct((frames...  11.8 us
    unnamed x10, local copies, waits for them, and re-layouts  2.03 us
  transfers between devices with their start and end apart: 8, of which 4 were waited for; matrix products, arithmetic and copies ran while one was open for 5% of the time, Pallas kernels for 13%

profile of v6, /device:TPU:57, one launch (start us, length us, event | category | flops | bytes accessed | tf_op | source)
XLA Modules:
  0.0 90.2 jit_solution(9660773853115008538)
XLA Ops:
  0.0 1.0 %fusion = (bf16[1,8,64,128]{3,2,1,0:T(8,128)(2,1)S(1)}, bf16[1,8,64,128]{3,2,1,0:T(8,128)(2,1)S(1)}) fusion(bf16[16,8,64,128]{3,2,1,0:T(8,128)(2,1)} %param.6), kind=kLoop, calls=%fused_computation.6 | loop fusion | bytes 524288 | tf_op jit(solution)/shard_map/slice | solution.py:153
  1.0 3.1 %collective-permute-start = (bf16[1,8,64,128]{3,2,1,0:T(8,128)(2,1)S(1)}, bf16[1,8,64,128]{3,2,1,0:T(8,128)(2,1)S(1)}, u32[]{:S(2)}, u32[]{:S(2)}) collective-permute-start(bf16[1,8,64,128]{3,2,1,0:T(8,128)(2,1)S(1)} %get-tuple-element.10), channel_id=1, source_target_pairs={{0,16},{16,32},{32,48},{48,64},{64,80},{80,96},{96,112},{1,17},{17... | collective-permute-start | bytes 393224 | tf_op jit(solution)/shard_map/ppermute | solution.py:27
  4.1 4.3 %collective-permute-start.1 = (bf16[1,8,64,128]{3,2,1,0:T(8,128)(2,1)S(1)}, bf16[1,8,64,128]{3,2,1,0:T(8,128)(2,1)S(1)}, u32[]{:S(2)}, u32[]{:S(2)}) collective-permute-start(bf16[1,8,64,128]{3,2,1,0:T(8,128)(2,1)S(1)} %get-tuple-element.9), channel_id=1, source_target_pairs={{16,0},{32,16},{48,32},{64,48},{80,64},{96,80},{112,96},{17,1},{33... | collective-permute-start | bytes 393224 | tf_op jit(solution)/shard_map/ppermute | solution.py:27
  8.4 1.0 %collective-permute-done = bf16[1,8,64,128]{3,2,1,0:T(8,128)(2,1)S(1)} collective-permute-done((bf16[1,8,64,128]{3,2,1,0:T(8,128)(2,1)S(1)}, bf16[1,8,64,128]{3,2,1,0:T(8,128)(2,1)S(1)}, u32[]{:S(2)}, u32[]{:S(2)}) %collective-permute-start) | collective-permute-done | bytes 131104 | tf_op jit(solution)/shard_map/ppermute | solution.py:27
  9.4 0.0 copy-start.3
  9.4 0.0 copy-start.2
  9.4 2.0 %constant_dynamic-update-slice_fusion.1 = bf16[18,8,64,128]{3,2,1,0:T(8,128)(2,1)S(1)} fusion(bf16[18,8,64,128]{3,2,1,0:T(8,128)(2,1)S(1)} %constant_dynamic-update-slice_fusion.2, bf16[16,8,64,128]{3,2,1,0:T(8,128)(2,1)} %param.6), kind=kLoop, calls=%fused_computation.4 | loop fusion | bytes 4194304
  11.4 0.0 collective-permute-done.1
  11.4 0.9 slice.40
  12.3 5.7 %collective-permute-start.2 = (bf16[18,2,64,128]{3,2,1,0:T(8,128)(2,1)}, bf16[18,2,64,128]{3,2,1,0:T(8,128)(2,1)S(1)}, u32[]{:S(2)}, u32[]{:S(2)}) collective-permute-start(bf16[18,2,64,128]{3,2,1,0:T(8,128)(2,1)} %slice.40), channel_id=1, source_target_pairs={{0,1},{1,2},{2,3},{3,4},{4,5},{5,6},{6,7},{7,8},{8,9},{9,10},{10,1... | collective-permute-start | bytes 1769480 | tf_op jit(solution)/shard_map/ppermute | solution.py:27
  18.0 0.7 slice.41
  18.7 1.9 %collective-permute-start.3 = (bf16[18,1,64,128]{3,2,1,0:T(8,128)(2,1)}, bf16[18,1,64,128]{3,2,1,0:T(8,128)(2,1)}, u32[]{:S(2)}, u32[]{:S(2)}) collective-permute-start(bf16[18,1,64,128]{3,2,1,0:T(8,128)(2,1)} %slice.41), channel_id=1, source_target_pairs={{1,0},{2,1},{3,2},{4,3},{5,4},{6,5},{7,6},{8,7},{9,8},{10,9},{11,1... | collective-permute-start | bytes 884744 | tf_op jit(solution)/shard_map/ppermute | solution.py:27
  20.6 0.0 copy-done.3
  20.7 0.1 copy.11
  20.8 0.1 reshape.20.t3_ref
  20.9 0.0 copy-done.2
  20.9 0.2 copy.12.w9_ref
  21.1 1.1 %copy.13.wd_ref = bf16[128,576]{1,0:T(8,128)(2,1)S(1)} copy(bf16[128,576]{0,1:T(8,128)(2,1)} %bitcast.17) | data formatting | bytes 294912 | tf_op jit(solution)/shard_map/reshape | solution.py:136
  22.1 8.6 %collective-permute-done.3 = bf16[18,1,64,128]{3,2,1,0:T(8,128)(2,1)} collective-permute-done((bf16[18,1,64,128]{3,2,1,0:T(8,128)(2,1)}, bf16[18,1,64,128]{3,2,1,0:T(8,128)(2,1)}, u32[]{:S(2)}, u32[]{:S(2)}) %collective-permute-start.3) | collective-permute-done | bytes 294944 | tf_op jit(solution)/shard_map/ppermute | solution.py:27
  30.7 0.0 collective-permute-done.2
  30.7 1.4 %pad_maximum_fusion.xp_ref = bf16[18,11,64,128]{3,2,1,0:T(8,128)(2,1)S(1)} fusion(bf16[18,1,64,128]{3,2,1,0:T(8,128)(2,1)} %collective-permute-done.3, bf16[18,8,64,128]{3,2,1,0:T(8,128)(2,1)S(1)} %constant_dynamic-update-slice_fusion, bf16[18,2,64,128]{3,2,1,0:T(8,128)(2,1)S(1)} %collective-permute-done.2), kind=kLoop, calls=%fused_computation | loop fusion | flops 3244032 | bytes 6488064 | tf_op jit(solution)/shard_map/concatenate | solution.py:157
  32.1 0.0 copy-start.1
  32.1 21.4 %shard_map.64 = bf16[16,4,64,128]{3,2,1,0:T(8,128)(2,1)S(1)} custom-call(s32[1]{0:T(128)} %bitcast.keep_ref, bf16[18,11,64,128]{3,2,1,0:T(8,128)(2,1)S(1)} %pad_maximum_fusion.xp_ref, bf16[144,576]{1,0:T(8,128)(2,1)S(1)} %copy.12.w9_ref, bf16[64,432]{1,0:T(8,128)(2,1)S(1)} %reshape.20.t3_ref, bf16[128,576]{1,0:T(8,128)(2,1)S(1)} %copy.13.wd_ref), custom_call_target="tpu_custom_call" | custom-call | tf_op jit(solution)/shard_map/pallas_call | solution.py:140
  53.4 0.8 fusion.1
  54.2 2.3 %collective-permute-start.4 = (bf16[16,1,64,128]{3,2,1,0:T(8,128)(2,1)}, bf16[16,1,64,128]{3,2,1,0:T(8,128)(2,1)S(1)}, u32[]{:S(2)}, u32[]{:S(2)}) collective-permute-start(bf16[16,1,64,128]{3,2,1,0:T(8,128)(2,1)} %get-tuple-element.11), channel_id=1, source_target_pairs={{0,1},{1,2},{2,3},{3,4},{4,5},{5,6},{6,7},{7,8},{8,9},{9,10},{10,1... | collective-permute-start | bytes 786440 | tf_op jit(solution)/shard_map/ppermute | solution.py:27
  56.5 2.0 %collective-permute-start.5 = (bf16[16,1,64,128]{3,2,1,0:T(8,128)(2,1)S(1)}, bf16[16,1,64,128]{3,2,1,0:T(8,128)(2,1)S(1)}, u32[]{:S(2)}, u32[]{:S(2)}) collective-permute-start(bf16[16,1,64,128]{3,2,1,0:T(8,128)(2,1)S(1)} %get-tuple-element.12), channel_id=1, source_target_pairs={{1,0},{2,1},{3,2},{4,3},{5,4},{6,5},{7,6},{8,7},{9,8},{10,9},{11,1... | collective-permute-start | bytes 786440 | tf_op jit(solution)/shard_map/ppermute | solution.py:27
  58.5 0.0 copy-done.1
  58.5 0.4 copy.14
  58.9 1.2 %collective-permute-done.4 = bf16[16,1,64,128]{3,2,1,0:T(8,128)(2,1)S(1)} collective-permute-done((bf16[16,1,64,128]{3,2,1,0:T(8,128)(2,1)}, bf16[16,1,64,128]{3,2,1,0:T(8,128)(2,1)S(1)}, u32[]{:S(2)}, u32[]{:S(2)}) %collective-permute-start.4) | collective-permute-done | bytes 262176 | tf_op jit(solution)/shard_map/ppermute | solution.py:27
  60.1 7.7 %collective-permute-done.5 = bf16[16,1,64,128]{3,2,1,0:T(8,128)(2,1)S(1)} collective-permute-done((bf16[16,1,64,128]{3,2,1,0:T(8,128)(2,1)S(1)}, bf16[16,1,64,128]{3,2,1,0:T(8,128)(2,1)S(1)}, u32[]{:S(2)}, u32[]{:S(2)}) %collective-permute-start.5) | collective-permute-done | bytes 262176 | tf_op jit(solution)/shard_map/ppermute | solution.py:27
  67.8 0.2 pad_maximum_fusion.1.xp_ref
  68.0 0.0 copy-start
  68.0 0.8 shard_map.65.edge_ref
  68.9 2.1 %collective-permute-start.6 = (bf16[1,256,288]{2,1,0:T(8,128)(2,1)S(1)}, bf16[1,256,288]{2,1,0:T(8,128)(2,1)S(1)}, u32[]{:S(2)}, u32[]{:S(2)}) collective-permute-start(bf16[1,256,288]{2,1,0:T(8,128)(2,1)S(1)} %get-tuple-element.14), channel_id=1, source_target_pairs={{0,16},{16,32},{32,48},{48,64},{64,80},{80,96},{96,112},{1,17},{17... | collective-permute-start | bytes 442376 | tf_op jit(solution)/shard_map/ppermute | solution.py:27
  71.0 5.8 %collective-permute-start.7 = (bf16[1,256,288]{2,1,0:T(8,128)(2,1)S(1)}, bf16[1,256,288]{2,1,0:T(8,128)(2,1)S(1)}, u32[]{:S(2)}, u32[]{:S(2)}) collective-permute-start(bf16[1,256,288]{2,1,0:T(8,128)(2,1)S(1)} %get-tuple-element.13), channel_id=1, source_target_pairs={{16,0},{32,16},{48,32},{64,48},{80,64},{96,80},{112,96},{17,1},{33... | collective-permute-start | bytes 442376 | tf_op jit(solution)/shard_map/ppermute | solution.py:27
  76.8 0.0 copy-done
  76.8 11.8 %shard_map.66 = (bf16[14,4,64,128]{3,2,1,0:T(8,128)(2,1)S(1)}, bf16[2,256,288]{2,1,0:T(8,128)(2,1)S(1)}) custom-call(bf16[16,6,64,128]{3,2,1,0:T(8,128)(2,1)S(1)} %pad_maximum_fusion.1.xp_ref, bf16[1152,288]{1,0:T(8,128)(2,1)S(1)} %bitcast.12, bf16[3,288,128]{2,1,0:T(8,128)(2,1)S(1)} %bitcast.13), custom_call_target="tpu_custom_call" | custom-call | flops 3623878656 | bytes 3145728 | tf_op jit(solution)/shard_map/pallas_call | solution.py:251
  88.6 0.0 collective-permute-done.6.before_ref
  88.6 0.0 collective-permute-done.7.after_ref
  88.6 0.5 shard_map.67
  89.1 1.1 %pad_maximum_fusion.2 = bf16[16,4,64,128]{3,2,1,0:T(8,128)(2,1)} fusion(bf16[1,4,64,128]{3,2,1,0:T(8,128)(2,1)S(1)} %get-tuple-element.16, bf16[14,4,64,128]{3,2,1,0:T(8,128)(2,1)S(1)} %get-tuple-element.8, bf16[1,4,64,128]{3,2,1,0:T(8,128)(2,1)S(1)} %get-tuple-element.15), kind=kLoop, calls=%fused_computation.2 | loop fusion | flops 1048576 | bytes 2097152 | tf_op jit(solution)/shard_map/concatenate | solution.py:274
  (4 shorter events, 0.1 us)
Async XLA Ops:
  1.0 8.4 %collective-permute-start = (bf16[1,8,64,128]{3,2,1,0:T(8,128)(2,1)S(1)}, bf16[1,8,64,128]{3,2,1,0:T(8,128)(2,1)S(1)}, u32[]{:S(2)}, u32[]{:S(2)}) collective-permute-start(bf16[1,8,64,128]{3,2,1,0:T(8,128)(2,1)S(1)} %get-tuple-element.10), channel_id=1, source_target_pairs={{0,16},{16,32},{32,48},{48,64},{64,80},{80,96},{96,112},{1,17},{17... | collective-permute-start | bytes 393224 | tf_op jit(solution)/shard_map/ppermute | solution.py:27
  4.1 7.3 %collective-permute-start.1 = (bf16[1,8,64,128]{3,2,1,0:T(8,128)(2,1)S(1)}, bf16[1,8,64,128]{3,2,1,0:T(8,128)(2,1)S(1)}, u32[]{:S(2)}, u32[]{:S(2)}) collective-permute-start(bf16[1,8,64,128]{3,2,1,0:T(8,128)(2,1)S(1)} %get-tuple-element.9), channel_id=1, source_target_pairs={{16,0},{32,16},{48,32},{64,48},{80,64},{96,80},{112,96},{17,1},{33... | collective-permute-start | bytes 393224 | tf_op jit(solution)/shard_map/ppermute | solution.py:27
  9.4 11.3 %copy-start.3 = (bf16[3,64,144]{2,1,0:T(8,128)(2,1)S(1)}, bf16[3,64,144]{2,1,0:T(8,128)(2,1)}, u32[]{:S(2)}) copy-start(bf16[3,64,144]{2,1,0:T(8,128)(2,1)} %param.8) | copy-start | bytes 165892
  9.4 11.5 %copy-start.2 = (bf16[3,3,144,64]{2,3,1,0:T(8,128)(2,1)S(1)}, bf16[3,3,144,64]{2,3,1,0:T(8,128)(2,1)}, u32[]{:S(2)}) copy-start(bf16[3,3,144,64]{2,3,1,0:T(8,128)(2,1)} %param.7) | copy-start | bytes 497668
  12.3 18.4 %collective-permute-start.2 = (bf16[18,2,64,128]{3,2,1,0:T(8,128)(2,1)}, bf16[18,2,64,128]{3,2,1,0:T(8,128)(2,1)S(1)}, u32[]{:S(2)}, u32[]{:S(2)}) collective-permute-start(bf16[18,2,64,128]{3,2,1,0:T(8,128)(2,1)} %slice.40), channel_id=1, source_target_pairs={{0,1},{1,2},{2,3},{3,4},{4,5},{5,6},{6,7},{7,8},{8,9},{9,10},{10,1... | collective-permute-start | bytes 1769480 | tf_op jit(solution)/shard_map/ppermute | solution.py:27
  18.7 12.0 %collective-permute-start.3 = (bf16[18,1,64,128]{3,2,1,0:T(8,128)(2,1)}, bf16[18,1,64,128]{3,2,1,0:T(8,128)(2,1)}, u32[]{:S(2)}, u32[]{:S(2)}) collective-permute-start(bf16[18,1,64,128]{3,2,1,0:T(8,128)(2,1)} %slice.41), channel_id=1, source_target_pairs={{1,0},{2,1},{3,2},{4,3},{5,4},{6,5},{7,6},{8,7},{9,8},{10,9},{11,1... | collective-permute-start | bytes 884744 | tf_op jit(solution)/shard_map/ppermute | solution.py:27
  32.1 26.5 %copy-start.1 = (bf16[3,3,288,128]{3,2,1,0:T(8,128)(2,1)S(1)}, bf16[3,3,288,128]{3,2,1,0:T(8,128)(2,1)}, u32[]{:S(2)}) copy-start(bf16[3,3,288,128]{3,2,1,0:T(8,128)(2,1)} %param.10) | copy-start | bytes 1990660
  54.2 5.9 %collective-permute-start.4 = (bf16[16,1,64,128]{3,2,1,0:T(8,128)(2,1)}, bf16[16,1,64,128]{3,2,1,0:T(8,128)(2,1)S(1)}, u32[]{:S(2)}, u32[]{:S(2)}) collective-permute-start(bf16[16,1,64,128]{3,2,1,0:T(8,128)(2,1)} %get-tuple-element.11), channel_id=1, source_target_pairs={{0,1},{1,2},{2,3},{3,4},{4,5},{5,6},{6,7},{7,8},{8,9},{9,10},{10,1... | collective-permute-start | bytes 786440 | tf_op jit(solution)/shard_map/ppermute | solution.py:27
  56.5 11.3 %collective-permute-start.5 = (bf16[16,1,64,128]{3,2,1,0:T(8,128)(2,1)S(1)}, bf16[16,1,64,128]{3,2,1,0:T(8,128)(2,1)S(1)}, u32[]{:S(2)}, u32[]{:S(2)}) collective-permute-start(bf16[16,1,64,128]{3,2,1,0:T(8,128)(2,1)S(1)} %get-tuple-element.12), channel_id=1, source_target_pairs={{1,0},{2,1},{3,2},{4,3},{5,4},{6,5},{7,6},{8,7},{9,8},{10,9},{11,1... | collective-permute-start | bytes 786440 | tf_op jit(solution)/shard_map/ppermute | solution.py:27
  68.0 8.8 %copy-start = (bf16[3,128,288]{1,2,0:T(8,128)(2,1)S(1)}, bf16[3,128,288]{1,2,0:T(8,128)(2,1)}, u32[]{:S(2)}) copy-start(bf16[3,128,288]{1,2,0:T(8,128)(2,1)} %param.11) | copy-start | bytes 663556
  68.9 19.7 %collective-permute-start.6 = (bf16[1,256,288]{2,1,0:T(8,128)(2,1)S(1)}, bf16[1,256,288]{2,1,0:T(8,128)(2,1)S(1)}, u32[]{:S(2)}, u32[]{:S(2)}) collective-permute-start(bf16[1,256,288]{2,1,0:T(8,128)(2,1)S(1)} %get-tuple-element.14), channel_id=1, source_target_pairs={{0,16},{16,32},{32,48},{48,64},{64,80},{80,96},{96,112},{1,17},{17... | collective-permute-start | bytes 442376 | tf_op jit(solution)/shard_map/ppermute | solution.py:27
  71.0 17.6 %collective-permute-start.7 = (bf16[1,256,288]{2,1,0:T(8,128)(2,1)S(1)}, bf16[1,256,288]{2,1,0:T(8,128)(2,1)S(1)}, u32[]{:S(2)}, u32[]{:S(2)}) collective-permute-start(bf16[1,256,288]{2,1,0:T(8,128)(2,1)S(1)} %get-tuple-element.13), channel_id=1, source_target_pairs={{16,0},{32,16},{48,32},{64,48},{80,64},{96,80},{112,96},{17,1},{33... | collective-permute-start | bytes 442376 | tf_op jit(solution)/shard_map/ppermute | solution.py:27

commit v7 on v6

--- a/solution.py
+++ b/solution.py
@@ -64,71 +64,88 @@
     return jnp.where(inside, rolled, jnp.zeros_like(rolled))
 
 
-def _block_one_kernel(keep_ref, xp_ref, w9_ref, t3_ref, wd_ref, out_ref, mid_ref):
-    frames_p, rows_p, channels, width = xp_ref.shape
-    rows = rows_p - 2
-    frames = frames_p - 2
+def _middle_one(xp_ref, f, w9_ref):
+    rows = xp_ref.shape[1] - 2
+    slab = xp_ref[f].astype(jnp.float32)
+    shifted = [_lane_shift(slab, b - 1).astype(jnp.bfloat16) for b in range(3)]
+    parts = []
+    for a in range(3):
+        for b in range(3):
+            parts.append(jnp.concatenate([shifted[b][h + a] for h in range(rows)], axis=1))
+    stacked = jnp.concatenate(parts, axis=0)
+    m = jnp.dot(w9_ref[...], stacked, preferred_element_type=jnp.float32)
+    return jnp.maximum(m, 0.0).astype(jnp.bfloat16)
+
+
+def _section_down(stacked, xp_ref, t, t3_ref, wd_ref, keep_ref, out_ref, slot):
+    rows = xp_ref.shape[1] - 2
+    width = xp_ref.shape[-1]
     reduced_rows = (rows - 1) // 2
-
-    def middle(f, carry):
-        slab = xp_ref[f].astype(jnp.float32)
-        shifted = [_lane_shift(slab, b - 1).astype(jnp.bfloat16) for b in range(3)]
-        parts = []
-        for a in range(3):
-            for b in range(3):
-                parts.append(jnp.concatenate([shifted[b][h + a] for h in range(rows)], axis=1))
-        stacked = jnp.concatenate(parts, axis=0)
-        m = jnp.dot(w9_ref[...], stacked, preferred_element_type=jnp.float32)
-        m = jnp.maximum(m, 0.0).astype(jnp.bfloat16)
-        for h in range(rows):
-            mid_ref[f, h] = m[:, h * width : (h + 1) * width]
-        return carry
-
-    lax.fori_loop(0, frames_p, middle, 0)
-
     lane = lax.broadcasted_iota(jnp.int32, (width // 2, width), 1)
     column = lax.broadcasted_iota(jnp.int32, (width // 2, width), 0)
     pick = (lane == 2 * column).astype(jnp.bfloat16)
-    keep_first = keep_ref[0].astype(jnp.float32)
+    s = jnp.dot(t3_ref[...], stacked, preferred_element_type=jnp.float32)
+    sec = []
+    for h in range(rows):
+        v = s[:, h * width : (h + 1) * width] + xp_ref[t, h + 1].astype(jnp.float32)
+        v = jnp.maximum(v, 0.0)
+        if h == 0:
+            v = v * keep_ref[0].astype(jnp.float32)
+        sec.append(v.astype(jnp.bfloat16).astype(jnp.float32))
+    shifted = [[_lane_shift(r, b - 1).astype(jnp.bfloat16) for b in range(3)] for r in sec]
+    parts = []
+    for a in range(3):
+        for b in range(3):
+            parts.append(jnp.concatenate([shifted[2 * i + a][b] for i in range(reduced_rows)], axis=1))
+    stacked = jnp.concatenate(parts, axis=0)
+    full = jnp.dot(wd_ref[...], stacked, preferred_element_type=jnp.float32)
+    full = jnp.maximum(full, 0.0).astype(jnp.bfloat16)
+    for i in range(reduced_rows):
+        r = lax.dot_general(
+            pick,
+            full[:, i * width : (i + 1) * width],
+            (((1,), (1,)), ((), ())),
+            preferred_element_type=jnp.float32,
+        )
+        out_ref[slot, i] = r.astype(out_ref.dtype)
+
+
+def _edges_one_kernel(xp_ref, w9_ref, edge_ref):
+    frames = xp_ref.shape[0]
+    edge_ref[0] = _middle_one(xp_ref, 0, w9_ref)
+    edge_ref[1] = _middle_one(xp_ref, frames - 1, w9_ref)
+
+
+def _inner_one_kernel(keep_ref, xp_ref, w9_ref, t3_ref, wd_ref, out_ref, side_ref, mid_ref):
+    frames = xp_ref.shape[0]
+
+    def middle(f, carry):
+        mid_ref[f] = _middle_one(xp_ref, f, w9_ref)
+        return carry
+
+    lax.fori_loop(0, frames, middle, 0)
+    side_ref[0] = mid_ref[1]
+    side_ref[1] = mid_ref[frames - 2]
 
     def section(t, carry):
-        parts = []
-        for k in range(3):
-            parts.append(jnp.concatenate([mid_ref[t + k, h] for h in range(rows)], axis=1))
-        stacked = jnp.concatenate(parts, axis=0)
-        s = jnp.dot(t3_ref[...], stacked, preferred_element_type=jnp.float32)
-        sec = []
-        for h in range(rows):
-            v = s[:, h * width : (h + 1) * width] + xp_ref[t + 1, h + 1].astype(jnp.float32)
-            v = jnp.maximum(v, 0.0)
-            if h == 0:
-                v = v * keep_first
-            sec.append(v.astype(jnp.bfloat16).astype(jnp.float32))
-        shifted = [[_lane_shift(r, b - 1).astype(jnp.bfloat16) for b in range(3)] for r in sec]
-        parts = []
-        for a in range(3):
-            for b in range(3):
-                parts.append(
-                    jnp.concatenate([shifted[2 * i + a][b] for i in range(reduced_rows)], axis=1)
-                )
-        stacked = jnp.concatenate(parts, axis=0)
-        full = jnp.dot(wd_ref[...], stacked, preferred_element_type=jnp.float32)
-        full = jnp.maximum(full, 0.0).astype(jnp.bfloat16)
-        for i in range(reduced_rows):
-            r = lax.dot_general(
-                pick,
-                full[:, i * width : (i + 1) * width],
-                (((1,), (1,)), ((), ())),
-                preferred_element_type=jnp.float32,
-            )
-            out_ref[t, i] = r.astype(out_ref.dtype)
+        stacked = jnp.concatenate([mid_ref[t - 1], mid_ref[t], mid_ref[t + 1]], axis=0)
+        _section_down(stacked, xp_ref, t, t3_ref, wd_ref, keep_ref, out_ref, t - 1)
         return carry
 
-    lax.fori_loop(0, frames, section, 0)
-
-
-def block_one(padded, keep_first, spatial_kernel, temporal_kernel, down_kernel):
-    frames_p, rows_p, channels, width = padded.shape
+    lax.fori_loop(1, frames - 1, section, 0)
+
+
+def _outer_one_kernel(keep_ref, xp_ref, t3_ref, wd_ref, before_ref, after_ref, edge_ref, side_ref, out_ref):
+    frames = xp_ref.shape[0]
+    stacked = jnp.concatenate([before_ref[0], edge_ref[0], side_ref[0]], axis=0)
+    _section_down(stacked, xp_ref, 0, t3_ref, wd_ref, keep_ref, out_ref, 0)
+    stacked = jnp.concatenate([side_ref[1], edge_ref[1], after_ref[0]], axis=0)
+    _section_down(stacked, xp_ref, frames - 1, t3_ref, wd_ref, keep_ref, out_ref, 1)
+
+
+def block_one(rowed, keep_first, spatial_kernel, temporal_kernel, down_kernel):
+    frames, rows_p, channels, width = rowed.shape
+    rows = rows_p - 2
     mids = spatial_kernel.shape[2]
     outs = down_kernel.shape[2]
     w9 = jnp.transpose(spatial_kernel, (2, 0, 1, 3)).reshape(mids, 9 * channels)
@@ -136,25 +153,46 @@
     wd = jnp.transpose(down_kernel, (2, 0, 1, 3)).reshape(outs, 9 * channels)
     vmem = pltpu.MemorySpace.VMEM if hasattr(pltpu, "MemorySpace") else pltpu.VMEM
     smem = pltpu.MemorySpace.SMEM if hasattr(pltpu, "MemorySpace") else pltpu.SMEM
-    reduced_rows = (rows_p - 3) // 2
-    return pl.pallas_call(
-        _block_one_kernel,
-        out_shape=jax.ShapeDtypeStruct((frames_p - 2, reduced_rows, width // 2, outs), padded.dtype),
-        in_specs=[pl.BlockSpec(memory_space=smem)] + [pl.BlockSpec(memory_space=vmem)] * 4,
-        out_specs=pl.BlockSpec(memory_space=vmem),
-        scratch_shapes=[pltpu.VMEM((frames_p, rows_p - 2, mids, width), jnp.bfloat16)],
-        compiler_params=pltpu.CompilerParams(vmem_limit_bytes=48 * 1024 * 1024),
-    )(keep_first, padded, w9, t3, wd)
-
-
-def with_halo_one(block):
-    frames, rows = block.shape[0], block.shape[1]
-    before = from_behind(block[frames - 1 :], "tm", 1)
-    after = from_behind(block[:1], "tm", -1)
-    block = jnp.concatenate([before, block, after], axis=0)
-    above = from_behind(block[:, rows - 2 :], "row", 1)
-    below = from_behind(block[:, :1], "row", -1)
-    return jnp.concatenate([above, block, below], axis=1)
+    params = pltpu.CompilerParams(vmem_limit_bytes=48 * 1024 * 1024)
+    spec = pl.BlockSpec(memory_space=vmem)
+    sspec = pl.BlockSpec(memory_space=smem)
+    reduced_rows = (rows - 1) // 2
+    plane = (mids, rows * width)
+    out_plane = (reduced_rows, width // 2, outs)
+    spatial_flops = 2 * rows * width * 9 * channels * mids
+    section_flops = 2 * rows * width * 3 * mids * channels + 2 * reduced_rows * width * 9 * channels * outs
+    edges = pl.pallas_call(
+        _edges_one_kernel,
+        out_shape=jax.ShapeDtypeStruct((2,) + plane, rowed.dtype),
+        in_specs=[spec] * 2,
+        out_specs=spec,
+        compiler_params=params,
+        cost_estimate=pl.CostEstimate(flops=2 * spatial_flops, bytes_accessed=2 * rowed.size, transcendentals=0),
+    )(rowed, w9)
+    before = from_behind(edges[1:], "tm", 1)
+    after = from_behind(edges[:1], "tm", -1)
+    inner, side = pl.pallas_call(
+        _inner_one_kernel,
+        out_shape=(
+            jax.ShapeDtypeStruct((frames - 2,) + out_plane, rowed.dtype),
+            jax.ShapeDtypeStruct((2,) + plane, rowed.dtype),
+        ),
+        in_specs=[sspec] + [spec] * 4,
+        out_specs=(spec, spec),
+        scratch_shapes=[pltpu.VMEM((frames,) + plane, jnp.bfloat16)],
+        compiler_params=params,
+        cost_estimate=pl.CostEstimate(
+            flops=frames * (spatial_flops + section_flops), bytes_accessed=4 * rowed.size, transcendentals=0
+        ),
+    )(keep_first, rowed, w9, t3, wd)
+    outer = pl.pallas_call(
+        _outer_one_kernel,
+        out_shape=jax.ShapeDtypeStruct((2,) + out_plane, rowed.dtype),
+        in_specs=[sspec] + [spec] * 7,
+        out_specs=spec,
+        compiler_params=params,
+    )(keep_first, rowed, t3, wd, before, after, edges, side)
+    return jnp.concatenate([outer[:1], inner, outer[1:]], axis=0)
 
 
 def _sublane_shift(x, by, axis):
@@ -275,7 +313,10 @@
 
 
 def on_device(video_clip, spatial_one, temporal_one, down_weight, spatial_two, temporal_two):
-    padded = with_halo_one(video_clip)
+    rows = video_clip.shape[1]
+    above = from_behind(video_clip[:, rows - 2 :], "row", 1)
+    below = from_behind(video_clip[:, :1], "row", -1)
+    padded = jnp.concatenate([above, video_clip, below], axis=1)
     keep_first = (lax.axis_index("row") > 0).astype(jnp.int32).reshape(1)
     reduced = block_one(padded, keep_first, spatial_one, temporal_one, down_weight)
     rows = reduced.shape[1]

time: 90.6 us -> 88.1 us (0.972)
  the two profiles are of different devices: /device:TPU:57 before, /device:TPU:96 now
where the time goes in v7:
time: 88.1 us; the launch traced here: 87.6 us
  Pallas kernels  34.2 us (39%)
  starting transfers between devices  33.7 us (38%)
  waiting for transfers between devices  9.4 us (11%)
  local copies, waits for them, and re-layouts  8 us (9%)
  other arithmetic  2.13 us (2%)
    ppermute x8, starting transfers between devices, from_behind(): return lax.ppermute(array, axis, pairs)  33.7 us
    pallas_call x1, Pallas kernels, block_one(): pl.pallas_call(_inner_one_kernel, out_shape=(jax.ShapeDtypeStruct((frames...  18.9 us
    pallas_call x1, Pallas kernels, block_two(): pl.pallas_call(_inner_two_kernel, out_shape=(jax.ShapeDtypeStruct((frames...  11.8 us
    ppermute x8, waiting for transfers between devices, from_behind(): return lax.ppermute(array, axis, pairs)  9.4 us
    slice x1, local copies, waits for them, and re-layouts, on_device(): above = from_behind(video_clip[:, rows - 2:], 'row', 1)  2.03 us
  transfers between devices with their start and end apart: 8, of which 4 were waited for; matrix products, arithmetic and copies ran while one was open for 7% of the time, Pallas kernels for 35%

profile of v7, /device:TPU:96, one launch (start us, length us, event | category | flops | bytes accessed | tf_op | source)
XLA Modules:
  0.0 87.6 jit_solution(2128377594760508954)
XLA Ops:
  0.0 0.0 copy-start.1
  0.0 2.0 %slice.36 = bf16[16,2,64,128]{3,2,1,0:T(8,128)(2,1)} slice(bf16[16,8,64,128]{3,2,1,0:T(8,128)(2,1)} %param.6), slice={[0:16], [6:8], [0:64], [0:128]} | slice | bytes 1048576 | tf_op jit(solution)/shard_map/slice | solution.py:317
  2.0 1.9 %collective-permute-start = (bf16[16,2,64,128]{3,2,1,0:T(8,128)(2,1)}, bf16[16,2,64,128]{3,2,1,0:T(8,128)(2,1)S(1)}, u32[]{:S(2)}, u32[]{:S(2)}) collective-permute-start(bf16[16,2,64,128]{3,2,1,0:T(8,128)(2,1)} %slice.36), channel_id=1, source_target_pairs={{0,1},{1,2},{2,3},{3,4},{4,5},{5,6},{6,7},{7,8},{8,9},{9,10},{10,1... | collective-permute-start | bytes 1572872 | tf_op jit(solution)/shard_map/ppermute | solution.py:27
  4.0 1.7 %slice.37 = bf16[16,1,64,128]{3,2,1,0:T(8,128)(2,1)} slice(bf16[16,8,64,128]{3,2,1,0:T(8,128)(2,1)} %param.6), slice={[0:16], [0:1], [0:64], [0:128]} | slice | bytes 524288 | tf_op jit(solution)/shard_map/slice | solution.py:318
  5.6 7.2 %collective-permute-start.1 = (bf16[16,1,64,128]{3,2,1,0:T(8,128)(2,1)}, bf16[16,1,64,128]{3,2,1,0:T(8,128)(2,1)S(1)}, u32[]{:S(2)}, u32[]{:S(2)}) collective-permute-start(bf16[16,1,64,128]{3,2,1,0:T(8,128)(2,1)} %slice.37), channel_id=1, source_target_pairs={{1,0},{2,1},{3,2},{4,3},{5,4},{6,5},{7,6},{8,7},{9,8},{10,9},{11,1... | collective-permute-start | bytes 786440 | tf_op jit(solution)/shard_map/ppermute | solution.py:27
  12.9 1.0 %copy.11 = bf16[64,3,144]{2,1,0:T(4,128)(2,1)S(1)} copy(bf16[64,3,144]{2,0,1:T(8,128)(2,1)} %bitcast.18) | data formatting | bytes 110592 | tf_op jit(solution)/shard_map/transpose | solution.py:152
  13.9 0.1 reshape.19.t3_ref
  14.0 1.1 %copy.15.wd_ref = bf16[128,576]{1,0:T(8,128)(2,1)S(1)} copy(bf16[128,576]{0,1:T(8,128)(2,1)} %bitcast.17) | data formatting | bytes 294912 | tf_op jit(solution)/shard_map/reshape | solution.py:153
  15.0 1.1 %copy.12.w9_ref = bf16[144,576]{1,0:T(8,128)(2,1)S(1)} copy(bf16[144,576]{0,1:T(8,128)(2,1)} %bitcast.16) | data formatting | bytes 331776 | tf_op jit(solution)/shard_map/reshape | solution.py:151
  16.2 0.2 collective-permute-done
  16.4 0.0 copy-done.1
  16.4 0.4 constant_dynamic-update-slice_fusion.1
  16.8 0.3 collective-permute-done.1
  17.1 0.8 shard_map.64.edge_ref
  17.9 0.1 fusion
  18.0 3.4 %collective-permute-start.2 = (bf16[1,144,1152]{2,1,0:T(8,128)(2,1)S(1)}, bf16[1,144,1152]{2,1,0:T(8,128)(2,1)S(1)}, u32[]{:S(2)}, u32[]{:S(2)}) collective-permute-start(bf16[1,144,1152]{2,1,0:T(8,128)(2,1)S(1)} %get-tuple-element.16), channel_id=1, source_target_pairs={{0,16},{16,32},{32,48},{48,64},{64,80},{80,96},{96,112},{1,17},{17... | collective-permute-start | bytes 995336 | tf_op jit(solution)/shard_map/ppermute | solution.py:27
  21.4 4.6 %collective-permute-start.3 = (bf16[1,144,1152]{2,1,0:T(8,128)(2,1)S(1)}, bf16[1,144,1152]{2,1,0:T(8,128)(2,1)S(1)}, u32[]{:S(2)}, u32[]{:S(2)}) collective-permute-start(bf16[1,144,1152]{2,1,0:T(8,128)(2,1)S(1)} %get-tuple-element.15), channel_id=1, source_target_pairs={{16,0},{32,16},{48,32},{64,48},{80,64},{96,80},{112,96},{17,1},{33... | collective-permute-start | bytes 995336 | tf_op jit(solution)/shard_map/ppermute | solution.py:27
  25.9 18.9 %shard_map.65 = (bf16[14,4,64,128]{3,2,1,0:T(8,128)(2,1)S(1)}, bf16[2,144,1152]{2,1,0:T(8,128)(2,1)S(1)}) custom-call(s32[1]{0:T(128)} %bitcast.keep_ref, bf16[16,11,64,128]{3,2,1,0:T(8,128)(2,1)S(1)} %constant_dynamic-update-slice_fusion.xp_ref, bf16[144,576]{1,0:T(8,128)(2,1)S(1)} %copy.12.w9_ref, bf16[64,432]{1,0:T(8,128)(2,1)S(1)} %reshape.19.t3_ref, ...), custom_call_target="tpu_custom_call" | custom-call | flops 5284823040 | bytes 5767168 | tf_op jit(solution)/shard_map/pallas_call | solution.py:174
  44.8 0.0 collective-permute-done.2.before_ref
  44.8 0.0 collective-permute-done.3.after_ref
  44.9 1.4 %shard_map.66 = bf16[2,4,64,128]{3,2,1,0:T(8,128)(2,1)S(1)} custom-call(s32[1]{0:T(128)} %bitcast.keep_ref, bf16[16,11,64,128]{3,2,1,0:T(8,128)(2,1)S(1)} %constant_dynamic-update-slice_fusion.xp_ref, bf16[64,432]{1,0:T(8,128)(2,1)S(1)} %reshape.19.t3_ref, bf16[128,576]{1,0:T(8,128)(2,1)S(1)} %copy.15.wd_ref, ...), custom_call_target="tpu_custom_call" | custom-call | tf_op jit(solution)/shard_map/pallas_call | solution.py:188
  46.2 0.0 copy-start.2
  46.3 0.8 pad_maximum_fusion.4
  47.1 6.7 %collective-permute-start.5 = (bf16[16,1,64,128]{3,2,1,0:T(8,128)(2,1)}, bf16[16,1,64,128]{3,2,1,0:T(8,128)(2,1)S(1)}, u32[]{:S(2)}, u32[]{:S(2)}) collective-permute-start(bf16[16,1,64,128]{3,2,1,0:T(8,128)(2,1)} %get-tuple-element.14), channel_id=1, source_target_pairs={{1,0},{2,1},{3,2},{4,3},{5,4},{6,5},{7,6},{8,7},{9,8},{10,9},{11,1... | collective-permute-start | bytes 786440 | tf_op jit(solution)/shard_map/ppermute | solution.py:27
  53.8 1.9 %collective-permute-start.4 = (bf16[16,1,64,128]{3,2,1,0:T(8,128)(2,1)S(1)}, bf16[16,1,64,128]{3,2,1,0:T(8,128)(2,1)S(1)}, u32[]{:S(2)}, u32[]{:S(2)}) collective-permute-start(bf16[16,1,64,128]{3,2,1,0:T(8,128)(2,1)S(1)} %get-tuple-element.13), channel_id=1, source_target_pairs={{0,1},{1,2},{2,3},{3,4},{4,5},{5,6},{6,7},{7,8},{8,9},{9,10},{10,1... | collective-permute-start | bytes 786440 | tf_op jit(solution)/shard_map/ppermute | solution.py:27
  55.7 0.0 copy-done.2
  55.8 0.4 copy.16
  56.2 1.8 %collective-permute-done.5 = bf16[16,1,64,128]{3,2,1,0:T(8,128)(2,1)S(1)} collective-permute-done((bf16[16,1,64,128]{3,2,1,0:T(8,128)(2,1)}, bf16[16,1,64,128]{3,2,1,0:T(8,128)(2,1)S(1)}, u32[]{:S(2)}, u32[]{:S(2)}) %collective-permute-start.5) | collective-permute-done | bytes 262176 | tf_op jit(solution)/shard_map/ppermute | solution.py:27
  58.0 7.1 %collective-permute-done.4 = bf16[16,1,64,128]{3,2,1,0:T(8,128)(2,1)S(1)} collective-permute-done((bf16[16,1,64,128]{3,2,1,0:T(8,128)(2,1)S(1)}, bf16[16,1,64,128]{3,2,1,0:T(8,128)(2,1)S(1)}, u32[]{:S(2)}, u32[]{:S(2)}) %collective-permute-start.4) | collective-permute-done | bytes 262176 | tf_op jit(solution)/shard_map/ppermute | solution.py:27
  65.1 0.3 pad_maximum_fusion.xp_ref
  65.4 0.0 copy-start
  65.4 0.8 shard_map.67.edge_ref
  66.3 1.9 %collective-permute-start.6 = (bf16[1,256,288]{2,1,0:T(8,128)(2,1)S(1)}, bf16[1,256,288]{2,1,0:T(8,128)(2,1)S(1)}, u32[]{:S(2)}, u32[]{:S(2)}) collective-permute-start(bf16[1,256,288]{2,1,0:T(8,128)(2,1)S(1)} %get-tuple-element.18), channel_id=1, source_target_pairs={{0,16},{16,32},{32,48},{48,64},{64,80},{80,96},{96,112},{1,17},{17... | collective-permute-start | bytes 442376 | tf_op jit(solution)/shard_map/ppermute | solution.py:27
  68.2 6.0 %collective-permute-start.7 = (bf16[1,256,288]{2,1,0:T(8,128)(2,1)S(1)}, bf16[1,256,288]{2,1,0:T(8,128)(2,1)S(1)}, u32[]{:S(2)}, u32[]{:S(2)}) collective-permute-start(bf16[1,256,288]{2,1,0:T(8,128)(2,1)S(1)} %get-tuple-element.17), channel_id=1, source_target_pairs={{16,0},{32,16},{48,32},{64,48},{80,64},{96,80},{112,96},{17,1},{33... | collective-permute-start | bytes 442376 | tf_op jit(solution)/shard_map/ppermute | solution.py:27
  74.2 0.0 copy-done
  74.2 11.8 %shard_map.68 = (bf16[14,4,64,128]{3,2,1,0:T(8,128)(2,1)S(1)}, bf16[2,256,288]{2,1,0:T(8,128)(2,1)S(1)}) custom-call(bf16[16,6,64,128]{3,2,1,0:T(8,128)(2,1)S(1)} %pad_maximum_fusion.xp_ref, bf16[1152,288]{1,0:T(8,128)(2,1)S(1)} %bitcast.12, bf16[3,288,128]{2,1,0:T(8,128)(2,1)S(1)} %bitcast.13), custom_call_target="tpu_custom_call" | custom-call | flops 3623878656 | bytes 3145728 | tf_op jit(solution)/shard_map/pallas_call | solution.py:289
  86.0 0.0 collective-permute-done.6.before_ref
  86.1 0.0 collective-permute-done.7.after_ref
  86.1 0.5 shard_map.69
  86.5 1.1 %pad_maximum_fusion.1 = bf16[16,4,64,128]{3,2,1,0:T(8,128)(2,1)} fusion(bf16[1,4,64,128]{3,2,1,0:T(8,128)(2,1)S(1)} %get-tuple-element.20, bf16[14,4,64,128]{3,2,1,0:T(8,128)(2,1)S(1)} %get-tuple-element.12, bf16[1,4,64,128]{3,2,1,0:T(8,128)(2,1)S(1)} %get-tuple-element.19), kind=kLoop, calls=%fused_computation.1 | loop fusion | flops 1048576 | bytes 2097152 | tf_op jit(solution)/shard_map/concatenate | solution.py:312
  (5 shorter events, 0.1 us)
Async XLA Ops:
  0.0 16.4 %copy-start.1 = (bf16[16,8,64,128]{3,2,1,0:T(8,128)(2,1)S(1)}, bf16[16,8,64,128]{3,2,1,0:T(8,128)(2,1)}, u32[]{:S(2)}) copy-start(bf16[16,8,64,128]{3,2,1,0:T(8,128)(2,1)} %param.6) | copy-start | bytes 6291460
  2.0 14.3 %collective-permute-start = (bf16[16,2,64,128]{3,2,1,0:T(8,128)(2,1)}, bf16[16,2,64,128]{3,2,1,0:T(8,128)(2,1)S(1)}, u32[]{:S(2)}, u32[]{:S(2)}) collective-permute-start(bf16[16,2,64,128]{3,2,1,0:T(8,128)(2,1)} %slice.36), channel_id=1, source_target_pairs={{0,1},{1,2},{2,3},{3,4},{4,5},{5,6},{6,7},{7,8},{8,9},{9,10},{10,1... | collective-permute-start | bytes 1572872 | tf_op jit(solution)/shard_map/ppermute | solution.py:27
  5.6 11.4 %collective-permute-start.1 = (bf16[16,1,64,128]{3,2,1,0:T(8,128)(2,1)}, bf16[16,1,64,128]{3,2,1,0:T(8,128)(2,1)S(1)}, u32[]{:S(2)}, u32[]{:S(2)}) collective-permute-start(bf16[16,1,64,128]{3,2,1,0:T(8,128)(2,1)} %slice.37), channel_id=1, source_target_pairs={{1,0},{2,1},{3,2},{4,3},{5,4},{6,5},{7,6},{8,7},{9,8},{10,9},{11,1... | collective-permute-start | bytes 786440 | tf_op jit(solution)/shard_map/ppermute | solution.py:27
  18.0 26.9 %collective-permute-start.2 = (bf16[1,144,1152]{2,1,0:T(8,128)(2,1)S(1)}, bf16[1,144,1152]{2,1,0:T(8,128)(2,1)S(1)}, u32[]{:S(2)}, u32[]{:S(2)}) collective-permute-start(bf16[1,144,1152]{2,1,0:T(8,128)(2,1)S(1)} %get-tuple-element.16), channel_id=1, source_target_pairs={{0,16},{16,32},{32,48},{48,64},{64,80},{80,96},{96,112},{1,17},{17... | collective-permute-start | bytes 995336 | tf_op jit(solution)/shard_map/ppermute | solution.py:27
  21.4 23.5 %collective-permute-start.3 = (bf16[1,144,1152]{2,1,0:T(8,128)(2,1)S(1)}, bf16[1,144,1152]{2,1,0:T(8,128)(2,1)S(1)}, u32[]{:S(2)}, u32[]{:S(2)}) collective-permute-start(bf16[1,144,1152]{2,1,0:T(8,128)(2,1)S(1)} %get-tuple-element.15), channel_id=1, source_target_pairs={{16,0},{32,16},{48,32},{64,48},{80,64},{96,80},{112,96},{17,1},{33... | collective-permute-start | bytes 995336 | tf_op jit(solution)/shard_map/ppermute | solution.py:27
  46.2 9.5 %copy-start.2 = (bf16[3,3,288,128]{3,2,1,0:T(8,128)(2,1)S(1)}, bf16[3,3,288,128]{3,2,1,0:T(8,128)(2,1)}, u32[]{:S(2)}) copy-start(bf16[3,3,288,128]{3,2,1,0:T(8,128)(2,1)} %param.10) | copy-start | bytes 1990660
  47.1 10.9 %collective-permute-start.5 = (bf16[16,1,64,128]{3,2,1,0:T(8,128)(2,1)}, bf16[16,1,64,128]{3,2,1,0:T(8,128)(2,1)S(1)}, u32[]{:S(2)}, u32[]{:S(2)}) collective-permute-start(bf16[16,1,64,128]{3,2,1,0:T(8,128)(2,1)} %get-tuple-element.14), channel_id=1, source_target_pairs={{1,0},{2,1},{3,2},{4,3},{5,4},{6,5},{7,6},{8,7},{9,8},{10,9},{11,1... | collective-permute-start | bytes 786440 | tf_op jit(solution)/shard_map/ppermute | solution.py:27
  53.8 11.3 %collective-permute-start.4 = (bf16[16,1,64,128]{3,2,1,0:T(8,128)(2,1)S(1)}, bf16[16,1,64,128]{3,2,1,0:T(8,128)(2,1)S(1)}, u32[]{:S(2)}, u32[]{:S(2)}) collective-permute-start(bf16[16,1,64,128]{3,2,1,0:T(8,128)(2,1)S(1)} %get-tuple-element.13), channel_id=1, source_target_pairs={{0,1},{1,2},{2,3},{3,4},{4,5},{5,6},{6,7},{7,8},{8,9},{9,10},{10,1... | collective-permute-start | bytes 786440 | tf_op jit(solution)/shard_map/ppermute | solution.py:27
  65.4 8.8 %copy-start = (bf16[3,128,288]{1,2,0:T(8,128)(2,1)S(1)}, bf16[3,128,288]{1,2,0:T(8,128)(2,1)}, u32[]{:S(2)}) copy-start(bf16[3,128,288]{1,2,0:T(8,128)(2,1)} %param.11) | copy-start | bytes 663556
  66.3 19.8 %collective-permute-start.6 = (bf16[1,256,288]{2,1,0:T(8,128)(2,1)S(1)}, bf16[1,256,288]{2,1,0:T(8,128)(2,1)S(1)}, u32[]{:S(2)}, u32[]{:S(2)}) collective-permute-start(bf16[1,256,288]{2,1,0:T(8,128)(2,1)S(1)} %get-tuple-element.18), channel_id=1, source_target_pairs={{0,16},{16,32},{32,48},{48,64},{64,80},{80,96},{96,112},{1,17},{17... | collective-permute-start | bytes 442376 | tf_op jit(solution)/shard_map/ppermute | solution.py:27
  68.2 17.9 %collective-permute-start.7 = (bf16[1,256,288]{2,1,0:T(8,128)(2,1)S(1)}, bf16[1,256,288]{2,1,0:T(8,128)(2,1)S(1)}, u32[]{:S(2)}, u32[]{:S(2)}) collective-permute-start(bf16[1,256,288]{2,1,0:T(8,128)(2,1)S(1)} %get-tuple-element.17), channel_id=1, source_target_pairs={{16,0},{32,16},{48,32},{64,48},{80,64},{96,80},{112,96},{17,1},{33... | collective-permute-start | bytes 442376 | tf_op jit(solution)/shard_map/ppermute | solution.py:27

commit v8 on v7

--- a/solution.py
+++ b/solution.py
@@ -64,9 +64,10 @@
     return jnp.where(inside, rolled, jnp.zeros_like(rolled))
 
 
-def _middle_one(xp_ref, f, w9_ref):
-    rows = xp_ref.shape[1] - 2
-    slab = xp_ref[f].astype(jnp.float32)
+def _middle_one(refs, f, w9_ref):
+    above_ref, xp_ref, below_ref = refs
+    rows = xp_ref.shape[1] + 1
+    slab = jnp.concatenate([above_ref[f], xp_ref[f], below_ref[f]], axis=0).astype(jnp.float32)
     shifted = [_lane_shift(slab, b - 1).astype(jnp.bfloat16) for b in range(3)]
     parts = []
     for a in range(3):
@@ -77,8 +78,9 @@
     return jnp.maximum(m, 0.0).astype(jnp.bfloat16)
 
 
-def _section_down(stacked, xp_ref, t, t3_ref, wd_ref, keep_ref, out_ref, slot):
-    rows = xp_ref.shape[1] - 2
+def _section_down(stacked, refs, t, t3_ref, wd_ref, keep_ref, out_ref, slot):
+    above_ref, xp_ref, _ = refs
+    rows = xp_ref.shape[1] + 1
     width = xp_ref.shape[-1]
     reduced_rows = (rows - 1) // 2
     lane = lax.broadcasted_iota(jnp.int32, (width // 2, width), 1)
@@ -87,7 +89,8 @@
     s = jnp.dot(t3_ref[...], stacked, preferred_element_type=jnp.float32)
     sec = []
     for h in range(rows):
-        v = s[:, h * width : (h + 1) * width] + xp_ref[t, h + 1].astype(jnp.float32)
+        own = above_ref[t, 1] if h == 0 else xp_ref[t, h - 1]
+        v = s[:, h * width : (h + 1) * width] + own.astype(jnp.float32)
         v = jnp.maximum(v, 0.0)
         if h == 0:
             v = v * keep_ref[0].astype(jnp.float32)
@@ -110,17 +113,19 @@
         out_ref[slot, i] = r.astype(out_ref.dtype)
 
 
-def _edges_one_kernel(xp_ref, w9_ref, edge_ref):
-    frames = xp_ref.shape[0]
-    edge_ref[0] = _middle_one(xp_ref, 0, w9_ref)
-    edge_ref[1] = _middle_one(xp_ref, frames - 1, w9_ref)
-
-
-def _inner_one_kernel(keep_ref, xp_ref, w9_ref, t3_ref, wd_ref, out_ref, side_ref, mid_ref):
+def _edges_one_kernel(above_ref, xp_ref, below_ref, w9_ref, edge_ref):
+    refs = (above_ref, xp_ref, below_ref)
+    frames = xp_ref.shape[0]
+    edge_ref[0] = _middle_one(refs, 0, w9_ref)
+    edge_ref[1] = _middle_one(refs, frames - 1, w9_ref)
+
+
+def _inner_one_kernel(keep_ref, above_ref, xp_ref, below_ref, w9_ref, t3_ref, wd_ref, out_ref, side_ref, mid_ref):
+    refs = (above_ref, xp_ref, below_ref)
     frames = xp_ref.shape[0]
 
     def middle(f, carry):
-        mid_ref[f] = _middle_one(xp_ref, f, w9_ref)
+        mid_ref[f] = _middle_one(refs, f, w9_ref)
         return carry
 
     lax.fori_loop(0, frames, middle, 0)
@@ -129,23 +134,26 @@
 
     def section(t, carry):
         stacked = jnp.concatenate([mid_ref[t - 1], mid_ref[t], mid_ref[t + 1]], axis=0)
-        _section_down(stacked, xp_ref, t, t3_ref, wd_ref, keep_ref, out_ref, t - 1)
+        _section_down(stacked, refs, t, t3_ref, wd_ref, keep_ref, out_ref, t - 1)
         return carry
 
     lax.fori_loop(1, frames - 1, section, 0)
 
 
-def _outer_one_kernel(keep_ref, xp_ref, t3_ref, wd_ref, before_ref, after_ref, edge_ref, side_ref, out_ref):
+def _outer_one_kernel(
+    keep_ref, above_ref, xp_ref, below_ref, t3_ref, wd_ref, before_ref, after_ref, edge_ref, side_ref, out_ref
+):
+    refs = (above_ref, xp_ref, below_ref)
     frames = xp_ref.shape[0]
     stacked = jnp.concatenate([before_ref[0], edge_ref[0], side_ref[0]], axis=0)
-    _section_down(stacked, xp_ref, 0, t3_ref, wd_ref, keep_ref, out_ref, 0)
+    _section_down(stacked, refs, 0, t3_ref, wd_ref, keep_ref, out_ref, 0)
     stacked = jnp.concatenate([side_ref[1], edge_ref[1], after_ref[0]], axis=0)
-    _section_down(stacked, xp_ref, frames - 1, t3_ref, wd_ref, keep_ref, out_ref, 1)
-
-
-def block_one(rowed, keep_first, spatial_kernel, temporal_kernel, down_kernel):
-    frames, rows_p, channels, width = rowed.shape
-    rows = rows_p - 2
+    _section_down(stacked, refs, frames - 1, t3_ref, wd_ref, keep_ref, out_ref, 1)
+
+
+def block_one(above, rowed, below, keep_first, spatial_kernel, temporal_kernel, down_kernel):
+    frames, rows, channels, width = rowed.shape
+    rows = rows + 1
     mids = spatial_kernel.shape[2]
     outs = down_kernel.shape[2]
     w9 = jnp.transpose(spatial_kernel, (2, 0, 1, 3)).reshape(mids, 9 * channels)
@@ -164,11 +172,11 @@
     edges = pl.pallas_call(
         _edges_one_kernel,
         out_shape=jax.ShapeDtypeStruct((2,) + plane, rowed.dtype),
-        in_specs=[spec] * 2,
+        in_specs=[spec] * 4,
         out_specs=spec,
         compiler_params=params,
         cost_estimate=pl.CostEstimate(flops=2 * spatial_flops, bytes_accessed=2 * rowed.size, transcendentals=0),
-    )(rowed, w9)
+    )(above, rowed, below, w9)
     before = from_behind(edges[1:], "tm", 1)
     after = from_behind(edges[:1], "tm", -1)
     inner, side = pl.pallas_call(
@@ -177,21 +185,21 @@
             jax.ShapeDtypeStruct((frames - 2,) + out_plane, rowed.dtype),
             jax.ShapeDtypeStruct((2,) + plane, rowed.dtype),
         ),
-        in_specs=[sspec] + [spec] * 4,
+        in_specs=[sspec] + [spec] * 6,
         out_specs=(spec, spec),
         scratch_shapes=[pltpu.VMEM((frames,) + plane, jnp.bfloat16)],
         compiler_params=params,
         cost_estimate=pl.CostEstimate(
             flops=frames * (spatial_flops + section_flops), bytes_accessed=4 * rowed.size, transcendentals=0
         ),
-    )(keep_first, rowed, w9, t3, wd)
+    )(keep_first, above, rowed, below, w9, t3, wd)
     outer = pl.pallas_call(
         _outer_one_kernel,
         out_shape=jax.ShapeDtypeStruct((2,) + out_plane, rowed.dtype),
-        in_specs=[sspec] + [spec] * 7,
+        in_specs=[sspec] + [spec] * 9,
         out_specs=spec,
         compiler_params=params,
-    )(keep_first, rowed, t3, wd, before, after, edges, side)
+    )(keep_first, above, rowed, below, t3, wd, before, after, edges, side)
     return jnp.concatenate([outer[:1], inner, outer[1:]], axis=0)
 
 
@@ -203,53 +211,68 @@
     return jnp.where(inside, rolled, jnp.zeros_like(rolled))
 
 
-def _middle_two(xp_ref, f, w9_ref):
-    rows = xp_ref.shape[1] - 2
-    slab = xp_ref[f].astype(jnp.float32)
-    shifted = [_sublane_shift(slab, b - 1, 1).astype(jnp.bfloat16) for b in range(3)]
-    stacked = jnp.concatenate(
-        [
-            jnp.concatenate([shifted[b][i + a] for a in range(3) for b in range(3)], axis=1)
-            for i in range(rows)
-        ],
-        axis=0,
-    )
+def _slab_two(above_ref, xp_ref, below_ref, f):
+    return jnp.concatenate([above_ref[f], xp_ref[f], below_ref[f]], axis=0).astype(jnp.float32)
+
+
+def _middle_two(slabs, w9_ref):
+    rows = slabs[0].shape[0] - 2
+    pieces = []
+    for slab in slabs:
+        shifted = [_sublane_shift(slab, b - 1, 1).astype(jnp.bfloat16) for b in range(3)]
+        for i in range(rows):
+            pieces.append(jnp.concatenate([shifted[b][i + a] for a in range(3) for b in range(3)], axis=1))
+    stacked = jnp.concatenate(pieces, axis=0)
     m = jnp.dot(stacked, w9_ref[...], preferred_element_type=jnp.float32)
     return jnp.maximum(m, 0.0).astype(jnp.bfloat16)
 
 
-def _edges_two_kernel(xp_ref, w9_ref, edge_ref):
-    frames = xp_ref.shape[0]
-    edge_ref[0] = _middle_two(xp_ref, 0, w9_ref)
-    edge_ref[1] = _middle_two(xp_ref, frames - 1, w9_ref)
+def _edges_two_kernel(above_ref, xp_ref, below_ref, w9_ref, edge_ref):
+    frames = xp_ref.shape[0]
+    plane = edge_ref.shape[1]
+    m = _middle_two(
+        [_slab_two(above_ref, xp_ref, below_ref, 0), _slab_two(above_ref, xp_ref, below_ref, frames - 1)], w9_ref
+    )
+    edge_ref[0] = m[:plane]
+    edge_ref[1] = m[plane:]
 
 
 def _finish(s, xp_ref, t, out_ref, slot):
-    rows, width = xp_ref.shape[1] - 2, xp_ref.shape[2]
+    rows, width = xp_ref.shape[1], xp_ref.shape[2]
     for i in range(rows):
-        v = s[i * width : (i + 1) * width] + xp_ref[t, i + 1].astype(jnp.float32)
+        v = s[i * width : (i + 1) * width] + xp_ref[t, i].astype(jnp.float32)
         out_ref[slot, i] = jnp.maximum(v, 0.0).astype(out_ref.dtype)
 
 
-def _inner_two_kernel(xp_ref, w9_ref, t3_ref, out_ref, side_ref, mid_ref):
-    frames = xp_ref.shape[0]
-
-    def middle(f, carry):
-        mid_ref[f] = _middle_two(xp_ref, f, w9_ref)
+def _inner_two_kernel(above_ref, xp_ref, below_ref, w9_ref, t3_ref, out_ref, side_ref, mid_ref):
+    frames = xp_ref.shape[0]
+    plane = mid_ref.shape[1]
+
+    def middle(g, carry):
+        f = 2 * g
+        m = _middle_two(
+            [_slab_two(above_ref, xp_ref, below_ref, f), _slab_two(above_ref, xp_ref, below_ref, f + 1)], w9_ref
+        )
+        mid_ref[f] = m[:plane]
+        mid_ref[f + 1] = m[plane:]
         return carry
 
-    lax.fori_loop(0, frames, middle, 0)
+    lax.fori_loop(0, frames // 2, middle, 0)
     side_ref[0] = mid_ref[1]
     side_ref[1] = mid_ref[frames - 2]
 
-    def section(t, carry):
-        s = jnp.dot(mid_ref[t - 1], t3_ref[0], preferred_element_type=jnp.float32)
-        s = s + jnp.dot(mid_ref[t], t3_ref[1], preferred_element_type=jnp.float32)
-        s = s + jnp.dot(mid_ref[t + 1], t3_ref[2], preferred_element_type=jnp.float32)
-        _finish(s, xp_ref, t, out_ref, t - 1)
+    def section(g, carry):
+        t = 2 * g + 1
+        s = None
+        for k in range(3):
+            pair = jnp.concatenate([mid_ref[t - 1 + k], mid_ref[t + k]], axis=0)
+            d = jnp.dot(pair, t3_ref[k], preferred_element_type=jnp.float32)
+            s = d if s is None else s + d
+        _finish(s[:plane], xp_ref, t, out_ref, t - 1)
+        _finish(s[plane:], xp_ref, t + 1, out_ref, t)
         return carry
 
-    lax.fori_loop(1, frames - 1, section, 0)
+    lax.fori_loop(0, (frames - 2) // 2, section, 0)
 
 
 def _outer_two_kernel(xp_ref, t3_ref, before_ref, after_ref, edge_ref, side_ref, out_ref):
@@ -264,9 +287,8 @@
     _finish(s, xp_ref, frames - 1, out_ref, 1)
 
 
-def block_two(rowed, spatial_kernel, temporal_kernel):
-    frames, rows_p, width, channels = rowed.shape
-    rows = rows_p - 2
+def block_two(above, rowed, below, spatial_kernel, temporal_kernel):
+    frames, rows, width, channels = rowed.shape
     mids = spatial_kernel.shape[2]
     w9 = jnp.transpose(spatial_kernel, (0, 1, 3, 2)).reshape(9 * channels, mids)
     t3 = jnp.transpose(temporal_kernel, (0, 2, 1))
@@ -277,13 +299,13 @@
     edges = pl.pallas_call(
         _edges_two_kernel,
         out_shape=jax.ShapeDtypeStruct((2,) + plane, rowed.dtype),
-        in_specs=[spec] * 2,
+        in_specs=[spec] * 4,
         out_specs=spec,
         compiler_params=params,
         cost_estimate=pl.CostEstimate(
             flops=2 * 2 * rows * width * 9 * channels * mids, bytes_accessed=2 * rowed.size, transcendentals=0
         ),
-    )(rowed, w9)
+    )(above, rowed, below, w9)
     before = from_behind(edges[1:], "tm", 1)
     after = from_behind(edges[:1], "tm", -1)
     inner, side = pl.pallas_call(
@@ -292,7 +314,7 @@
             jax.ShapeDtypeStruct((frames - 2, rows, width, channels), rowed.dtype),
             jax.ShapeDtypeStruct((2,) + plane, rowed.dtype),
         ),
-        in_specs=[spec] * 3,
+        in_specs=[spec] * 5,
         out_specs=(spec, spec),
         scratch_shapes=[pltpu.VMEM((frames,) + plane, jnp.bfloat16)],
         compiler_params=params,
@@ -301,7 +323,7 @@
             bytes_accessed=4 * rowed.size,
             transcendentals=0,
         ),
-    )(rowed, w9, t3)
+    )(above, rowed, below, w9, t3)
     outer = pl.pallas_call(
         _outer_two_kernel,
         out_shape=jax.ShapeDtypeStruct((2, rows, width, channels), rowed.dtype),
@@ -316,13 +338,12 @@
     rows = video_clip.shape[1]
     above = from_behind(video_clip[:, rows - 2 :], "row", 1)
     below = from_behind(video_clip[:, :1], "row", -1)
-    padded = jnp.concatenate([above, video_clip, below], axis=1)
     keep_first = (lax.axis_index("row") > 0).astype(jnp.int32).reshape(1)
-    reduced = block_one(padded, keep_first, spatial_one, temporal_one, down_weight)
+    reduced = block_one(above, video_clip, below, keep_first, spatial_one, temporal_one, down_weight)
     rows = reduced.shape[1]
     above = from_behind(reduced[:, rows - 1 :], "row", 1)
     below = from_behind(reduced[:, :1], "row", -1)
-    return block_two(jnp.concatenate([above, reduced, below], axis=1), spatial_two, temporal_two)
+    return block_two(above, reduced, below, spatial_two, temporal_two)
 
 
 def solution(mesh):

time: 88.1 us -> 83.2 us (0.944)
  the two profiles are of different devices: /device:TPU:96 before, /device:TPU:57 now
where the time goes in v8:
time: 83.2 us; the launch traced here: 82.8 us
  Pallas kernels  32 us (38%)
  starting transfers between devices  25.8 us (31%)
  waiting for transfers between devices  16.1 us (19%)
  local copies, waits for them, and re-layouts  7.4 us (9%)
  other arithmetic  1.24 us (1%)
    ppermute x8, starting transfers between devices, from_behind(): return lax.ppermute(array, axis, pairs)  25.8 us
    pallas_call x1, Pallas kernels, block_one(): pl.pallas_call(_inner_one_kernel, out_shape=(jax.ShapeDtypeStruct((frames...  18.9 us
    ppermute x8, waiting for transfers between devices, from_behind(): return lax.ppermute(array, axis, pairs)  16.1 us
    pallas_call x1, Pallas kernels, block_two(): pl.pallas_call(_inner_two_kernel, out_shape=(jax.ShapeDtypeStruct((frames...  9.62 us
    slice x1, local copies, waits for them, and re-layouts, on_device(): above = from_behind(video_clip[:, rows - 2:], 'row', 1)  2.04 us
    slice x1, local copies, waits for them, and re-layouts, on_device(): below = from_behind(video_clip[:, :1], 'row', -1)  1.68 us
  transfers between devices with their start and end apart: 8, of which 3 were waited for; matrix products, arithmetic and copies ran while one was open for 5% of the time, Pallas kernels for 34%

profile of v8, /device:TPU:57, one launch (start us, length us, event | category | flops | bytes accessed | tf_op | source)
XLA Modules:
  0.0 82.8 jit_solution(426871226685949165)
XLA Ops:
  0.0 0.0 copy-start
  0.0 0.0 copy-start.3
  0.0 2.0 %slice.36 = bf16[16,2,64,128]{3,2,1,0:T(8,128)(2,1)} slice(bf16[16,8,64,128]{3,2,1,0:T(8,128)(2,1)} %xp_ref.5), slice={[0:16], [6:8], [0:64], [0:128]} | slice | bytes 1048576 | tf_op jit(solution)/shard_map/slice | solution.py:339
  2.0 4.8 %collective-permute-start = (bf16[16,2,64,128]{3,2,1,0:T(8,128)(2,1)}, bf16[16,2,64,128]{3,2,1,0:T(8,128)(2,1)S(1)}, u32[]{:S(2)}, u32[]{:S(2)}) collective-permute-start(bf16[16,2,64,128]{3,2,1,0:T(8,128)(2,1)} %slice.36), channel_id=1, source_target_pairs={{0,1},{1,2},{2,3},{3,4},{4,5},{5,6},{6,7},{7,8},{8,9},{9,10},{10,1... | collective-permute-start | bytes 1572872 | tf_op jit(solution)/shard_map/ppermute | solution.py:27
  6.9 1.7 %slice.37 = bf16[16,1,64,128]{3,2,1,0:T(8,128)(2,1)} slice(bf16[16,8,64,128]{3,2,1,0:T(8,128)(2,1)} %xp_ref.5), slice={[0:16], [0:1], [0:64], [0:128]} | slice | bytes 524288 | tf_op jit(solution)/shard_map/slice | solution.py:340
  8.5 1.9 %collective-permute-start.1 = (bf16[16,1,64,128]{3,2,1,0:T(8,128)(2,1)}, bf16[16,1,64,128]{3,2,1,0:T(8,128)(2,1)S(1)}, u32[]{:S(2)}, u32[]{:S(2)}) collective-permute-start(bf16[16,1,64,128]{3,2,1,0:T(8,128)(2,1)} %slice.37), channel_id=1, source_target_pairs={{1,0},{2,1},{3,2},{4,3},{5,4},{6,5},{7,6},{8,7},{9,8},{10,9},{11,1... | collective-permute-start | bytes 786440 | tf_op jit(solution)/shard_map/ppermute | solution.py:27
  10.5 1.0 %copy.11 = bf16[64,3,144]{2,1,0:T(4,128)(2,1)S(1)} copy(bf16[64,3,144]{2,0,1:T(8,128)(2,1)} %bitcast.18) | data formatting | bytes 110592 | tf_op jit(solution)/shard_map/transpose | solution.py:160
  11.4 0.1 reshape.19.t3_ref
  11.6 1.1 %copy.12.w9_ref = bf16[144,576]{1,0:T(8,128)(2,1)S(1)} copy(bf16[144,576]{0,1:T(8,128)(2,1)} %bitcast.16) | data formatting | bytes 331776 | tf_op jit(solution)/shard_map/reshape | solution.py:159
  12.7 0.0 copy-done.3
  12.7 0.2 copy.15.wd_ref
  12.9 7.2 %collective-permute-done.1.below_ref = bf16[16,1,64,128]{3,2,1,0:T(8,128)(2,1)S(1)} collective-permute-done((bf16[16,1,64,128]{3,2,1,0:T(8,128)(2,1)}, bf16[16,1,64,128]{3,2,1,0:T(8,128)(2,1)S(1)}, u32[]{:S(2)}, u32[]{:S(2)}) %collective-permute-start.1) | collective-permute-done | bytes 262176 | tf_op jit(solution)/shard_map/ppermute | solution.py:27
  20.0 0.0 collective-permute-done.above_ref
  20.1 0.0 copy-done
  20.1 0.8 shard_map.64.edge_ref
  20.9 0.1 fusion.1
  20.9 3.1 %collective-permute-start.2 = (bf16[1,144,1152]{2,1,0:T(8,128)(2,1)S(1)}, bf16[1,144,1152]{2,1,0:T(8,128)(2,1)S(1)}, u32[]{:S(2)}, u32[]{:S(2)}) collective-permute-start(bf16[1,144,1152]{2,1,0:T(8,128)(2,1)S(1)} %get-tuple-element.16), channel_id=1, source_target_pairs={{0,16},{16,32},{32,48},{48,64},{64,80},{80,96},{96,112},{1,17},{17... | collective-permute-start | bytes 995336 | tf_op jit(solution)/shard_map/ppermute | solution.py:27
  24.1 4.3 %collective-permute-start.3 = (bf16[1,144,1152]{2,1,0:T(8,128)(2,1)S(1)}, bf16[1,144,1152]{2,1,0:T(8,128)(2,1)S(1)}, u32[]{:S(2)}, u32[]{:S(2)}) collective-permute-start(bf16[1,144,1152]{2,1,0:T(8,128)(2,1)S(1)} %get-tuple-element.15), channel_id=1, source_target_pairs={{16,0},{32,16},{48,32},{64,48},{80,64},{96,80},{112,96},{17,1},{33... | collective-permute-start | bytes 995336 | tf_op jit(solution)/shard_map/ppermute | solution.py:27
  28.4 18.9 %shard_map.65 = (bf16[14,4,64,128]{3,2,1,0:T(8,128)(2,1)S(1)}, bf16[2,144,1152]{2,1,0:T(8,128)(2,1)S(1)}) custom-call(s32[1]{0:T(128)} %bitcast.keep_ref, bf16[16,2,64,128]{3,2,1,0:T(8,128)(2,1)S(1)} %collective-permute-done.above_ref, bf16[16,8,64,128]{3,2,1,0:T(8,128)(2,1)S(1)} %copy-done, bf16[16,1,64,128]{3,2,1,0:T(8,128)(2,1)S(1)} %collective-permute-done.1.below_ref, ...), custom_call_target="tpu_custom_call" | custom-call | flops 5284823040 | bytes 4194304 | tf_op jit(solution)/shard_map/pallas_call | solution.py:182
  47.2 0.0 collective-permute-done.2.before_ref
  47.2 0.0 collective-permute-done.3.after_ref
  47.3 1.4 %shard_map.66 = bf16[2,4,64,128]{3,2,1,0:T(8,128)(2,1)S(1)} custom-call(s32[1]{0:T(128)} %bitcast.keep_ref, bf16[16,2,64,128]{3,2,1,0:T(8,128)(2,1)S(1)} %collective-permute-done.above_ref, bf16[16,8,64,128]{3,2,1,0:T(8,128)(2,1)S(1)} %copy-done, bf16[16,1,64,128]{3,2,1,0:T(8,128)(2,1)S(1)} %collective-permute-done.1.below_ref, ...), custom_call_target="tpu_custom_call" | custom-call | tf_op jit(solution)/shard_map/pallas_call | solution.py:196
  48.7 0.0 copy-start.2
  48.7 0.1 pad_maximum_fusion.xp_ref
  48.8 0.7 fusion
  49.6 2.4 %collective-permute-start.4 = (bf16[16,1,64,128]{3,2,1,0:T(8,128)(2,1)}, bf16[16,1,64,128]{3,2,1,0:T(8,128)(2,1)S(1)}, u32[]{:S(2)}, u32[]{:S(2)}) collective-permute-start(bf16[16,1,64,128]{3,2,1,0:T(8,128)(2,1)} %get-tuple-element.14), channel_id=1, source_target_pairs={{0,1},{1,2},{2,3},{3,4},{4,5},{5,6},{6,7},{7,8},{8,9},{9,10},{10,1... | collective-permute-start | bytes 786440 | tf_op jit(solution)/shard_map/ppermute | solution.py:27
  52.0 1.9 %collective-permute-start.5 = (bf16[16,1,64,128]{3,2,1,0:T(8,128)(2,1)S(1)}, bf16[16,1,64,128]{3,2,1,0:T(8,128)(2,1)S(1)}, u32[]{:S(2)}, u32[]{:S(2)}) collective-permute-start(bf16[16,1,64,128]{3,2,1,0:T(8,128)(2,1)S(1)} %get-tuple-element.13), channel_id=1, source_target_pairs={{1,0},{2,1},{3,2},{4,3},{5,4},{6,5},{7,6},{8,7},{9,8},{10,9},{11,1... | collective-permute-start | bytes 786440 | tf_op jit(solution)/shard_map/ppermute | solution.py:27
  53.9 0.0 copy-done.2
  53.9 0.4 copy.16
  54.3 0.0 copy-start.1
  54.3 1.3 %collective-permute-done.4.above_ref = bf16[16,1,64,128]{3,2,1,0:T(8,128)(2,1)S(1)} collective-permute-done((bf16[16,1,64,128]{3,2,1,0:T(8,128)(2,1)}, bf16[16,1,64,128]{3,2,1,0:T(8,128)(2,1)S(1)}, u32[]{:S(2)}, u32[]{:S(2)}) %collective-permute-start.4) | collective-permute-done | bytes 262176 | tf_op jit(solution)/shard_map/ppermute | solution.py:27
  55.6 7.7 %collective-permute-done.5.below_ref = bf16[16,1,64,128]{3,2,1,0:T(8,128)(2,1)S(1)} collective-permute-done((bf16[16,1,64,128]{3,2,1,0:T(8,128)(2,1)S(1)}, bf16[16,1,64,128]{3,2,1,0:T(8,128)(2,1)S(1)}, u32[]{:S(2)}, u32[]{:S(2)}) %collective-permute-start.5) | collective-permute-done | bytes 262176 | tf_op jit(solution)/shard_map/ppermute | solution.py:27
  63.3 0.8 shard_map.67.edge_ref
  64.1 1.9 %collective-permute-start.6 = (bf16[1,256,288]{2,1,0:T(8,128)(2,1)S(1)}, bf16[1,256,288]{2,1,0:T(8,128)(2,1)S(1)}, u32[]{:S(2)}, u32[]{:S(2)}) collective-permute-start(bf16[1,256,288]{2,1,0:T(8,128)(2,1)S(1)} %get-tuple-element.18), channel_id=1, source_target_pairs={{0,16},{16,32},{32,48},{48,64},{64,80},{80,96},{96,112},{1,17},{17... | collective-permute-start | bytes 442376 | tf_op jit(solution)/shard_map/ppermute | solution.py:27
  66.1 5.5 %collective-permute-start.7 = (bf16[1,256,288]{2,1,0:T(8,128)(2,1)S(1)}, bf16[1,256,288]{2,1,0:T(8,128)(2,1)S(1)}, u32[]{:S(2)}, u32[]{:S(2)}) collective-permute-start(bf16[1,256,288]{2,1,0:T(8,128)(2,1)S(1)} %get-tuple-element.17), channel_id=1, source_target_pairs={{16,0},{32,16},{48,32},{64,48},{80,64},{96,80},{112,96},{17,1},{33... | collective-permute-start | bytes 442376 | tf_op jit(solution)/shard_map/ppermute | solution.py:27
  71.5 0.0 copy-done.1
  71.6 9.6 %shard_map.68 = (bf16[14,4,64,128]{3,2,1,0:T(8,128)(2,1)S(1)}, bf16[2,256,288]{2,1,0:T(8,128)(2,1)S(1)}) custom-call(bf16[16,1,64,128]{3,2,1,0:T(8,128)(2,1)S(1)} %collective-permute-done.4.above_ref, bf16[16,4,64,128]{3,2,1,0:T(8,128)(2,1)S(1)} %pad_maximum_fusion.xp_ref, bf16[16,1,64,128]{3,2,1,0:T(8,128)(2,1)S(1)} %collective-permute-done.5.below_ref, ...), custom_call_target="tpu_custom_call" | custom-call | flops 3623878656 | bytes 2097152 | tf_op jit(solution)/shard_map/pallas_call | solution.py:311
  81.2 0.0 collective-permute-done.6.before_ref
  81.2 0.0 collective-permute-done.7.after_ref
  81.2 0.5 shard_map.69
  81.7 1.1 %pad_maximum_fusion.1 = bf16[16,4,64,128]{3,2,1,0:T(8,128)(2,1)} fusion(bf16[1,4,64,128]{3,2,1,0:T(8,128)(2,1)S(1)} %get-tuple-element.20, bf16[14,4,64,128]{3,2,1,0:T(8,128)(2,1)S(1)} %get-tuple-element.12, bf16[1,4,64,128]{3,2,1,0:T(8,128)(2,1)S(1)} %get-tuple-element.19), kind=kLoop, calls=%fused_computation.1 | loop fusion | flops 1048576 | bytes 2097152 | tf_op jit(solution)/shard_map/concatenate | solution.py:334
  (3 shorter events, 0.1 us)
Async XLA Ops:
  0.0 20.1 %copy-start = (bf16[16,8,64,128]{3,2,1,0:T(8,128)(2,1)S(1)}, bf16[16,8,64,128]{3,2,1,0:T(8,128)(2,1)}, u32[]{:S(2)}) copy-start(bf16[16,8,64,128]{3,2,1,0:T(8,128)(2,1)} %xp_ref.5) | copy-start | bytes 6291460
  0.0 12.7 %copy-start.3 = (bf16[3,3,128,64]{2,3,1,0:T(8,128)(2,1)S(1)}, bf16[3,3,128,64]{2,3,1,0:T(8,128)(2,1)}, u32[]{:S(2)}) copy-start(bf16[3,3,128,64]{2,3,1,0:T(8,128)(2,1)} %param.9) | copy-start | bytes 442372
  2.0 18.0 %collective-permute-start = (bf16[16,2,64,128]{3,2,1,0:T(8,128)(2,1)}, bf16[16,2,64,128]{3,2,1,0:T(8,128)(2,1)S(1)}, u32[]{:S(2)}, u32[]{:S(2)}) collective-permute-start(bf16[16,2,64,128]{3,2,1,0:T(8,128)(2,1)} %slice.36), channel_id=1, source_target_pairs={{0,1},{1,2},{2,3},{3,4},{4,5},{5,6},{6,7},{7,8},{8,9},{9,10},{10,1... | collective-permute-start | bytes 1572872 | tf_op jit(solution)/shard_map/ppermute | solution.py:27
  8.5 11.5 %collective-permute-start.1 = (bf16[16,1,64,128]{3,2,1,0:T(8,128)(2,1)}, bf16[16,1,64,128]{3,2,1,0:T(8,128)(2,1)S(1)}, u32[]{:S(2)}, u32[]{:S(2)}) collective-permute-start(bf16[16,1,64,128]{3,2,1,0:T(8,128)(2,1)} %slice.37), channel_id=1, source_target_pairs={{1,0},{2,1},{3,2},{4,3},{5,4},{6,5},{7,6},{8,7},{9,8},{10,9},{11,1... | collective-permute-start | bytes 786440 | tf_op jit(solution)/shard_map/ppermute | solution.py:27
  20.9 26.3 %collective-permute-start.2 = (bf16[1,144,1152]{2,1,0:T(8,128)(2,1)S(1)}, bf16[1,144,1152]{2,1,0:T(8,128)(2,1)S(1)}, u32[]{:S(2)}, u32[]{:S(2)}) collective-permute-start(bf16[1,144,1152]{2,1,0:T(8,128)(2,1)S(1)} %get-tuple-element.16), channel_id=1, source_target_pairs={{0,16},{16,32},{32,48},{48,64},{64,80},{80,96},{96,112},{1,17},{17... | collective-permute-start | bytes 995336 | tf_op jit(solution)/shard_map/ppermute | solution.py:27
  24.1 23.2 %collective-permute-start.3 = (bf16[1,144,1152]{2,1,0:T(8,128)(2,1)S(1)}, bf16[1,144,1152]{2,1,0:T(8,128)(2,1)S(1)}, u32[]{:S(2)}, u32[]{:S(2)}) collective-permute-start(bf16[1,144,1152]{2,1,0:T(8,128)(2,1)S(1)} %get-tuple-element.15), channel_id=1, source_target_pairs={{16,0},{32,16},{48,32},{64,48},{80,64},{96,80},{112,96},{17,1},{33... | collective-permute-start | bytes 995336 | tf_op jit(solution)/shard_map/ppermute | solution.py:27
  48.7 5.3 %copy-start.2 = (bf16[3,3,288,128]{3,2,1,0:T(8,128)(2,1)S(1)}, bf16[3,3,288,128]{3,2,1,0:T(8,128)(2,1)}, u32[]{:S(2)}) copy-start(bf16[3,3,288,128]{3,2,1,0:T(8,128)(2,1)} %param.10) | copy-start | bytes 1990660
  49.6 6.0 %collective-permute-start.4 = (bf16[16,1,64,128]{3,2,1,0:T(8,128)(2,1)}, bf16[16,1,64,128]{3,2,1,0:T(8,128)(2,1)S(1)}, u32[]{:S(2)}, u32[]{:S(2)}) collective-permute-start(bf16[16,1,64,128]{3,2,1,0:T(8,128)(2,1)} %get-tuple-element.14), channel_id=1, source_target_pairs={{0,1},{1,2},{2,3},{3,4},{4,5},{5,6},{6,7},{7,8},{8,9},{9,10},{10,1... | collective-permute-start | bytes 786440 | tf_op jit(solution)/shard_map/ppermute | solution.py:27
  52.0 11.3 %collective-permute-start.5 = (bf16[16,1,64,128]{3,2,1,0:T(8,128)(2,1)S(1)}, bf16[16,1,64,128]{3,2,1,0:T(8,128)(2,1)S(1)}, u32[]{:S(2)}, u32[]{:S(2)}) collective-permute-start(bf16[16,1,64,128]{3,2,1,0:T(8,128)(2,1)S(1)} %get-tuple-element.13), channel_id=1, source_target_pairs={{1,0},{2,1},{3,2},{4,3},{5,4},{6,5},{7,6},{8,7},{9,8},{10,9},{11,1... | collective-permute-start | bytes 786440 | tf_op jit(solution)/shard_map/ppermute | solution.py:27
  54.3 17.2 %copy-start.1 = (bf16[3,128,288]{1,2,0:T(8,128)(2,1)S(1)}, bf16[3,128,288]{1,2,0:T(8,128)(2,1)}, u32[]{:S(2)}) copy-start(bf16[3,128,288]{1,2,0:T(8,128)(2,1)} %param.11) | copy-start | bytes 663556
  64.1 17.1 %collective-permute-start.6 = (bf16[1,256,288]{2,1,0:T(8,128)(2,1)S(1)}, bf16[1,256,288]{2,1,0:T(8,128)(2,1)S(1)}, u32[]{:S(2)}, u32[]{:S(2)}) collective-permute-start(bf16[1,256,288]{2,1,0:T(8,128)(2,1)S(1)} %get-tuple-element.18), channel_id=1, source_target_pairs={{0,16},{16,32},{32,48},{48,64},{64,80},{80,96},{96,112},{1,17},{17... | collective-permute-start | bytes 442376 | tf_op jit(solution)/shard_map/ppermute | solution.py:27
  66.1 15.1 %collective-permute-start.7 = (bf16[1,256,288]{2,1,0:T(8,128)(2,1)S(1)}, bf16[1,256,288]{2,1,0:T(8,128)(2,1)S(1)}, u32[]{:S(2)}, u32[]{:S(2)}) collective-permute-start(bf16[1,256,288]{2,1,0:T(8,128)(2,1)S(1)} %get-tuple-element.17), channel_id=1, source_target_pairs={{16,0},{32,16},{48,32},{64,48},{80,64},{96,80},{112,96},{17,1},{33... | collective-permute-start | bytes 442376 | tf_op jit(solution)/shard_map/ppermute | solution.py:27

commit v9 on v8

--- a/solution.py
+++ b/solution.py
@@ -54,6 +54,9 @@
     framed = jax.nn.relu(spatial(padded, spatial_kernel, space_layout)).astype(jnp.bfloat16)
     summed = source.astype(jnp.float32) + temporal(framed, temporal_kernel, time_layout)
     return jax.nn.relu(summed).astype(jnp.bfloat16)
+
+
+_ANY = pl.ANY
 
 
 def _lane_shift(x, by):
@@ -134,21 +137,23 @@
 
     def section(t, carry):
         stacked = jnp.concatenate([mid_ref[t - 1], mid_ref[t], mid_ref[t + 1]], axis=0)
-        _section_down(stacked, refs, t, t3_ref, wd_ref, keep_ref, out_ref, t - 1)
+        _section_down(stacked, refs, t, t3_ref, wd_ref, keep_ref, out_ref, t)
         return carry
 
     lax.fori_loop(1, frames - 1, section, 0)
 
 
 def _outer_one_kernel(
-    keep_ref, above_ref, xp_ref, below_ref, t3_ref, wd_ref, before_ref, after_ref, edge_ref, side_ref, out_ref
+    keep_ref, above_ref, xp_ref, below_ref, t3_ref, wd_ref, before_ref, after_ref, edge_ref, side_ref, full_ref,
+    out_ref, buf, sem
 ):
     refs = (above_ref, xp_ref, below_ref)
     frames = xp_ref.shape[0]
     stacked = jnp.concatenate([before_ref[0], edge_ref[0], side_ref[0]], axis=0)
-    _section_down(stacked, refs, 0, t3_ref, wd_ref, keep_ref, out_ref, 0)
+    _section_down(stacked, refs, 0, t3_ref, wd_ref, keep_ref, buf, 0)
     stacked = jnp.concatenate([side_ref[1], edge_ref[1], after_ref[0]], axis=0)
-    _section_down(stacked, refs, frames - 1, t3_ref, wd_ref, keep_ref, out_ref, 1)
+    _section_down(stacked, refs, frames - 1, t3_ref, wd_ref, keep_ref, buf, 1)
+    _put_ends(buf, out_ref, sem)
 
 
 def block_one(above, rowed, below, keep_first, spatial_kernel, temporal_kernel, down_kernel):
@@ -182,7 +187,7 @@
     inner, side = pl.pallas_call(
         _inner_one_kernel,
         out_shape=(
-            jax.ShapeDtypeStruct((frames - 2,) + out_plane, rowed.dtype),
+            jax.ShapeDtypeStruct((frames,) + out_plane, rowed.dtype),
             jax.ShapeDtypeStruct((2,) + plane, rowed.dtype),
         ),
         in_specs=[sspec] + [spec] * 6,
@@ -193,14 +198,16 @@
             flops=frames * (spatial_flops + section_flops), bytes_accessed=4 * rowed.size, transcendentals=0
         ),
     )(keep_first, above, rowed, below, w9, t3, wd)
-    outer = pl.pallas_call(
+    anywhere = pl.BlockSpec(memory_space=_ANY)
+    return pl.pallas_call(
         _outer_one_kernel,
-        out_shape=jax.ShapeDtypeStruct((2,) + out_plane, rowed.dtype),
-        in_specs=[sspec] + [spec] * 9,
-        out_specs=spec,
-        compiler_params=params,
-    )(keep_first, above, rowed, below, t3, wd, before, after, edges, side)
-    return jnp.concatenate([outer[:1], inner, outer[1:]], axis=0)
+        out_shape=jax.ShapeDtypeStruct(inner.shape, rowed.dtype),
+        in_specs=[sspec] + [spec] * 9 + [anywhere],
+        out_specs=anywhere,
+        scratch_shapes=[pltpu.VMEM((2,) + out_plane, rowed.dtype), pltpu.SemaphoreType.DMA((2,))],
+        input_output_aliases={10: 0},
+        compiler_params=params,
+    )(keep_first, above, rowed, below, t3, wd, before, after, edges, side, inner)
 
 
 def _sublane_shift(x, by, axis):
@@ -268,23 +275,34 @@
             pair = jnp.concatenate([mid_ref[t - 1 + k], mid_ref[t + k]], axis=0)
             d = jnp.dot(pair, t3_ref[k], preferred_element_type=jnp.float32)
             s = d if s is None else s + d
-        _finish(s[:plane], xp_ref, t, out_ref, t - 1)
-        _finish(s[plane:], xp_ref, t + 1, out_ref, t)
+        _finish(s[:plane], xp_ref, t, out_ref, t)
+        _finish(s[plane:], xp_ref, t + 1, out_ref, t + 1)
         return carry
 
     lax.fori_loop(0, (frames - 2) // 2, section, 0)
 
 
-def _outer_two_kernel(xp_ref, t3_ref, before_ref, after_ref, edge_ref, side_ref, out_ref):
+def _outer_two_kernel(xp_ref, t3_ref, before_ref, after_ref, edge_ref, side_ref, full_ref, out_ref, buf, sem):
     frames = xp_ref.shape[0]
     s = jnp.dot(before_ref[0], t3_ref[0], preferred_element_type=jnp.float32)
     s = s + jnp.dot(edge_ref[0], t3_ref[1], preferred_element_type=jnp.float32)
     s = s + jnp.dot(side_ref[0], t3_ref[2], preferred_element_type=jnp.float32)
-    _finish(s, xp_ref, 0, out_ref, 0)
+    _finish(s, xp_ref, 0, buf, 0)
     s = jnp.dot(side_ref[1], t3_ref[0], preferred_element_type=jnp.float32)
     s = s + jnp.dot(edge_ref[1], t3_ref[1], preferred_element_type=jnp.float32)
     s = s + jnp.dot(after_ref[0], t3_ref[2], preferred_element_type=jnp.float32)
-    _finish(s, xp_ref, frames - 1, out_ref, 1)
+    _finish(s, xp_ref, frames - 1, buf, 1)
+    _put_ends(buf, out_ref, sem)
+
+
+def _put_ends(buf, out_ref, sem):
+    frames = out_ref.shape[0]
+    first = pltpu.make_async_copy(buf.at[0], out_ref.at[0], sem.at[0])
+    last = pltpu.make_async_copy(buf.at[1], out_ref.at[frames - 1], sem.at[1])
+    first.start()
+    last.start()
+    first.wait()
+    last.wait()
 
 
 def block_two(above, rowed, below, spatial_kernel, temporal_kernel):
@@ -311,7 +329,7 @@
     inner, side = pl.pallas_call(
         _inner_two_kernel,
         out_shape=(
-            jax.ShapeDtypeStruct((frames - 2, rows, width, channels), rowed.dtype),
+            jax.ShapeDtypeStruct((frames, rows, width, channels), rowed.dtype),
             jax.ShapeDtypeStruct((2,) + plane, rowed.dtype),
         ),
         in_specs=[spec] * 5,
@@ -324,14 +342,16 @@
             transcendentals=0,
         ),
     )(above, rowed, below, w9, t3)
-    outer = pl.pallas_call(
+    anywhere = pl.BlockSpec(memory_space=_ANY)
+    return pl.pallas_call(
         _outer_two_kernel,
-        out_shape=jax.ShapeDtypeStruct((2, rows, width, channels), rowed.dtype),
-        in_specs=[spec] * 6,
-        out_specs=spec,
-        compiler_params=params,
-    )(rowed, t3, before, after, edges, side)
-    return jnp.concatenate([outer[:1], inner, outer[1:]], axis=0)
+        out_shape=jax.ShapeDtypeStruct(inner.shape, rowed.dtype),
+        in_specs=[spec] * 6 + [anywhere],
+        out_specs=anywhere,
+        scratch_shapes=[pltpu.VMEM((2, rows, width, channels), rowed.dtype), pltpu.SemaphoreType.DMA((2,))],
+        input_output_aliases={6: 0},
+        compiler_params=params,
+    )(rowed, t3, before, after, edges, side, inner)
 
 
 def on_device(video_clip, spatial_one, temporal_one, down_weight, spatial_two, temporal_two):

time: 83.2 us -> 84.4 us (1.014)
  local copies, waits for them, and re-layouts: 7.4 us -> 10.6 us
  waiting for transfers between devices: 16.1 us -> 13.2 us
  Pallas kernels: 32 us -> 33.8 us
  other arithmetic: 1.24 us -> 0 us
    ppermute x8, waiting for transfers between devices: 16.1 us -> 13.2 us  [from_behind(): return lax.ppermute(array, axis, pairs)]
    unnamed x8 -> x14, local copies, waits for them, and re-layouts: 0.03 us -> 1.98 us
    reshape x1, local copies, waits for them, and re-layouts: 0.16 us -> 1.78 us  [block_one(): wd = jnp.transpose(down_kernel, (2, 0, 1, 3)).reshape(outs, 9 * channels)]
    concatenate x2 -> x0, other arithmetic: 1.24 us -> none  [the longest x1 1.1 us: block_two(): return jnp.concatenate([outer[:1], inner, outer[1:]], axis=0)]
    transpose x1, local copies, waits for them, and re-layouts: 0.41 us -> 1.49 us  [block_two(): w9 = jnp.transpose(spatial_kernel, (0, 1, 3, 2)).reshape(9 * channels, mids)]
    pallas_call x1, Pallas kernels: 9.62 us -> 10.6 us  [block_two(): pl.pallas_call(_inner_two_kernel, out_shape=(jax.ShapeDtypeStruct((frames...]
    pallas_call x2, Pallas kernels: 1.85 us -> 2.7 us  [the longest x1 1.59 us: block_one(): pl.pallas_call(_outer_one_kernel, out_shape=jax.ShapeDtypeStruct(inner.sh...]
  transfers between devices with their start and end apart: 8 -> 8, of which waited for: 3 -> 2; matrix products, arithmetic and copies ran while one was open for 5% -> 8% of each run, Pallas kernels for 34% -> 35%
where the time goes in v9:
time: 84.4 us; the launch traced here: 83.9 us
  Pallas kernels  33.8 us (40%)
  starting transfers between devices  26 us (31%)
  waiting for transfers between devices  13.2 us (16%)
  local copies, waits for them, and re-layouts  10.6 us (13%)
    ppermute x8, starting transfers between devices, from_behind(): return lax.ppermute(array, axis, pairs)  26 us
    pallas_call x1, Pallas kernels, block_one(): pl.pallas_call(_inner_one_kernel, out_shape=(jax.ShapeDtypeStruct((frames...  18.9 us
    ppermute x8, waiting for transfers between devices, from_behind(): return lax.ppermute(array, axis, pairs)  13.2 us
    pallas_call x1, Pallas kernels, block_two(): pl.pallas_call(_inner_two_kernel, out_shape=(jax.ShapeDtypeStruct((frames...  10.6 us
    slice x1, local copies, waits for them, and re-layouts, on_device(): above = from_behind(video_clip[:, rows - 2:], 'row', 1)  2.03 us
    unnamed x14, local copies, waits for them, and re-layouts  1.98 us
    reshape x1, local copies, waits for them, and re-layouts, block_one(): wd = jnp.transpose(down_kernel, (2, 0, 1, 3)).reshape(outs, 9 * channels)  1.78 us
  transfers between devices with their start and end apart: 8, of which 2 were waited for; matrix products, arithmetic and copies ran while one was open for 8% of the time, Pallas kernels for 35%

profile of v9, /device:TPU:57, one launch (start us, length us, event | category | flops | bytes accessed | tf_op | source)
XLA Modules:
  0.0 83.9 jit_solution(5548430279795693713)
XLA Ops:
  0.0 0.0 copy-start
  0.0 2.0 %slice.24 = bf16[16,2,64,128]{3,2,1,0:T(8,128)(2,1)} slice(bf16[16,8,64,128]{3,2,1,0:T(8,128)(2,1)} %xp_ref.5), slice={[0:16], [6:8], [0:64], [0:128]} | slice | bytes 1048576 | tf_op jit(solution)/shard_map/slice | solution.py:359
  2.0 4.8 %collective-permute-start = (bf16[16,2,64,128]{3,2,1,0:T(8,128)(2,1)}, bf16[16,2,64,128]{3,2,1,0:T(8,128)(2,1)S(1)}, u32[]{:S(2)}, u32[]{:S(2)}) collective-permute-start(bf16[16,2,64,128]{3,2,1,0:T(8,128)(2,1)} %slice.24), channel_id=1, source_target_pairs={{0,1},{1,2},{2,3},{3,4},{4,5},{5,6},{6,7},{7,8},{8,9},{9,10},{10,1... | collective-permute-start | bytes 1572872 | tf_op jit(solution)/shard_map/ppermute | solution.py:27
  6.9 1.0 %slice.25 = bf16[16,1,64,128]{3,2,1,0:T(8,128)(2,1)S(1)} slice(bf16[16,8,64,128]{3,2,1,0:T(8,128)(2,1)} %xp_ref.5), slice={[0:16], [0:1], [0:64], [0:128]} | slice | bytes 524288 | tf_op jit(solution)/shard_map/slice | solution.py:360
  7.8 1.9 %collective-permute-start.1 = (bf16[16,1,64,128]{3,2,1,0:T(8,128)(2,1)S(1)}, bf16[16,1,64,128]{3,2,1,0:T(8,128)(2,1)S(1)}, u32[]{:S(2)}, u32[]{:S(2)}) collective-permute-start(bf16[16,1,64,128]{3,2,1,0:T(8,128)(2,1)S(1)} %slice.25), channel_id=1, source_target_pairs={{1,0},{2,1},{3,2},{4,3},{5,4},{6,5},{7,6},{8,7},{9,8},{10,9},{11,1... | collective-permute-start | bytes 786440 | tf_op jit(solution)/shard_map/ppermute | solution.py:27
  9.8 1.0 %copy.13 = bf16[64,3,144]{2,1,0:T(4,128)(2,1)S(1)} copy(bf16[64,3,144]{2,0,1:T(8,128)(2,1)} %bitcast.18) | data formatting | bytes 110592 | tf_op jit(solution)/shard_map/transpose | solution.py:165
  10.7 0.1 reshape.19.t3_ref
  10.9 1.1 %copy.14.w9_ref = bf16[144,576]{1,0:T(8,128)(2,1)S(1)} copy(bf16[144,576]{0,1:T(8,128)(2,1)} %bitcast.16) | data formatting | bytes 331776 | tf_op jit(solution)/shard_map/reshape | solution.py:164
  12.0 0.0 copy-start.3
  12.0 1.8 %copy.17.wd_ref = bf16[128,576]{1,0:T(8,128)(2,1)} copy(bf16[128,576]{0,1:T(8,128)(2,1)} %bitcast.17) | data formatting | bytes 294912 | tf_op jit(solution)/shard_map/reshape | solution.py:166
  13.8 0.0 copy-start.5
  13.8 5.3 %collective-permute-done.1.below_ref = bf16[16,1,64,128]{3,2,1,0:T(8,128)(2,1)S(1)} collective-permute-done((bf16[16,1,64,128]{3,2,1,0:T(8,128)(2,1)S(1)}, bf16[16,1,64,128]{3,2,1,0:T(8,128)(2,1)S(1)}, u32[]{:S(2)}, u32[]{:S(2)}) %collective-permute-start.1) | collective-permute-done | bytes 262176 | tf_op jit(solution)/shard_map/ppermute | solution.py:27
  19.1 0.0 collective-permute-done.above_ref
  19.1 0.0 copy-done
  19.1 0.0 copy-start.1
  19.1 0.8 shard_map.64.edge_ref
  20.0 0.1 fusion.1
  20.0 0.0 copy-done.3
  20.1 0.0 copy-done.1
  20.1 3.1 %collective-permute-start.2 = (bf16[1,144,1152]{2,1,0:T(8,128)(2,1)S(1)}, bf16[1,144,1152]{2,1,0:T(8,128)(2,1)S(1)}, u32[]{:S(2)}, u32[]{:S(2)}) collective-permute-start(bf16[1,144,1152]{2,1,0:T(8,128)(2,1)S(1)} %get-tuple-element.16), channel_id=1, source_target_pairs={{0,16},{16,32},{32,48},{48,64},{64,80},{80,96},{96,112},{1,17},{17... | collective-permute-start | bytes 995336 | tf_op jit(solution)/shard_map/ppermute | solution.py:27
  23.2 4.3 %collective-permute-start.3 = (bf16[1,144,1152]{2,1,0:T(8,128)(2,1)S(1)}, bf16[1,144,1152]{2,1,0:T(8,128)(2,1)S(1)}, u32[]{:S(2)}, u32[]{:S(2)}) collective-permute-start(bf16[1,144,1152]{2,1,0:T(8,128)(2,1)S(1)} %get-tuple-element.15), channel_id=1, source_target_pairs={{16,0},{32,16},{48,32},{64,48},{80,64},{96,80},{112,96},{17,1},{33... | collective-permute-start | bytes 995336 | tf_op jit(solution)/shard_map/ppermute | solution.py:27
  27.5 0.0 copy-done.5
  27.5 0.0 copy-start.2
  27.5 1.0 %copy-done.2 = bf16[16,2,64,128]{3,2,1,0:T(8,128)(2,1)S(1)} copy-done((bf16[16,2,64,128]{3,2,1,0:T(8,128)(2,1)S(1)}, bf16[16,2,64,128]{3,2,1,0:T(8,128)(2,1)}, u32[]{:S(2)}) %copy-start.2) | copy-done | bytes 524312
  28.5 0.0 copy-start.4
  28.5 0.9 %copy-done.4 = bf16[144,576]{1,0:T(8,128)(2,1)S(1)} copy-done((bf16[144,576]{1,0:T(8,128)(2,1)S(1)}, bf16[144,576]{1,0:T(8,128)(2,1)}, u32[]{:S(2)}) %copy-start.4) | copy-done | bytes 165912
  29.4 18.9 %shard_map.65 = (bf16[16,4,64,128]{3,2,1,0:T(8,128)(2,1)S(1)}, bf16[2,144,1152]{2,1,0:T(8,128)(2,1)S(1)}) custom-call(s32[1]{0:T(128)} %bitcast.keep_ref, bf16[16,2,64,128]{3,2,1,0:T(8,128)(2,1)S(1)} %copy-done.2, bf16[16,8,64,128]{3,2,1,0:T(8,128)(2,1)S(1)} %copy-done, bf16[16,1,64,128]{3,2,1,0:T(8,128)(2,1)S(1)} %collective-permute-done.1.below_ref, ...), custom_call_target="tpu_custom_call" | custom-call | flops 5284823040 | bytes 4194304 | tf_op jit(solution)/shard_map/pallas_call | solution.py:187
  48.3 0.0 collective-permute-done.2.before_ref
  48.3 0.0 collective-permute-done.3.after_ref
  48.3 1.6 %shard_map.66.xp_ref = bf16[16,4,64,128]{3,2,1,0:T(8,128)(2,1)S(1)} custom-call(s32[1]{0:T(128)} %bitcast.keep_ref, bf16[16,2,64,128]{3,2,1,0:T(8,128)(2,1)S(1)} %copy-done.2, bf16[16,8,64,128]{3,2,1,0:T(8,128)(2,1)S(1)} %copy-done, bf16[16,1,64,128]{3,2,1,0:T(8,128)(2,1)S(1)} %collective-permute-done.1.below_ref, ...), custom_call_target="tpu_custom_call", output_to_operand_aliasing={{}: (10, {})} | custom-call | tf_op jit(solution)/shard_map/pallas_call | solution.py:202
  50.0 2.6 %collective-permute-start.4 = (bf16[16,1,64,128]{3,2,1,0:T(8,128)(2,1)S(1)}, bf16[16,1,64,128]{3,2,1,0:T(8,128)(2,1)S(1)}, u32[]{:S(2)}, u32[]{:S(2)}) collective-permute-start(bf16[16,1,64,128]{3,2,1,0:T(8,128)(2,1)S(1)} %get-tuple-element.14), channel_id=1, source_target_pairs={{0,1},{1,2},{2,3},{3,4},{4,5},{5,6},{6,7},{7,8},{8,9},{9,10},{10,1... | collective-permute-start | bytes 786440 | tf_op jit(solution)/shard_map/ppermute | solution.py:27
  52.6 1.9 %collective-permute-start.5 = (bf16[16,1,64,128]{3,2,1,0:T(8,128)(2,1)S(1)}, bf16[16,1,64,128]{3,2,1,0:T(8,128)(2,1)S(1)}, u32[]{:S(2)}, u32[]{:S(2)}) collective-permute-start(bf16[16,1,64,128]{3,2,1,0:T(8,128)(2,1)S(1)} %get-tuple-element.13), channel_id=1, source_target_pairs={{1,0},{2,1},{3,2},{4,3},{5,4},{6,5},{7,6},{8,7},{9,8},{10,9},{11,1... | collective-permute-start | bytes 786440 | tf_op jit(solution)/shard_map/ppermute | solution.py:27
  54.5 1.5 %copy.18 = bf16[3,3,128,288]{3,2,1,0:T(8,128)(2,1)S(1)} copy(bf16[3,3,128,288]{2,3,1,0:T(8,128)(2,1)} %bitcast.15) | data formatting | bytes 1327104 | tf_op jit(solution)/shard_map/transpose | solution.py:311
  56.0 0.0 copy-start.6
  56.0 0.0 collective-permute-done.4.above_ref
  56.0 7.9 %collective-permute-done.5.below_ref = bf16[16,1,64,128]{3,2,1,0:T(8,128)(2,1)S(1)} collective-permute-done((bf16[16,1,64,128]{3,2,1,0:T(8,128)(2,1)S(1)}, bf16[16,1,64,128]{3,2,1,0:T(8,128)(2,1)S(1)}, u32[]{:S(2)}, u32[]{:S(2)}) %collective-permute-start.5) | collective-permute-done | bytes 262176 | tf_op jit(solution)/shard_map/ppermute | solution.py:27
  63.9 0.8 shard_map.67.edge_ref
  64.7 1.9 %collective-permute-start.6 = (bf16[1,256,288]{2,1,0:T(8,128)(2,1)S(1)}, bf16[1,256,288]{2,1,0:T(8,128)(2,1)S(1)}, u32[]{:S(2)}, u32[]{:S(2)}) collective-permute-start(bf16[1,256,288]{2,1,0:T(8,128)(2,1)S(1)} %get-tuple-element.18), channel_id=1, source_target_pairs={{0,16},{16,32},{32,48},{48,64},{64,80},{80,96},{96,112},{1,17},{17... | collective-permute-start | bytes 442376 | tf_op jit(solution)/shard_map/ppermute | solution.py:27
  66.7 5.5 %collective-permute-start.7 = (bf16[1,256,288]{2,1,0:T(8,128)(2,1)S(1)}, bf16[1,256,288]{2,1,0:T(8,128)(2,1)S(1)}, u32[]{:S(2)}, u32[]{:S(2)}) collective-permute-start(bf16[1,256,288]{2,1,0:T(8,128)(2,1)S(1)} %get-tuple-element.17), channel_id=1, source_target_pairs={{16,0},{32,16},{48,32},{64,48},{80,64},{96,80},{112,96},{17,1},{33... | collective-permute-start | bytes 442376 | tf_op jit(solution)/shard_map/ppermute | solution.py:27
  72.1 0.0 copy-done.6
  72.2 10.6 %shard_map.68 = (bf16[16,4,64,128]{3,2,1,0:T(8,128)(2,1)}, bf16[2,256,288]{2,1,0:T(8,128)(2,1)S(1)}) custom-call(bf16[16,1,64,128]{3,2,1,0:T(8,128)(2,1)S(1)} %collective-permute-done.4.above_ref, bf16[16,4,64,128]{3,2,1,0:T(8,128)(2,1)S(1)} %shard_map.66.xp_ref, bf16[16,1,64,128]{3,2,1,0:T(8,128)(2,1)S(1)} %collective-permute-done.5.below_ref, ...), custom_call_target="tpu_custom_call" | custom-call | flops 3623878656 | bytes 2097152 | tf_op jit(solution)/shard_map/pallas_call | solution.py:329
  82.8 0.0 collective-permute-done.6.before_ref
  82.8 0.0 collective-permute-done.7.after_ref
  82.8 1.1 %shard_map.69 = bf16[16,4,64,128]{3,2,1,0:T(8,128)(2,1)} custom-call(bf16[16,4,64,128]{3,2,1,0:T(8,128)(2,1)S(1)} %shard_map.66.xp_ref, bf16[3,288,128]{2,1,0:T(8,128)(2,1)S(1)} %bitcast.14, bf16[1,256,288]{2,1,0:T(8,128)(2,1)S(1)} %collective-permute-done.6.before_ref, ...), custom_call_target="tpu_custom_call", output_to_operand_aliasing={{}: (6, {})} | custom-call | tf_op jit(solution)/shard_map/pallas_call | solution.py:346
  (2 shorter events, 0.1 us)
Async XLA Ops:
  0.0 19.1 %copy-start = (bf16[16,8,64,128]{3,2,1,0:T(8,128)(2,1)S(1)}, bf16[16,8,64,128]{3,2,1,0:T(8,128)(2,1)}, u32[]{:S(2)}) copy-start(bf16[16,8,64,128]{3,2,1,0:T(8,128)(2,1)} %xp_ref.5) | copy-start | bytes 6291460
  2.0 17.1 %collective-permute-start = (bf16[16,2,64,128]{3,2,1,0:T(8,128)(2,1)}, bf16[16,2,64,128]{3,2,1,0:T(8,128)(2,1)S(1)}, u32[]{:S(2)}, u32[]{:S(2)}) collective-permute-start(bf16[16,2,64,128]{3,2,1,0:T(8,128)(2,1)} %slice.24), channel_id=1, source_target_pairs={{0,1},{1,2},{2,3},{3,4},{4,5},{5,6},{6,7},{7,8},{8,9},{9,10},{10,1... | collective-permute-start | bytes 1572872 | tf_op jit(solution)/shard_map/ppermute | solution.py:27
  7.8 11.3 %collective-permute-start.1 = (bf16[16,1,64,128]{3,2,1,0:T(8,128)(2,1)S(1)}, bf16[16,1,64,128]{3,2,1,0:T(8,128)(2,1)S(1)}, u32[]{:S(2)}, u32[]{:S(2)}) collective-permute-start(bf16[16,1,64,128]{3,2,1,0:T(8,128)(2,1)S(1)} %slice.25), channel_id=1, source_target_pairs={{1,0},{2,1},{3,2},{4,3},{5,4},{6,5},{7,6},{8,7},{9,8},{10,9},{11,1... | collective-permute-start | bytes 786440 | tf_op jit(solution)/shard_map/ppermute | solution.py:27
  12.0 8.0 %copy-start.3 = (bf16[144,576]{1,0:T(8,128)(2,1)}, bf16[144,576]{1,0:T(8,128)(2,1)S(1)}, u32[]{:S(2)}) copy-start(bf16[144,576]{1,0:T(8,128)(2,1)S(1)} %copy.14.w9_ref) | copy-start | bytes 497668
  13.8 13.7 %copy-start.5 = (bf16[128,576]{1,0:T(8,128)(2,1)S(1)}, bf16[128,576]{1,0:T(8,128)(2,1)}, u32[]{:S(2)}) copy-start(bf16[128,576]{1,0:T(8,128)(2,1)} %copy.17.wd_ref) | copy-start | bytes 442372
  19.1 0.9 %copy-start.1 = (bf16[16,2,64,128]{3,2,1,0:T(8,128)(2,1)}, bf16[16,2,64,128]{3,2,1,0:T(8,128)(2,1)S(1)}, u32[]{:S(2)}) copy-start(bf16[16,2,64,128]{3,2,1,0:T(8,128)(2,1)S(1)} %collective-permute-done.above_ref) | copy-start | bytes 1572868
  20.1 28.3 %collective-permute-start.2 = (bf16[1,144,1152]{2,1,0:T(8,128)(2,1)S(1)}, bf16[1,144,1152]{2,1,0:T(8,128)(2,1)S(1)}, u32[]{:S(2)}, u32[]{:S(2)}) collective-permute-start(bf16[1,144,1152]{2,1,0:T(8,128)(2,1)S(1)} %get-tuple-element.16), channel_id=1, source_target_pairs={{0,16},{16,32},{32,48},{48,64},{64,80},{80,96},{96,112},{1,17},{17... | collective-permute-start | bytes 995336 | tf_op jit(solution)/shard_map/ppermute | solution.py:27
  23.2 25.1 %collective-permute-start.3 = (bf16[1,144,1152]{2,1,0:T(8,128)(2,1)S(1)}, bf16[1,144,1152]{2,1,0:T(8,128)(2,1)S(1)}, u32[]{:S(2)}, u32[]{:S(2)}) collective-permute-start(bf16[1,144,1152]{2,1,0:T(8,128)(2,1)S(1)} %get-tuple-element.15), channel_id=1, source_target_pairs={{16,0},{32,16},{48,32},{64,48},{80,64},{96,80},{112,96},{17,1},{33... | collective-permute-start | bytes 995336 | tf_op jit(solution)/shard_map/ppermute | solution.py:27
  27.5 1.0 %copy-start.2 = (bf16[16,2,64,128]{3,2,1,0:T(8,128)(2,1)S(1)}, bf16[16,2,64,128]{3,2,1,0:T(8,128)(2,1)}, u32[]{:S(2)}) copy-start(bf16[16,2,64,128]{3,2,1,0:T(8,128)(2,1)} %copy-done.1) | copy-start | bytes 1572868
  28.5 0.9 %copy-start.4 = (bf16[144,576]{1,0:T(8,128)(2,1)S(1)}, bf16[144,576]{1,0:T(8,128)(2,1)}, u32[]{:S(2)}) copy-start(bf16[144,576]{1,0:T(8,128)(2,1)} %copy-done.3) | copy-start | bytes 497668
  50.0 6.0 %collective-permute-start.4 = (bf16[16,1,64,128]{3,2,1,0:T(8,128)(2,1)S(1)}, bf16[16,1,64,128]{3,2,1,0:T(8,128)(2,1)S(1)}, u32[]{:S(2)}, u32[]{:S(2)}) collective-permute-start(bf16[16,1,64,128]{3,2,1,0:T(8,128)(2,1)S(1)} %get-tuple-element.14), channel_id=1, source_target_pairs={{0,1},{1,2},{2,3},{3,4},{4,5},{5,6},{6,7},{7,8},{8,9},{9,10},{10,1... | collective-permute-start | bytes 786440 | tf_op jit(solution)/shard_map/ppermute | solution.py:27
  52.6 11.3 %collective-permute-start.5 = (bf16[16,1,64,128]{3,2,1,0:T(8,128)(2,1)S(1)}, bf16[16,1,64,128]{3,2,1,0:T(8,128)(2,1)S(1)}, u32[]{:S(2)}, u32[]{:S(2)}) collective-permute-start(bf16[16,1,64,128]{3,2,1,0:T(8,128)(2,1)S(1)} %get-tuple-element.13), channel_id=1, source_target_pairs={{1,0},{2,1},{3,2},{4,3},{5,4},{6,5},{7,6},{8,7},{9,8},{10,9},{11,1... | collective-permute-start | bytes 786440 | tf_op jit(solution)/shard_map/ppermute | solution.py:27
  56.0 16.1 %copy-start.6 = (bf16[3,128,288]{1,2,0:T(8,128)(2,1)S(1)}, bf16[3,128,288]{1,2,0:T(8,128)(2,1)}, u32[]{:S(2)}) copy-start(bf16[3,128,288]{1,2,0:T(8,128)(2,1)} %param.11) | copy-start | bytes 663556
  64.7 18.0 %collective-permute-start.6 = (bf16[1,256,288]{2,1,0:T(8,128)(2,1)S(1)}, bf16[1,256,288]{2,1,0:T(8,128)(2,1)S(1)}, u32[]{:S(2)}, u32[]{:S(2)}) collective-permute-start(bf16[1,256,288]{2,1,0:T(8,128)(2,1)S(1)} %get-tuple-element.18), channel_id=1, source_target_pairs={{0,16},{16,32},{32,48},{48,64},{64,80},{80,96},{96,112},{1,17},{17... | collective-permute-start | bytes 442376 | tf_op jit(solution)/shard_map/ppermute | solution.py:27
  66.7 16.1 %collective-permute-start.7 = (bf16[1,256,288]{2,1,0:T(8,128)(2,1)S(1)}, bf16[1,256,288]{2,1,0:T(8,128)(2,1)S(1)}, u32[]{:S(2)}, u32[]{:S(2)}) collective-permute-start(bf16[1,256,288]{2,1,0:T(8,128)(2,1)S(1)} %get-tuple-element.17), channel_id=1, source_target_pairs={{16,0},{32,16},{48,32},{64,48},{80,64},{96,80},{112,96},{17,1},{33... | collective-permute-start | bytes 442376 | tf_op jit(solution)/shard_map/ppermute | solution.py:27

commit v10 on v8

--- a/solution.py
+++ b/solution.py
@@ -334,10 +334,32 @@
     return jnp.concatenate([outer[:1], inner, outer[1:]], axis=0)
 
 
+def _copy_kernel(top_ref, bottom_ref, top_out, bottom_out):
+    top_out[...] = top_ref[...]
+    bottom_out[...] = bottom_ref[...]
+
+
+def edge_rows(block, top, bottom):
+    frames, rows, channels, width = block.shape
+    top_spec = pl.BlockSpec((frames, top, channels, width), lambda i: (0, rows // top - 1, 0, 0))
+    bottom_spec = pl.BlockSpec((frames, bottom, channels, width), lambda i: (0, 0, 0, 0))
+    return pl.pallas_call(
+        _copy_kernel,
+        grid=(1,),
+        out_shape=(
+            jax.ShapeDtypeStruct((frames, top, channels, width), block.dtype),
+            jax.ShapeDtypeStruct((frames, bottom, channels, width), block.dtype),
+        ),
+        in_specs=[top_spec, bottom_spec],
+        out_specs=(pl.BlockSpec((frames, top, channels, width), lambda i: (0, 0, 0, 0)), bottom_spec),
+    )(block, block)
+
+
 def on_device(video_clip, spatial_one, temporal_one, down_weight, spatial_two, temporal_two):
     rows = video_clip.shape[1]
-    above = from_behind(video_clip[:, rows - 2 :], "row", 1)
-    below = from_behind(video_clip[:, :1], "row", -1)
+    top, bottom = edge_rows(video_clip, 2, 1)
+    above = from_behind(top, "row", 1)
+    below = from_behind(bottom, "row", -1)
     keep_first = (lax.axis_index("row") > 0).astype(jnp.int32).reshape(1)
     reduced = block_one(above, video_clip, below, keep_first, spatial_one, temporal_one, down_weight)
     rows = reduced.shape[1]

time: 83.2 us -> 82.5 us (level)
  local copies, waits for them, and re-layouts: 7.4 us -> 2.79 us
  Pallas kernels: 32 us -> 34.1 us
  starting transfers between devices: 25.8 us -> 26.8 us
  waiting for transfers between devices: 16.1 us -> 17 us
    slice x2 -> x0, local copies, waits for them, and re-layouts: 3.72 us -> none  [the longest x1 2.04 us: on_device(): above = from_behind(video_clip[:, rows - 2:], 'row', 1)]
    pallas_call x0 -> x1, Pallas kernels: none -> 2.17 us  [edge_rows(): pl.pallas_call(_copy_kernel, grid=(1,), out_shape=(jax.ShapeDtypeStruct((...]
    ppermute x8, starting transfers between devices: 25.8 us -> 26.8 us  [from_behind(): return lax.ppermute(array, axis, pairs)]
    transpose x1, local copies, waits for them, and re-layouts: 0.98 us -> 0.09 us  [block_one(): t3 = jnp.transpose(temporal_kernel, (1, 0, 2)).reshape(channels, 3 * mids)]
    ppermute x8, waiting for transfers between devices: 16.1 us -> 17 us  [from_behind(): return lax.ppermute(array, axis, pairs)]
  transfers between devices with their start and end apart: 8 -> 8, of which waited for: 3 -> 3; matrix products, arithmetic and copies ran while one was open for 5% -> 2% of each run, Pallas kernels for 34% -> 35%
where the time goes in v10:
time: 82.5 us; the launch traced here: 82.2 us
  Pallas kernels  34.1 us (41%)
  starting transfers between devices  26.8 us (32%)
  waiting for transfers between devices  17 us (21%)
  local copies, waits for them, and re-layouts  2.79 us (3%)
  other arithmetic  1.24 us (2%)
    ppermute x8, starting transfers between devices, from_behind(): return lax.ppermute(array, axis, pairs)  26.8 us
    pallas_call x1, Pallas kernels, block_one(): pl.pallas_call(_inner_one_kernel, out_shape=(jax.ShapeDtypeStruct((frames...  18.9 us
    ppermute x8, waiting for transfers between devices, from_behind(): return lax.ppermute(array, axis, pairs)  17 us
    pallas_call x1, Pallas kernels, block_two(): pl.pallas_call(_inner_two_kernel, out_shape=(jax.ShapeDtypeStruct((frames...  9.62 us
    pallas_call x1, Pallas kernels, edge_rows(): pl.pallas_call(_copy_kernel, grid=(1,), out_shape=(jax.ShapeDtypeStruct((...  2.17 us
  transfers between devices with their start and end apart: 8, of which 3 were waited for; matrix products, arithmetic and copies ran while one was open for 2% of the time, Pallas kernels for 35%

profile of v10, /device:TPU:57, one launch (start us, length us, event | category | flops | bytes accessed | tf_op | source)
XLA Modules:
  0.0 82.2 jit_solution(3165759179469727926)
XLA Ops:
  0.0 0.0 copy-start
  0.0 0.0 copy-start.4
  0.0 0.0 copy-start.3
  0.0 2.2 %shard_map.64 = (bf16[16,2,64,128]{3,2,1,0:T(8,128)(2,1)}, bf16[16,1,64,128]{3,2,1,0:T(8,128)(2,1)}) custom-call(bf16[16,8,64,128]{3,2,1,0:T(8,128)(2,1)} %xp_ref.5, bf16[16,8,64,128]{3,2,1,0:T(8,128)(2,1)} %xp_ref.5), custom_call_target="tpu_custom_call" | custom-call | tf_op jit(solution)/shard_map/pallas_call | solution.py:346
  2.2 4.8 %collective-permute-start = (bf16[16,2,64,128]{3,2,1,0:T(8,128)(2,1)}, bf16[16,2,64,128]{3,2,1,0:T(8,128)(2,1)S(1)}, u32[]{:S(2)}, u32[]{:S(2)}) collective-permute-start(bf16[16,2,64,128]{3,2,1,0:T(8,128)(2,1)} %get-tuple-element.11), channel_id=1, source_target_pairs={{0,1},{1,2},{2,3},{3,4},{4,5},{5,6},{6,7},{7,8},{8,9},{9,10},{10,1... | collective-permute-start | bytes 1572872 | tf_op jit(solution)/shard_map/ppermute | solution.py:27
  7.0 1.9 %collective-permute-start.1 = (bf16[16,1,64,128]{3,2,1,0:T(8,128)(2,1)}, bf16[16,1,64,128]{3,2,1,0:T(8,128)(2,1)S(1)}, u32[]{:S(2)}, u32[]{:S(2)}) collective-permute-start(bf16[16,1,64,128]{3,2,1,0:T(8,128)(2,1)} %get-tuple-element.12), channel_id=1, source_target_pairs={{1,0},{2,1},{3,2},{4,3},{5,4},{6,5},{7,6},{8,7},{9,8},{10,9},{11,1... | collective-permute-start | bytes 786440 | tf_op jit(solution)/shard_map/ppermute | solution.py:27
  8.9 0.0 copy-done.4
  8.9 0.1 copy.11
  9.0 0.1 reshape.19.t3_ref
  9.2 1.1 %copy.12.w9_ref = bf16[144,576]{1,0:T(8,128)(2,1)S(1)} copy(bf16[144,576]{0,1:T(8,128)(2,1)} %bitcast.16) | data formatting | bytes 331776 | tf_op jit(solution)/shard_map/reshape | solution.py:159
  10.3 0.0 copy-done.3
  10.3 0.2 copy.15.wd_ref
  10.5 8.0 %collective-permute-done.1.below_ref = bf16[16,1,64,128]{3,2,1,0:T(8,128)(2,1)S(1)} collective-permute-done((bf16[16,1,64,128]{3,2,1,0:T(8,128)(2,1)}, bf16[16,1,64,128]{3,2,1,0:T(8,128)(2,1)S(1)}, u32[]{:S(2)}, u32[]{:S(2)}) %collective-permute-start.1) | collective-permute-done | bytes 262176 | tf_op jit(solution)/shard_map/ppermute | solution.py:27
  18.5 0.0 collective-permute-done.above_ref
  18.5 0.0 copy-done
  18.5 0.8 %shard_map.65.edge_ref = bf16[2,144,1152]{2,1,0:T(8,128)(2,1)S(1)} custom-call(bf16[16,2,64,128]{3,2,1,0:T(8,128)(2,1)S(1)} %collective-permute-done.above_ref, bf16[16,8,64,128]{3,2,1,0:T(8,128)(2,1)S(1)} %copy-done, bf16[16,1,64,128]{3,2,1,0:T(8,128)(2,1)S(1)} %collective-permute-done.1.below_ref, bf16[144,576]{1,0:T(8,128)(2,1)S(1)} %copy.12.w9_ref), custom_call_target="tpu_custom_call" | custom-call | flops 382205952 | bytes 2097152 | tf_op jit(solution)/shard_map/pallas_call | solution.py:172
  19.4 0.1 fusion.1
  19.4 3.1 %collective-permute-start.2 = (bf16[1,144,1152]{2,1,0:T(8,128)(2,1)S(1)}, bf16[1,144,1152]{2,1,0:T(8,128)(2,1)S(1)}, u32[]{:S(2)}, u32[]{:S(2)}) collective-permute-start(bf16[1,144,1152]{2,1,0:T(8,128)(2,1)S(1)} %get-tuple-element.20), channel_id=1, source_target_pairs={{0,16},{16,32},{32,48},{48,64},{64,80},{80,96},{96,112},{1,17},{17... | collective-permute-start | bytes 995336 | tf_op jit(solution)/shard_map/ppermute | solution.py:27
  22.5 4.3 %collective-permute-start.3 = (bf16[1,144,1152]{2,1,0:T(8,128)(2,1)S(1)}, bf16[1,144,1152]{2,1,0:T(8,128)(2,1)S(1)}, u32[]{:S(2)}, u32[]{:S(2)}) collective-permute-start(bf16[1,144,1152]{2,1,0:T(8,128)(2,1)S(1)} %get-tuple-element.19), channel_id=1, source_target_pairs={{16,0},{32,16},{48,32},{64,48},{80,64},{96,80},{112,96},{17,1},{33... | collective-permute-start | bytes 995336 | tf_op jit(solution)/shard_map/ppermute | solution.py:27
  26.8 18.9 %shard_map.66 = (bf16[14,4,64,128]{3,2,1,0:T(8,128)(2,1)S(1)}, bf16[2,144,1152]{2,1,0:T(8,128)(2,1)S(1)}) custom-call(s32[1]{0:T(128)} %bitcast.keep_ref, bf16[16,2,64,128]{3,2,1,0:T(8,128)(2,1)S(1)} %collective-permute-done.above_ref, bf16[16,8,64,128]{3,2,1,0:T(8,128)(2,1)S(1)} %copy-done, bf16[16,1,64,128]{3,2,1,0:T(8,128)(2,1)S(1)} %collective-permute-done.1.below_ref, ...), custom_call_target="tpu_custom_call" | custom-call | flops 5284823040 | bytes 4194304 | tf_op jit(solution)/shard_map/pallas_call | solution.py:182
  45.7 0.0 collective-permute-done.2.before_ref
  45.7 0.0 collective-permute-done.3.after_ref
  45.7 1.4 %shard_map.67 = bf16[2,4,64,128]{3,2,1,0:T(8,128)(2,1)S(1)} custom-call(s32[1]{0:T(128)} %bitcast.keep_ref, bf16[16,2,64,128]{3,2,1,0:T(8,128)(2,1)S(1)} %collective-permute-done.above_ref, bf16[16,8,64,128]{3,2,1,0:T(8,128)(2,1)S(1)} %copy-done, bf16[16,1,64,128]{3,2,1,0:T(8,128)(2,1)S(1)} %collective-permute-done.1.below_ref, ...), custom_call_target="tpu_custom_call" | custom-call | tf_op jit(solution)/shard_map/pallas_call | solution.py:196
  47.1 0.0 copy-start.2
  47.2 0.1 pad_maximum_fusion.xp_ref
  47.3 0.7 fusion
  48.0 3.3 %collective-permute-start.4 = (bf16[16,1,64,128]{3,2,1,0:T(8,128)(2,1)}, bf16[16,1,64,128]{3,2,1,0:T(8,128)(2,1)S(1)}, u32[]{:S(2)}, u32[]{:S(2)}) collective-permute-start(bf16[16,1,64,128]{3,2,1,0:T(8,128)(2,1)} %get-tuple-element.18), channel_id=1, source_target_pairs={{0,1},{1,2},{2,3},{3,4},{4,5},{5,6},{6,7},{7,8},{8,9},{9,10},{10,1... | collective-permute-start | bytes 786440 | tf_op jit(solution)/shard_map/ppermute | solution.py:27
  51.4 1.9 %collective-permute-start.5 = (bf16[16,1,64,128]{3,2,1,0:T(8,128)(2,1)S(1)}, bf16[16,1,64,128]{3,2,1,0:T(8,128)(2,1)S(1)}, u32[]{:S(2)}, u32[]{:S(2)}) collective-permute-start(bf16[16,1,64,128]{3,2,1,0:T(8,128)(2,1)S(1)} %get-tuple-element.17), channel_id=1, source_target_pairs={{1,0},{2,1},{3,2},{4,3},{5,4},{6,5},{7,6},{8,7},{9,8},{10,9},{11,1... | collective-permute-start | bytes 786440 | tf_op jit(solution)/shard_map/ppermute | solution.py:27
  53.3 0.0 copy-done.2
  53.3 0.4 copy.16
  53.7 0.0 copy-start.1
  53.8 1.3 %collective-permute-done.4.above_ref = bf16[16,1,64,128]{3,2,1,0:T(8,128)(2,1)S(1)} collective-permute-done((bf16[16,1,64,128]{3,2,1,0:T(8,128)(2,1)}, bf16[16,1,64,128]{3,2,1,0:T(8,128)(2,1)S(1)}, u32[]{:S(2)}, u32[]{:S(2)}) %collective-permute-start.4) | collective-permute-done | bytes 262176 | tf_op jit(solution)/shard_map/ppermute | solution.py:27
  55.0 7.7 %collective-permute-done.5.below_ref = bf16[16,1,64,128]{3,2,1,0:T(8,128)(2,1)S(1)} collective-permute-done((bf16[16,1,64,128]{3,2,1,0:T(8,128)(2,1)S(1)}, bf16[16,1,64,128]{3,2,1,0:T(8,128)(2,1)S(1)}, u32[]{:S(2)}, u32[]{:S(2)}) %collective-permute-start.5) | collective-permute-done | bytes 262176 | tf_op jit(solution)/shard_map/ppermute | solution.py:27
  62.7 0.8 shard_map.68.edge_ref
  63.6 1.9 %collective-permute-start.6 = (bf16[1,256,288]{2,1,0:T(8,128)(2,1)S(1)}, bf16[1,256,288]{2,1,0:T(8,128)(2,1)S(1)}, u32[]{:S(2)}, u32[]{:S(2)}) collective-permute-start(bf16[1,256,288]{2,1,0:T(8,128)(2,1)S(1)} %get-tuple-element.22), channel_id=1, source_target_pairs={{0,16},{16,32},{32,48},{48,64},{64,80},{80,96},{96,112},{1,17},{17... | collective-permute-start | bytes 442376 | tf_op jit(solution)/shard_map/ppermute | solution.py:27
  65.5 5.5 %collective-permute-start.7 = (bf16[1,256,288]{2,1,0:T(8,128)(2,1)S(1)}, bf16[1,256,288]{2,1,0:T(8,128)(2,1)S(1)}, u32[]{:S(2)}, u32[]{:S(2)}) collective-permute-start(bf16[1,256,288]{2,1,0:T(8,128)(2,1)S(1)} %get-tuple-element.21), channel_id=1, source_target_pairs={{16,0},{32,16},{48,32},{64,48},{80,64},{96,80},{112,96},{17,1},{33... | collective-permute-start | bytes 442376 | tf_op jit(solution)/shard_map/ppermute | solution.py:27
  71.0 0.0 copy-done.1
  71.0 9.6 %shard_map.69 = (bf16[14,4,64,128]{3,2,1,0:T(8,128)(2,1)S(1)}, bf16[2,256,288]{2,1,0:T(8,128)(2,1)S(1)}) custom-call(bf16[16,1,64,128]{3,2,1,0:T(8,128)(2,1)S(1)} %collective-permute-done.4.above_ref, bf16[16,4,64,128]{3,2,1,0:T(8,128)(2,1)S(1)} %pad_maximum_fusion.xp_ref, bf16[16,1,64,128]{3,2,1,0:T(8,128)(2,1)S(1)} %collective-permute-done.5.below_ref, ...), custom_call_target="tpu_custom_call" | custom-call | flops 3623878656 | bytes 2097152 | tf_op jit(solution)/shard_map/pallas_call | solution.py:311
  80.6 0.0 collective-permute-done.6.before_ref
  80.6 0.0 collective-permute-done.7.after_ref
  80.6 0.5 shard_map.70
  81.1 1.1 %pad_maximum_fusion.1 = bf16[16,4,64,128]{3,2,1,0:T(8,128)(2,1)} fusion(bf16[1,4,64,128]{3,2,1,0:T(8,128)(2,1)S(1)} %get-tuple-element.24, bf16[14,4,64,128]{3,2,1,0:T(8,128)(2,1)S(1)} %get-tuple-element.16, bf16[1,4,64,128]{3,2,1,0:T(8,128)(2,1)S(1)} %get-tuple-element.23), kind=kLoop, calls=%fused_computation.1 | loop fusion | flops 1048576 | bytes 2097152 | tf_op jit(solution)/shard_map/concatenate | solution.py:334
  (3 shorter events, 0.1 us)
Async XLA Ops:
  0.0 18.5 %copy-start = (bf16[16,8,64,128]{3,2,1,0:T(8,128)(2,1)S(1)}, bf16[16,8,64,128]{3,2,1,0:T(8,128)(2,1)}, u32[]{:S(2)}) copy-start(bf16[16,8,64,128]{3,2,1,0:T(8,128)(2,1)} %xp_ref.5) | copy-start | bytes 6291460
  0.0 8.9 %copy-start.4 = (bf16[3,64,144]{2,1,0:T(8,128)(2,1)S(1)}, bf16[3,64,144]{2,1,0:T(8,128)(2,1)}, u32[]{:S(2)}) copy-start(bf16[3,64,144]{2,1,0:T(8,128)(2,1)} %param.8) | copy-start | bytes 165892
  0.0 10.3 %copy-start.3 = (bf16[3,3,128,64]{2,3,1,0:T(8,128)(2,1)S(1)}, bf16[3,3,128,64]{2,3,1,0:T(8,128)(2,1)}, u32[]{:S(2)}) copy-start(bf16[3,3,128,64]{2,3,1,0:T(8,128)(2,1)} %param.9) | copy-start | bytes 442372
  2.2 16.3 %collective-permute-start = (bf16[16,2,64,128]{3,2,1,0:T(8,128)(2,1)}, bf16[16,2,64,128]{3,2,1,0:T(8,128)(2,1)S(1)}, u32[]{:S(2)}, u32[]{:S(2)}) collective-permute-start(bf16[16,2,64,128]{3,2,1,0:T(8,128)(2,1)} %get-tuple-element.11), channel_id=1, source_target_pairs={{0,1},{1,2},{2,3},{3,4},{4,5},{5,6},{6,7},{7,8},{8,9},{9,10},{10,1... | collective-permute-start | bytes 1572872 | tf_op jit(solution)/shard_map/ppermute | solution.py:27
  7.0 11.5 %collective-permute-start.1 = (bf16[16,1,64,128]{3,2,1,0:T(8,128)(2,1)}, bf16[16,1,64,128]{3,2,1,0:T(8,128)(2,1)S(1)}, u32[]{:S(2)}, u32[]{:S(2)}) collective-permute-start(bf16[16,1,64,128]{3,2,1,0:T(8,128)(2,1)} %get-tuple-element.12), channel_id=1, source_target_pairs={{1,0},{2,1},{3,2},{4,3},{5,4},{6,5},{7,6},{8,7},{9,8},{10,9},{11,1... | collective-permute-start | bytes 786440 | tf_op jit(solution)/shard_map/ppermute | solution.py:27
  19.4 26.3 %collective-permute-start.2 = (bf16[1,144,1152]{2,1,0:T(8,128)(2,1)S(1)}, bf16[1,144,1152]{2,1,0:T(8,128)(2,1)S(1)}, u32[]{:S(2)}, u32[]{:S(2)}) collective-permute-start(bf16[1,144,1152]{2,1,0:T(8,128)(2,1)S(1)} %get-tuple-element.20), channel_id=1, source_target_pairs={{0,16},{16,32},{32,48},{48,64},{64,80},{80,96},{96,112},{1,17},{17... | collective-permute-start | bytes 995336 | tf_op jit(solution)/shard_map/ppermute | solution.py:27
  22.5 23.2 %collective-permute-start.3 = (bf16[1,144,1152]{2,1,0:T(8,128)(2,1)S(1)}, bf16[1,144,1152]{2,1,0:T(8,128)(2,1)S(1)}, u32[]{:S(2)}, u32[]{:S(2)}) collective-permute-start(bf16[1,144,1152]{2,1,0:T(8,128)(2,1)S(1)} %get-tuple-element.19), channel_id=1, source_target_pairs={{16,0},{32,16},{48,32},{64,48},{80,64},{96,80},{112,96},{17,1},{33... | collective-permute-start | bytes 995336 | tf_op jit(solution)/shard_map/ppermute | solution.py:27
  47.1 6.2 %copy-start.2 = (bf16[3,3,288,128]{3,2,1,0:T(8,128)(2,1)S(1)}, bf16[3,3,288,128]{3,2,1,0:T(8,128)(2,1)}, u32[]{:S(2)}) copy-start(bf16[3,3,288,128]{3,2,1,0:T(8,128)(2,1)} %param.10) | copy-start | bytes 1990660
  48.0 7.0 %collective-permute-start.4 = (bf16[16,1,64,128]{3,2,1,0:T(8,128)(2,1)}, bf16[16,1,64,128]{3,2,1,0:T(8,128)(2,1)S(1)}, u32[]{:S(2)}, u32[]{:S(2)}) collective-permute-start(bf16[16,1,64,128]{3,2,1,0:T(8,128)(2,1)} %get-tuple-element.18), channel_id=1, source_target_pairs={{0,1},{1,2},{2,3},{3,4},{4,5},{5,6},{6,7},{7,8},{8,9},{9,10},{10,1... | collective-permute-start | bytes 786440 | tf_op jit(solution)/shard_map/ppermute | solution.py:27
  51.4 11.3 %collective-permute-start.5 = (bf16[16,1,64,128]{3,2,1,0:T(8,128)(2,1)S(1)}, bf16[16,1,64,128]{3,2,1,0:T(8,128)(2,1)S(1)}, u32[]{:S(2)}, u32[]{:S(2)}) collective-permute-start(bf16[16,1,64,128]{3,2,1,0:T(8,128)(2,1)S(1)} %get-tuple-element.17), channel_id=1, source_target_pairs={{1,0},{2,1},{3,2},{4,3},{5,4},{6,5},{7,6},{8,7},{9,8},{10,9},{11,1... | collective-permute-start | bytes 786440 | tf_op jit(solution)/shard_map/ppermute | solution.py:27
  53.7 17.2 %copy-start.1 = (bf16[3,128,288]{1,2,0:T(8,128)(2,1)S(1)}, bf16[3,128,288]{1,2,0:T(8,128)(2,1)}, u32[]{:S(2)}) copy-start(bf16[3,128,288]{1,2,0:T(8,128)(2,1)} %param.11) | copy-start | bytes 663556
  63.6 17.1 %collective-permute-start.6 = (bf16[1,256,288]{2,1,0:T(8,128)(2,1)S(1)}, bf16[1,256,288]{2,1,0:T(8,128)(2,1)S(1)}, u32[]{:S(2)}, u32[]{:S(2)}) collective-permute-start(bf16[1,256,288]{2,1,0:T(8,128)(2,1)S(1)} %get-tuple-element.22), channel_id=1, source_target_pairs={{0,16},{16,32},{32,48},{48,64},{64,80},{80,96},{96,112},{1,17},{17... | collective-permute-start | bytes 442376 | tf_op jit(solution)/shard_map/ppermute | solution.py:27
  65.5 15.1 %collective-permute-start.7 = (bf16[1,256,288]{2,1,0:T(8,128)(2,1)S(1)}, bf16[1,256,288]{2,1,0:T(8,128)(2,1)S(1)}, u32[]{:S(2)}, u32[]{:S(2)}) collective-permute-start(bf16[1,256,288]{2,1,0:T(8,128)(2,1)S(1)} %get-tuple-element.21), channel_id=1, source_target_pairs={{16,0},{32,16},{48,32},{64,48},{80,64},{96,80},{112,96},{17,1},{33... | collective-permute-start | bytes 442376 | tf_op jit(solution)/shard_map/ppermute | solution.py:27

commit v11 on v10

--- a/solution.py
+++ b/solution.py
@@ -248,16 +248,16 @@
     frames = xp_ref.shape[0]
     plane = mid_ref.shape[1]
 
+    group = 4 if frames % 4 == 0 else 2
+
     def middle(g, carry):
-        f = 2 * g
-        m = _middle_two(
-            [_slab_two(above_ref, xp_ref, below_ref, f), _slab_two(above_ref, xp_ref, below_ref, f + 1)], w9_ref
-        )
-        mid_ref[f] = m[:plane]
-        mid_ref[f + 1] = m[plane:]
+        f = group * g
+        m = _middle_two([_slab_two(above_ref, xp_ref, below_ref, f + k) for k in range(group)], w9_ref)
+        for k in range(group):
+            mid_ref[f + k] = m[k * plane : (k + 1) * plane]
         return carry
 
-    lax.fori_loop(0, frames // 2, middle, 0)
+    lax.fori_loop(0, frames // group, middle, 0)
     side_ref[0] = mid_ref[1]
     side_ref[1] = mid_ref[frames - 2]
 

time: 82.5 us -> 81.9 us (level)
  transfers between devices with their start and end apart: 8 -> 8, of which waited for: 3 -> 3; matrix products, arithmetic and copies ran while one was open for 2% -> 2% of each run, Pallas kernels for 35% -> 34%
where the time goes in v11:
time: 81.9 us; the launch traced here: 81.6 us
  Pallas kernels  33.5 us (41%)
  starting transfers between devices  26.8 us (33%)
  waiting for transfers between devices  17 us (21%)
  local copies, waits for them, and re-layouts  2.79 us (3%)
  other arithmetic  1.24 us (2%)
    ppermute x8, starting transfers between devices, from_behind(): return lax.ppermute(array, axis, pairs)  26.8 us
    pallas_call x1, Pallas kernels, block_one(): pl.pallas_call(_inner_one_kernel, out_shape=(jax.ShapeDtypeStruct((frames...  18.9 us
    ppermute x8, waiting for transfers between devices, from_behind(): return lax.ppermute(array, axis, pairs)  17 us
    pallas_call x1, Pallas kernels, block_two(): pl.pallas_call(_inner_two_kernel, out_shape=(jax.ShapeDtypeStruct((frames...  9.03 us
    pallas_call x1, Pallas kernels, edge_rows(): pl.pallas_call(_copy_kernel, grid=(1,), out_shape=(jax.ShapeDtypeStruct((...  2.17 us
  transfers between devices with their start and end apart: 8, of which 3 were waited for; matrix products, arithmetic and copies ran while one was open for 2% of the time, Pallas kernels for 34%

profile of v11, /device:TPU:57, one launch (start us, length us, event | category | flops | bytes accessed | tf_op | source)
XLA Modules:
  0.0 81.6 jit_solution(15702829286670300945)
XLA Ops:
  0.0 0.0 copy-start
  0.0 0.0 copy-start.4
  0.0 0.0 copy-start.3
  0.0 2.2 %shard_map.64 = (bf16[16,2,64,128]{3,2,1,0:T(8,128)(2,1)}, bf16[16,1,64,128]{3,2,1,0:T(8,128)(2,1)}) custom-call(bf16[16,8,64,128]{3,2,1,0:T(8,128)(2,1)} %xp_ref.5, bf16[16,8,64,128]{3,2,1,0:T(8,128)(2,1)} %xp_ref.5), custom_call_target="tpu_custom_call" | custom-call | tf_op jit(solution)/shard_map/pallas_call | solution.py:346
  2.2 4.8 %collective-permute-start = (bf16[16,2,64,128]{3,2,1,0:T(8,128)(2,1)}, bf16[16,2,64,128]{3,2,1,0:T(8,128)(2,1)S(1)}, u32[]{:S(2)}, u32[]{:S(2)}) collective-permute-start(bf16[16,2,64,128]{3,2,1,0:T(8,128)(2,1)} %get-tuple-element.11), channel_id=1, source_target_pairs={{0,1},{1,2},{2,3},{3,4},{4,5},{5,6},{6,7},{7,8},{8,9},{9,10},{10,1... | collective-permute-start | bytes 1572872 | tf_op jit(solution)/shard_map/ppermute | solution.py:27
  7.0 1.9 %collective-permute-start.1 = (bf16[16,1,64,128]{3,2,1,0:T(8,128)(2,1)}, bf16[16,1,64,128]{3,2,1,0:T(8,128)(2,1)S(1)}, u32[]{:S(2)}, u32[]{:S(2)}) collective-permute-start(bf16[16,1,64,128]{3,2,1,0:T(8,128)(2,1)} %get-tuple-element.12), channel_id=1, source_target_pairs={{1,0},{2,1},{3,2},{4,3},{5,4},{6,5},{7,6},{8,7},{9,8},{10,9},{11,1... | collective-permute-start | bytes 786440 | tf_op jit(solution)/shard_map/ppermute | solution.py:27
  8.9 0.0 copy-done.4
  8.9 0.1 copy.11
  9.0 0.1 reshape.19.t3_ref
  9.2 1.1 %copy.12.w9_ref = bf16[144,576]{1,0:T(8,128)(2,1)S(1)} copy(bf16[144,576]{0,1:T(8,128)(2,1)} %bitcast.16) | data formatting | bytes 331776 | tf_op jit(solution)/shard_map/reshape | solution.py:159
  10.3 0.0 copy-done.3
  10.3 0.2 copy.15.wd_ref
  10.5 8.0 %collective-permute-done.1.below_ref = bf16[16,1,64,128]{3,2,1,0:T(8,128)(2,1)S(1)} collective-permute-done((bf16[16,1,64,128]{3,2,1,0:T(8,128)(2,1)}, bf16[16,1,64,128]{3,2,1,0:T(8,128)(2,1)S(1)}, u32[]{:S(2)}, u32[]{:S(2)}) %collective-permute-start.1) | collective-permute-done | bytes 262176 | tf_op jit(solution)/shard_map/ppermute | solution.py:27
  18.5 0.0 collective-permute-done.above_ref
  18.5 0.0 copy-done
  18.5 0.8 %shard_map.65.edge_ref = bf16[2,144,1152]{2,1,0:T(8,128)(2,1)S(1)} custom-call(bf16[16,2,64,128]{3,2,1,0:T(8,128)(2,1)S(1)} %collective-permute-done.above_ref, bf16[16,8,64,128]{3,2,1,0:T(8,128)(2,1)S(1)} %copy-done, bf16[16,1,64,128]{3,2,1,0:T(8,128)(2,1)S(1)} %collective-permute-done.1.below_ref, bf16[144,576]{1,0:T(8,128)(2,1)S(1)} %copy.12.w9_ref), custom_call_target="tpu_custom_call" | custom-call | flops 382205952 | bytes 2097152 | tf_op jit(solution)/shard_map/pallas_call | solution.py:172
  19.4 0.1 fusion.1
  19.4 3.1 %collective-permute-start.2 = (bf16[1,144,1152]{2,1,0:T(8,128)(2,1)S(1)}, bf16[1,144,1152]{2,1,0:T(8,128)(2,1)S(1)}, u32[]{:S(2)}, u32[]{:S(2)}) collective-permute-start(bf16[1,144,1152]{2,1,0:T(8,128)(2,1)S(1)} %get-tuple-element.20), channel_id=1, source_target_pairs={{0,16},{16,32},{32,48},{48,64},{64,80},{80,96},{96,112},{1,17},{17... | collective-permute-start | bytes 995336 | tf_op jit(solution)/shard_map/ppermute | solution.py:27
  22.5 4.3 %collective-permute-start.3 = (bf16[1,144,1152]{2,1,0:T(8,128)(2,1)S(1)}, bf16[1,144,1152]{2,1,0:T(8,128)(2,1)S(1)}, u32[]{:S(2)}, u32[]{:S(2)}) collective-permute-start(bf16[1,144,1152]{2,1,0:T(8,128)(2,1)S(1)} %get-tuple-element.19), channel_id=1, source_target_pairs={{16,0},{32,16},{48,32},{64,48},{80,64},{96,80},{112,96},{17,1},{33... | collective-permute-start | bytes 995336 | tf_op jit(solution)/shard_map/ppermute | solution.py:27
  26.8 18.9 %shard_map.66 = (bf16[14,4,64,128]{3,2,1,0:T(8,128)(2,1)S(1)}, bf16[2,144,1152]{2,1,0:T(8,128)(2,1)S(1)}) custom-call(s32[1]{0:T(128)} %bitcast.keep_ref, bf16[16,2,64,128]{3,2,1,0:T(8,128)(2,1)S(1)} %collective-permute-done.above_ref, bf16[16,8,64,128]{3,2,1,0:T(8,128)(2,1)S(1)} %copy-done, bf16[16,1,64,128]{3,2,1,0:T(8,128)(2,1)S(1)} %collective-permute-done.1.below_ref, ...), custom_call_target="tpu_custom_call" | custom-call | flops 5284823040 | bytes 4194304 | tf_op jit(solution)/shard_map/pallas_call | solution.py:182
  45.7 0.0 collective-permute-done.2.before_ref
  45.7 0.0 collective-permute-done.3.after_ref
  45.7 1.4 %shard_map.67 = bf16[2,4,64,128]{3,2,1,0:T(8,128)(2,1)S(1)} custom-call(s32[1]{0:T(128)} %bitcast.keep_ref, bf16[16,2,64,128]{3,2,1,0:T(8,128)(2,1)S(1)} %collective-permute-done.above_ref, bf16[16,8,64,128]{3,2,1,0:T(8,128)(2,1)S(1)} %copy-done, bf16[16,1,64,128]{3,2,1,0:T(8,128)(2,1)S(1)} %collective-permute-done.1.below_ref, ...), custom_call_target="tpu_custom_call" | custom-call | tf_op jit(solution)/shard_map/pallas_call | solution.py:196
  47.1 0.0 copy-start.2
  47.2 0.1 pad_maximum_fusion.xp_ref
  47.3 0.7 fusion
  48.0 3.3 %collective-permute-start.4 = (bf16[16,1,64,128]{3,2,1,0:T(8,128)(2,1)}, bf16[16,1,64,128]{3,2,1,0:T(8,128)(2,1)S(1)}, u32[]{:S(2)}, u32[]{:S(2)}) collective-permute-start(bf16[16,1,64,128]{3,2,1,0:T(8,128)(2,1)} %get-tuple-element.18), channel_id=1, source_target_pairs={{0,1},{1,2},{2,3},{3,4},{4,5},{5,6},{6,7},{7,8},{8,9},{9,10},{10,1... | collective-permute-start | bytes 786440 | tf_op jit(solution)/shard_map/ppermute | solution.py:27
  51.4 1.9 %collective-permute-start.5 = (bf16[16,1,64,128]{3,2,1,0:T(8,128)(2,1)S(1)}, bf16[16,1,64,128]{3,2,1,0:T(8,128)(2,1)S(1)}, u32[]{:S(2)}, u32[]{:S(2)}) collective-permute-start(bf16[16,1,64,128]{3,2,1,0:T(8,128)(2,1)S(1)} %get-tuple-element.17), channel_id=1, source_target_pairs={{1,0},{2,1},{3,2},{4,3},{5,4},{6,5},{7,6},{8,7},{9,8},{10,9},{11,1... | collective-permute-start | bytes 786440 | tf_op jit(solution)/shard_map/ppermute | solution.py:27
  53.3 0.0 copy-done.2
  53.3 0.4 copy.16
  53.7 0.0 copy-start.1
  53.8 1.3 %collective-permute-done.4.above_ref = bf16[16,1,64,128]{3,2,1,0:T(8,128)(2,1)S(1)} collective-permute-done((bf16[16,1,64,128]{3,2,1,0:T(8,128)(2,1)}, bf16[16,1,64,128]{3,2,1,0:T(8,128)(2,1)S(1)}, u32[]{:S(2)}, u32[]{:S(2)}) %collective-permute-start.4) | collective-permute-done | bytes 262176 | tf_op jit(solution)/shard_map/ppermute | solution.py:27
  55.0 7.7 %collective-permute-done.5.below_ref = bf16[16,1,64,128]{3,2,1,0:T(8,128)(2,1)S(1)} collective-permute-done((bf16[16,1,64,128]{3,2,1,0:T(8,128)(2,1)S(1)}, bf16[16,1,64,128]{3,2,1,0:T(8,128)(2,1)S(1)}, u32[]{:S(2)}, u32[]{:S(2)}) %collective-permute-start.5) | collective-permute-done | bytes 262176 | tf_op jit(solution)/shard_map/ppermute | solution.py:27
  62.7 0.8 shard_map.68.edge_ref
  63.6 1.9 %collective-permute-start.6 = (bf16[1,256,288]{2,1,0:T(8,128)(2,1)S(1)}, bf16[1,256,288]{2,1,0:T(8,128)(2,1)S(1)}, u32[]{:S(2)}, u32[]{:S(2)}) collective-permute-start(bf16[1,256,288]{2,1,0:T(8,128)(2,1)S(1)} %get-tuple-element.22), channel_id=1, source_target_pairs={{0,16},{16,32},{32,48},{48,64},{64,80},{80,96},{96,112},{1,17},{17... | collective-permute-start | bytes 442376 | tf_op jit(solution)/shard_map/ppermute | solution.py:27
  65.5 5.5 %collective-permute-start.7 = (bf16[1,256,288]{2,1,0:T(8,128)(2,1)S(1)}, bf16[1,256,288]{2,1,0:T(8,128)(2,1)S(1)}, u32[]{:S(2)}, u32[]{:S(2)}) collective-permute-start(bf16[1,256,288]{2,1,0:T(8,128)(2,1)S(1)} %get-tuple-element.21), channel_id=1, source_target_pairs={{16,0},{32,16},{48,32},{64,48},{80,64},{96,80},{112,96},{17,1},{33... | collective-permute-start | bytes 442376 | tf_op jit(solution)/shard_map/ppermute | solution.py:27
  71.0 0.0 copy-done.1
  71.0 9.0 %shard_map.69 = (bf16[14,4,64,128]{3,2,1,0:T(8,128)(2,1)S(1)}, bf16[2,256,288]{2,1,0:T(8,128)(2,1)S(1)}) custom-call(bf16[16,1,64,128]{3,2,1,0:T(8,128)(2,1)S(1)} %collective-permute-done.4.above_ref, bf16[16,4,64,128]{3,2,1,0:T(8,128)(2,1)S(1)} %pad_maximum_fusion.xp_ref, bf16[16,1,64,128]{3,2,1,0:T(8,128)(2,1)S(1)} %collective-permute-done.5.below_ref, ...), custom_call_target="tpu_custom_call" | custom-call | flops 3623878656 | bytes 2097152 | tf_op jit(solution)/shard_map/pallas_call | solution.py:311
  80.0 0.0 collective-permute-done.6.before_ref
  80.0 0.0 collective-permute-done.7.after_ref
  80.0 0.5 shard_map.70
  80.5 1.1 %pad_maximum_fusion.1 = bf16[16,4,64,128]{3,2,1,0:T(8,128)(2,1)} fusion(bf16[1,4,64,128]{3,2,1,0:T(8,128)(2,1)S(1)} %get-tuple-element.24, bf16[14,4,64,128]{3,2,1,0:T(8,128)(2,1)S(1)} %get-tuple-element.16, bf16[1,4,64,128]{3,2,1,0:T(8,128)(2,1)S(1)} %get-tuple-element.23), kind=kLoop, calls=%fused_computation.1 | loop fusion | flops 1048576 | bytes 2097152 | tf_op jit(solution)/shard_map/concatenate | solution.py:334
  (3 shorter events, 0.1 us)
Async XLA Ops:
  0.0 18.5 %copy-start = (bf16[16,8,64,128]{3,2,1,0:T(8,128)(2,1)S(1)}, bf16[16,8,64,128]{3,2,1,0:T(8,128)(2,1)}, u32[]{:S(2)}) copy-start(bf16[16,8,64,128]{3,2,1,0:T(8,128)(2,1)} %xp_ref.5) | copy-start | bytes 6291460
  0.0 8.9 %copy-start.4 = (bf16[3,64,144]{2,1,0:T(8,128)(2,1)S(1)}, bf16[3,64,144]{2,1,0:T(8,128)(2,1)}, u32[]{:S(2)}) copy-start(bf16[3,64,144]{2,1,0:T(8,128)(2,1)} %param.8) | copy-start | bytes 165892
  0.0 10.3 %copy-start.3 = (bf16[3,3,128,64]{2,3,1,0:T(8,128)(2,1)S(1)}, bf16[3,3,128,64]{2,3,1,0:T(8,128)(2,1)}, u32[]{:S(2)}) copy-start(bf16[3,3,128,64]{2,3,1,0:T(8,128)(2,1)} %param.9) | copy-start | bytes 442372
  2.2 16.3 %collective-permute-start = (bf16[16,2,64,128]{3,2,1,0:T(8,128)(2,1)}, bf16[16,2,64,128]{3,2,1,0:T(8,128)(2,1)S(1)}, u32[]{:S(2)}, u32[]{:S(2)}) collective-permute-start(bf16[16,2,64,128]{3,2,1,0:T(8,128)(2,1)} %get-tuple-element.11), channel_id=1, source_target_pairs={{0,1},{1,2},{2,3},{3,4},{4,5},{5,6},{6,7},{7,8},{8,9},{9,10},{10,1... | collective-permute-start | bytes 1572872 | tf_op jit(solution)/shard_map/ppermute | solution.py:27
  7.0 11.5 %collective-permute-start.1 = (bf16[16,1,64,128]{3,2,1,0:T(8,128)(2,1)}, bf16[16,1,64,128]{3,2,1,0:T(8,128)(2,1)S(1)}, u32[]{:S(2)}, u32[]{:S(2)}) collective-permute-start(bf16[16,1,64,128]{3,2,1,0:T(8,128)(2,1)} %get-tuple-element.12), channel_id=1, source_target_pairs={{1,0},{2,1},{3,2},{4,3},{5,4},{6,5},{7,6},{8,7},{9,8},{10,9},{11,1... | collective-permute-start | bytes 786440 | tf_op jit(solution)/shard_map/ppermute | solution.py:27
  19.4 26.3 %collective-permute-start.2 = (bf16[1,144,1152]{2,1,0:T(8,128)(2,1)S(1)}, bf16[1,144,1152]{2,1,0:T(8,128)(2,1)S(1)}, u32[]{:S(2)}, u32[]{:S(2)}) collective-permute-start(bf16[1,144,1152]{2,1,0:T(8,128)(2,1)S(1)} %get-tuple-element.20), channel_id=1, source_target_pairs={{0,16},{16,32},{32,48},{48,64},{64,80},{80,96},{96,112},{1,17},{17... | collective-permute-start | bytes 995336 | tf_op jit(solution)/shard_map/ppermute | solution.py:27
  22.5 23.2 %collective-permute-start.3 = (bf16[1,144,1152]{2,1,0:T(8,128)(2,1)S(1)}, bf16[1,144,1152]{2,1,0:T(8,128)(2,1)S(1)}, u32[]{:S(2)}, u32[]{:S(2)}) collective-permute-start(bf16[1,144,1152]{2,1,0:T(8,128)(2,1)S(1)} %get-tuple-element.19), channel_id=1, source_target_pairs={{16,0},{32,16},{48,32},{64,48},{80,64},{96,80},{112,96},{17,1},{33... | collective-permute-start | bytes 995336 | tf_op jit(solution)/shard_map/ppermute | solution.py:27
  47.1 6.2 %copy-start.2 = (bf16[3,3,288,128]{3,2,1,0:T(8,128)(2,1)S(1)}, bf16[3,3,288,128]{3,2,1,0:T(8,128)(2,1)}, u32[]{:S(2)}) copy-start(bf16[3,3,288,128]{3,2,1,0:T(8,128)(2,1)} %param.10) | copy-start | bytes 1990660
  48.0 7.0 %collective-permute-start.4 = (bf16[16,1,64,128]{3,2,1,0:T(8,128)(2,1)}, bf16[16,1,64,128]{3,2,1,0:T(8,128)(2,1)S(1)}, u32[]{:S(2)}, u32[]{:S(2)}) collective-permute-start(bf16[16,1,64,128]{3,2,1,0:T(8,128)(2,1)} %get-tuple-element.18), channel_id=1, source_target_pairs={{0,1},{1,2},{2,3},{3,4},{4,5},{5,6},{6,7},{7,8},{8,9},{9,10},{10,1... | collective-permute-start | bytes 786440 | tf_op jit(solution)/shard_map/ppermute | solution.py:27
  51.4 11.3 %collective-permute-start.5 = (bf16[16,1,64,128]{3,2,1,0:T(8,128)(2,1)S(1)}, bf16[16,1,64,128]{3,2,1,0:T(8,128)(2,1)S(1)}, u32[]{:S(2)}, u32[]{:S(2)}) collective-permute-start(bf16[16,1,64,128]{3,2,1,0:T(8,128)(2,1)S(1)} %get-tuple-element.17), channel_id=1, source_target_pairs={{1,0},{2,1},{3,2},{4,3},{5,4},{6,5},{7,6},{8,7},{9,8},{10,9},{11,1... | collective-permute-start | bytes 786440 | tf_op jit(solution)/shard_map/ppermute | solution.py:27
  53.7 17.2 %copy-start.1 = (bf16[3,128,288]{1,2,0:T(8,128)(2,1)S(1)}, bf16[3,128,288]{1,2,0:T(8,128)(2,1)}, u32[]{:S(2)}) copy-start(bf16[3,128,288]{1,2,0:T(8,128)(2,1)} %param.11) | copy-start | bytes 663556
  63.6 16.5 %collective-permute-start.6 = (bf16[1,256,288]{2,1,0:T(8,128)(2,1)S(1)}, bf16[1,256,288]{2,1,0:T(8,128)(2,1)S(1)}, u32[]{:S(2)}, u32[]{:S(2)}) collective-permute-start(bf16[1,256,288]{2,1,0:T(8,128)(2,1)S(1)} %get-tuple-element.22), channel_id=1, source_target_pairs={{0,16},{16,32},{32,48},{48,64},{64,80},{80,96},{96,112},{1,17},{17... | collective-permute-start | bytes 442376 | tf_op jit(solution)/shard_map/ppermute | solution.py:27
  65.5 14.5 %collective-permute-start.7 = (bf16[1,256,288]{2,1,0:T(8,128)(2,1)S(1)}, bf16[1,256,288]{2,1,0:T(8,128)(2,1)S(1)}, u32[]{:S(2)}, u32[]{:S(2)}) collective-permute-start(bf16[1,256,288]{2,1,0:T(8,128)(2,1)S(1)} %get-tuple-element.21), channel_id=1, source_target_pairs={{16,0},{32,16},{48,32},{64,48},{80,64},{96,80},{112,96},{17,1},{33... | collective-permute-start | bytes 442376 | tf_op jit(solution)/shard_map/ppermute | solution.py:27

commit v12 on v11

--- a/solution.py
+++ b/solution.py
@@ -78,14 +78,11 @@
     return jnp.maximum(m, 0.0).astype(jnp.bfloat16)
 
 
-def _section_down(stacked, refs, t, t3_ref, wd_ref, keep_ref, out_ref, slot):
+def _section_down(stacked, refs, t, t3_ref, wd_ref, keep_ref, out_ref, slot, full_ref):
     above_ref, xp_ref, _ = refs
     rows = xp_ref.shape[1] + 1
     width = xp_ref.shape[-1]
     reduced_rows = (rows - 1) // 2
-    lane = lax.broadcasted_iota(jnp.int32, (width // 2, width), 1)
-    column = lax.broadcasted_iota(jnp.int32, (width // 2, width), 0)
-    pick = (lane == 2 * column).astype(jnp.bfloat16)
     s = jnp.dot(t3_ref[...], stacked, preferred_element_type=jnp.float32)
     sec = []
     for h in range(rows):
@@ -101,16 +98,11 @@
         for b in range(3):
             parts.append(jnp.concatenate([shifted[2 * i + a][b] for i in range(reduced_rows)], axis=1))
     stacked = jnp.concatenate(parts, axis=0)
-    full = jnp.dot(wd_ref[...], stacked, preferred_element_type=jnp.float32)
-    full = jnp.maximum(full, 0.0).astype(jnp.bfloat16)
+    full = lax.dot_general(stacked, wd_ref[...], (((0,), (0,)), ((), ())), preferred_element_type=jnp.float32)
+    full_ref[...] = jnp.maximum(full, 0.0)
     for i in range(reduced_rows):
-        r = lax.dot_general(
-            pick,
-            full[:, i * width : (i + 1) * width],
-            (((1,), (1,)), ((), ())),
-            preferred_element_type=jnp.float32,
-        )
-        out_ref[slot, i] = r.astype(out_ref.dtype)
+        picked = full_ref[pl.ds(i * width, width // 2, stride=2), :]
+        out_ref[slot, i] = picked.astype(out_ref.dtype)
 
 
 def _edges_one_kernel(above_ref, xp_ref, below_ref, w9_ref, edge_ref):
@@ -120,7 +112,9 @@
     edge_ref[1] = _middle_one(refs, frames - 1, w9_ref)
 
 
-def _inner_one_kernel(keep_ref, above_ref, xp_ref, below_ref, w9_ref, t3_ref, wd_ref, out_ref, side_ref, mid_ref):
+def _inner_one_kernel(
+    keep_ref, above_ref, xp_ref, below_ref, w9_ref, t3_ref, wd_ref, out_ref, side_ref, mid_ref, full_ref
+):
     refs = (above_ref, xp_ref, below_ref)
     frames = xp_ref.shape[0]
 
@@ -134,21 +128,21 @@
 
     def section(t, carry):
         stacked = jnp.concatenate([mid_ref[t - 1], mid_ref[t], mid_ref[t + 1]], axis=0)
-        _section_down(stacked, refs, t, t3_ref, wd_ref, keep_ref, out_ref, t - 1)
+        _section_down(stacked, refs, t, t3_ref, wd_ref, keep_ref, out_ref, t - 1, full_ref)
         return carry
 
     lax.fori_loop(1, frames - 1, section, 0)
 
 
 def _outer_one_kernel(
-    keep_ref, above_ref, xp_ref, below_ref, t3_ref, wd_ref, before_ref, after_ref, edge_ref, side_ref, out_ref
+    keep_ref, above_ref, xp_ref, below_ref, t3_ref, wd_ref, before_ref, after_ref, edge_ref, side_ref, out_ref, full_ref
 ):
     refs = (above_ref, xp_ref, below_ref)
     frames = xp_ref.shape[0]
     stacked = jnp.concatenate([before_ref[0], edge_ref[0], side_ref[0]], axis=0)
-    _section_down(stacked, refs, 0, t3_ref, wd_ref, keep_ref, out_ref, 0)
+    _section_down(stacked, refs, 0, t3_ref, wd_ref, keep_ref, out_ref, 0, full_ref)
     stacked = jnp.concatenate([side_ref[1], edge_ref[1], after_ref[0]], axis=0)
-    _section_down(stacked, refs, frames - 1, t3_ref, wd_ref, keep_ref, out_ref, 1)
+    _section_down(stacked, refs, frames - 1, t3_ref, wd_ref, keep_ref, out_ref, 1, full_ref)
 
 
 def block_one(above, rowed, below, keep_first, spatial_kernel, temporal_kernel, down_kernel):
@@ -158,7 +152,7 @@
     outs = down_kernel.shape[2]
     w9 = jnp.transpose(spatial_kernel, (2, 0, 1, 3)).reshape(mids, 9 * channels)
     t3 = jnp.transpose(temporal_kernel, (1, 0, 2)).reshape(channels, 3 * mids)
-    wd = jnp.transpose(down_kernel, (2, 0, 1, 3)).reshape(outs, 9 * channels)
+    wd = jnp.transpose(down_kernel, (0, 1, 3, 2)).reshape(9 * channels, outs)
     vmem = pltpu.MemorySpace.VMEM if hasattr(pltpu, "MemorySpace") else pltpu.VMEM
     smem = pltpu.MemorySpace.SMEM if hasattr(pltpu, "MemorySpace") else pltpu.SMEM
     params = pltpu.CompilerParams(vmem_limit_bytes=48 * 1024 * 1024)
@@ -187,7 +181,7 @@
         ),
         in_specs=[sspec] + [spec] * 6,
         out_specs=(spec, spec),
-        scratch_shapes=[pltpu.VMEM((frames,) + plane, jnp.bfloat16)],
+        scratch_shapes=[pltpu.VMEM((frames,) + plane, jnp.bfloat16), pltpu.VMEM((reduced_rows * width, outs), jnp.float32)],
         compiler_params=params,
         cost_estimate=pl.CostEstimate(
             flops=frames * (spatial_flops + section_flops), bytes_accessed=4 * rowed.size, transcendentals=0
@@ -198,6 +192,7 @@
         out_shape=jax.ShapeDtypeStruct((2,) + out_plane, rowed.dtype),
         in_specs=[sspec] + [spec] * 9,
         out_specs=spec,
+        scratch_shapes=[pltpu.VMEM((reduced_rows * width, outs), jnp.float32)],
         compiler_params=params,
     )(keep_first, above, rowed, below, t3, wd, before, after, edges, side)
     return jnp.concatenate([outer[:1], inner, outer[1:]], axis=0)

time: 81.9 us -> 82.5 us (level)
  local copies, waits for them, and re-layouts: 2.79 us -> 1.66 us
  waiting for transfers between devices: 17 us -> 18.1 us
    ppermute x8, waiting for transfers between devices: 17 us -> 18.1 us  [from_behind(): return lax.ppermute(array, axis, pairs)]
    reshape x1, local copies, waits for them, and re-layouts: 1.12 us -> 0.16 us  [block_one(): w9 = jnp.transpose(spatial_kernel, (2, 0, 1, 3)).reshape(mids, 9 * channels)]
  transfers between devices with their start and end apart: 8 -> 8, of which waited for: 3 -> 3; matrix products, arithmetic and copies ran while one was open for 2% -> 1% of each run, Pallas kernels for 34% -> 35%
where the time goes in v12:
time: 82.5 us; the launch traced here: 82.2 us
  Pallas kernels  34.1 us (41%)
  starting transfers between devices  26.8 us (32%)
  waiting for transfers between devices  18.1 us (22%)
  local copies, waits for them, and re-layouts  1.66 us (2%)
  other arithmetic  1.24 us (2%)
    ppermute x8, starting transfers between devices, from_behind(): return lax.ppermute(array, axis, pairs)  26.8 us
    pallas_call x1, Pallas kernels, block_one(): pl.pallas_call(_inner_one_kernel, out_shape=(jax.ShapeDtypeStruct((frames...  19.4 us
    ppermute x8, waiting for transfers between devices, from_behind(): return lax.ppermute(array, axis, pairs)  18.1 us
    pallas_call x1, Pallas kernels, block_two(): pl.pallas_call(_inner_two_kernel, out_shape=(jax.ShapeDtypeStruct((frames...  9.02 us
    pallas_call x1, Pallas kernels, edge_rows(): pl.pallas_call(_copy_kernel, grid=(1,), out_shape=(jax.ShapeDtypeStruct((...  2.17 us
  transfers between devices with their start and end apart: 8, of which 3 were waited for; matrix products, arithmetic and copies ran while one was open for 1% of the time, Pallas kernels for 35%

profile of v12, /device:TPU:57, one launch (start us, length us, event | category | flops | bytes accessed | tf_op | source)
XLA Modules:
  0.0 82.2 jit_solution(7208356590529052586)
XLA Ops:
  0.0 0.0 copy-start
  0.0 0.0 copy-start.5
  0.0 0.0 copy-start.4
  0.0 2.2 %shard_map.64 = (bf16[16,2,64,128]{3,2,1,0:T(8,128)(2,1)}, bf16[16,1,64,128]{3,2,1,0:T(8,128)(2,1)}) custom-call(bf16[16,8,64,128]{3,2,1,0:T(8,128)(2,1)} %xp_ref.5, bf16[16,8,64,128]{3,2,1,0:T(8,128)(2,1)} %xp_ref.5), custom_call_target="tpu_custom_call" | custom-call | tf_op jit(solution)/shard_map/pallas_call | solution.py:341
  2.2 4.8 %collective-permute-start = (bf16[16,2,64,128]{3,2,1,0:T(8,128)(2,1)}, bf16[16,2,64,128]{3,2,1,0:T(8,128)(2,1)S(1)}, u32[]{:S(2)}, u32[]{:S(2)}) collective-permute-start(bf16[16,2,64,128]{3,2,1,0:T(8,128)(2,1)} %get-tuple-element.11), channel_id=1, source_target_pairs={{0,1},{1,2},{2,3},{3,4},{4,5},{5,6},{6,7},{7,8},{8,9},{9,10},{10,1... | collective-permute-start | bytes 1572872 | tf_op jit(solution)/shard_map/ppermute | solution.py:27
  7.0 1.9 %collective-permute-start.1 = (bf16[16,1,64,128]{3,2,1,0:T(8,128)(2,1)}, bf16[16,1,64,128]{3,2,1,0:T(8,128)(2,1)S(1)}, u32[]{:S(2)}, u32[]{:S(2)}) collective-permute-start(bf16[16,1,64,128]{3,2,1,0:T(8,128)(2,1)} %get-tuple-element.12), channel_id=1, source_target_pairs={{1,0},{2,1},{3,2},{4,3},{5,4},{6,5},{7,6},{8,7},{9,8},{10,9},{11,1... | collective-permute-start | bytes 786440 | tf_op jit(solution)/shard_map/ppermute | solution.py:27
  8.9 0.0 copy-done.5
  8.9 0.1 copy.10
  9.0 0.1 reshape.19.t3_ref
  9.2 0.0 copy-done.4
  9.2 0.2 copy.11.w9_ref
  9.3 0.0 copy-start.2
  9.4 9.2 %collective-permute-done.1.below_ref = bf16[16,1,64,128]{3,2,1,0:T(8,128)(2,1)S(1)} collective-permute-done((bf16[16,1,64,128]{3,2,1,0:T(8,128)(2,1)}, bf16[16,1,64,128]{3,2,1,0:T(8,128)(2,1)S(1)}, u32[]{:S(2)}, u32[]{:S(2)}) %collective-permute-start.1) | collective-permute-done | bytes 262176 | tf_op jit(solution)/shard_map/ppermute | solution.py:27
  18.5 0.0 collective-permute-done.above_ref
  18.5 0.0 copy-done
  18.5 0.8 %shard_map.65.edge_ref = bf16[2,144,1152]{2,1,0:T(8,128)(2,1)S(1)} custom-call(bf16[16,2,64,128]{3,2,1,0:T(8,128)(2,1)S(1)} %collective-permute-done.above_ref, bf16[16,8,64,128]{3,2,1,0:T(8,128)(2,1)S(1)} %copy-done, bf16[16,1,64,128]{3,2,1,0:T(8,128)(2,1)S(1)} %collective-permute-done.1.below_ref, bf16[144,576]{1,0:T(8,128)(2,1)S(1)} %copy.11.w9_ref), custom_call_target="tpu_custom_call" | custom-call | flops 382205952 | bytes 2097152 | tf_op jit(solution)/shard_map/pallas_call | solution.py:166
  19.4 0.1 fusion.1
  19.4 3.1 %collective-permute-start.2 = (bf16[1,144,1152]{2,1,0:T(8,128)(2,1)S(1)}, bf16[1,144,1152]{2,1,0:T(8,128)(2,1)S(1)}, u32[]{:S(2)}, u32[]{:S(2)}) collective-permute-start(bf16[1,144,1152]{2,1,0:T(8,128)(2,1)S(1)} %get-tuple-element.20), channel_id=1, source_target_pairs={{0,16},{16,32},{32,48},{48,64},{64,80},{80,96},{96,112},{1,17},{17... | collective-permute-start | bytes 995336 | tf_op jit(solution)/shard_map/ppermute | solution.py:27
  22.5 4.3 %collective-permute-start.3 = (bf16[1,144,1152]{2,1,0:T(8,128)(2,1)S(1)}, bf16[1,144,1152]{2,1,0:T(8,128)(2,1)S(1)}, u32[]{:S(2)}, u32[]{:S(2)}) collective-permute-start(bf16[1,144,1152]{2,1,0:T(8,128)(2,1)S(1)} %get-tuple-element.19), channel_id=1, source_target_pairs={{16,0},{32,16},{48,32},{64,48},{80,64},{96,80},{112,96},{17,1},{33... | collective-permute-start | bytes 995336 | tf_op jit(solution)/shard_map/ppermute | solution.py:27
  26.8 0.0 copy-done.2
  26.8 19.4 %shard_map.66 = (bf16[14,4,64,128]{3,2,1,0:T(8,128)(2,1)S(1)}, bf16[2,144,1152]{2,1,0:T(8,128)(2,1)S(1)}) custom-call(s32[1]{0:T(128)} %bitcast.keep_ref, bf16[16,2,64,128]{3,2,1,0:T(8,128)(2,1)S(1)} %collective-permute-done.above_ref, bf16[16,8,64,128]{3,2,1,0:T(8,128)(2,1)S(1)} %copy-done, bf16[16,1,64,128]{3,2,1,0:T(8,128)(2,1)S(1)} %collective-permute-done.1.below_ref, ...), custom_call_target="tpu_custom_call" | custom-call | flops 5284823040 | bytes 4194304 | tf_op jit(solution)/shard_map/pallas_call | solution.py:176
  46.2 0.0 collective-permute-done.2.before_ref
  46.2 0.0 collective-permute-done.3.after_ref
  46.2 1.5 %shard_map.67 = bf16[2,4,64,128]{3,2,1,0:T(8,128)(2,1)S(1)} custom-call(s32[1]{0:T(128)} %bitcast.keep_ref, bf16[16,2,64,128]{3,2,1,0:T(8,128)(2,1)S(1)} %collective-permute-done.above_ref, bf16[16,8,64,128]{3,2,1,0:T(8,128)(2,1)S(1)} %copy-done, bf16[16,1,64,128]{3,2,1,0:T(8,128)(2,1)S(1)} %collective-permute-done.1.below_ref, ...), custom_call_target="tpu_custom_call" | custom-call | tf_op jit(solution)/shard_map/pallas_call | solution.py:190
  47.7 0.0 copy-start.3
  47.7 0.1 pad_maximum_fusion.xp_ref
  47.9 0.7 fusion
  48.6 3.3 %collective-permute-start.4 = (bf16[16,1,64,128]{3,2,1,0:T(8,128)(2,1)}, bf16[16,1,64,128]{3,2,1,0:T(8,128)(2,1)S(1)}, u32[]{:S(2)}, u32[]{:S(2)}) collective-permute-start(bf16[16,1,64,128]{3,2,1,0:T(8,128)(2,1)} %get-tuple-element.18), channel_id=1, source_target_pairs={{0,1},{1,2},{2,3},{3,4},{4,5},{5,6},{6,7},{7,8},{8,9},{9,10},{10,1... | collective-permute-start | bytes 786440 | tf_op jit(solution)/shard_map/ppermute | solution.py:27
  52.0 1.9 %collective-permute-start.5 = (bf16[16,1,64,128]{3,2,1,0:T(8,128)(2,1)S(1)}, bf16[16,1,64,128]{3,2,1,0:T(8,128)(2,1)S(1)}, u32[]{:S(2)}, u32[]{:S(2)}) collective-permute-start(bf16[16,1,64,128]{3,2,1,0:T(8,128)(2,1)S(1)} %get-tuple-element.17), channel_id=1, source_target_pairs={{1,0},{2,1},{3,2},{4,3},{5,4},{6,5},{7,6},{8,7},{9,8},{10,9},{11,1... | collective-permute-start | bytes 786440 | tf_op jit(solution)/shard_map/ppermute | solution.py:27
  53.9 0.0 copy-done.3
  53.9 0.4 copy.13
  54.3 0.0 copy-start.1
  54.3 1.3 %collective-permute-done.4.above_ref = bf16[16,1,64,128]{3,2,1,0:T(8,128)(2,1)S(1)} collective-permute-done((bf16[16,1,64,128]{3,2,1,0:T(8,128)(2,1)}, bf16[16,1,64,128]{3,2,1,0:T(8,128)(2,1)S(1)}, u32[]{:S(2)}, u32[]{:S(2)}) %collective-permute-start.4) | collective-permute-done | bytes 262176 | tf_op jit(solution)/shard_map/ppermute | solution.py:27
  55.6 7.7 %collective-permute-done.5.below_ref = bf16[16,1,64,128]{3,2,1,0:T(8,128)(2,1)S(1)} collective-permute-done((bf16[16,1,64,128]{3,2,1,0:T(8,128)(2,1)S(1)}, bf16[16,1,64,128]{3,2,1,0:T(8,128)(2,1)S(1)}, u32[]{:S(2)}, u32[]{:S(2)}) %collective-permute-start.5) | collective-permute-done | bytes 262176 | tf_op jit(solution)/shard_map/ppermute | solution.py:27
  63.3 0.8 shard_map.68.edge_ref
  64.1 1.9 %collective-permute-start.6 = (bf16[1,256,288]{2,1,0:T(8,128)(2,1)S(1)}, bf16[1,256,288]{2,1,0:T(8,128)(2,1)S(1)}, u32[]{:S(2)}, u32[]{:S(2)}) collective-permute-start(bf16[1,256,288]{2,1,0:T(8,128)(2,1)S(1)} %get-tuple-element.22), channel_id=1, source_target_pairs={{0,16},{16,32},{32,48},{48,64},{64,80},{80,96},{96,112},{1,17},{17... | collective-permute-start | bytes 442376 | tf_op jit(solution)/shard_map/ppermute | solution.py:27
  66.1 5.5 %collective-permute-start.7 = (bf16[1,256,288]{2,1,0:T(8,128)(2,1)S(1)}, bf16[1,256,288]{2,1,0:T(8,128)(2,1)S(1)}, u32[]{:S(2)}, u32[]{:S(2)}) collective-permute-start(bf16[1,256,288]{2,1,0:T(8,128)(2,1)S(1)} %get-tuple-element.21), channel_id=1, source_target_pairs={{16,0},{32,16},{48,32},{64,48},{80,64},{96,80},{112,96},{17,1},{33... | collective-permute-start | bytes 442376 | tf_op jit(solution)/shard_map/ppermute | solution.py:27
  71.5 0.0 copy-done.1
  71.6 9.0 %shard_map.69 = (bf16[14,4,64,128]{3,2,1,0:T(8,128)(2,1)S(1)}, bf16[2,256,288]{2,1,0:T(8,128)(2,1)S(1)}) custom-call(bf16[16,1,64,128]{3,2,1,0:T(8,128)(2,1)S(1)} %collective-permute-done.4.above_ref, bf16[16,4,64,128]{3,2,1,0:T(8,128)(2,1)S(1)} %pad_maximum_fusion.xp_ref, bf16[16,1,64,128]{3,2,1,0:T(8,128)(2,1)S(1)} %collective-permute-done.5.below_ref, ...), custom_call_target="tpu_custom_call" | custom-call | flops 3623878656 | bytes 2097152 | tf_op jit(solution)/shard_map/pallas_call | solution.py:306
  80.6 0.0 collective-permute-done.6.before_ref
  80.6 0.0 collective-permute-done.7.after_ref
  80.6 0.5 shard_map.70
  81.1 1.1 %pad_maximum_fusion.1 = bf16[16,4,64,128]{3,2,1,0:T(8,128)(2,1)} fusion(bf16[1,4,64,128]{3,2,1,0:T(8,128)(2,1)S(1)} %get-tuple-element.24, bf16[14,4,64,128]{3,2,1,0:T(8,128)(2,1)S(1)} %get-tuple-element.16, bf16[1,4,64,128]{3,2,1,0:T(8,128)(2,1)S(1)} %get-tuple-element.23), kind=kLoop, calls=%fused_computation.1 | loop fusion | flops 1048576 | bytes 2097152 | tf_op jit(solution)/shard_map/concatenate | solution.py:329
  (3 shorter events, 0.1 us)
Async XLA Ops:
  0.0 18.5 %copy-start = (bf16[16,8,64,128]{3,2,1,0:T(8,128)(2,1)S(1)}, bf16[16,8,64,128]{3,2,1,0:T(8,128)(2,1)}, u32[]{:S(2)}) copy-start(bf16[16,8,64,128]{3,2,1,0:T(8,128)(2,1)} %xp_ref.5) | copy-start | bytes 6291460
  0.0 8.9 %copy-start.5 = (bf16[3,64,144]{2,1,0:T(8,128)(2,1)S(1)}, bf16[3,64,144]{2,1,0:T(8,128)(2,1)}, u32[]{:S(2)}) copy-start(bf16[3,64,144]{2,1,0:T(8,128)(2,1)} %param.8) | copy-start | bytes 165892
  0.0 9.2 %copy-start.4 = (bf16[3,3,144,64]{2,3,1,0:T(8,128)(2,1)S(1)}, bf16[3,3,144,64]{2,3,1,0:T(8,128)(2,1)}, u32[]{:S(2)}) copy-start(bf16[3,3,144,64]{2,3,1,0:T(8,128)(2,1)} %param.7) | copy-start | bytes 497668
  2.2 16.3 %collective-permute-start = (bf16[16,2,64,128]{3,2,1,0:T(8,128)(2,1)}, bf16[16,2,64,128]{3,2,1,0:T(8,128)(2,1)S(1)}, u32[]{:S(2)}, u32[]{:S(2)}) collective-permute-start(bf16[16,2,64,128]{3,2,1,0:T(8,128)(2,1)} %get-tuple-element.11), channel_id=1, source_target_pairs={{0,1},{1,2},{2,3},{3,4},{4,5},{5,6},{6,7},{7,8},{8,9},{9,10},{10,1... | collective-permute-start | bytes 1572872 | tf_op jit(solution)/shard_map/ppermute | solution.py:27
  7.0 11.5 %collective-permute-start.1 = (bf16[16,1,64,128]{3,2,1,0:T(8,128)(2,1)}, bf16[16,1,64,128]{3,2,1,0:T(8,128)(2,1)S(1)}, u32[]{:S(2)}, u32[]{:S(2)}) collective-permute-start(bf16[16,1,64,128]{3,2,1,0:T(8,128)(2,1)} %get-tuple-element.12), channel_id=1, source_target_pairs={{1,0},{2,1},{3,2},{4,3},{5,4},{6,5},{7,6},{8,7},{9,8},{10,9},{11,1... | collective-permute-start | bytes 786440 | tf_op jit(solution)/shard_map/ppermute | solution.py:27
  9.3 17.5 %copy-start.2 = (bf16[3,3,128,64]{2,3,1,0:T(8,128)(2,1)S(1)}, bf16[3,3,128,64]{2,3,1,0:T(8,128)(2,1)}, u32[]{:S(2)}) copy-start(bf16[3,3,128,64]{2,3,1,0:T(8,128)(2,1)} %param.9) | copy-start | bytes 442372
  19.4 26.8 %collective-permute-start.2 = (bf16[1,144,1152]{2,1,0:T(8,128)(2,1)S(1)}, bf16[1,144,1152]{2,1,0:T(8,128)(2,1)S(1)}, u32[]{:S(2)}, u32[]{:S(2)}) collective-permute-start(bf16[1,144,1152]{2,1,0:T(8,128)(2,1)S(1)} %get-tuple-element.20), channel_id=1, source_target_pairs={{0,16},{16,32},{32,48},{48,64},{64,80},{80,96},{96,112},{1,17},{17... | collective-permute-start | bytes 995336 | tf_op jit(solution)/shard_map/ppermute | solution.py:27
  22.5 23.7 %collective-permute-start.3 = (bf16[1,144,1152]{2,1,0:T(8,128)(2,1)S(1)}, bf16[1,144,1152]{2,1,0:T(8,128)(2,1)S(1)}, u32[]{:S(2)}, u32[]{:S(2)}) collective-permute-start(bf16[1,144,1152]{2,1,0:T(8,128)(2,1)S(1)} %get-tuple-element.19), channel_id=1, source_target_pairs={{16,0},{32,16},{48,32},{64,48},{80,64},{96,80},{112,96},{17,1},{33... | collective-permute-start | bytes 995336 | tf_op jit(solution)/shard_map/ppermute | solution.py:27
  47.7 6.2 %copy-start.3 = (bf16[3,3,288,128]{3,2,1,0:T(8,128)(2,1)S(1)}, bf16[3,3,288,128]{3,2,1,0:T(8,128)(2,1)}, u32[]{:S(2)}) copy-start(bf16[3,3,288,128]{3,2,1,0:T(8,128)(2,1)} %param.10) | copy-start | bytes 1990660
  48.6 7.0 %collective-permute-start.4 = (bf16[16,1,64,128]{3,2,1,0:T(8,128)(2,1)}, bf16[16,1,64,128]{3,2,1,0:T(8,128)(2,1)S(1)}, u32[]{:S(2)}, u32[]{:S(2)}) collective-permute-start(bf16[16,1,64,128]{3,2,1,0:T(8,128)(2,1)} %get-tuple-element.18), channel_id=1, source_target_pairs={{0,1},{1,2},{2,3},{3,4},{4,5},{5,6},{6,7},{7,8},{8,9},{9,10},{10,1... | collective-permute-start | bytes 786440 | tf_op jit(solution)/shard_map/ppermute | solution.py:27
  52.0 11.3 %collective-permute-start.5 = (bf16[16,1,64,128]{3,2,1,0:T(8,128)(2,1)S(1)}, bf16[16,1,64,128]{3,2,1,0:T(8,128)(2,1)S(1)}, u32[]{:S(2)}, u32[]{:S(2)}) collective-permute-start(bf16[16,1,64,128]{3,2,1,0:T(8,128)(2,1)S(1)} %get-tuple-element.17), channel_id=1, source_target_pairs={{1,0},{2,1},{3,2},{4,3},{5,4},{6,5},{7,6},{8,7},{9,8},{10,9},{11,1... | collective-permute-start | bytes 786440 | tf_op jit(solution)/shard_map/ppermute | solution.py:27
  54.3 17.2 %copy-start.1 = (bf16[3,128,288]{1,2,0:T(8,128)(2,1)S(1)}, bf16[3,128,288]{1,2,0:T(8,128)(2,1)}, u32[]{:S(2)}) copy-start(bf16[3,128,288]{1,2,0:T(8,128)(2,1)} %param.11) | copy-start | bytes 663556
  64.1 16.4 %collective-permute-start.6 = (bf16[1,256,288]{2,1,0:T(8,128)(2,1)S(1)}, bf16[1,256,288]{2,1,0:T(8,128)(2,1)S(1)}, u32[]{:S(2)}, u32[]{:S(2)}) collective-permute-start(bf16[1,256,288]{2,1,0:T(8,128)(2,1)S(1)} %get-tuple-element.22), channel_id=1, source_target_pairs={{0,16},{16,32},{32,48},{48,64},{64,80},{80,96},{96,112},{1,17},{17... | collective-permute-start | bytes 442376 | tf_op jit(solution)/shard_map/ppermute | solution.py:27
  66.1 14.5 %collective-permute-start.7 = (bf16[1,256,288]{2,1,0:T(8,128)(2,1)S(1)}, bf16[1,256,288]{2,1,0:T(8,128)(2,1)S(1)}, u32[]{:S(2)}, u32[]{:S(2)}) collective-permute-start(bf16[1,256,288]{2,1,0:T(8,128)(2,1)S(1)} %get-tuple-element.21), channel_id=1, source_target_pairs={{16,0},{32,16},{48,32},{64,48},{80,64},{96,80},{112,96},{17,1},{33... | collective-permute-start | bytes 442376 | tf_op jit(solution)/shard_map/ppermute | solution.py:27

commit v13 on v11

--- a/solution.py
+++ b/solution.py
@@ -79,6 +79,11 @@
 
 
 def _section_down(stacked, refs, t, t3_ref, wd_ref, keep_ref, out_ref, slot):
+    s = jnp.dot(t3_ref[...], stacked, preferred_element_type=jnp.float32)
+    _down(s, refs, t, wd_ref, keep_ref, out_ref, slot)
+
+
+def _down(s, refs, t, wd_ref, keep_ref, out_ref, slot):
     above_ref, xp_ref, _ = refs
     rows = xp_ref.shape[1] + 1
     width = xp_ref.shape[-1]
@@ -86,7 +91,6 @@
     lane = lax.broadcasted_iota(jnp.int32, (width // 2, width), 1)
     column = lax.broadcasted_iota(jnp.int32, (width // 2, width), 0)
     pick = (lane == 2 * column).astype(jnp.bfloat16)
-    s = jnp.dot(t3_ref[...], stacked, preferred_element_type=jnp.float32)
     sec = []
     for h in range(rows):
         own = above_ref[t, 1] if h == 0 else xp_ref[t, h - 1]
@@ -132,12 +136,17 @@
     side_ref[0] = mid_ref[1]
     side_ref[1] = mid_ref[frames - 2]
 
-    def section(t, carry):
-        stacked = jnp.concatenate([mid_ref[t - 1], mid_ref[t], mid_ref[t + 1]], axis=0)
-        _section_down(stacked, refs, t, t3_ref, wd_ref, keep_ref, out_ref, t - 1)
+    channels = t3_ref.shape[0] // 2
+
+    def section(g, carry):
+        t = 2 * g + 1
+        stacked = jnp.concatenate([mid_ref[t - 1], mid_ref[t], mid_ref[t + 1], mid_ref[t + 2]], axis=0)
+        s = jnp.dot(t3_ref[...], stacked, preferred_element_type=jnp.float32)
+        _down(s[:channels], refs, t, wd_ref, keep_ref, out_ref, t - 1)
+        _down(s[channels:], refs, t + 1, wd_ref, keep_ref, out_ref, t)
         return carry
 
-    lax.fori_loop(1, frames - 1, section, 0)
+    lax.fori_loop(0, (frames - 2) // 2, section, 0)
 
 
 def _outer_one_kernel(
@@ -159,6 +168,10 @@
     w9 = jnp.transpose(spatial_kernel, (2, 0, 1, 3)).reshape(mids, 9 * channels)
     t3 = jnp.transpose(temporal_kernel, (1, 0, 2)).reshape(channels, 3 * mids)
     wd = jnp.transpose(down_kernel, (2, 0, 1, 3)).reshape(outs, 9 * channels)
+    gap = jnp.zeros((channels, mids), t3.dtype)
+    t4 = jnp.concatenate(
+        [jnp.concatenate([t3, gap], axis=1), jnp.concatenate([gap, t3], axis=1)], axis=0
+    )
     vmem = pltpu.MemorySpace.VMEM if hasattr(pltpu, "MemorySpace") else pltpu.VMEM
     smem = pltpu.MemorySpace.SMEM if hasattr(pltpu, "MemorySpace") else pltpu.SMEM
     params = pltpu.CompilerParams(vmem_limit_bytes=48 * 1024 * 1024)
@@ -192,7 +205,7 @@
         cost_estimate=pl.CostEstimate(
             flops=frames * (spatial_flops + section_flops), bytes_accessed=4 * rowed.size, transcendentals=0
         ),
-    )(keep_first, above, rowed, below, w9, t3, wd)
+    )(keep_first, above, rowed, below, w9, t4, wd)
     outer = pl.pallas_call(
         _outer_one_kernel,
         out_shape=jax.ShapeDtypeStruct((2,) + out_plane, rowed.dtype),

time: 81.9 us -> 79.5 us (0.971)
  Pallas kernels: 33.5 us -> 31.1 us
    pallas_call x1, Pallas kernels: 18.9 us -> 16.4 us  [block_one(): pl.pallas_call(_inner_one_kernel, out_shape=(jax.ShapeDtypeStruct((frames...]
  transfers between devices with their start and end apart: 8 -> 8, of which waited for: 3 -> 3; matrix products, arithmetic and copies ran while one was open for 2% -> 3% of each run, Pallas kernels for 34% -> 32%
where the time goes in v13:
time: 79.5 us; the launch traced here: 79.2 us
  Pallas kernels  31.1 us (39%)
  starting transfers between devices  26.8 us (34%)
  waiting for transfers between devices  16.9 us (21%)
  local copies, waits for them, and re-layouts  2.79 us (4%)
  other arithmetic  1.33 us (2%)
    ppermute x8, starting transfers between devices, from_behind(): return lax.ppermute(array, axis, pairs)  26.8 us
    ppermute x8, waiting for transfers between devices, from_behind(): return lax.ppermute(array, axis, pairs)  16.9 us
    pallas_call x1, Pallas kernels, block_one(): pl.pallas_call(_inner_one_kernel, out_shape=(jax.ShapeDtypeStruct((frames...  16.4 us
    pallas_call x1, Pallas kernels, block_two(): pl.pallas_call(_inner_two_kernel, out_shape=(jax.ShapeDtypeStruct((frames...  9.01 us
    pallas_call x1, Pallas kernels, edge_rows(): pl.pallas_call(_copy_kernel, grid=(1,), out_shape=(jax.ShapeDtypeStruct((...  2.17 us
  transfers between devices with their start and end apart: 8, of which 3 were waited for; matrix products, arithmetic and copies ran while one was open for 3% of the time, Pallas kernels for 32%

profile of v13, /device:TPU:57, one launch (start us, length us, event | category | flops | bytes accessed | tf_op | source)
XLA Modules:
  0.0 79.2 jit_solution(12076582192566210163)
XLA Ops:
  0.0 0.0 copy-start
  0.0 0.0 copy-start.4
  0.0 0.0 copy-start.3
  0.0 2.2 %shard_map.64 = (bf16[16,2,64,128]{3,2,1,0:T(8,128)(2,1)}, bf16[16,1,64,128]{3,2,1,0:T(8,128)(2,1)}) custom-call(bf16[16,8,64,128]{3,2,1,0:T(8,128)(2,1)} %xp_ref.5, bf16[16,8,64,128]{3,2,1,0:T(8,128)(2,1)} %xp_ref.5), custom_call_target="tpu_custom_call" | custom-call | tf_op jit(solution)/shard_map/pallas_call | solution.py:359
  2.2 4.8 %collective-permute-start = (bf16[16,2,64,128]{3,2,1,0:T(8,128)(2,1)}, bf16[16,2,64,128]{3,2,1,0:T(8,128)(2,1)S(1)}, u32[]{:S(2)}, u32[]{:S(2)}) collective-permute-start(bf16[16,2,64,128]{3,2,1,0:T(8,128)(2,1)} %get-tuple-element.11), channel_id=1, source_target_pairs={{0,1},{1,2},{2,3},{3,4},{4,5},{5,6},{6,7},{7,8},{8,9},{9,10},{10,1... | collective-permute-start | bytes 1572872 | tf_op jit(solution)/shard_map/ppermute | solution.py:27
  7.0 1.9 %collective-permute-start.1 = (bf16[16,1,64,128]{3,2,1,0:T(8,128)(2,1)}, bf16[16,1,64,128]{3,2,1,0:T(8,128)(2,1)S(1)}, u32[]{:S(2)}, u32[]{:S(2)}) collective-permute-start(bf16[16,1,64,128]{3,2,1,0:T(8,128)(2,1)} %get-tuple-element.12), channel_id=1, source_target_pairs={{1,0},{2,1},{3,2},{4,3},{5,4},{6,5},{7,6},{8,7},{9,8},{10,9},{11,1... | collective-permute-start | bytes 786440 | tf_op jit(solution)/shard_map/ppermute | solution.py:27
  8.9 0.0 copy-done.4
  8.9 0.1 copy.11
  9.0 0.1 reshape.19.t3_ref
  9.2 1.1 %copy.12.w9_ref = bf16[144,576]{1,0:T(8,128)(2,1)S(1)} copy(bf16[144,576]{0,1:T(8,128)(2,1)} %bitcast.16) | data formatting | bytes 331776 | tf_op jit(solution)/shard_map/reshape | solution.py:168
  10.3 0.0 copy-done.3
  10.3 0.2 copy.15.wd_ref
  10.5 0.1 fusion.2.t3_ref
  10.6 8.0 %collective-permute-done.1.below_ref = bf16[16,1,64,128]{3,2,1,0:T(8,128)(2,1)S(1)} collective-permute-done((bf16[16,1,64,128]{3,2,1,0:T(8,128)(2,1)}, bf16[16,1,64,128]{3,2,1,0:T(8,128)(2,1)S(1)}, u32[]{:S(2)}, u32[]{:S(2)}) %collective-permute-start.1) | collective-permute-done | bytes 262176 | tf_op jit(solution)/shard_map/ppermute | solution.py:27
  18.5 0.0 collective-permute-done.above_ref
  18.5 0.0 copy-done
  18.5 0.8 %shard_map.65.edge_ref = bf16[2,144,1152]{2,1,0:T(8,128)(2,1)S(1)} custom-call(bf16[16,2,64,128]{3,2,1,0:T(8,128)(2,1)S(1)} %collective-permute-done.above_ref, bf16[16,8,64,128]{3,2,1,0:T(8,128)(2,1)S(1)} %copy-done, bf16[16,1,64,128]{3,2,1,0:T(8,128)(2,1)S(1)} %collective-permute-done.1.below_ref, bf16[144,576]{1,0:T(8,128)(2,1)S(1)} %copy.12.w9_ref), custom_call_target="tpu_custom_call" | custom-call | flops 382205952 | bytes 2097152 | tf_op jit(solution)/shard_map/pallas_call | solution.py:185
  19.4 0.1 fusion.4
  19.4 3.1 %collective-permute-start.2 = (bf16[1,144,1152]{2,1,0:T(8,128)(2,1)S(1)}, bf16[1,144,1152]{2,1,0:T(8,128)(2,1)S(1)}, u32[]{:S(2)}, u32[]{:S(2)}) collective-permute-start(bf16[1,144,1152]{2,1,0:T(8,128)(2,1)S(1)} %get-tuple-element.20), channel_id=1, source_target_pairs={{0,16},{16,32},{32,48},{48,64},{64,80},{80,96},{96,112},{1,17},{17... | collective-permute-start | bytes 995336 | tf_op jit(solution)/shard_map/ppermute | solution.py:27
  22.5 4.3 %collective-permute-start.3 = (bf16[1,144,1152]{2,1,0:T(8,128)(2,1)S(1)}, bf16[1,144,1152]{2,1,0:T(8,128)(2,1)S(1)}, u32[]{:S(2)}, u32[]{:S(2)}) collective-permute-start(bf16[1,144,1152]{2,1,0:T(8,128)(2,1)S(1)} %get-tuple-element.19), channel_id=1, source_target_pairs={{16,0},{32,16},{48,32},{64,48},{80,64},{96,80},{112,96},{17,1},{33... | collective-permute-start | bytes 995336 | tf_op jit(solution)/shard_map/ppermute | solution.py:27
  26.8 16.4 %shard_map.66 = (bf16[14,4,64,128]{3,2,1,0:T(8,128)(2,1)S(1)}, bf16[2,144,1152]{2,1,0:T(8,128)(2,1)S(1)}) custom-call(s32[1]{0:T(128)} %bitcast.keep_ref, bf16[16,2,64,128]{3,2,1,0:T(8,128)(2,1)S(1)} %collective-permute-done.above_ref, bf16[16,8,64,128]{3,2,1,0:T(8,128)(2,1)S(1)} %copy-done, bf16[16,1,64,128]{3,2,1,0:T(8,128)(2,1)S(1)} %collective-permute-done.1.below_ref, ...), custom_call_target="tpu_custom_call" | custom-call | flops 5284823040 | bytes 4194304 | tf_op jit(solution)/shard_map/pallas_call | solution.py:195
  43.2 0.0 collective-permute-done.2.before_ref
  43.3 0.0 collective-permute-done.3.after_ref
  43.3 1.4 %shard_map.67 = bf16[2,4,64,128]{3,2,1,0:T(8,128)(2,1)S(1)} custom-call(s32[1]{0:T(128)} %bitcast.keep_ref, bf16[16,2,64,128]{3,2,1,0:T(8,128)(2,1)S(1)} %collective-permute-done.above_ref, bf16[16,8,64,128]{3,2,1,0:T(8,128)(2,1)S(1)} %copy-done, bf16[16,1,64,128]{3,2,1,0:T(8,128)(2,1)S(1)} %collective-permute-done.1.below_ref, ...), custom_call_target="tpu_custom_call" | custom-call | tf_op jit(solution)/shard_map/pallas_call | solution.py:209
  44.7 0.0 copy-start.2
  44.7 0.1 pad_maximum_fusion.xp_ref
  44.9 0.7 fusion.3
  45.6 3.4 %collective-permute-start.4 = (bf16[16,1,64,128]{3,2,1,0:T(8,128)(2,1)}, bf16[16,1,64,128]{3,2,1,0:T(8,128)(2,1)S(1)}, u32[]{:S(2)}, u32[]{:S(2)}) collective-permute-start(bf16[16,1,64,128]{3,2,1,0:T(8,128)(2,1)} %get-tuple-element.18), channel_id=1, source_target_pairs={{0,1},{1,2},{2,3},{3,4},{4,5},{5,6},{6,7},{7,8},{8,9},{9,10},{10,1... | collective-permute-start | bytes 786440 | tf_op jit(solution)/shard_map/ppermute | solution.py:27
  49.0 1.9 %collective-permute-start.5 = (bf16[16,1,64,128]{3,2,1,0:T(8,128)(2,1)S(1)}, bf16[16,1,64,128]{3,2,1,0:T(8,128)(2,1)S(1)}, u32[]{:S(2)}, u32[]{:S(2)}) collective-permute-start(bf16[16,1,64,128]{3,2,1,0:T(8,128)(2,1)S(1)} %get-tuple-element.17), channel_id=1, source_target_pairs={{1,0},{2,1},{3,2},{4,3},{5,4},{6,5},{7,6},{8,7},{9,8},{10,9},{11,1... | collective-permute-start | bytes 786440 | tf_op jit(solution)/shard_map/ppermute | solution.py:27
  50.9 0.0 copy-done.2
  50.9 0.4 copy.16
  51.3 0.0 copy-start.1
  51.3 1.3 %collective-permute-done.4.above_ref = bf16[16,1,64,128]{3,2,1,0:T(8,128)(2,1)S(1)} collective-permute-done((bf16[16,1,64,128]{3,2,1,0:T(8,128)(2,1)}, bf16[16,1,64,128]{3,2,1,0:T(8,128)(2,1)S(1)}, u32[]{:S(2)}, u32[]{:S(2)}) %collective-permute-start.4) | collective-permute-done | bytes 262176 | tf_op jit(solution)/shard_map/ppermute | solution.py:27
  52.6 7.7 %collective-permute-done.5.below_ref = bf16[16,1,64,128]{3,2,1,0:T(8,128)(2,1)S(1)} collective-permute-done((bf16[16,1,64,128]{3,2,1,0:T(8,128)(2,1)S(1)}, bf16[16,1,64,128]{3,2,1,0:T(8,128)(2,1)S(1)}, u32[]{:S(2)}, u32[]{:S(2)}) %collective-permute-start.5) | collective-permute-done | bytes 262176 | tf_op jit(solution)/shard_map/ppermute | solution.py:27
  60.3 0.8 %shard_map.68.edge_ref = bf16[2,256,288]{2,1,0:T(8,128)(2,1)S(1)} custom-call(bf16[16,1,64,128]{3,2,1,0:T(8,128)(2,1)S(1)} %collective-permute-done.4.above_ref, bf16[16,4,64,128]{3,2,1,0:T(8,128)(2,1)S(1)} %pad_maximum_fusion.xp_ref, bf16[16,1,64,128]{3,2,1,0:T(8,128)(2,1)S(1)} %collective-permute-done.5.below_ref, bf16[1152,288]{1,0:T(8,128)(2,1)S(1)} %bitcast.11), custom_call_target="tpu_custom_call" | custom-call | flops 339738624 | bytes 1048576 | tf_op jit(solution)/shard_map/pallas_call | solution.py:312
  61.1 1.9 %collective-permute-start.6 = (bf16[1,256,288]{2,1,0:T(8,128)(2,1)S(1)}, bf16[1,256,288]{2,1,0:T(8,128)(2,1)S(1)}, u32[]{:S(2)}, u32[]{:S(2)}) collective-permute-start(bf16[1,256,288]{2,1,0:T(8,128)(2,1)S(1)} %get-tuple-element.22), channel_id=1, source_target_pairs={{0,16},{16,32},{32,48},{48,64},{64,80},{80,96},{96,112},{1,17},{17... | collective-permute-start | bytes 442376 | tf_op jit(solution)/shard_map/ppermute | solution.py:27
  63.1 5.5 %collective-permute-start.7 = (bf16[1,256,288]{2,1,0:T(8,128)(2,1)S(1)}, bf16[1,256,288]{2,1,0:T(8,128)(2,1)S(1)}, u32[]{:S(2)}, u32[]{:S(2)}) collective-permute-start(bf16[1,256,288]{2,1,0:T(8,128)(2,1)S(1)} %get-tuple-element.21), channel_id=1, source_target_pairs={{16,0},{32,16},{48,32},{64,48},{80,64},{96,80},{112,96},{17,1},{33... | collective-permute-start | bytes 442376 | tf_op jit(solution)/shard_map/ppermute | solution.py:27
  68.5 0.0 copy-done.1
  68.5 9.0 %shard_map.69 = (bf16[14,4,64,128]{3,2,1,0:T(8,128)(2,1)S(1)}, bf16[2,256,288]{2,1,0:T(8,128)(2,1)S(1)}) custom-call(bf16[16,1,64,128]{3,2,1,0:T(8,128)(2,1)S(1)} %collective-permute-done.4.above_ref, bf16[16,4,64,128]{3,2,1,0:T(8,128)(2,1)S(1)} %pad_maximum_fusion.xp_ref, bf16[16,1,64,128]{3,2,1,0:T(8,128)(2,1)S(1)} %collective-permute-done.5.below_ref, ...), custom_call_target="tpu_custom_call" | custom-call | flops 3623878656 | bytes 2097152 | tf_op jit(solution)/shard_map/pallas_call | solution.py:324
  77.6 0.0 collective-permute-done.6.before_ref
  77.6 0.0 collective-permute-done.7.after_ref
  77.6 0.4 shard_map.70
  78.1 1.1 %pad_maximum_fusion.1 = bf16[16,4,64,128]{3,2,1,0:T(8,128)(2,1)} fusion(bf16[1,4,64,128]{3,2,1,0:T(8,128)(2,1)S(1)} %get-tuple-element.24, bf16[14,4,64,128]{3,2,1,0:T(8,128)(2,1)S(1)} %get-tuple-element.16, bf16[1,4,64,128]{3,2,1,0:T(8,128)(2,1)S(1)} %get-tuple-element.23), kind=kLoop, calls=%fused_computation.1 | loop fusion | flops 1048576 | bytes 2097152 | tf_op jit(solution)/shard_map/concatenate | solution.py:347
  (3 shorter events, 0.1 us)
Async XLA Ops:
  0.0 18.5 %copy-start = (bf16[16,8,64,128]{3,2,1,0:T(8,128)(2,1)S(1)}, bf16[16,8,64,128]{3,2,1,0:T(8,128)(2,1)}, u32[]{:S(2)}) copy-start(bf16[16,8,64,128]{3,2,1,0:T(8,128)(2,1)} %xp_ref.5) | copy-start | bytes 6291460
  0.0 8.9 %copy-start.4 = (bf16[3,64,144]{2,1,0:T(8,128)(2,1)S(1)}, bf16[3,64,144]{2,1,0:T(8,128)(2,1)}, u32[]{:S(2)}) copy-start(bf16[3,64,144]{2,1,0:T(8,128)(2,1)} %param.8) | copy-start | bytes 165892
  0.0 10.3 %copy-start.3 = (bf16[3,3,128,64]{2,3,1,0:T(8,128)(2,1)S(1)}, bf16[3,3,128,64]{2,3,1,0:T(8,128)(2,1)}, u32[]{:S(2)}) copy-start(bf16[3,3,128,64]{2,3,1,0:T(8,128)(2,1)} %param.9) | copy-start | bytes 442372
  2.2 16.3 %collective-permute-start = (bf16[16,2,64,128]{3,2,1,0:T(8,128)(2,1)}, bf16[16,2,64,128]{3,2,1,0:T(8,128)(2,1)S(1)}, u32[]{:S(2)}, u32[]{:S(2)}) collective-permute-start(bf16[16,2,64,128]{3,2,1,0:T(8,128)(2,1)} %get-tuple-element.11), channel_id=1, source_target_pairs={{0,1},{1,2},{2,3},{3,4},{4,5},{5,6},{6,7},{7,8},{8,9},{9,10},{10,1... | collective-permute-start | bytes 1572872 | tf_op jit(solution)/shard_map/ppermute | solution.py:27
  7.0 11.5 %collective-permute-start.1 = (bf16[16,1,64,128]{3,2,1,0:T(8,128)(2,1)}, bf16[16,1,64,128]{3,2,1,0:T(8,128)(2,1)S(1)}, u32[]{:S(2)}, u32[]{:S(2)}) collective-permute-start(bf16[16,1,64,128]{3,2,1,0:T(8,128)(2,1)} %get-tuple-element.12), channel_id=1, source_target_pairs={{1,0},{2,1},{3,2},{4,3},{5,4},{6,5},{7,6},{8,7},{9,8},{10,9},{11,1... | collective-permute-start | bytes 786440 | tf_op jit(solution)/shard_map/ppermute | solution.py:27
  19.4 23.8 %collective-permute-start.2 = (bf16[1,144,1152]{2,1,0:T(8,128)(2,1)S(1)}, bf16[1,144,1152]{2,1,0:T(8,128)(2,1)S(1)}, u32[]{:S(2)}, u32[]{:S(2)}) collective-permute-start(bf16[1,144,1152]{2,1,0:T(8,128)(2,1)S(1)} %get-tuple-element.20), channel_id=1, source_target_pairs={{0,16},{16,32},{32,48},{48,64},{64,80},{80,96},{96,112},{1,17},{17... | collective-permute-start | bytes 995336 | tf_op jit(solution)/shard_map/ppermute | solution.py:27
  22.5 20.7 %collective-permute-start.3 = (bf16[1,144,1152]{2,1,0:T(8,128)(2,1)S(1)}, bf16[1,144,1152]{2,1,0:T(8,128)(2,1)S(1)}, u32[]{:S(2)}, u32[]{:S(2)}) collective-permute-start(bf16[1,144,1152]{2,1,0:T(8,128)(2,1)S(1)} %get-tuple-element.19), channel_id=1, source_target_pairs={{16,0},{32,16},{48,32},{64,48},{80,64},{96,80},{112,96},{17,1},{33... | collective-permute-start | bytes 995336 | tf_op jit(solution)/shard_map/ppermute | solution.py:27
  44.7 6.2 %copy-start.2 = (bf16[3,3,288,128]{3,2,1,0:T(8,128)(2,1)S(1)}, bf16[3,3,288,128]{3,2,1,0:T(8,128)(2,1)}, u32[]{:S(2)}) copy-start(bf16[3,3,288,128]{3,2,1,0:T(8,128)(2,1)} %param.10) | copy-start | bytes 1990660
  45.6 7.0 %collective-permute-start.4 = (bf16[16,1,64,128]{3,2,1,0:T(8,128)(2,1)}, bf16[16,1,64,128]{3,2,1,0:T(8,128)(2,1)S(1)}, u32[]{:S(2)}, u32[]{:S(2)}) collective-permute-start(bf16[16,1,64,128]{3,2,1,0:T(8,128)(2,1)} %get-tuple-element.18), channel_id=1, source_target_pairs={{0,1},{1,2},{2,3},{3,4},{4,5},{5,6},{6,7},{7,8},{8,9},{9,10},{10,1... | collective-permute-start | bytes 786440 | tf_op jit(solution)/shard_map/ppermute | solution.py:27
  49.0 11.3 %collective-permute-start.5 = (bf16[16,1,64,128]{3,2,1,0:T(8,128)(2,1)S(1)}, bf16[16,1,64,128]{3,2,1,0:T(8,128)(2,1)S(1)}, u32[]{:S(2)}, u32[]{:S(2)}) collective-permute-start(bf16[16,1,64,128]{3,2,1,0:T(8,128)(2,1)S(1)} %get-tuple-element.17), channel_id=1, source_target_pairs={{1,0},{2,1},{3,2},{4,3},{5,4},{6,5},{7,6},{8,7},{9,8},{10,9},{11,1... | collective-permute-start | bytes 786440 | tf_op jit(solution)/shard_map/ppermute | solution.py:27
  51.3 17.2 %copy-start.1 = (bf16[3,128,288]{1,2,0:T(8,128)(2,1)S(1)}, bf16[3,128,288]{1,2,0:T(8,128)(2,1)}, u32[]{:S(2)}) copy-start(bf16[3,128,288]{1,2,0:T(8,128)(2,1)} %param.11) | copy-start | bytes 663556
  61.1 16.4 %collective-permute-start.6 = (bf16[1,256,288]{2,1,0:T(8,128)(2,1)S(1)}, bf16[1,256,288]{2,1,0:T(8,128)(2,1)S(1)}, u32[]{:S(2)}, u32[]{:S(2)}) collective-permute-start(bf16[1,256,288]{2,1,0:T(8,128)(2,1)S(1)} %get-tuple-element.22), channel_id=1, source_target_pairs={{0,16},{16,32},{32,48},{48,64},{64,80},{80,96},{96,112},{1,17},{17... | collective-permute-start | bytes 442376 | tf_op jit(solution)/shard_map/ppermute | solution.py:27
  63.1 14.5 %collective-permute-start.7 = (bf16[1,256,288]{2,1,0:T(8,128)(2,1)S(1)}, bf16[1,256,288]{2,1,0:T(8,128)(2,1)S(1)}, u32[]{:S(2)}, u32[]{:S(2)}) collective-permute-start(bf16[1,256,288]{2,1,0:T(8,128)(2,1)S(1)} %get-tuple-element.21), channel_id=1, source_target_pairs={{16,0},{32,16},{48,32},{64,48},{80,64},{96,80},{112,96},{17,1},{33... | collective-permute-start | bytes 442376 | tf_op jit(solution)/shard_map/ppermute | solution.py:27

commit v14 on v13

--- a/solution.py
+++ b/solution.py
@@ -67,14 +67,17 @@
 def _middle_one(refs, f, w9_ref):
     above_ref, xp_ref, below_ref = refs
     rows = xp_ref.shape[1] + 1
+    width = xp_ref.shape[-1]
+    mids = w9_ref.shape[0] // 3
     slab = jnp.concatenate([above_ref[f], xp_ref[f], below_ref[f]], axis=0).astype(jnp.float32)
     shifted = [_lane_shift(slab, b - 1).astype(jnp.bfloat16) for b in range(3)]
-    parts = []
-    for a in range(3):
-        for b in range(3):
-            parts.append(jnp.concatenate([shifted[b][h + a] for h in range(rows)], axis=1))
-    stacked = jnp.concatenate(parts, axis=0)
-    m = jnp.dot(w9_ref[...], stacked, preferred_element_type=jnp.float32)
+    stacked = jnp.concatenate(
+        [jnp.concatenate([shifted[b][r] for b in range(3)], axis=0) for r in range(rows + 2)], axis=1
+    )
+    q = jnp.dot(w9_ref[...], stacked, preferred_element_type=jnp.float32)
+    m = q[:mids, : rows * width]
+    for a in range(1, 3):
+        m = m + q[a * mids : (a + 1) * mids, a * width : (a + rows) * width]
     return jnp.maximum(m, 0.0).astype(jnp.bfloat16)
 
 
@@ -165,7 +168,7 @@
     rows = rows + 1
     mids = spatial_kernel.shape[2]
     outs = down_kernel.shape[2]
-    w9 = jnp.transpose(spatial_kernel, (2, 0, 1, 3)).reshape(mids, 9 * channels)
+    w9 = jnp.transpose(spatial_kernel, (0, 2, 1, 3)).reshape(3 * mids, 3 * channels)
     t3 = jnp.transpose(temporal_kernel, (1, 0, 2)).reshape(channels, 3 * mids)
     wd = jnp.transpose(down_kernel, (2, 0, 1, 3)).reshape(outs, 9 * channels)
     gap = jnp.zeros((channels, mids), t3.dtype)

time: 79.5 us -> 80.9 us (1.018)
  local copies, waits for them, and re-layouts: 2.79 us -> 4.98 us
  waiting for transfers between devices: 16.9 us -> 14.8 us
  Pallas kernels: 31.1 us -> 32.3 us
    ppermute x8, waiting for transfers between devices: 16.9 us -> 14.8 us  [from_behind(): return lax.ppermute(array, axis, pairs)]
    pallas_call x1, Pallas kernels: 16.4 us -> 17.6 us  [block_one(): pl.pallas_call(_inner_one_kernel, out_shape=(jax.ShapeDtypeStruct((frames...]
    reshape x1, local copies, waits for them, and re-layouts: 0.16 us -> 1.06 us  [block_one(): wd = jnp.transpose(down_kernel, (2, 0, 1, 3)).reshape(outs, 9 * channels)]
    transpose x1, local copies, waits for them, and re-layouts: 0.09 us -> 0.99 us  [block_one(): t3 = jnp.transpose(temporal_kernel, (1, 0, 2)).reshape(channels, 3 * mids)]
  transfers between devices with their start and end apart: 8 -> 8, of which waited for: 3 -> 3; matrix products, arithmetic and copies ran while one was open for 3% -> 5% of each run, Pallas kernels for 32% -> 33%
where the time goes in v14:
time: 80.9 us; the launch traced here: 80.5 us
  Pallas kernels  32.3 us (40%)
  starting transfers between devices  26.9 us (33%)
  waiting for transfers between devices  14.8 us (18%)
  local copies, waits for them, and re-layouts  4.98 us (6%)
  other arithmetic  1.33 us (2%)
    ppermute x8, starting transfers between devices, from_behind(): return lax.ppermute(array, axis, pairs)  26.9 us
    pallas_call x1, Pallas kernels, block_one(): pl.pallas_call(_inner_one_kernel, out_shape=(jax.ShapeDtypeStruct((frames...  17.6 us
    ppermute x8, waiting for transfers between devices, from_behind(): return lax.ppermute(array, axis, pairs)  14.8 us
    pallas_call x1, Pallas kernels, block_two(): pl.pallas_call(_inner_two_kernel, out_shape=(jax.ShapeDtypeStruct((frames...  9.03 us
    pallas_call x1, Pallas kernels, edge_rows(): pl.pallas_call(_copy_kernel, grid=(1,), out_shape=(jax.ShapeDtypeStruct((...  2.02 us
  transfers between devices with their start and end apart: 8, of which 3 were waited for; matrix products, arithmetic and copies ran while one was open for 5% of the time, Pallas kernels for 33%

profile of v14, /device:TPU:57, one launch (start us, length us, event | category | flops | bytes accessed | tf_op | source)
XLA Modules:
  0.0 80.5 jit_solution(5809595554512603966)
XLA Ops:
  0.0 2.0 %shard_map.64 = (bf16[16,2,64,128]{3,2,1,0:T(8,128)(2,1)}, bf16[16,1,64,128]{3,2,1,0:T(8,128)(2,1)}) custom-call(bf16[16,8,64,128]{3,2,1,0:T(8,128)(2,1)} %xp_ref.5, bf16[16,8,64,128]{3,2,1,0:T(8,128)(2,1)} %xp_ref.5), custom_call_target="tpu_custom_call" | custom-call | tf_op jit(solution)/shard_map/pallas_call | solution.py:362
  2.0 0.0 copy-start
  2.0 4.9 %collective-permute-start = (bf16[16,2,64,128]{3,2,1,0:T(8,128)(2,1)}, bf16[16,2,64,128]{3,2,1,0:T(8,128)(2,1)S(1)}, u32[]{:S(2)}, u32[]{:S(2)}) collective-permute-start(bf16[16,2,64,128]{3,2,1,0:T(8,128)(2,1)} %get-tuple-element.11), channel_id=1, source_target_pairs={{0,1},{1,2},{2,3},{3,4},{4,5},{5,6},{6,7},{7,8},{8,9},{9,10},{10,1... | collective-permute-start | bytes 1572872 | tf_op jit(solution)/shard_map/ppermute | solution.py:27
  7.0 1.9 %collective-permute-start.1 = (bf16[16,1,64,128]{3,2,1,0:T(8,128)(2,1)}, bf16[16,1,64,128]{3,2,1,0:T(8,128)(2,1)S(1)}, u32[]{:S(2)}, u32[]{:S(2)}) collective-permute-start(bf16[16,1,64,128]{3,2,1,0:T(8,128)(2,1)} %get-tuple-element.12), channel_id=1, source_target_pairs={{1,0},{2,1},{3,2},{4,3},{5,4},{6,5},{7,6},{8,7},{9,8},{10,9},{11,1... | collective-permute-start | bytes 786440 | tf_op jit(solution)/shard_map/ppermute | solution.py:27
  8.9 1.2 %copy.18 = bf16[3,144,3,64]{3,2,1,0:T(4,128)(2,1)S(1)} copy(bf16[3,144,3,64]{1,3,2,0:T(8,128)(2,1)} %bitcast.14) | data formatting | bytes 331776 | tf_op jit(solution)/shard_map/reshape | solution.py:171
  10.2 0.3 reshape.25.w9_ref
  10.4 1.0 %copy.11 = bf16[64,3,144]{2,1,0:T(4,128)(2,1)S(1)} copy(bf16[64,3,144]{2,0,1:T(8,128)(2,1)} %bitcast.16) | data formatting | bytes 110592 | tf_op jit(solution)/shard_map/transpose | solution.py:172
  11.4 0.1 reshape.19.t3_ref
  11.6 1.1 %copy.16.wd_ref = bf16[128,576]{1,0:T(8,128)(2,1)S(1)} copy(bf16[128,576]{0,1:T(8,128)(2,1)} %bitcast.15) | data formatting | bytes 294912 | tf_op jit(solution)/shard_map/reshape | solution.py:173
  12.6 0.1 fusion.2.t3_ref
  12.7 5.8 %collective-permute-done.1.below_ref = bf16[16,1,64,128]{3,2,1,0:T(8,128)(2,1)S(1)} collective-permute-done((bf16[16,1,64,128]{3,2,1,0:T(8,128)(2,1)}, bf16[16,1,64,128]{3,2,1,0:T(8,128)(2,1)S(1)}, u32[]{:S(2)}, u32[]{:S(2)}) %collective-permute-start.1) | collective-permute-done | bytes 262176 | tf_op jit(solution)/shard_map/ppermute | solution.py:27
  18.5 0.0 collective-permute-done.above_ref
  18.5 0.0 copy-done
  18.5 0.9 %shard_map.65.edge_ref = bf16[2,144,1152]{2,1,0:T(8,128)(2,1)S(1)} custom-call(bf16[16,2,64,128]{3,2,1,0:T(8,128)(2,1)S(1)} %collective-permute-done.above_ref, bf16[16,8,64,128]{3,2,1,0:T(8,128)(2,1)S(1)} %copy-done, bf16[16,1,64,128]{3,2,1,0:T(8,128)(2,1)S(1)} %collective-permute-done.1.below_ref, bf16[432,192]{1,0:T(8,128)(2,1)S(1)} %reshape.25.w9_ref), custom_call_target="tpu_custom_call" | custom-call | flops 382205952 | bytes 2097152 | tf_op jit(solution)/shard_map/pallas_call | solution.py:188
  19.4 0.1 fusion.4
  19.5 3.1 %collective-permute-start.2 = (bf16[1,144,1152]{2,1,0:T(8,128)(2,1)S(1)}, bf16[1,144,1152]{2,1,0:T(8,128)(2,1)S(1)}, u32[]{:S(2)}, u32[]{:S(2)}) collective-permute-start(bf16[1,144,1152]{2,1,0:T(8,128)(2,1)S(1)} %get-tuple-element.20), channel_id=1, source_target_pairs={{0,16},{16,32},{32,48},{48,64},{64,80},{80,96},{96,112},{1,17},{17... | collective-permute-start | bytes 995336 | tf_op jit(solution)/shard_map/ppermute | solution.py:27
  22.6 4.3 %collective-permute-start.3 = (bf16[1,144,1152]{2,1,0:T(8,128)(2,1)S(1)}, bf16[1,144,1152]{2,1,0:T(8,128)(2,1)S(1)}, u32[]{:S(2)}, u32[]{:S(2)}) collective-permute-start(bf16[1,144,1152]{2,1,0:T(8,128)(2,1)S(1)} %get-tuple-element.19), channel_id=1, source_target_pairs={{16,0},{32,16},{48,32},{64,48},{80,64},{96,80},{112,96},{17,1},{33... | collective-permute-start | bytes 995336 | tf_op jit(solution)/shard_map/ppermute | solution.py:27
  26.9 17.6 %shard_map.66 = (bf16[14,4,64,128]{3,2,1,0:T(8,128)(2,1)S(1)}, bf16[2,144,1152]{2,1,0:T(8,128)(2,1)S(1)}) custom-call(s32[1]{0:T(128)} %bitcast.keep_ref, bf16[16,2,64,128]{3,2,1,0:T(8,128)(2,1)S(1)} %collective-permute-done.above_ref, bf16[16,8,64,128]{3,2,1,0:T(8,128)(2,1)S(1)} %copy-done, bf16[16,1,64,128]{3,2,1,0:T(8,128)(2,1)S(1)} %collective-permute-done.1.below_ref, ...), custom_call_target="tpu_custom_call" | custom-call | flops 5284823040 | bytes 4194304 | tf_op jit(solution)/shard_map/pallas_call | solution.py:198
  44.5 0.0 collective-permute-done.2.before_ref
  44.6 0.0 collective-permute-done.3.after_ref
  44.6 1.4 %shard_map.67 = bf16[2,4,64,128]{3,2,1,0:T(8,128)(2,1)S(1)} custom-call(s32[1]{0:T(128)} %bitcast.keep_ref, bf16[16,2,64,128]{3,2,1,0:T(8,128)(2,1)S(1)} %collective-permute-done.above_ref, bf16[16,8,64,128]{3,2,1,0:T(8,128)(2,1)S(1)} %copy-done, bf16[16,1,64,128]{3,2,1,0:T(8,128)(2,1)S(1)} %collective-permute-done.1.below_ref, ...), custom_call_target="tpu_custom_call" | custom-call | tf_op jit(solution)/shard_map/pallas_call | solution.py:212
  46.0 0.0 copy-start.2
  46.0 0.1 pad_maximum_fusion.xp_ref
  46.2 0.7 fusion.3
  46.9 3.3 %collective-permute-start.4 = (bf16[16,1,64,128]{3,2,1,0:T(8,128)(2,1)}, bf16[16,1,64,128]{3,2,1,0:T(8,128)(2,1)S(1)}, u32[]{:S(2)}, u32[]{:S(2)}) collective-permute-start(bf16[16,1,64,128]{3,2,1,0:T(8,128)(2,1)} %get-tuple-element.18), channel_id=1, source_target_pairs={{0,1},{1,2},{2,3},{3,4},{4,5},{5,6},{6,7},{7,8},{8,9},{9,10},{10,1... | collective-permute-start | bytes 786440 | tf_op jit(solution)/shard_map/ppermute | solution.py:27
  50.2 1.9 %collective-permute-start.5 = (bf16[16,1,64,128]{3,2,1,0:T(8,128)(2,1)S(1)}, bf16[16,1,64,128]{3,2,1,0:T(8,128)(2,1)S(1)}, u32[]{:S(2)}, u32[]{:S(2)}) collective-permute-start(bf16[16,1,64,128]{3,2,1,0:T(8,128)(2,1)S(1)} %get-tuple-element.17), channel_id=1, source_target_pairs={{1,0},{2,1},{3,2},{4,3},{5,4},{6,5},{7,6},{8,7},{9,8},{10,9},{11,1... | collective-permute-start | bytes 786440 | tf_op jit(solution)/shard_map/ppermute | solution.py:27
  52.2 0.0 copy-done.2
  52.2 0.4 copy.17
  52.6 0.0 copy-start.1
  52.6 1.3 %collective-permute-done.4.above_ref = bf16[16,1,64,128]{3,2,1,0:T(8,128)(2,1)S(1)} collective-permute-done((bf16[16,1,64,128]{3,2,1,0:T(8,128)(2,1)}, bf16[16,1,64,128]{3,2,1,0:T(8,128)(2,1)S(1)}, u32[]{:S(2)}, u32[]{:S(2)}) %collective-permute-start.4) | collective-permute-done | bytes 262176 | tf_op jit(solution)/shard_map/ppermute | solution.py:27
  53.9 7.7 %collective-permute-done.5.below_ref = bf16[16,1,64,128]{3,2,1,0:T(8,128)(2,1)S(1)} collective-permute-done((bf16[16,1,64,128]{3,2,1,0:T(8,128)(2,1)S(1)}, bf16[16,1,64,128]{3,2,1,0:T(8,128)(2,1)S(1)}, u32[]{:S(2)}, u32[]{:S(2)}) %collective-permute-start.5) | collective-permute-done | bytes 262176 | tf_op jit(solution)/shard_map/ppermute | solution.py:27
  61.5 0.8 shard_map.68.edge_ref
  62.4 1.9 %collective-permute-start.6 = (bf16[1,256,288]{2,1,0:T(8,128)(2,1)S(1)}, bf16[1,256,288]{2,1,0:T(8,128)(2,1)S(1)}, u32[]{:S(2)}, u32[]{:S(2)}) collective-permute-start(bf16[1,256,288]{2,1,0:T(8,128)(2,1)S(1)} %get-tuple-element.22), channel_id=1, source_target_pairs={{0,16},{16,32},{32,48},{48,64},{64,80},{80,96},{96,112},{1,17},{17... | collective-permute-start | bytes 442376 | tf_op jit(solution)/shard_map/ppermute | solution.py:27
  64.3 5.5 %collective-permute-start.7 = (bf16[1,256,288]{2,1,0:T(8,128)(2,1)S(1)}, bf16[1,256,288]{2,1,0:T(8,128)(2,1)S(1)}, u32[]{:S(2)}, u32[]{:S(2)}) collective-permute-start(bf16[1,256,288]{2,1,0:T(8,128)(2,1)S(1)} %get-tuple-element.21), channel_id=1, source_target_pairs={{16,0},{32,16},{48,32},{64,48},{80,64},{96,80},{112,96},{17,1},{33... | collective-permute-start | bytes 442376 | tf_op jit(solution)/shard_map/ppermute | solution.py:27
  69.8 0.0 copy-done.1
  69.8 9.0 %shard_map.69 = (bf16[14,4,64,128]{3,2,1,0:T(8,128)(2,1)S(1)}, bf16[2,256,288]{2,1,0:T(8,128)(2,1)S(1)}) custom-call(bf16[16,1,64,128]{3,2,1,0:T(8,128)(2,1)S(1)} %collective-permute-done.4.above_ref, bf16[16,4,64,128]{3,2,1,0:T(8,128)(2,1)S(1)} %pad_maximum_fusion.xp_ref, bf16[16,1,64,128]{3,2,1,0:T(8,128)(2,1)S(1)} %collective-permute-done.5.below_ref, ...), custom_call_target="tpu_custom_call" | custom-call | flops 3623878656 | bytes 2097152 | tf_op jit(solution)/shard_map/pallas_call | solution.py:327
  78.9 0.0 collective-permute-done.6.before_ref
  78.9 0.0 collective-permute-done.7.after_ref
  78.9 0.4 shard_map.70
  79.4 1.1 %pad_maximum_fusion.1 = bf16[16,4,64,128]{3,2,1,0:T(8,128)(2,1)} fusion(bf16[1,4,64,128]{3,2,1,0:T(8,128)(2,1)S(1)} %get-tuple-element.24, bf16[14,4,64,128]{3,2,1,0:T(8,128)(2,1)S(1)} %get-tuple-element.16, bf16[1,4,64,128]{3,2,1,0:T(8,128)(2,1)S(1)} %get-tuple-element.23), kind=kLoop, calls=%fused_computation.1 | loop fusion | flops 1048576 | bytes 2097152 | tf_op jit(solution)/shard_map/concatenate | solution.py:350
  (3 shorter events, 0.1 us)
Async XLA Ops:
  2.0 16.5 %copy-start = (bf16[16,8,64,128]{3,2,1,0:T(8,128)(2,1)S(1)}, bf16[16,8,64,128]{3,2,1,0:T(8,128)(2,1)}, u32[]{:S(2)}) copy-start(bf16[16,8,64,128]{3,2,1,0:T(8,128)(2,1)} %xp_ref.5) | copy-start | bytes 6291460
  2.0 16.5 %collective-permute-start = (bf16[16,2,64,128]{3,2,1,0:T(8,128)(2,1)}, bf16[16,2,64,128]{3,2,1,0:T(8,128)(2,1)S(1)}, u32[]{:S(2)}, u32[]{:S(2)}) collective-permute-start(bf16[16,2,64,128]{3,2,1,0:T(8,128)(2,1)} %get-tuple-element.11), channel_id=1, source_target_pairs={{0,1},{1,2},{2,3},{3,4},{4,5},{5,6},{6,7},{7,8},{8,9},{9,10},{10,1... | collective-permute-start | bytes 1572872 | tf_op jit(solution)/shard_map/ppermute | solution.py:27
  7.0 11.5 %collective-permute-start.1 = (bf16[16,1,64,128]{3,2,1,0:T(8,128)(2,1)}, bf16[16,1,64,128]{3,2,1,0:T(8,128)(2,1)S(1)}, u32[]{:S(2)}, u32[]{:S(2)}) collective-permute-start(bf16[16,1,64,128]{3,2,1,0:T(8,128)(2,1)} %get-tuple-element.12), channel_id=1, source_target_pairs={{1,0},{2,1},{3,2},{4,3},{5,4},{6,5},{7,6},{8,7},{9,8},{10,9},{11,1... | collective-permute-start | bytes 786440 | tf_op jit(solution)/shard_map/ppermute | solution.py:27
  19.5 25.1 %collective-permute-start.2 = (bf16[1,144,1152]{2,1,0:T(8,128)(2,1)S(1)}, bf16[1,144,1152]{2,1,0:T(8,128)(2,1)S(1)}, u32[]{:S(2)}, u32[]{:S(2)}) collective-permute-start(bf16[1,144,1152]{2,1,0:T(8,128)(2,1)S(1)} %get-tuple-element.20), channel_id=1, source_target_pairs={{0,16},{16,32},{32,48},{48,64},{64,80},{80,96},{96,112},{1,17},{17... | collective-permute-start | bytes 995336 | tf_op jit(solution)/shard_map/ppermute | solution.py:27
  22.6 22.0 %collective-permute-start.3 = (bf16[1,144,1152]{2,1,0:T(8,128)(2,1)S(1)}, bf16[1,144,1152]{2,1,0:T(8,128)(2,1)S(1)}, u32[]{:S(2)}, u32[]{:S(2)}) collective-permute-start(bf16[1,144,1152]{2,1,0:T(8,128)(2,1)S(1)} %get-tuple-element.19), channel_id=1, source_target_pairs={{16,0},{32,16},{48,32},{64,48},{80,64},{96,80},{112,96},{17,1},{33... | collective-permute-start | bytes 995336 | tf_op jit(solution)/shard_map/ppermute | solution.py:27
  46.0 6.2 %copy-start.2 = (bf16[3,3,288,128]{3,2,1,0:T(8,128)(2,1)S(1)}, bf16[3,3,288,128]{3,2,1,0:T(8,128)(2,1)}, u32[]{:S(2)}) copy-start(bf16[3,3,288,128]{3,2,1,0:T(8,128)(2,1)} %param.10) | copy-start | bytes 1990660
  46.9 6.9 %collective-permute-start.4 = (bf16[16,1,64,128]{3,2,1,0:T(8,128)(2,1)}, bf16[16,1,64,128]{3,2,1,0:T(8,128)(2,1)S(1)}, u32[]{:S(2)}, u32[]{:S(2)}) collective-permute-start(bf16[16,1,64,128]{3,2,1,0:T(8,128)(2,1)} %get-tuple-element.18), channel_id=1, source_target_pairs={{0,1},{1,2},{2,3},{3,4},{4,5},{5,6},{6,7},{7,8},{8,9},{9,10},{10,1... | collective-permute-start | bytes 786440 | tf_op jit(solution)/shard_map/ppermute | solution.py:27
  50.2 11.3 %collective-permute-start.5 = (bf16[16,1,64,128]{3,2,1,0:T(8,128)(2,1)S(1)}, bf16[16,1,64,128]{3,2,1,0:T(8,128)(2,1)S(1)}, u32[]{:S(2)}, u32[]{:S(2)}) collective-permute-start(bf16[16,1,64,128]{3,2,1,0:T(8,128)(2,1)S(1)} %get-tuple-element.17), channel_id=1, source_target_pairs={{1,0},{2,1},{3,2},{4,3},{5,4},{6,5},{7,6},{8,7},{9,8},{10,9},{11,1... | collective-permute-start | bytes 786440 | tf_op jit(solution)/shard_map/ppermute | solution.py:27
  52.6 17.2 %copy-start.1 = (bf16[3,128,288]{1,2,0:T(8,128)(2,1)S(1)}, bf16[3,128,288]{1,2,0:T(8,128)(2,1)}, u32[]{:S(2)}) copy-start(bf16[3,128,288]{1,2,0:T(8,128)(2,1)} %param.11) | copy-start | bytes 663556
  62.4 16.5 %collective-permute-start.6 = (bf16[1,256,288]{2,1,0:T(8,128)(2,1)S(1)}, bf16[1,256,288]{2,1,0:T(8,128)(2,1)S(1)}, u32[]{:S(2)}, u32[]{:S(2)}) collective-permute-start(bf16[1,256,288]{2,1,0:T(8,128)(2,1)S(1)} %get-tuple-element.22), channel_id=1, source_target_pairs={{0,16},{16,32},{32,48},{48,64},{64,80},{80,96},{96,112},{1,17},{17... | collective-permute-start | bytes 442376 | tf_op jit(solution)/shard_map/ppermute | solution.py:27
  64.3 14.5 %collective-permute-start.7 = (bf16[1,256,288]{2,1,0:T(8,128)(2,1)S(1)}, bf16[1,256,288]{2,1,0:T(8,128)(2,1)S(1)}, u32[]{:S(2)}, u32[]{:S(2)}) collective-permute-start(bf16[1,256,288]{2,1,0:T(8,128)(2,1)S(1)} %get-tuple-element.21), channel_id=1, source_target_pairs={{16,0},{32,16},{48,32},{64,48},{80,64},{96,80},{112,96},{17,1},{33... | collective-permute-start | bytes 442376 | tf_op jit(solution)/shard_map/ppermute | solution.py:27

commit v15 on v13

--- a/solution.py
+++ b/solution.py
@@ -107,14 +107,11 @@
     stacked = jnp.concatenate(parts, axis=0)
     full = jnp.dot(wd_ref[...], stacked, preferred_element_type=jnp.float32)
     full = jnp.maximum(full, 0.0).astype(jnp.bfloat16)
+    outs = full.shape[0]
+    rows_by_d = jnp.concatenate([full[:, i * width : (i + 1) * width] for i in range(reduced_rows)], axis=0)
+    r = lax.dot_general(pick, rows_by_d, (((1,), (1,)), ((), ())), preferred_element_type=jnp.float32)
     for i in range(reduced_rows):
-        r = lax.dot_general(
-            pick,
-            full[:, i * width : (i + 1) * width],
-            (((1,), (1,)), ((), ())),
-            preferred_element_type=jnp.float32,
-        )
-        out_ref[slot, i] = r.astype(out_ref.dtype)
+        out_ref[slot, i] = r[:, i * outs : (i + 1) * outs].astype(out_ref.dtype)
 
 
 def _edges_one_kernel(above_ref, xp_ref, below_ref, w9_ref, edge_ref):

time: 79.5 us -> 79.2 us (level)
  no operation moved by 1% of the time
where the time goes in v15:
time: 79.2 us; the launch traced here: 78.8 us
  Pallas kernels  30.7 us (39%)
  starting transfers between devices  26.8 us (34%)
  waiting for transfers between devices  16.9 us (21%)
  local copies, waits for them, and re-layouts  2.78 us (4%)
  other arithmetic  1.33 us (2%)
    ppermute x8, starting transfers between devices, from_behind(): return lax.ppermute(array, axis, pairs)  26.8 us
    ppermute x8, waiting for transfers between devices, from_behind(): return lax.ppermute(array, axis, pairs)  16.9 us
    pallas_call x1, Pallas kernels, block_one(): pl.pallas_call(_inner_one_kernel, out_shape=(jax.ShapeDtypeStruct((frames...  16.1 us
    pallas_call x1, Pallas kernels, block_two(): pl.pallas_call(_inner_two_kernel, out_shape=(jax.ShapeDtypeStruct((frames...  9.03 us
    pallas_call x1, Pallas kernels, edge_rows(): pl.pallas_call(_copy_kernel, grid=(1,), out_shape=(jax.ShapeDtypeStruct((...  2.17 us
  transfers between devices with their start and end apart: 8, of which 3 were waited for; matrix products, arithmetic and copies ran while one was open for 3% of the time, Pallas kernels for 32%

profile of v15, /device:TPU:57, one launch (start us, length us, event | category | flops | bytes accessed | tf_op | source)
XLA Modules:
  0.0 78.8 jit_solution(6500169410285872617)
XLA Ops:
  0.0 0.0 copy-start
  0.0 0.0 copy-start.4
  0.0 0.0 copy-start.3
  0.0 2.2 %shard_map.64 = (bf16[16,2,64,128]{3,2,1,0:T(8,128)(2,1)}, bf16[16,1,64,128]{3,2,1,0:T(8,128)(2,1)}) custom-call(bf16[16,8,64,128]{3,2,1,0:T(8,128)(2,1)} %xp_ref.5, bf16[16,8,64,128]{3,2,1,0:T(8,128)(2,1)} %xp_ref.5), custom_call_target="tpu_custom_call" | custom-call | tf_op jit(solution)/shard_map/pallas_call | solution.py:356
  2.2 4.8 %collective-permute-start = (bf16[16,2,64,128]{3,2,1,0:T(8,128)(2,1)}, bf16[16,2,64,128]{3,2,1,0:T(8,128)(2,1)S(1)}, u32[]{:S(2)}, u32[]{:S(2)}) collective-permute-start(bf16[16,2,64,128]{3,2,1,0:T(8,128)(2,1)} %get-tuple-element.11), channel_id=1, source_target_pairs={{0,1},{1,2},{2,3},{3,4},{4,5},{5,6},{6,7},{7,8},{8,9},{9,10},{10,1... | collective-permute-start | bytes 1572872 | tf_op jit(solution)/shard_map/ppermute | solution.py:27
  7.0 1.9 %collective-permute-start.1 = (bf16[16,1,64,128]{3,2,1,0:T(8,128)(2,1)}, bf16[16,1,64,128]{3,2,1,0:T(8,128)(2,1)S(1)}, u32[]{:S(2)}, u32[]{:S(2)}) collective-permute-start(bf16[16,1,64,128]{3,2,1,0:T(8,128)(2,1)} %get-tuple-element.12), channel_id=1, source_target_pairs={{1,0},{2,1},{3,2},{4,3},{5,4},{6,5},{7,6},{8,7},{9,8},{10,9},{11,1... | collective-permute-start | bytes 786440 | tf_op jit(solution)/shard_map/ppermute | solution.py:27
  8.9 0.0 copy-done.4
  8.9 0.1 copy.11
  9.0 0.1 reshape.19.t3_ref
  9.2 1.1 %copy.12.w9_ref = bf16[144,576]{1,0:T(8,128)(2,1)S(1)} copy(bf16[144,576]{0,1:T(8,128)(2,1)} %bitcast.16) | data formatting | bytes 331776 | tf_op jit(solution)/shard_map/reshape | solution.py:165
  10.3 0.0 copy-done.3
  10.3 0.2 copy.15.wd_ref
  10.5 0.1 fusion.2.t3_ref
  10.6 8.0 %collective-permute-done.1.below_ref = bf16[16,1,64,128]{3,2,1,0:T(8,128)(2,1)S(1)} collective-permute-done((bf16[16,1,64,128]{3,2,1,0:T(8,128)(2,1)}, bf16[16,1,64,128]{3,2,1,0:T(8,128)(2,1)S(1)}, u32[]{:S(2)}, u32[]{:S(2)}) %collective-permute-start.1) | collective-permute-done | bytes 262176 | tf_op jit(solution)/shard_map/ppermute | solution.py:27
  18.5 0.0 collective-permute-done.above_ref
  18.5 0.0 copy-done
  18.5 0.8 %shard_map.65.edge_ref = bf16[2,144,1152]{2,1,0:T(8,128)(2,1)S(1)} custom-call(bf16[16,2,64,128]{3,2,1,0:T(8,128)(2,1)S(1)} %collective-permute-done.above_ref, bf16[16,8,64,128]{3,2,1,0:T(8,128)(2,1)S(1)} %copy-done, bf16[16,1,64,128]{3,2,1,0:T(8,128)(2,1)S(1)} %collective-permute-done.1.below_ref, bf16[144,576]{1,0:T(8,128)(2,1)S(1)} %copy.12.w9_ref), custom_call_target="tpu_custom_call" | custom-call | flops 382205952 | bytes 2097152 | tf_op jit(solution)/shard_map/pallas_call | solution.py:182
  19.4 0.1 fusion.4
  19.4 3.1 %collective-permute-start.2 = (bf16[1,144,1152]{2,1,0:T(8,128)(2,1)S(1)}, bf16[1,144,1152]{2,1,0:T(8,128)(2,1)S(1)}, u32[]{:S(2)}, u32[]{:S(2)}) collective-permute-start(bf16[1,144,1152]{2,1,0:T(8,128)(2,1)S(1)} %get-tuple-element.20), channel_id=1, source_target_pairs={{0,16},{16,32},{32,48},{48,64},{64,80},{80,96},{96,112},{1,17},{17... | collective-permute-start | bytes 995336 | tf_op jit(solution)/shard_map/ppermute | solution.py:27
  22.5 4.3 %collective-permute-start.3 = (bf16[1,144,1152]{2,1,0:T(8,128)(2,1)S(1)}, bf16[1,144,1152]{2,1,0:T(8,128)(2,1)S(1)}, u32[]{:S(2)}, u32[]{:S(2)}) collective-permute-start(bf16[1,144,1152]{2,1,0:T(8,128)(2,1)S(1)} %get-tuple-element.19), channel_id=1, source_target_pairs={{16,0},{32,16},{48,32},{64,48},{80,64},{96,80},{112,96},{17,1},{33... | collective-permute-start | bytes 995336 | tf_op jit(solution)/shard_map/ppermute | solution.py:27
  26.8 16.1 %shard_map.66 = (bf16[14,4,64,128]{3,2,1,0:T(8,128)(2,1)S(1)}, bf16[2,144,1152]{2,1,0:T(8,128)(2,1)S(1)}) custom-call(s32[1]{0:T(128)} %bitcast.keep_ref, bf16[16,2,64,128]{3,2,1,0:T(8,128)(2,1)S(1)} %collective-permute-done.above_ref, bf16[16,8,64,128]{3,2,1,0:T(8,128)(2,1)S(1)} %copy-done, bf16[16,1,64,128]{3,2,1,0:T(8,128)(2,1)S(1)} %collective-permute-done.1.below_ref, ...), custom_call_target="tpu_custom_call" | custom-call | flops 5284823040 | bytes 4194304 | tf_op jit(solution)/shard_map/pallas_call | solution.py:192
  43.0 0.0 collective-permute-done.2.before_ref
  43.0 0.0 collective-permute-done.3.after_ref
  43.0 1.3 %shard_map.67 = bf16[2,4,64,128]{3,2,1,0:T(8,128)(2,1)S(1)} custom-call(s32[1]{0:T(128)} %bitcast.keep_ref, bf16[16,2,64,128]{3,2,1,0:T(8,128)(2,1)S(1)} %collective-permute-done.above_ref, bf16[16,8,64,128]{3,2,1,0:T(8,128)(2,1)S(1)} %copy-done, bf16[16,1,64,128]{3,2,1,0:T(8,128)(2,1)S(1)} %collective-permute-done.1.below_ref, ...), custom_call_target="tpu_custom_call" | custom-call | tf_op jit(solution)/shard_map/pallas_call | solution.py:206
  44.3 0.0 copy-start.2
  44.4 0.1 pad_maximum_fusion.xp_ref
  44.5 0.7 fusion.3
  45.3 3.3 %collective-permute-start.4 = (bf16[16,1,64,128]{3,2,1,0:T(8,128)(2,1)}, bf16[16,1,64,128]{3,2,1,0:T(8,128)(2,1)S(1)}, u32[]{:S(2)}, u32[]{:S(2)}) collective-permute-start(bf16[16,1,64,128]{3,2,1,0:T(8,128)(2,1)} %get-tuple-element.18), channel_id=1, source_target_pairs={{0,1},{1,2},{2,3},{3,4},{4,5},{5,6},{6,7},{7,8},{8,9},{9,10},{10,1... | collective-permute-start | bytes 786440 | tf_op jit(solution)/shard_map/ppermute | solution.py:27
  48.6 1.9 %collective-permute-start.5 = (bf16[16,1,64,128]{3,2,1,0:T(8,128)(2,1)S(1)}, bf16[16,1,64,128]{3,2,1,0:T(8,128)(2,1)S(1)}, u32[]{:S(2)}, u32[]{:S(2)}) collective-permute-start(bf16[16,1,64,128]{3,2,1,0:T(8,128)(2,1)S(1)} %get-tuple-element.17), channel_id=1, source_target_pairs={{1,0},{2,1},{3,2},{4,3},{5,4},{6,5},{7,6},{8,7},{9,8},{10,9},{11,1... | collective-permute-start | bytes 786440 | tf_op jit(solution)/shard_map/ppermute | solution.py:27
  50.5 0.0 copy-done.2
  50.5 0.4 copy.16
  51.0 0.0 copy-start.1
  51.0 1.3 %collective-permute-done.4.above_ref = bf16[16,1,64,128]{3,2,1,0:T(8,128)(2,1)S(1)} collective-permute-done((bf16[16,1,64,128]{3,2,1,0:T(8,128)(2,1)}, bf16[16,1,64,128]{3,2,1,0:T(8,128)(2,1)S(1)}, u32[]{:S(2)}, u32[]{:S(2)}) %collective-permute-start.4) | collective-permute-done | bytes 262176 | tf_op jit(solution)/shard_map/ppermute | solution.py:27
  52.2 7.7 %collective-permute-done.5.below_ref = bf16[16,1,64,128]{3,2,1,0:T(8,128)(2,1)S(1)} collective-permute-done((bf16[16,1,64,128]{3,2,1,0:T(8,128)(2,1)S(1)}, bf16[16,1,64,128]{3,2,1,0:T(8,128)(2,1)S(1)}, u32[]{:S(2)}, u32[]{:S(2)}) %collective-permute-start.5) | collective-permute-done | bytes 262176 | tf_op jit(solution)/shard_map/ppermute | solution.py:27
  59.9 0.8 %shard_map.68.edge_ref = bf16[2,256,288]{2,1,0:T(8,128)(2,1)S(1)} custom-call(bf16[16,1,64,128]{3,2,1,0:T(8,128)(2,1)S(1)} %collective-permute-done.4.above_ref, bf16[16,4,64,128]{3,2,1,0:T(8,128)(2,1)S(1)} %pad_maximum_fusion.xp_ref, bf16[16,1,64,128]{3,2,1,0:T(8,128)(2,1)S(1)} %collective-permute-done.5.below_ref, bf16[1152,288]{1,0:T(8,128)(2,1)S(1)} %bitcast.11), custom_call_target="tpu_custom_call" | custom-call | flops 339738624 | bytes 1048576 | tf_op jit(solution)/shard_map/pallas_call | solution.py:309
  60.8 1.9 %collective-permute-start.6 = (bf16[1,256,288]{2,1,0:T(8,128)(2,1)S(1)}, bf16[1,256,288]{2,1,0:T(8,128)(2,1)S(1)}, u32[]{:S(2)}, u32[]{:S(2)}) collective-permute-start(bf16[1,256,288]{2,1,0:T(8,128)(2,1)S(1)} %get-tuple-element.22), channel_id=1, source_target_pairs={{0,16},{16,32},{32,48},{48,64},{64,80},{80,96},{96,112},{1,17},{17... | collective-permute-start | bytes 442376 | tf_op jit(solution)/shard_map/ppermute | solution.py:27
  62.7 5.5 %collective-permute-start.7 = (bf16[1,256,288]{2,1,0:T(8,128)(2,1)S(1)}, bf16[1,256,288]{2,1,0:T(8,128)(2,1)S(1)}, u32[]{:S(2)}, u32[]{:S(2)}) collective-permute-start(bf16[1,256,288]{2,1,0:T(8,128)(2,1)S(1)} %get-tuple-element.21), channel_id=1, source_target_pairs={{16,0},{32,16},{48,32},{64,48},{80,64},{96,80},{112,96},{17,1},{33... | collective-permute-start | bytes 442376 | tf_op jit(solution)/shard_map/ppermute | solution.py:27
  68.2 0.0 copy-done.1
  68.2 9.0 %shard_map.69 = (bf16[14,4,64,128]{3,2,1,0:T(8,128)(2,1)S(1)}, bf16[2,256,288]{2,1,0:T(8,128)(2,1)S(1)}) custom-call(bf16[16,1,64,128]{3,2,1,0:T(8,128)(2,1)S(1)} %collective-permute-done.4.above_ref, bf16[16,4,64,128]{3,2,1,0:T(8,128)(2,1)S(1)} %pad_maximum_fusion.xp_ref, bf16[16,1,64,128]{3,2,1,0:T(8,128)(2,1)S(1)} %collective-permute-done.5.below_ref, ...), custom_call_target="tpu_custom_call" | custom-call | flops 3623878656 | bytes 2097152 | tf_op jit(solution)/shard_map/pallas_call | solution.py:321
  77.2 0.0 collective-permute-done.6.before_ref
  77.2 0.0 collective-permute-done.7.after_ref
  77.2 0.4 shard_map.70
  77.7 1.1 %pad_maximum_fusion.1 = bf16[16,4,64,128]{3,2,1,0:T(8,128)(2,1)} fusion(bf16[1,4,64,128]{3,2,1,0:T(8,128)(2,1)S(1)} %get-tuple-element.24, bf16[14,4,64,128]{3,2,1,0:T(8,128)(2,1)S(1)} %get-tuple-element.16, bf16[1,4,64,128]{3,2,1,0:T(8,128)(2,1)S(1)} %get-tuple-element.23), kind=kLoop, calls=%fused_computation.1 | loop fusion | flops 1048576 | bytes 2097152 | tf_op jit(solution)/shard_map/concatenate | solution.py:344
  (3 shorter events, 0.1 us)
Async XLA Ops:
  0.0 18.5 %copy-start = (bf16[16,8,64,128]{3,2,1,0:T(8,128)(2,1)S(1)}, bf16[16,8,64,128]{3,2,1,0:T(8,128)(2,1)}, u32[]{:S(2)}) copy-start(bf16[16,8,64,128]{3,2,1,0:T(8,128)(2,1)} %xp_ref.5) | copy-start | bytes 6291460
  0.0 8.9 %copy-start.4 = (bf16[3,64,144]{2,1,0:T(8,128)(2,1)S(1)}, bf16[3,64,144]{2,1,0:T(8,128)(2,1)}, u32[]{:S(2)}) copy-start(bf16[3,64,144]{2,1,0:T(8,128)(2,1)} %param.8) | copy-start | bytes 165892
  0.0 10.3 %copy-start.3 = (bf16[3,3,128,64]{2,3,1,0:T(8,128)(2,1)S(1)}, bf16[3,3,128,64]{2,3,1,0:T(8,128)(2,1)}, u32[]{:S(2)}) copy-start(bf16[3,3,128,64]{2,3,1,0:T(8,128)(2,1)} %param.9) | copy-start | bytes 442372
  2.2 16.3 %collective-permute-start = (bf16[16,2,64,128]{3,2,1,0:T(8,128)(2,1)}, bf16[16,2,64,128]{3,2,1,0:T(8,128)(2,1)S(1)}, u32[]{:S(2)}, u32[]{:S(2)}) collective-permute-start(bf16[16,2,64,128]{3,2,1,0:T(8,128)(2,1)} %get-tuple-element.11), channel_id=1, source_target_pairs={{0,1},{1,2},{2,3},{3,4},{4,5},{5,6},{6,7},{7,8},{8,9},{9,10},{10,1... | collective-permute-start | bytes 1572872 | tf_op jit(solution)/shard_map/ppermute | solution.py:27
  7.0 11.5 %collective-permute-start.1 = (bf16[16,1,64,128]{3,2,1,0:T(8,128)(2,1)}, bf16[16,1,64,128]{3,2,1,0:T(8,128)(2,1)S(1)}, u32[]{:S(2)}, u32[]{:S(2)}) collective-permute-start(bf16[16,1,64,128]{3,2,1,0:T(8,128)(2,1)} %get-tuple-element.12), channel_id=1, source_target_pairs={{1,0},{2,1},{3,2},{4,3},{5,4},{6,5},{7,6},{8,7},{9,8},{10,9},{11,1... | collective-permute-start | bytes 786440 | tf_op jit(solution)/shard_map/ppermute | solution.py:27
  19.4 23.5 %collective-permute-start.2 = (bf16[1,144,1152]{2,1,0:T(8,128)(2,1)S(1)}, bf16[1,144,1152]{2,1,0:T(8,128)(2,1)S(1)}, u32[]{:S(2)}, u32[]{:S(2)}) collective-permute-start(bf16[1,144,1152]{2,1,0:T(8,128)(2,1)S(1)} %get-tuple-element.20), channel_id=1, source_target_pairs={{0,16},{16,32},{32,48},{48,64},{64,80},{80,96},{96,112},{1,17},{17... | collective-permute-start | bytes 995336 | tf_op jit(solution)/shard_map/ppermute | solution.py:27
  22.5 20.4 %collective-permute-start.3 = (bf16[1,144,1152]{2,1,0:T(8,128)(2,1)S(1)}, bf16[1,144,1152]{2,1,0:T(8,128)(2,1)S(1)}, u32[]{:S(2)}, u32[]{:S(2)}) collective-permute-start(bf16[1,144,1152]{2,1,0:T(8,128)(2,1)S(1)} %get-tuple-element.19), channel_id=1, source_target_pairs={{16,0},{32,16},{48,32},{64,48},{80,64},{96,80},{112,96},{17,1},{33... | collective-permute-start | bytes 995336 | tf_op jit(solution)/shard_map/ppermute | solution.py:27
  44.3 6.2 %copy-start.2 = (bf16[3,3,288,128]{3,2,1,0:T(8,128)(2,1)S(1)}, bf16[3,3,288,128]{3,2,1,0:T(8,128)(2,1)}, u32[]{:S(2)}) copy-start(bf16[3,3,288,128]{3,2,1,0:T(8,128)(2,1)} %param.10) | copy-start | bytes 1990660
  45.3 7.0 %collective-permute-start.4 = (bf16[16,1,64,128]{3,2,1,0:T(8,128)(2,1)}, bf16[16,1,64,128]{3,2,1,0:T(8,128)(2,1)S(1)}, u32[]{:S(2)}, u32[]{:S(2)}) collective-permute-start(bf16[16,1,64,128]{3,2,1,0:T(8,128)(2,1)} %get-tuple-element.18), channel_id=1, source_target_pairs={{0,1},{1,2},{2,3},{3,4},{4,5},{5,6},{6,7},{7,8},{8,9},{9,10},{10,1... | collective-permute-start | bytes 786440 | tf_op jit(solution)/shard_map/ppermute | solution.py:27
  48.6 11.3 %collective-permute-start.5 = (bf16[16,1,64,128]{3,2,1,0:T(8,128)(2,1)S(1)}, bf16[16,1,64,128]{3,2,1,0:T(8,128)(2,1)S(1)}, u32[]{:S(2)}, u32[]{:S(2)}) collective-permute-start(bf16[16,1,64,128]{3,2,1,0:T(8,128)(2,1)S(1)} %get-tuple-element.17), channel_id=1, source_target_pairs={{1,0},{2,1},{3,2},{4,3},{5,4},{6,5},{7,6},{8,7},{9,8},{10,9},{11,1... | collective-permute-start | bytes 786440 | tf_op jit(solution)/shard_map/ppermute | solution.py:27
  51.0 17.2 %copy-start.1 = (bf16[3,128,288]{1,2,0:T(8,128)(2,1)S(1)}, bf16[3,128,288]{1,2,0:T(8,128)(2,1)}, u32[]{:S(2)}) copy-start(bf16[3,128,288]{1,2,0:T(8,128)(2,1)} %param.11) | copy-start | bytes 663556
  60.8 16.5 %collective-permute-start.6 = (bf16[1,256,288]{2,1,0:T(8,128)(2,1)S(1)}, bf16[1,256,288]{2,1,0:T(8,128)(2,1)S(1)}, u32[]{:S(2)}, u32[]{:S(2)}) collective-permute-start(bf16[1,256,288]{2,1,0:T(8,128)(2,1)S(1)} %get-tuple-element.22), channel_id=1, source_target_pairs={{0,16},{16,32},{32,48},{48,64},{64,80},{80,96},{96,112},{1,17},{17... | collective-permute-start | bytes 442376 | tf_op jit(solution)/shard_map/ppermute | solution.py:27
  62.7 14.5 %collective-permute-start.7 = (bf16[1,256,288]{2,1,0:T(8,128)(2,1)S(1)}, bf16[1,256,288]{2,1,0:T(8,128)(2,1)S(1)}, u32[]{:S(2)}, u32[]{:S(2)}) collective-permute-start(bf16[1,256,288]{2,1,0:T(8,128)(2,1)S(1)} %get-tuple-element.21), channel_id=1, source_target_pairs={{16,0},{32,16},{48,32},{64,48},{80,64},{96,80},{112,96},{17,1},{33... | collective-permute-start | bytes 442376 | tf_op jit(solution)/shard_map/ppermute | solution.py:27

commit v16 on v15

--- a/solution.py
+++ b/solution.py
@@ -64,16 +64,19 @@
     return jnp.where(inside, rolled, jnp.zeros_like(rolled))
 
 
-def _middle_one(refs, f, w9_ref):
+def _middle_one(refs, f, w9_ref, count=1):
     above_ref, xp_ref, below_ref = refs
     rows = xp_ref.shape[1] + 1
-    slab = jnp.concatenate([above_ref[f], xp_ref[f], below_ref[f]], axis=0).astype(jnp.float32)
-    shifted = [_lane_shift(slab, b - 1).astype(jnp.bfloat16) for b in range(3)]
-    parts = []
-    for a in range(3):
-        for b in range(3):
-            parts.append(jnp.concatenate([shifted[b][h + a] for h in range(rows)], axis=1))
-    stacked = jnp.concatenate(parts, axis=0)
+    columns = []
+    for k in range(count):
+        slab = jnp.concatenate([above_ref[f + k], xp_ref[f + k], below_ref[f + k]], axis=0).astype(jnp.float32)
+        shifted = [_lane_shift(slab, b - 1).astype(jnp.bfloat16) for b in range(3)]
+        parts = []
+        for a in range(3):
+            for b in range(3):
+                parts.append(jnp.concatenate([shifted[b][h + a] for h in range(rows)], axis=1))
+        columns.append(jnp.concatenate(parts, axis=0))
+    stacked = columns[0] if count == 1 else jnp.concatenate(columns, axis=1)
     m = jnp.dot(w9_ref[...], stacked, preferred_element_type=jnp.float32)
     return jnp.maximum(m, 0.0).astype(jnp.bfloat16)
 
@@ -125,11 +128,15 @@
     refs = (above_ref, xp_ref, below_ref)
     frames = xp_ref.shape[0]
 
-    def middle(f, carry):
-        mid_ref[f] = _middle_one(refs, f, w9_ref)
+    span = mid_ref.shape[-1]
+
+    def middle(g, carry):
+        m = _middle_one(refs, 2 * g, w9_ref, 2)
+        mid_ref[2 * g] = m[:, :span]
+        mid_ref[2 * g + 1] = m[:, span:]
         return carry
 
-    lax.fori_loop(0, frames, middle, 0)
+    lax.fori_loop(0, frames // 2, middle, 0)
     side_ref[0] = mid_ref[1]
     side_ref[1] = mid_ref[frames - 2]
 

time: 79.2 us -> 77.1 us (0.973)
  Pallas kernels: 30.7 us -> 28.7 us
    pallas_call x1, Pallas kernels: 16.1 us -> 14.1 us  [block_one(): pl.pallas_call(_inner_one_kernel, out_shape=(jax.ShapeDtypeStruct((frames...]
  transfers between devices with their start and end apart: 8 -> 8, of which waited for: 3 -> 3; matrix products, arithmetic and copies ran while one was open for 3% -> 3% of each run, Pallas kernels for 32% -> 30%
where the time goes in v16:
time: 77.1 us; the launch traced here: 76.7 us
  Pallas kernels  28.7 us (37%)
  starting transfers between devices  26.8 us (35%)
  waiting for transfers between devices  16.9 us (22%)
  local copies, waits for them, and re-layouts  2.78 us (4%)
  other arithmetic  1.33 us (2%)
    ppermute x8, starting transfers between devices, from_behind(): return lax.ppermute(array, axis, pairs)  26.8 us
    ppermute x8, waiting for transfers between devices, from_behind(): return lax.ppermute(array, axis, pairs)  16.9 us
    pallas_call x1, Pallas kernels, block_one(): pl.pallas_call(_inner_one_kernel, out_shape=(jax.ShapeDtypeStruct((frames...  14.1 us
    pallas_call x1, Pallas kernels, block_two(): pl.pallas_call(_inner_two_kernel, out_shape=(jax.ShapeDtypeStruct((frames...  9.03 us
    pallas_call x1, Pallas kernels, edge_rows(): pl.pallas_call(_copy_kernel, grid=(1,), out_shape=(jax.ShapeDtypeStruct((...  2.17 us
  transfers between devices with their start and end apart: 8, of which 3 were waited for; matrix products, arithmetic and copies ran while one was open for 3% of the time, Pallas kernels for 30%

profile of v16, /device:TPU:57, one launch (start us, length us, event | category | flops | bytes accessed | tf_op | source)
XLA Modules:
  0.0 76.7 jit_solution(5017418811843408044)
XLA Ops:
  0.0 0.0 copy-start
  0.0 0.0 copy-start.4
  0.0 0.0 copy-start.3
  0.0 2.2 %shard_map.64 = (bf16[16,2,64,128]{3,2,1,0:T(8,128)(2,1)}, bf16[16,1,64,128]{3,2,1,0:T(8,128)(2,1)}) custom-call(bf16[16,8,64,128]{3,2,1,0:T(8,128)(2,1)} %xp_ref.5, bf16[16,8,64,128]{3,2,1,0:T(8,128)(2,1)} %xp_ref.5), custom_call_target="tpu_custom_call" | custom-call | tf_op jit(solution)/shard_map/pallas_call | solution.py:363
  2.2 4.8 %collective-permute-start = (bf16[16,2,64,128]{3,2,1,0:T(8,128)(2,1)}, bf16[16,2,64,128]{3,2,1,0:T(8,128)(2,1)S(1)}, u32[]{:S(2)}, u32[]{:S(2)}) collective-permute-start(bf16[16,2,64,128]{3,2,1,0:T(8,128)(2,1)} %get-tuple-element.11), channel_id=1, source_target_pairs={{0,1},{1,2},{2,3},{3,4},{4,5},{5,6},{6,7},{7,8},{8,9},{9,10},{10,1... | collective-permute-start | bytes 1572872 | tf_op jit(solution)/shard_map/ppermute | solution.py:27
  7.0 1.9 %collective-permute-start.1 = (bf16[16,1,64,128]{3,2,1,0:T(8,128)(2,1)}, bf16[16,1,64,128]{3,2,1,0:T(8,128)(2,1)S(1)}, u32[]{:S(2)}, u32[]{:S(2)}) collective-permute-start(bf16[16,1,64,128]{3,2,1,0:T(8,128)(2,1)} %get-tuple-element.12), channel_id=1, source_target_pairs={{1,0},{2,1},{3,2},{4,3},{5,4},{6,5},{7,6},{8,7},{9,8},{10,9},{11,1... | collective-permute-start | bytes 786440 | tf_op jit(solution)/shard_map/ppermute | solution.py:27
  8.9 0.0 copy-done.4
  8.9 0.1 copy.11
  9.0 0.1 reshape.19.t3_ref
  9.2 1.1 %copy.12.w9_ref = bf16[144,576]{1,0:T(8,128)(2,1)S(1)} copy(bf16[144,576]{0,1:T(8,128)(2,1)} %bitcast.16) | data formatting | bytes 331776 | tf_op jit(solution)/shard_map/reshape | solution.py:172
  10.3 0.0 copy-done.3
  10.3 0.2 copy.15.wd_ref
  10.5 0.1 fusion.2.t3_ref
  10.6 8.0 %collective-permute-done.1.below_ref = bf16[16,1,64,128]{3,2,1,0:T(8,128)(2,1)S(1)} collective-permute-done((bf16[16,1,64,128]{3,2,1,0:T(8,128)(2,1)}, bf16[16,1,64,128]{3,2,1,0:T(8,128)(2,1)S(1)}, u32[]{:S(2)}, u32[]{:S(2)}) %collective-permute-start.1) | collective-permute-done | bytes 262176 | tf_op jit(solution)/shard_map/ppermute | solution.py:27
  18.5 0.0 collective-permute-done.above_ref
  18.5 0.0 copy-done
  18.5 0.8 %shard_map.65.edge_ref = bf16[2,144,1152]{2,1,0:T(8,128)(2,1)S(1)} custom-call(bf16[16,2,64,128]{3,2,1,0:T(8,128)(2,1)S(1)} %collective-permute-done.above_ref, bf16[16,8,64,128]{3,2,1,0:T(8,128)(2,1)S(1)} %copy-done, bf16[16,1,64,128]{3,2,1,0:T(8,128)(2,1)S(1)} %collective-permute-done.1.below_ref, bf16[144,576]{1,0:T(8,128)(2,1)S(1)} %copy.12.w9_ref), custom_call_target="tpu_custom_call" | custom-call | flops 382205952 | bytes 2097152 | tf_op jit(solution)/shard_map/pallas_call | solution.py:189
  19.4 0.1 fusion.4
  19.4 3.1 %collective-permute-start.2 = (bf16[1,144,1152]{2,1,0:T(8,128)(2,1)S(1)}, bf16[1,144,1152]{2,1,0:T(8,128)(2,1)S(1)}, u32[]{:S(2)}, u32[]{:S(2)}) collective-permute-start(bf16[1,144,1152]{2,1,0:T(8,128)(2,1)S(1)} %get-tuple-element.20), channel_id=1, source_target_pairs={{0,16},{16,32},{32,48},{48,64},{64,80},{80,96},{96,112},{1,17},{17... | collective-permute-start | bytes 995336 | tf_op jit(solution)/shard_map/ppermute | solution.py:27
  22.5 4.3 %collective-permute-start.3 = (bf16[1,144,1152]{2,1,0:T(8,128)(2,1)S(1)}, bf16[1,144,1152]{2,1,0:T(8,128)(2,1)S(1)}, u32[]{:S(2)}, u32[]{:S(2)}) collective-permute-start(bf16[1,144,1152]{2,1,0:T(8,128)(2,1)S(1)} %get-tuple-element.19), channel_id=1, source_target_pairs={{16,0},{32,16},{48,32},{64,48},{80,64},{96,80},{112,96},{17,1},{33... | collective-permute-start | bytes 995336 | tf_op jit(solution)/shard_map/ppermute | solution.py:27
  26.8 14.1 %shard_map.66 = (bf16[14,4,64,128]{3,2,1,0:T(8,128)(2,1)S(1)}, bf16[2,144,1152]{2,1,0:T(8,128)(2,1)S(1)}) custom-call(s32[1]{0:T(128)} %bitcast.keep_ref, bf16[16,2,64,128]{3,2,1,0:T(8,128)(2,1)S(1)} %collective-permute-done.above_ref, bf16[16,8,64,128]{3,2,1,0:T(8,128)(2,1)S(1)} %copy-done, bf16[16,1,64,128]{3,2,1,0:T(8,128)(2,1)S(1)} %collective-permute-done.1.below_ref, ...), custom_call_target="tpu_custom_call" | custom-call | flops 5284823040 | bytes 4194304 | tf_op jit(solution)/shard_map/pallas_call | solution.py:199
  40.9 0.0 collective-permute-done.2.before_ref
  40.9 0.0 collective-permute-done.3.after_ref
  40.9 1.3 %shard_map.67 = bf16[2,4,64,128]{3,2,1,0:T(8,128)(2,1)S(1)} custom-call(s32[1]{0:T(128)} %bitcast.keep_ref, bf16[16,2,64,128]{3,2,1,0:T(8,128)(2,1)S(1)} %collective-permute-done.above_ref, bf16[16,8,64,128]{3,2,1,0:T(8,128)(2,1)S(1)} %copy-done, bf16[16,1,64,128]{3,2,1,0:T(8,128)(2,1)S(1)} %collective-permute-done.1.below_ref, ...), custom_call_target="tpu_custom_call" | custom-call | tf_op jit(solution)/shard_map/pallas_call | solution.py:213
  42.3 0.0 copy-start.2
  42.3 0.1 pad_maximum_fusion.xp_ref
  42.4 0.7 fusion.3
  43.2 3.3 %collective-permute-start.4 = (bf16[16,1,64,128]{3,2,1,0:T(8,128)(2,1)}, bf16[16,1,64,128]{3,2,1,0:T(8,128)(2,1)S(1)}, u32[]{:S(2)}, u32[]{:S(2)}) collective-permute-start(bf16[16,1,64,128]{3,2,1,0:T(8,128)(2,1)} %get-tuple-element.18), channel_id=1, source_target_pairs={{0,1},{1,2},{2,3},{3,4},{4,5},{5,6},{6,7},{7,8},{8,9},{9,10},{10,1... | collective-permute-start | bytes 786440 | tf_op jit(solution)/shard_map/ppermute | solution.py:27
  46.5 1.9 %collective-permute-start.5 = (bf16[16,1,64,128]{3,2,1,0:T(8,128)(2,1)S(1)}, bf16[16,1,64,128]{3,2,1,0:T(8,128)(2,1)S(1)}, u32[]{:S(2)}, u32[]{:S(2)}) collective-permute-start(bf16[16,1,64,128]{3,2,1,0:T(8,128)(2,1)S(1)} %get-tuple-element.17), channel_id=1, source_target_pairs={{1,0},{2,1},{3,2},{4,3},{5,4},{6,5},{7,6},{8,7},{9,8},{10,9},{11,1... | collective-permute-start | bytes 786440 | tf_op jit(solution)/shard_map/ppermute | solution.py:27
  48.5 0.0 copy-done.2
  48.5 0.4 copy.16
  48.9 0.0 copy-start.1
  48.9 1.3 %collective-permute-done.4.above_ref = bf16[16,1,64,128]{3,2,1,0:T(8,128)(2,1)S(1)} collective-permute-done((bf16[16,1,64,128]{3,2,1,0:T(8,128)(2,1)}, bf16[16,1,64,128]{3,2,1,0:T(8,128)(2,1)S(1)}, u32[]{:S(2)}, u32[]{:S(2)}) %collective-permute-start.4) | collective-permute-done | bytes 262176 | tf_op jit(solution)/shard_map/ppermute | solution.py:27
  50.1 7.7 %collective-permute-done.5.below_ref = bf16[16,1,64,128]{3,2,1,0:T(8,128)(2,1)S(1)} collective-permute-done((bf16[16,1,64,128]{3,2,1,0:T(8,128)(2,1)S(1)}, bf16[16,1,64,128]{3,2,1,0:T(8,128)(2,1)S(1)}, u32[]{:S(2)}, u32[]{:S(2)}) %collective-permute-start.5) | collective-permute-done | bytes 262176 | tf_op jit(solution)/shard_map/ppermute | solution.py:27
  57.8 0.8 %shard_map.68.edge_ref = bf16[2,256,288]{2,1,0:T(8,128)(2,1)S(1)} custom-call(bf16[16,1,64,128]{3,2,1,0:T(8,128)(2,1)S(1)} %collective-permute-done.4.above_ref, bf16[16,4,64,128]{3,2,1,0:T(8,128)(2,1)S(1)} %pad_maximum_fusion.xp_ref, bf16[16,1,64,128]{3,2,1,0:T(8,128)(2,1)S(1)} %collective-permute-done.5.below_ref, bf16[1152,288]{1,0:T(8,128)(2,1)S(1)} %bitcast.11), custom_call_target="tpu_custom_call" | custom-call | flops 339738624 | bytes 1048576 | tf_op jit(solution)/shard_map/pallas_call | solution.py:316
  58.7 1.9 %collective-permute-start.6 = (bf16[1,256,288]{2,1,0:T(8,128)(2,1)S(1)}, bf16[1,256,288]{2,1,0:T(8,128)(2,1)S(1)}, u32[]{:S(2)}, u32[]{:S(2)}) collective-permute-start(bf16[1,256,288]{2,1,0:T(8,128)(2,1)S(1)} %get-tuple-element.22), channel_id=1, source_target_pairs={{0,16},{16,32},{32,48},{48,64},{64,80},{80,96},{96,112},{1,17},{17... | collective-permute-start | bytes 442376 | tf_op jit(solution)/shard_map/ppermute | solution.py:27
  60.6 5.5 %collective-permute-start.7 = (bf16[1,256,288]{2,1,0:T(8,128)(2,1)S(1)}, bf16[1,256,288]{2,1,0:T(8,128)(2,1)S(1)}, u32[]{:S(2)}, u32[]{:S(2)}) collective-permute-start(bf16[1,256,288]{2,1,0:T(8,128)(2,1)S(1)} %get-tuple-element.21), channel_id=1, source_target_pairs={{16,0},{32,16},{48,32},{64,48},{80,64},{96,80},{112,96},{17,1},{33... | collective-permute-start | bytes 442376 | tf_op jit(solution)/shard_map/ppermute | solution.py:27
  66.1 0.0 copy-done.1
  66.1 9.0 %shard_map.69 = (bf16[14,4,64,128]{3,2,1,0:T(8,128)(2,1)S(1)}, bf16[2,256,288]{2,1,0:T(8,128)(2,1)S(1)}) custom-call(bf16[16,1,64,128]{3,2,1,0:T(8,128)(2,1)S(1)} %collective-permute-done.4.above_ref, bf16[16,4,64,128]{3,2,1,0:T(8,128)(2,1)S(1)} %pad_maximum_fusion.xp_ref, bf16[16,1,64,128]{3,2,1,0:T(8,128)(2,1)S(1)} %collective-permute-done.5.below_ref, ...), custom_call_target="tpu_custom_call" | custom-call | flops 3623878656 | bytes 2097152 | tf_op jit(solution)/shard_map/pallas_call | solution.py:328
  75.1 0.0 collective-permute-done.6.before_ref
  75.2 0.0 collective-permute-done.7.after_ref
  75.2 0.4 shard_map.70
  75.6 1.1 %pad_maximum_fusion.1 = bf16[16,4,64,128]{3,2,1,0:T(8,128)(2,1)} fusion(bf16[1,4,64,128]{3,2,1,0:T(8,128)(2,1)S(1)} %get-tuple-element.24, bf16[14,4,64,128]{3,2,1,0:T(8,128)(2,1)S(1)} %get-tuple-element.16, bf16[1,4,64,128]{3,2,1,0:T(8,128)(2,1)S(1)} %get-tuple-element.23), kind=kLoop, calls=%fused_computation.1 | loop fusion | flops 1048576 | bytes 2097152 | tf_op jit(solution)/shard_map/concatenate | solution.py:351
  (3 shorter events, 0.1 us)
Async XLA Ops:
  0.0 18.5 %copy-start = (bf16[16,8,64,128]{3,2,1,0:T(8,128)(2,1)S(1)}, bf16[16,8,64,128]{3,2,1,0:T(8,128)(2,1)}, u32[]{:S(2)}) copy-start(bf16[16,8,64,128]{3,2,1,0:T(8,128)(2,1)} %xp_ref.5) | copy-start | bytes 6291460
  0.0 8.9 %copy-start.4 = (bf16[3,64,144]{2,1,0:T(8,128)(2,1)S(1)}, bf16[3,64,144]{2,1,0:T(8,128)(2,1)}, u32[]{:S(2)}) copy-start(bf16[3,64,144]{2,1,0:T(8,128)(2,1)} %param.8) | copy-start | bytes 165892
  0.0 10.3 %copy-start.3 = (bf16[3,3,128,64]{2,3,1,0:T(8,128)(2,1)S(1)}, bf16[3,3,128,64]{2,3,1,0:T(8,128)(2,1)}, u32[]{:S(2)}) copy-start(bf16[3,3,128,64]{2,3,1,0:T(8,128)(2,1)} %param.9) | copy-start | bytes 442372
  2.2 16.3 %collective-permute-start = (bf16[16,2,64,128]{3,2,1,0:T(8,128)(2,1)}, bf16[16,2,64,128]{3,2,1,0:T(8,128)(2,1)S(1)}, u32[]{:S(2)}, u32[]{:S(2)}) collective-permute-start(bf16[16,2,64,128]{3,2,1,0:T(8,128)(2,1)} %get-tuple-element.11), channel_id=1, source_target_pairs={{0,1},{1,2},{2,3},{3,4},{4,5},{5,6},{6,7},{7,8},{8,9},{9,10},{10,1... | collective-permute-start | bytes 1572872 | tf_op jit(solution)/shard_map/ppermute | solution.py:27
  7.0 11.5 %collective-permute-start.1 = (bf16[16,1,64,128]{3,2,1,0:T(8,128)(2,1)}, bf16[16,1,64,128]{3,2,1,0:T(8,128)(2,1)S(1)}, u32[]{:S(2)}, u32[]{:S(2)}) collective-permute-start(bf16[16,1,64,128]{3,2,1,0:T(8,128)(2,1)} %get-tuple-element.12), channel_id=1, source_target_pairs={{1,0},{2,1},{3,2},{4,3},{5,4},{6,5},{7,6},{8,7},{9,8},{10,9},{11,1... | collective-permute-start | bytes 786440 | tf_op jit(solution)/shard_map/ppermute | solution.py:27
  19.4 21.5 %collective-permute-start.2 = (bf16[1,144,1152]{2,1,0:T(8,128)(2,1)S(1)}, bf16[1,144,1152]{2,1,0:T(8,128)(2,1)S(1)}, u32[]{:S(2)}, u32[]{:S(2)}) collective-permute-start(bf16[1,144,1152]{2,1,0:T(8,128)(2,1)S(1)} %get-tuple-element.20), channel_id=1, source_target_pairs={{0,16},{16,32},{32,48},{48,64},{64,80},{80,96},{96,112},{1,17},{17... | collective-permute-start | bytes 995336 | tf_op jit(solution)/shard_map/ppermute | solution.py:27
  22.5 18.4 %collective-permute-start.3 = (bf16[1,144,1152]{2,1,0:T(8,128)(2,1)S(1)}, bf16[1,144,1152]{2,1,0:T(8,128)(2,1)S(1)}, u32[]{:S(2)}, u32[]{:S(2)}) collective-permute-start(bf16[1,144,1152]{2,1,0:T(8,128)(2,1)S(1)} %get-tuple-element.19), channel_id=1, source_target_pairs={{16,0},{32,16},{48,32},{64,48},{80,64},{96,80},{112,96},{17,1},{33... | collective-permute-start | bytes 995336 | tf_op jit(solution)/shard_map/ppermute | solution.py:27
  42.3 6.2 %copy-start.2 = (bf16[3,3,288,128]{3,2,1,0:T(8,128)(2,1)S(1)}, bf16[3,3,288,128]{3,2,1,0:T(8,128)(2,1)}, u32[]{:S(2)}) copy-start(bf16[3,3,288,128]{3,2,1,0:T(8,128)(2,1)} %param.10) | copy-start | bytes 1990660
  43.2 7.0 %collective-permute-start.4 = (bf16[16,1,64,128]{3,2,1,0:T(8,128)(2,1)}, bf16[16,1,64,128]{3,2,1,0:T(8,128)(2,1)S(1)}, u32[]{:S(2)}, u32[]{:S(2)}) collective-permute-start(bf16[16,1,64,128]{3,2,1,0:T(8,128)(2,1)} %get-tuple-element.18), channel_id=1, source_target_pairs={{0,1},{1,2},{2,3},{3,4},{4,5},{5,6},{6,7},{7,8},{8,9},{9,10},{10,1... | collective-permute-start | bytes 786440 | tf_op jit(solution)/shard_map/ppermute | solution.py:27
  46.5 11.3 %collective-permute-start.5 = (bf16[16,1,64,128]{3,2,1,0:T(8,128)(2,1)S(1)}, bf16[16,1,64,128]{3,2,1,0:T(8,128)(2,1)S(1)}, u32[]{:S(2)}, u32[]{:S(2)}) collective-permute-start(bf16[16,1,64,128]{3,2,1,0:T(8,128)(2,1)S(1)} %get-tuple-element.17), channel_id=1, source_target_pairs={{1,0},{2,1},{3,2},{4,3},{5,4},{6,5},{7,6},{8,7},{9,8},{10,9},{11,1... | collective-permute-start | bytes 786440 | tf_op jit(solution)/shard_map/ppermute | solution.py:27
  48.9 17.2 %copy-start.1 = (bf16[3,128,288]{1,2,0:T(8,128)(2,1)S(1)}, bf16[3,128,288]{1,2,0:T(8,128)(2,1)}, u32[]{:S(2)}) copy-start(bf16[3,128,288]{1,2,0:T(8,128)(2,1)} %param.11) | copy-start | bytes 663556
  58.7 16.5 %collective-permute-start.6 = (bf16[1,256,288]{2,1,0:T(8,128)(2,1)S(1)}, bf16[1,256,288]{2,1,0:T(8,128)(2,1)S(1)}, u32[]{:S(2)}, u32[]{:S(2)}) collective-permute-start(bf16[1,256,288]{2,1,0:T(8,128)(2,1)S(1)} %get-tuple-element.22), channel_id=1, source_target_pairs={{0,16},{16,32},{32,48},{48,64},{64,80},{80,96},{96,112},{1,17},{17... | collective-permute-start | bytes 442376 | tf_op jit(solution)/shard_map/ppermute | solution.py:27
  60.6 14.5 %collective-permute-start.7 = (bf16[1,256,288]{2,1,0:T(8,128)(2,1)S(1)}, bf16[1,256,288]{2,1,0:T(8,128)(2,1)S(1)}, u32[]{:S(2)}, u32[]{:S(2)}) collective-permute-start(bf16[1,256,288]{2,1,0:T(8,128)(2,1)S(1)} %get-tuple-element.21), channel_id=1, source_target_pairs={{16,0},{32,16},{48,32},{64,48},{80,64},{96,80},{112,96},{17,1},{33... | collective-permute-start | bytes 442376 | tf_op jit(solution)/shard_map/ppermute | solution.py:27

commit v17 on v16

--- a/solution.py
+++ b/solution.py
@@ -129,14 +129,15 @@
     frames = xp_ref.shape[0]
 
     span = mid_ref.shape[-1]
+    group = 4 if frames % 4 == 0 else 2
 
     def middle(g, carry):
-        m = _middle_one(refs, 2 * g, w9_ref, 2)
-        mid_ref[2 * g] = m[:, :span]
-        mid_ref[2 * g + 1] = m[:, span:]
+        m = _middle_one(refs, group * g, w9_ref, group)
+        for k in range(group):
+            mid_ref[group * g + k] = m[:, k * span : (k + 1) * span]
         return carry
 
-    lax.fori_loop(0, frames // 2, middle, 0)
+    lax.fori_loop(0, frames // group, middle, 0)
     side_ref[0] = mid_ref[1]
     side_ref[1] = mid_ref[frames - 2]
 

time: 77.1 us -> 76.1 us (0.987)
  Pallas kernels: 28.7 us -> 27.7 us
    pallas_call x1, Pallas kernels: 14.1 us -> 13.1 us  [block_one(): pl.pallas_call(_inner_one_kernel, out_shape=(jax.ShapeDtypeStruct((frames...]
  transfers between devices with their start and end apart: 8 -> 8, of which waited for: 3 -> 3; matrix products, arithmetic and copies ran while one was open for 3% -> 3% of each run, Pallas kernels for 30% -> 29%
where the time goes in v17:
time: 76.1 us; the launch traced here: 75.8 us
  Pallas kernels  27.7 us (36%)
  starting transfers between devices  26.8 us (35%)
  waiting for transfers between devices  16.9 us (22%)
  local copies, waits for them, and re-layouts  2.78 us (4%)
  other arithmetic  1.33 us (2%)
    ppermute x8, starting transfers between devices, from_behind(): return lax.ppermute(array, axis, pairs)  26.8 us
    ppermute x8, waiting for transfers between devices, from_behind(): return lax.ppermute(array, axis, pairs)  16.9 us
    pallas_call x1, Pallas kernels, block_one(): pl.pallas_call(_inner_one_kernel, out_shape=(jax.ShapeDtypeStruct((frames...  13.1 us
    pallas_call x1, Pallas kernels, block_two(): pl.pallas_call(_inner_two_kernel, out_shape=(jax.ShapeDtypeStruct((frames...  9.03 us
    pallas_call x1, Pallas kernels, edge_rows(): pl.pallas_call(_copy_kernel, grid=(1,), out_shape=(jax.ShapeDtypeStruct((...  2.17 us
  transfers between devices with their start and end apart: 8, of which 3 were waited for; matrix products, arithmetic and copies ran while one was open for 3% of the time, Pallas kernels for 29%

profile of v17, /device:TPU:57, one launch (start us, length us, event | category | flops | bytes accessed | tf_op | source)
XLA Modules:
  0.0 75.8 jit_solution(8141997277629584623)
XLA Ops:
  0.0 0.0 copy-start
  0.0 0.0 copy-start.4
  0.0 0.0 copy-start.3
  0.0 2.2 %shard_map.64 = (bf16[16,2,64,128]{3,2,1,0:T(8,128)(2,1)}, bf16[16,1,64,128]{3,2,1,0:T(8,128)(2,1)}) custom-call(bf16[16,8,64,128]{3,2,1,0:T(8,128)(2,1)} %xp_ref.5, bf16[16,8,64,128]{3,2,1,0:T(8,128)(2,1)} %xp_ref.5), custom_call_target="tpu_custom_call" | custom-call | tf_op jit(solution)/shard_map/pallas_call | solution.py:364
  2.2 4.8 %collective-permute-start = (bf16[16,2,64,128]{3,2,1,0:T(8,128)(2,1)}, bf16[16,2,64,128]{3,2,1,0:T(8,128)(2,1)S(1)}, u32[]{:S(2)}, u32[]{:S(2)}) collective-permute-start(bf16[16,2,64,128]{3,2,1,0:T(8,128)(2,1)} %get-tuple-element.11), channel_id=1, source_target_pairs={{0,1},{1,2},{2,3},{3,4},{4,5},{5,6},{6,7},{7,8},{8,9},{9,10},{10,1... | collective-permute-start | bytes 1572872 | tf_op jit(solution)/shard_map/ppermute | solution.py:27
  7.0 1.9 %collective-permute-start.1 = (bf16[16,1,64,128]{3,2,1,0:T(8,128)(2,1)}, bf16[16,1,64,128]{3,2,1,0:T(8,128)(2,1)S(1)}, u32[]{:S(2)}, u32[]{:S(2)}) collective-permute-start(bf16[16,1,64,128]{3,2,1,0:T(8,128)(2,1)} %get-tuple-element.12), channel_id=1, source_target_pairs={{1,0},{2,1},{3,2},{4,3},{5,4},{6,5},{7,6},{8,7},{9,8},{10,9},{11,1... | collective-permute-start | bytes 786440 | tf_op jit(solution)/shard_map/ppermute | solution.py:27
  8.9 0.0 copy-done.4
  8.9 0.1 copy.11
  9.0 0.1 reshape.19.t3_ref
  9.2 1.1 %copy.12.w9_ref = bf16[144,576]{1,0:T(8,128)(2,1)S(1)} copy(bf16[144,576]{0,1:T(8,128)(2,1)} %bitcast.16) | data formatting | bytes 331776 | tf_op jit(solution)/shard_map/reshape | solution.py:173
  10.3 0.0 copy-done.3
  10.3 0.2 copy.15.wd_ref
  10.5 0.1 fusion.2.t3_ref
  10.6 8.0 %collective-permute-done.1.below_ref = bf16[16,1,64,128]{3,2,1,0:T(8,128)(2,1)S(1)} collective-permute-done((bf16[16,1,64,128]{3,2,1,0:T(8,128)(2,1)}, bf16[16,1,64,128]{3,2,1,0:T(8,128)(2,1)S(1)}, u32[]{:S(2)}, u32[]{:S(2)}) %collective-permute-start.1) | collective-permute-done | bytes 262176 | tf_op jit(solution)/shard_map/ppermute | solution.py:27
  18.5 0.0 collective-permute-done.above_ref
  18.5 0.0 copy-done
  18.5 0.8 %shard_map.65.edge_ref = bf16[2,144,1152]{2,1,0:T(8,128)(2,1)S(1)} custom-call(bf16[16,2,64,128]{3,2,1,0:T(8,128)(2,1)S(1)} %collective-permute-done.above_ref, bf16[16,8,64,128]{3,2,1,0:T(8,128)(2,1)S(1)} %copy-done, bf16[16,1,64,128]{3,2,1,0:T(8,128)(2,1)S(1)} %collective-permute-done.1.below_ref, bf16[144,576]{1,0:T(8,128)(2,1)S(1)} %copy.12.w9_ref), custom_call_target="tpu_custom_call" | custom-call | flops 382205952 | bytes 2097152 | tf_op jit(solution)/shard_map/pallas_call | solution.py:190
  19.4 0.1 fusion.4
  19.4 3.1 %collective-permute-start.2 = (bf16[1,144,1152]{2,1,0:T(8,128)(2,1)S(1)}, bf16[1,144,1152]{2,1,0:T(8,128)(2,1)S(1)}, u32[]{:S(2)}, u32[]{:S(2)}) collective-permute-start(bf16[1,144,1152]{2,1,0:T(8,128)(2,1)S(1)} %get-tuple-element.20), channel_id=1, source_target_pairs={{0,16},{16,32},{32,48},{48,64},{64,80},{80,96},{96,112},{1,17},{17... | collective-permute-start | bytes 995336 | tf_op jit(solution)/shard_map/ppermute | solution.py:27
  22.5 4.3 %collective-permute-start.3 = (bf16[1,144,1152]{2,1,0:T(8,128)(2,1)S(1)}, bf16[1,144,1152]{2,1,0:T(8,128)(2,1)S(1)}, u32[]{:S(2)}, u32[]{:S(2)}) collective-permute-start(bf16[1,144,1152]{2,1,0:T(8,128)(2,1)S(1)} %get-tuple-element.19), channel_id=1, source_target_pairs={{16,0},{32,16},{48,32},{64,48},{80,64},{96,80},{112,96},{17,1},{33... | collective-permute-start | bytes 995336 | tf_op jit(solution)/shard_map/ppermute | solution.py:27
  26.8 13.1 %shard_map.66 = (bf16[14,4,64,128]{3,2,1,0:T(8,128)(2,1)S(1)}, bf16[2,144,1152]{2,1,0:T(8,128)(2,1)S(1)}) custom-call(s32[1]{0:T(128)} %bitcast.keep_ref, bf16[16,2,64,128]{3,2,1,0:T(8,128)(2,1)S(1)} %collective-permute-done.above_ref, bf16[16,8,64,128]{3,2,1,0:T(8,128)(2,1)S(1)} %copy-done, bf16[16,1,64,128]{3,2,1,0:T(8,128)(2,1)S(1)} %collective-permute-done.1.below_ref, ...), custom_call_target="tpu_custom_call" | custom-call | flops 5284823040 | bytes 4194304 | tf_op jit(solution)/shard_map/pallas_call | solution.py:200
  39.9 0.0 collective-permute-done.2.before_ref
  39.9 0.0 collective-permute-done.3.after_ref
  39.9 1.3 %shard_map.67 = bf16[2,4,64,128]{3,2,1,0:T(8,128)(2,1)S(1)} custom-call(s32[1]{0:T(128)} %bitcast.keep_ref, bf16[16,2,64,128]{3,2,1,0:T(8,128)(2,1)S(1)} %collective-permute-done.above_ref, bf16[16,8,64,128]{3,2,1,0:T(8,128)(2,1)S(1)} %copy-done, bf16[16,1,64,128]{3,2,1,0:T(8,128)(2,1)S(1)} %collective-permute-done.1.below_ref, ...), custom_call_target="tpu_custom_call" | custom-call | tf_op jit(solution)/shard_map/pallas_call | solution.py:214
  41.3 0.0 copy-start.2
  41.3 0.1 pad_maximum_fusion.xp_ref
  41.5 0.7 fusion.3
  42.2 3.3 %collective-permute-start.4 = (bf16[16,1,64,128]{3,2,1,0:T(8,128)(2,1)}, bf16[16,1,64,128]{3,2,1,0:T(8,128)(2,1)S(1)}, u32[]{:S(2)}, u32[]{:S(2)}) collective-permute-start(bf16[16,1,64,128]{3,2,1,0:T(8,128)(2,1)} %get-tuple-element.18), channel_id=1, source_target_pairs={{0,1},{1,2},{2,3},{3,4},{4,5},{5,6},{6,7},{7,8},{8,9},{9,10},{10,1... | collective-permute-start | bytes 786440 | tf_op jit(solution)/shard_map/ppermute | solution.py:27
  45.6 1.9 %collective-permute-start.5 = (bf16[16,1,64,128]{3,2,1,0:T(8,128)(2,1)S(1)}, bf16[16,1,64,128]{3,2,1,0:T(8,128)(2,1)S(1)}, u32[]{:S(2)}, u32[]{:S(2)}) collective-permute-start(bf16[16,1,64,128]{3,2,1,0:T(8,128)(2,1)S(1)} %get-tuple-element.17), channel_id=1, source_target_pairs={{1,0},{2,1},{3,2},{4,3},{5,4},{6,5},{7,6},{8,7},{9,8},{10,9},{11,1... | collective-permute-start | bytes 786440 | tf_op jit(solution)/shard_map/ppermute | solution.py:27
  47.5 0.0 copy-done.2
  47.5 0.4 copy.16
  47.9 0.0 copy-start.1
  47.9 1.3 %collective-permute-done.4.above_ref = bf16[16,1,64,128]{3,2,1,0:T(8,128)(2,1)S(1)} collective-permute-done((bf16[16,1,64,128]{3,2,1,0:T(8,128)(2,1)}, bf16[16,1,64,128]{3,2,1,0:T(8,128)(2,1)S(1)}, u32[]{:S(2)}, u32[]{:S(2)}) %collective-permute-start.4) | collective-permute-done | bytes 262176 | tf_op jit(solution)/shard_map/ppermute | solution.py:27
  49.2 7.7 %collective-permute-done.5.below_ref = bf16[16,1,64,128]{3,2,1,0:T(8,128)(2,1)S(1)} collective-permute-done((bf16[16,1,64,128]{3,2,1,0:T(8,128)(2,1)S(1)}, bf16[16,1,64,128]{3,2,1,0:T(8,128)(2,1)S(1)}, u32[]{:S(2)}, u32[]{:S(2)}) %collective-permute-start.5) | collective-permute-done | bytes 262176 | tf_op jit(solution)/shard_map/ppermute | solution.py:27
  56.9 0.8 %shard_map.68.edge_ref = bf16[2,256,288]{2,1,0:T(8,128)(2,1)S(1)} custom-call(bf16[16,1,64,128]{3,2,1,0:T(8,128)(2,1)S(1)} %collective-permute-done.4.above_ref, bf16[16,4,64,128]{3,2,1,0:T(8,128)(2,1)S(1)} %pad_maximum_fusion.xp_ref, bf16[16,1,64,128]{3,2,1,0:T(8,128)(2,1)S(1)} %collective-permute-done.5.below_ref, bf16[1152,288]{1,0:T(8,128)(2,1)S(1)} %bitcast.11), custom_call_target="tpu_custom_call" | custom-call | flops 339738624 | bytes 1048576 | tf_op jit(solution)/shard_map/pallas_call | solution.py:317
  57.7 1.9 %collective-permute-start.6 = (bf16[1,256,288]{2,1,0:T(8,128)(2,1)S(1)}, bf16[1,256,288]{2,1,0:T(8,128)(2,1)S(1)}, u32[]{:S(2)}, u32[]{:S(2)}) collective-permute-start(bf16[1,256,288]{2,1,0:T(8,128)(2,1)S(1)} %get-tuple-element.22), channel_id=1, source_target_pairs={{0,16},{16,32},{32,48},{48,64},{64,80},{80,96},{96,112},{1,17},{17... | collective-permute-start | bytes 442376 | tf_op jit(solution)/shard_map/ppermute | solution.py:27
  59.6 5.5 %collective-permute-start.7 = (bf16[1,256,288]{2,1,0:T(8,128)(2,1)S(1)}, bf16[1,256,288]{2,1,0:T(8,128)(2,1)S(1)}, u32[]{:S(2)}, u32[]{:S(2)}) collective-permute-start(bf16[1,256,288]{2,1,0:T(8,128)(2,1)S(1)} %get-tuple-element.21), channel_id=1, source_target_pairs={{16,0},{32,16},{48,32},{64,48},{80,64},{96,80},{112,96},{17,1},{33... | collective-permute-start | bytes 442376 | tf_op jit(solution)/shard_map/ppermute | solution.py:27
  65.1 0.0 copy-done.1
  65.1 9.0 %shard_map.69 = (bf16[14,4,64,128]{3,2,1,0:T(8,128)(2,1)S(1)}, bf16[2,256,288]{2,1,0:T(8,128)(2,1)S(1)}) custom-call(bf16[16,1,64,128]{3,2,1,0:T(8,128)(2,1)S(1)} %collective-permute-done.4.above_ref, bf16[16,4,64,128]{3,2,1,0:T(8,128)(2,1)S(1)} %pad_maximum_fusion.xp_ref, bf16[16,1,64,128]{3,2,1,0:T(8,128)(2,1)S(1)} %collective-permute-done.5.below_ref, ...), custom_call_target="tpu_custom_call" | custom-call | flops 3623878656 | bytes 2097152 | tf_op jit(solution)/shard_map/pallas_call | solution.py:329
  74.2 0.0 collective-permute-done.6.before_ref
  74.2 0.0 collective-permute-done.7.after_ref
  74.2 0.4 shard_map.70
  74.7 1.1 %pad_maximum_fusion.1 = bf16[16,4,64,128]{3,2,1,0:T(8,128)(2,1)} fusion(bf16[1,4,64,128]{3,2,1,0:T(8,128)(2,1)S(1)} %get-tuple-element.24, bf16[14,4,64,128]{3,2,1,0:T(8,128)(2,1)S(1)} %get-tuple-element.16, bf16[1,4,64,128]{3,2,1,0:T(8,128)(2,1)S(1)} %get-tuple-element.23), kind=kLoop, calls=%fused_computation.1 | loop fusion | flops 1048576 | bytes 2097152 | tf_op jit(solution)/shard_map/concatenate | solution.py:352
  (3 shorter events, 0.1 us)
Async XLA Ops:
  0.0 18.5 %copy-start = (bf16[16,8,64,128]{3,2,1,0:T(8,128)(2,1)S(1)}, bf16[16,8,64,128]{3,2,1,0:T(8,128)(2,1)}, u32[]{:S(2)}) copy-start(bf16[16,8,64,128]{3,2,1,0:T(8,128)(2,1)} %xp_ref.5) | copy-start | bytes 6291460
  0.0 8.9 %copy-start.4 = (bf16[3,64,144]{2,1,0:T(8,128)(2,1)S(1)}, bf16[3,64,144]{2,1,0:T(8,128)(2,1)}, u32[]{:S(2)}) copy-start(bf16[3,64,144]{2,1,0:T(8,128)(2,1)} %param.8) | copy-start | bytes 165892
  0.0 10.3 %copy-start.3 = (bf16[3,3,128,64]{2,3,1,0:T(8,128)(2,1)S(1)}, bf16[3,3,128,64]{2,3,1,0:T(8,128)(2,1)}, u32[]{:S(2)}) copy-start(bf16[3,3,128,64]{2,3,1,0:T(8,128)(2,1)} %param.9) | copy-start | bytes 442372
  2.2 16.3 %collective-permute-start = (bf16[16,2,64,128]{3,2,1,0:T(8,128)(2,1)}, bf16[16,2,64,128]{3,2,1,0:T(8,128)(2,1)S(1)}, u32[]{:S(2)}, u32[]{:S(2)}) collective-permute-start(bf16[16,2,64,128]{3,2,1,0:T(8,128)(2,1)} %get-tuple-element.11), channel_id=1, source_target_pairs={{0,1},{1,2},{2,3},{3,4},{4,5},{5,6},{6,7},{7,8},{8,9},{9,10},{10,1... | collective-permute-start | bytes 1572872 | tf_op jit(solution)/shard_map/ppermute | solution.py:27
  7.0 11.5 %collective-permute-start.1 = (bf16[16,1,64,128]{3,2,1,0:T(8,128)(2,1)}, bf16[16,1,64,128]{3,2,1,0:T(8,128)(2,1)S(1)}, u32[]{:S(2)}, u32[]{:S(2)}) collective-permute-start(bf16[16,1,64,128]{3,2,1,0:T(8,128)(2,1)} %get-tuple-element.12), channel_id=1, source_target_pairs={{1,0},{2,1},{3,2},{4,3},{5,4},{6,5},{7,6},{8,7},{9,8},{10,9},{11,1... | collective-permute-start | bytes 786440 | tf_op jit(solution)/shard_map/ppermute | solution.py:27
  19.4 20.5 %collective-permute-start.2 = (bf16[1,144,1152]{2,1,0:T(8,128)(2,1)S(1)}, bf16[1,144,1152]{2,1,0:T(8,128)(2,1)S(1)}, u32[]{:S(2)}, u32[]{:S(2)}) collective-permute-start(bf16[1,144,1152]{2,1,0:T(8,128)(2,1)S(1)} %get-tuple-element.20), channel_id=1, source_target_pairs={{0,16},{16,32},{32,48},{48,64},{64,80},{80,96},{96,112},{1,17},{17... | collective-permute-start | bytes 995336 | tf_op jit(solution)/shard_map/ppermute | solution.py:27
  22.5 17.4 %collective-permute-start.3 = (bf16[1,144,1152]{2,1,0:T(8,128)(2,1)S(1)}, bf16[1,144,1152]{2,1,0:T(8,128)(2,1)S(1)}, u32[]{:S(2)}, u32[]{:S(2)}) collective-permute-start(bf16[1,144,1152]{2,1,0:T(8,128)(2,1)S(1)} %get-tuple-element.19), channel_id=1, source_target_pairs={{16,0},{32,16},{48,32},{64,48},{80,64},{96,80},{112,96},{17,1},{33... | collective-permute-start | bytes 995336 | tf_op jit(solution)/shard_map/ppermute | solution.py:27
  41.3 6.2 %copy-start.2 = (bf16[3,3,288,128]{3,2,1,0:T(8,128)(2,1)S(1)}, bf16[3,3,288,128]{3,2,1,0:T(8,128)(2,1)}, u32[]{:S(2)}) copy-start(bf16[3,3,288,128]{3,2,1,0:T(8,128)(2,1)} %param.10) | copy-start | bytes 1990660
  42.2 7.0 %collective-permute-start.4 = (bf16[16,1,64,128]{3,2,1,0:T(8,128)(2,1)}, bf16[16,1,64,128]{3,2,1,0:T(8,128)(2,1)S(1)}, u32[]{:S(2)}, u32[]{:S(2)}) collective-permute-start(bf16[16,1,64,128]{3,2,1,0:T(8,128)(2,1)} %get-tuple-element.18), channel_id=1, source_target_pairs={{0,1},{1,2},{2,3},{3,4},{4,5},{5,6},{6,7},{7,8},{8,9},{9,10},{10,1... | collective-permute-start | bytes 786440 | tf_op jit(solution)/shard_map/ppermute | solution.py:27
  45.6 11.3 %collective-permute-start.5 = (bf16[16,1,64,128]{3,2,1,0:T(8,128)(2,1)S(1)}, bf16[16,1,64,128]{3,2,1,0:T(8,128)(2,1)S(1)}, u32[]{:S(2)}, u32[]{:S(2)}) collective-permute-start(bf16[16,1,64,128]{3,2,1,0:T(8,128)(2,1)S(1)} %get-tuple-element.17), channel_id=1, source_target_pairs={{1,0},{2,1},{3,2},{4,3},{5,4},{6,5},{7,6},{8,7},{9,8},{10,9},{11,1... | collective-permute-start | bytes 786440 | tf_op jit(solution)/shard_map/ppermute | solution.py:27
  47.9 17.2 %copy-start.1 = (bf16[3,128,288]{1,2,0:T(8,128)(2,1)S(1)}, bf16[3,128,288]{1,2,0:T(8,128)(2,1)}, u32[]{:S(2)}) copy-start(bf16[3,128,288]{1,2,0:T(8,128)(2,1)} %param.11) | copy-start | bytes 663556
  57.7 16.5 %collective-permute-start.6 = (bf16[1,256,288]{2,1,0:T(8,128)(2,1)S(1)}, bf16[1,256,288]{2,1,0:T(8,128)(2,1)S(1)}, u32[]{:S(2)}, u32[]{:S(2)}) collective-permute-start(bf16[1,256,288]{2,1,0:T(8,128)(2,1)S(1)} %get-tuple-element.22), channel_id=1, source_target_pairs={{0,16},{16,32},{32,48},{48,64},{64,80},{80,96},{96,112},{1,17},{17... | collective-permute-start | bytes 442376 | tf_op jit(solution)/shard_map/ppermute | solution.py:27
  59.6 14.5 %collective-permute-start.7 = (bf16[1,256,288]{2,1,0:T(8,128)(2,1)S(1)}, bf16[1,256,288]{2,1,0:T(8,128)(2,1)S(1)}, u32[]{:S(2)}, u32[]{:S(2)}) collective-permute-start(bf16[1,256,288]{2,1,0:T(8,128)(2,1)S(1)} %get-tuple-element.21), channel_id=1, source_target_pairs={{16,0},{32,16},{48,32},{64,48},{80,64},{96,80},{112,96},{17,1},{33... | collective-permute-start | bytes 442376 | tf_op jit(solution)/shard_map/ppermute | solution.py:27

commit v18 on v17

--- a/solution.py
+++ b/solution.py
@@ -64,19 +64,19 @@
     return jnp.where(inside, rolled, jnp.zeros_like(rolled))
 
 
-def _middle_one(refs, f, w9_ref, count=1):
+def _middle_one(refs, fs, w9_ref):
     above_ref, xp_ref, below_ref = refs
     rows = xp_ref.shape[1] + 1
     columns = []
-    for k in range(count):
-        slab = jnp.concatenate([above_ref[f + k], xp_ref[f + k], below_ref[f + k]], axis=0).astype(jnp.float32)
+    for f in fs:
+        slab = jnp.concatenate([above_ref[f], xp_ref[f], below_ref[f]], axis=0).astype(jnp.float32)
         shifted = [_lane_shift(slab, b - 1).astype(jnp.bfloat16) for b in range(3)]
         parts = []
         for a in range(3):
             for b in range(3):
                 parts.append(jnp.concatenate([shifted[b][h + a] for h in range(rows)], axis=1))
         columns.append(jnp.concatenate(parts, axis=0))
-    stacked = columns[0] if count == 1 else jnp.concatenate(columns, axis=1)
+    stacked = columns[0] if len(columns) == 1 else jnp.concatenate(columns, axis=1)
     m = jnp.dot(w9_ref[...], stacked, preferred_element_type=jnp.float32)
     return jnp.maximum(m, 0.0).astype(jnp.bfloat16)
 
@@ -120,8 +120,10 @@
 def _edges_one_kernel(above_ref, xp_ref, below_ref, w9_ref, edge_ref):
     refs = (above_ref, xp_ref, below_ref)
     frames = xp_ref.shape[0]
-    edge_ref[0] = _middle_one(refs, 0, w9_ref)
-    edge_ref[1] = _middle_one(refs, frames - 1, w9_ref)
+    span = edge_ref.shape[-1]
+    m = _middle_one(refs, [0, frames - 1], w9_ref)
+    edge_ref[0] = m[:, :span]
+    edge_ref[1] = m[:, span:]
 
 
 def _inner_one_kernel(keep_ref, above_ref, xp_ref, below_ref, w9_ref, t3_ref, wd_ref, out_ref, side_ref, mid_ref):
@@ -132,7 +134,7 @@
     group = 4 if frames % 4 == 0 else 2
 
     def middle(g, carry):
-        m = _middle_one(refs, group * g, w9_ref, group)
+        m = _middle_one(refs, [group * g + k for k in range(group)], w9_ref)
         for k in range(group):
             mid_ref[group * g + k] = m[:, k * span : (k + 1) * span]
         return carry
@@ -266,7 +268,7 @@
     frames = xp_ref.shape[0]
     plane = mid_ref.shape[1]
 
-    group = 4 if frames % 4 == 0 else 2
+    group = 8 if frames % 8 == 0 else 2
 
     def middle(g, carry):
         f = group * g

time: 76.1 us -> 75.8 us (level)
  no operation moved by 1% of the time
where the time goes in v18:
time: 75.8 us; the launch traced here: 75.4 us
  Pallas kernels  27.4 us (36%)
  starting transfers between devices  26.8 us (35%)
  waiting for transfers between devices  16.9 us (22%)
  local copies, waits for them, and re-layouts  2.78 us (4%)
  other arithmetic  1.33 us (2%)
    ppermute x8, starting transfers between devices, from_behind(): return lax.ppermute(array, axis, pairs)  26.8 us
    ppermute x8, waiting for transfers between devices, from_behind(): return lax.ppermute(array, axis, pairs)  16.9 us
    pallas_call x1, Pallas kernels, block_one(): pl.pallas_call(_inner_one_kernel, out_shape=(jax.ShapeDtypeStruct((frames...  13.1 us
    pallas_call x1, Pallas kernels, block_two(): pl.pallas_call(_inner_two_kernel, out_shape=(jax.ShapeDtypeStruct((frames...  8.75 us
    pallas_call x1, Pallas kernels, edge_rows(): pl.pallas_call(_copy_kernel, grid=(1,), out_shape=(jax.ShapeDtypeStruct((...  2.17 us
  transfers between devices with their start and end apart: 8, of which 3 were waited for; matrix products, arithmetic and copies ran while one was open for 3% of the time, Pallas kernels for 29%

profile of v18, /device:TPU:57, one launch (start us, length us, event | category | flops | bytes accessed | tf_op | source)
XLA Modules:
  0.0 75.4 jit_solution(4939905655574575412)
XLA Ops:
  0.0 0.0 copy-start
  0.0 0.0 copy-start.4
  0.0 0.0 copy-start.3
  0.0 2.2 %shard_map.64 = (bf16[16,2,64,128]{3,2,1,0:T(8,128)(2,1)}, bf16[16,1,64,128]{3,2,1,0:T(8,128)(2,1)}) custom-call(bf16[16,8,64,128]{3,2,1,0:T(8,128)(2,1)} %xp_ref.5, bf16[16,8,64,128]{3,2,1,0:T(8,128)(2,1)} %xp_ref.5), custom_call_target="tpu_custom_call" | custom-call | tf_op jit(solution)/shard_map/pallas_call | solution.py:366
  2.2 4.8 %collective-permute-start = (bf16[16,2,64,128]{3,2,1,0:T(8,128)(2,1)}, bf16[16,2,64,128]{3,2,1,0:T(8,128)(2,1)S(1)}, u32[]{:S(2)}, u32[]{:S(2)}) collective-permute-start(bf16[16,2,64,128]{3,2,1,0:T(8,128)(2,1)} %get-tuple-element.11), channel_id=1, source_target_pairs={{0,1},{1,2},{2,3},{3,4},{4,5},{5,6},{6,7},{7,8},{8,9},{9,10},{10,1... | collective-permute-start | bytes 1572872 | tf_op jit(solution)/shard_map/ppermute | solution.py:27
  7.0 1.9 %collective-permute-start.1 = (bf16[16,1,64,128]{3,2,1,0:T(8,128)(2,1)}, bf16[16,1,64,128]{3,2,1,0:T(8,128)(2,1)S(1)}, u32[]{:S(2)}, u32[]{:S(2)}) collective-permute-start(bf16[16,1,64,128]{3,2,1,0:T(8,128)(2,1)} %get-tuple-element.12), channel_id=1, source_target_pairs={{1,0},{2,1},{3,2},{4,3},{5,4},{6,5},{7,6},{8,7},{9,8},{10,9},{11,1... | collective-permute-start | bytes 786440 | tf_op jit(solution)/shard_map/ppermute | solution.py:27
  8.9 0.0 copy-done.4
  8.9 0.1 copy.11
  9.0 0.1 reshape.19.t3_ref
  9.2 1.1 %copy.12.w9_ref = bf16[144,576]{1,0:T(8,128)(2,1)S(1)} copy(bf16[144,576]{0,1:T(8,128)(2,1)} %bitcast.16) | data formatting | bytes 331776 | tf_op jit(solution)/shard_map/reshape | solution.py:175
  10.3 0.0 copy-done.3
  10.3 0.2 copy.15.wd_ref
  10.5 0.1 fusion.2.t3_ref
  10.6 8.0 %collective-permute-done.1.below_ref = bf16[16,1,64,128]{3,2,1,0:T(8,128)(2,1)S(1)} collective-permute-done((bf16[16,1,64,128]{3,2,1,0:T(8,128)(2,1)}, bf16[16,1,64,128]{3,2,1,0:T(8,128)(2,1)S(1)}, u32[]{:S(2)}, u32[]{:S(2)}) %collective-permute-start.1) | collective-permute-done | bytes 262176 | tf_op jit(solution)/shard_map/ppermute | solution.py:27
  18.5 0.0 collective-permute-done.above_ref
  18.5 0.0 copy-done
  18.5 0.8 %shard_map.65.edge_ref = bf16[2,144,1152]{2,1,0:T(8,128)(2,1)S(1)} custom-call(bf16[16,2,64,128]{3,2,1,0:T(8,128)(2,1)S(1)} %collective-permute-done.above_ref, bf16[16,8,64,128]{3,2,1,0:T(8,128)(2,1)S(1)} %copy-done, bf16[16,1,64,128]{3,2,1,0:T(8,128)(2,1)S(1)} %collective-permute-done.1.below_ref, bf16[144,576]{1,0:T(8,128)(2,1)S(1)} %copy.12.w9_ref), custom_call_target="tpu_custom_call" | custom-call | flops 382205952 | bytes 2097152 | tf_op jit(solution)/shard_map/pallas_call | solution.py:192
  19.3 0.1 fusion.4
  19.4 3.1 %collective-permute-start.2 = (bf16[1,144,1152]{2,1,0:T(8,128)(2,1)S(1)}, bf16[1,144,1152]{2,1,0:T(8,128)(2,1)S(1)}, u32[]{:S(2)}, u32[]{:S(2)}) collective-permute-start(bf16[1,144,1152]{2,1,0:T(8,128)(2,1)S(1)} %get-tuple-element.20), channel_id=1, source_target_pairs={{0,16},{16,32},{32,48},{48,64},{64,80},{80,96},{96,112},{1,17},{17... | collective-permute-start | bytes 995336 | tf_op jit(solution)/shard_map/ppermute | solution.py:27
  22.5 4.3 %collective-permute-start.3 = (bf16[1,144,1152]{2,1,0:T(8,128)(2,1)S(1)}, bf16[1,144,1152]{2,1,0:T(8,128)(2,1)S(1)}, u32[]{:S(2)}, u32[]{:S(2)}) collective-permute-start(bf16[1,144,1152]{2,1,0:T(8,128)(2,1)S(1)} %get-tuple-element.19), channel_id=1, source_target_pairs={{16,0},{32,16},{48,32},{64,48},{80,64},{96,80},{112,96},{17,1},{33... | collective-permute-start | bytes 995336 | tf_op jit(solution)/shard_map/ppermute | solution.py:27
  26.8 13.1 %shard_map.66 = (bf16[14,4,64,128]{3,2,1,0:T(8,128)(2,1)S(1)}, bf16[2,144,1152]{2,1,0:T(8,128)(2,1)S(1)}) custom-call(s32[1]{0:T(128)} %bitcast.keep_ref, bf16[16,2,64,128]{3,2,1,0:T(8,128)(2,1)S(1)} %collective-permute-done.above_ref, bf16[16,8,64,128]{3,2,1,0:T(8,128)(2,1)S(1)} %copy-done, bf16[16,1,64,128]{3,2,1,0:T(8,128)(2,1)S(1)} %collective-permute-done.1.below_ref, ...), custom_call_target="tpu_custom_call" | custom-call | flops 5284823040 | bytes 4194304 | tf_op jit(solution)/shard_map/pallas_call | solution.py:202
  39.9 0.0 collective-permute-done.2.before_ref
  39.9 0.0 collective-permute-done.3.after_ref
  39.9 1.3 %shard_map.67 = bf16[2,4,64,128]{3,2,1,0:T(8,128)(2,1)S(1)} custom-call(s32[1]{0:T(128)} %bitcast.keep_ref, bf16[16,2,64,128]{3,2,1,0:T(8,128)(2,1)S(1)} %collective-permute-done.above_ref, bf16[16,8,64,128]{3,2,1,0:T(8,128)(2,1)S(1)} %copy-done, bf16[16,1,64,128]{3,2,1,0:T(8,128)(2,1)S(1)} %collective-permute-done.1.below_ref, ...), custom_call_target="tpu_custom_call" | custom-call | tf_op jit(solution)/shard_map/pallas_call | solution.py:216
  41.2 0.0 copy-start.2
  41.3 0.1 pad_maximum_fusion.xp_ref
  41.4 0.7 fusion.3
  42.1 3.4 %collective-permute-start.4 = (bf16[16,1,64,128]{3,2,1,0:T(8,128)(2,1)}, bf16[16,1,64,128]{3,2,1,0:T(8,128)(2,1)S(1)}, u32[]{:S(2)}, u32[]{:S(2)}) collective-permute-start(bf16[16,1,64,128]{3,2,1,0:T(8,128)(2,1)} %get-tuple-element.18), channel_id=1, source_target_pairs={{0,1},{1,2},{2,3},{3,4},{4,5},{5,6},{6,7},{7,8},{8,9},{9,10},{10,1... | collective-permute-start | bytes 786440 | tf_op jit(solution)/shard_map/ppermute | solution.py:27
  45.5 1.9 %collective-permute-start.5 = (bf16[16,1,64,128]{3,2,1,0:T(8,128)(2,1)S(1)}, bf16[16,1,64,128]{3,2,1,0:T(8,128)(2,1)S(1)}, u32[]{:S(2)}, u32[]{:S(2)}) collective-permute-start(bf16[16,1,64,128]{3,2,1,0:T(8,128)(2,1)S(1)} %get-tuple-element.17), channel_id=1, source_target_pairs={{1,0},{2,1},{3,2},{4,3},{5,4},{6,5},{7,6},{8,7},{9,8},{10,9},{11,1... | collective-permute-start | bytes 786440 | tf_op jit(solution)/shard_map/ppermute | solution.py:27
  47.4 0.0 copy-done.2
  47.4 0.4 copy.16
  47.9 0.0 copy-start.1
  47.9 1.3 %collective-permute-done.4.above_ref = bf16[16,1,64,128]{3,2,1,0:T(8,128)(2,1)S(1)} collective-permute-done((bf16[16,1,64,128]{3,2,1,0:T(8,128)(2,1)}, bf16[16,1,64,128]{3,2,1,0:T(8,128)(2,1)S(1)}, u32[]{:S(2)}, u32[]{:S(2)}) %collective-permute-start.4) | collective-permute-done | bytes 262176 | tf_op jit(solution)/shard_map/ppermute | solution.py:27
  49.1 7.7 %collective-permute-done.5.below_ref = bf16[16,1,64,128]{3,2,1,0:T(8,128)(2,1)S(1)} collective-permute-done((bf16[16,1,64,128]{3,2,1,0:T(8,128)(2,1)S(1)}, bf16[16,1,64,128]{3,2,1,0:T(8,128)(2,1)S(1)}, u32[]{:S(2)}, u32[]{:S(2)}) %collective-permute-start.5) | collective-permute-done | bytes 262176 | tf_op jit(solution)/shard_map/ppermute | solution.py:27
  56.8 0.8 %shard_map.68.edge_ref = bf16[2,256,288]{2,1,0:T(8,128)(2,1)S(1)} custom-call(bf16[16,1,64,128]{3,2,1,0:T(8,128)(2,1)S(1)} %collective-permute-done.4.above_ref, bf16[16,4,64,128]{3,2,1,0:T(8,128)(2,1)S(1)} %pad_maximum_fusion.xp_ref, bf16[16,1,64,128]{3,2,1,0:T(8,128)(2,1)S(1)} %collective-permute-done.5.below_ref, bf16[1152,288]{1,0:T(8,128)(2,1)S(1)} %bitcast.11), custom_call_target="tpu_custom_call" | custom-call | flops 339738624 | bytes 1048576 | tf_op jit(solution)/shard_map/pallas_call | solution.py:319
  57.7 1.9 %collective-permute-start.6 = (bf16[1,256,288]{2,1,0:T(8,128)(2,1)S(1)}, bf16[1,256,288]{2,1,0:T(8,128)(2,1)S(1)}, u32[]{:S(2)}, u32[]{:S(2)}) collective-permute-start(bf16[1,256,288]{2,1,0:T(8,128)(2,1)S(1)} %get-tuple-element.22), channel_id=1, source_target_pairs={{0,16},{16,32},{32,48},{48,64},{64,80},{80,96},{96,112},{1,17},{17... | collective-permute-start | bytes 442376 | tf_op jit(solution)/shard_map/ppermute | solution.py:27
  59.6 5.5 %collective-permute-start.7 = (bf16[1,256,288]{2,1,0:T(8,128)(2,1)S(1)}, bf16[1,256,288]{2,1,0:T(8,128)(2,1)S(1)}, u32[]{:S(2)}, u32[]{:S(2)}) collective-permute-start(bf16[1,256,288]{2,1,0:T(8,128)(2,1)S(1)} %get-tuple-element.21), channel_id=1, source_target_pairs={{16,0},{32,16},{48,32},{64,48},{80,64},{96,80},{112,96},{17,1},{33... | collective-permute-start | bytes 442376 | tf_op jit(solution)/shard_map/ppermute | solution.py:27
  65.1 0.0 copy-done.1
  65.1 8.7 %shard_map.69 = (bf16[14,4,64,128]{3,2,1,0:T(8,128)(2,1)S(1)}, bf16[2,256,288]{2,1,0:T(8,128)(2,1)S(1)}) custom-call(bf16[16,1,64,128]{3,2,1,0:T(8,128)(2,1)S(1)} %collective-permute-done.4.above_ref, bf16[16,4,64,128]{3,2,1,0:T(8,128)(2,1)S(1)} %pad_maximum_fusion.xp_ref, bf16[16,1,64,128]{3,2,1,0:T(8,128)(2,1)S(1)} %collective-permute-done.5.below_ref, ...), custom_call_target="tpu_custom_call" | custom-call | flops 3623878656 | bytes 2097152 | tf_op jit(solution)/shard_map/pallas_call | solution.py:331
  73.8 0.0 collective-permute-done.6.before_ref
  73.8 0.0 collective-permute-done.7.after_ref
  73.9 0.4 shard_map.70
  74.3 1.1 %pad_maximum_fusion.1 = bf16[16,4,64,128]{3,2,1,0:T(8,128)(2,1)} fusion(bf16[1,4,64,128]{3,2,1,0:T(8,128)(2,1)S(1)} %get-tuple-element.24, bf16[14,4,64,128]{3,2,1,0:T(8,128)(2,1)S(1)} %get-tuple-element.16, bf16[1,4,64,128]{3,2,1,0:T(8,128)(2,1)S(1)} %get-tuple-element.23), kind=kLoop, calls=%fused_computation.1 | loop fusion | flops 1048576 | bytes 2097152 | tf_op jit(solution)/shard_map/concatenate | solution.py:354
  (3 shorter events, 0.1 us)
Async XLA Ops:
  0.0 18.5 %copy-start = (bf16[16,8,64,128]{3,2,1,0:T(8,128)(2,1)S(1)}, bf16[16,8,64,128]{3,2,1,0:T(8,128)(2,1)}, u32[]{:S(2)}) copy-start(bf16[16,8,64,128]{3,2,1,0:T(8,128)(2,1)} %xp_ref.5) | copy-start | bytes 6291460
  0.0 8.9 %copy-start.4 = (bf16[3,64,144]{2,1,0:T(8,128)(2,1)S(1)}, bf16[3,64,144]{2,1,0:T(8,128)(2,1)}, u32[]{:S(2)}) copy-start(bf16[3,64,144]{2,1,0:T(8,128)(2,1)} %param.8) | copy-start | bytes 165892
  0.0 10.3 %copy-start.3 = (bf16[3,3,128,64]{2,3,1,0:T(8,128)(2,1)S(1)}, bf16[3,3,128,64]{2,3,1,0:T(8,128)(2,1)}, u32[]{:S(2)}) copy-start(bf16[3,3,128,64]{2,3,1,0:T(8,128)(2,1)} %param.9) | copy-start | bytes 442372
  2.2 16.3 %collective-permute-start = (bf16[16,2,64,128]{3,2,1,0:T(8,128)(2,1)}, bf16[16,2,64,128]{3,2,1,0:T(8,128)(2,1)S(1)}, u32[]{:S(2)}, u32[]{:S(2)}) collective-permute-start(bf16[16,2,64,128]{3,2,1,0:T(8,128)(2,1)} %get-tuple-element.11), channel_id=1, source_target_pairs={{0,1},{1,2},{2,3},{3,4},{4,5},{5,6},{6,7},{7,8},{8,9},{9,10},{10,1... | collective-permute-start | bytes 1572872 | tf_op jit(solution)/shard_map/ppermute | solution.py:27
  7.0 11.5 %collective-permute-start.1 = (bf16[16,1,64,128]{3,2,1,0:T(8,128)(2,1)}, bf16[16,1,64,128]{3,2,1,0:T(8,128)(2,1)S(1)}, u32[]{:S(2)}, u32[]{:S(2)}) collective-permute-start(bf16[16,1,64,128]{3,2,1,0:T(8,128)(2,1)} %get-tuple-element.12), channel_id=1, source_target_pairs={{1,0},{2,1},{3,2},{4,3},{5,4},{6,5},{7,6},{8,7},{9,8},{10,9},{11,1... | collective-permute-start | bytes 786440 | tf_op jit(solution)/shard_map/ppermute | solution.py:27
  19.4 20.5 %collective-permute-start.2 = (bf16[1,144,1152]{2,1,0:T(8,128)(2,1)S(1)}, bf16[1,144,1152]{2,1,0:T(8,128)(2,1)S(1)}, u32[]{:S(2)}, u32[]{:S(2)}) collective-permute-start(bf16[1,144,1152]{2,1,0:T(8,128)(2,1)S(1)} %get-tuple-element.20), channel_id=1, source_target_pairs={{0,16},{16,32},{32,48},{48,64},{64,80},{80,96},{96,112},{1,17},{17... | collective-permute-start | bytes 995336 | tf_op jit(solution)/shard_map/ppermute | solution.py:27
  22.5 17.4 %collective-permute-start.3 = (bf16[1,144,1152]{2,1,0:T(8,128)(2,1)S(1)}, bf16[1,144,1152]{2,1,0:T(8,128)(2,1)S(1)}, u32[]{:S(2)}, u32[]{:S(2)}) collective-permute-start(bf16[1,144,1152]{2,1,0:T(8,128)(2,1)S(1)} %get-tuple-element.19), channel_id=1, source_target_pairs={{16,0},{32,16},{48,32},{64,48},{80,64},{96,80},{112,96},{17,1},{33... | collective-permute-start | bytes 995336 | tf_op jit(solution)/shard_map/ppermute | solution.py:27
  41.2 6.2 %copy-start.2 = (bf16[3,3,288,128]{3,2,1,0:T(8,128)(2,1)S(1)}, bf16[3,3,288,128]{3,2,1,0:T(8,128)(2,1)}, u32[]{:S(2)}) copy-start(bf16[3,3,288,128]{3,2,1,0:T(8,128)(2,1)} %param.10) | copy-start | bytes 1990660
  42.1 7.0 %collective-permute-start.4 = (bf16[16,1,64,128]{3,2,1,0:T(8,128)(2,1)}, bf16[16,1,64,128]{3,2,1,0:T(8,128)(2,1)S(1)}, u32[]{:S(2)}, u32[]{:S(2)}) collective-permute-start(bf16[16,1,64,128]{3,2,1,0:T(8,128)(2,1)} %get-tuple-element.18), channel_id=1, source_target_pairs={{0,1},{1,2},{2,3},{3,4},{4,5},{5,6},{6,7},{7,8},{8,9},{9,10},{10,1... | collective-permute-start | bytes 786440 | tf_op jit(solution)/shard_map/ppermute | solution.py:27
  45.5 11.3 %collective-permute-start.5 = (bf16[16,1,64,128]{3,2,1,0:T(8,128)(2,1)S(1)}, bf16[16,1,64,128]{3,2,1,0:T(8,128)(2,1)S(1)}, u32[]{:S(2)}, u32[]{:S(2)}) collective-permute-start(bf16[16,1,64,128]{3,2,1,0:T(8,128)(2,1)S(1)} %get-tuple-element.17), channel_id=1, source_target_pairs={{1,0},{2,1},{3,2},{4,3},{5,4},{6,5},{7,6},{8,7},{9,8},{10,9},{11,1... | collective-permute-start | bytes 786440 | tf_op jit(solution)/shard_map/ppermute | solution.py:27
  47.9 17.2 %copy-start.1 = (bf16[3,128,288]{1,2,0:T(8,128)(2,1)S(1)}, bf16[3,128,288]{1,2,0:T(8,128)(2,1)}, u32[]{:S(2)}) copy-start(bf16[3,128,288]{1,2,0:T(8,128)(2,1)} %param.11) | copy-start | bytes 663556
  57.7 16.2 %collective-permute-start.6 = (bf16[1,256,288]{2,1,0:T(8,128)(2,1)S(1)}, bf16[1,256,288]{2,1,0:T(8,128)(2,1)S(1)}, u32[]{:S(2)}, u32[]{:S(2)}) collective-permute-start(bf16[1,256,288]{2,1,0:T(8,128)(2,1)S(1)} %get-tuple-element.22), channel_id=1, source_target_pairs={{0,16},{16,32},{32,48},{48,64},{64,80},{80,96},{96,112},{1,17},{17... | collective-permute-start | bytes 442376 | tf_op jit(solution)/shard_map/ppermute | solution.py:27
  59.6 14.3 %collective-permute-start.7 = (bf16[1,256,288]{2,1,0:T(8,128)(2,1)S(1)}, bf16[1,256,288]{2,1,0:T(8,128)(2,1)S(1)}, u32[]{:S(2)}, u32[]{:S(2)}) collective-permute-start(bf16[1,256,288]{2,1,0:T(8,128)(2,1)S(1)} %get-tuple-element.21), channel_id=1, source_target_pairs={{16,0},{32,16},{48,32},{64,48},{80,64},{96,80},{112,96},{17,1},{33... | collective-permute-start | bytes 442376 | tf_op jit(solution)/shard_map/ppermute | solution.py:27

commit v19 on v18

--- a/solution.py
+++ b/solution.py
@@ -281,18 +281,23 @@
     side_ref[0] = mid_ref[1]
     side_ref[1] = mid_ref[frames - 2]
 
-    def section(g, carry):
-        t = 2 * g + 1
+    def run(t, count):
         s = None
         for k in range(3):
-            pair = jnp.concatenate([mid_ref[t - 1 + k], mid_ref[t + k]], axis=0)
-            d = jnp.dot(pair, t3_ref[k], preferred_element_type=jnp.float32)
+            rows = jnp.concatenate([mid_ref[t - 1 + k + j] for j in range(count)], axis=0)
+            d = jnp.dot(rows, t3_ref[k], preferred_element_type=jnp.float32)
             s = d if s is None else s + d
-        _finish(s[:plane], xp_ref, t, out_ref, t - 1)
-        _finish(s[plane:], xp_ref, t + 1, out_ref, t)
+        for j in range(count):
+            _finish(s[j * plane : (j + 1) * plane], xp_ref, t + j, out_ref, t + j - 1)
+
+    def section(g, carry):
+        run(4 * g + 1, 4)
         return carry
 
-    lax.fori_loop(0, (frames - 2) // 2, section, 0)
+    lax.fori_loop(0, (frames - 2) // 4, section, 0)
+    left = (frames - 2) % 4
+    if left:
+        run(frames - 1 - left, left)
 
 
 def _outer_two_kernel(xp_ref, t3_ref, before_ref, after_ref, edge_ref, side_ref, out_ref):

time: 75.8 us -> 75.3 us (level)
  transfers between devices with their start and end apart: 8 -> 8, of which waited for: 3 -> 3; matrix products, arithmetic and copies ran while one was open for 3% -> 3% of each run, Pallas kernels for 29% -> 28%
where the time goes in v19:
time: 75.3 us; the launch traced here: 75 us
  Pallas kernels  26.9 us (36%)
  starting transfers between devices  26.8 us (36%)
  waiting for transfers between devices  16.9 us (22%)
  local copies, waits for them, and re-layouts  2.78 us (4%)
  other arithmetic  1.33 us (2%)
    ppermute x8, starting transfers between devices, from_behind(): return lax.ppermute(array, axis, pairs)  26.8 us
    ppermute x8, waiting for transfers between devices, from_behind(): return lax.ppermute(array, axis, pairs)  16.9 us
    pallas_call x1, Pallas kernels, block_one(): pl.pallas_call(_inner_one_kernel, out_shape=(jax.ShapeDtypeStruct((frames...  13.1 us
    pallas_call x1, Pallas kernels, block_two(): pl.pallas_call(_inner_two_kernel, out_shape=(jax.ShapeDtypeStruct((frames...  8.27 us
    pallas_call x1, Pallas kernels, edge_rows(): pl.pallas_call(_copy_kernel, grid=(1,), out_shape=(jax.ShapeDtypeStruct((...  2.17 us
  transfers between devices with their start and end apart: 8, of which 3 were waited for; matrix products, arithmetic and copies ran while one was open for 3% of the time, Pallas kernels for 28%

profile of v19, /device:TPU:57, one launch (start us, length us, event | category | flops | bytes accessed | tf_op | source)
XLA Modules:
  0.0 75.0 jit_solution(12178359516250585896)
XLA Ops:
  0.0 0.0 copy-start
  0.0 0.0 copy-start.4
  0.0 0.0 copy-start.3
  0.0 2.2 %shard_map.64 = (bf16[16,2,64,128]{3,2,1,0:T(8,128)(2,1)}, bf16[16,1,64,128]{3,2,1,0:T(8,128)(2,1)}) custom-call(bf16[16,8,64,128]{3,2,1,0:T(8,128)(2,1)} %xp_ref.5, bf16[16,8,64,128]{3,2,1,0:T(8,128)(2,1)} %xp_ref.5), custom_call_target="tpu_custom_call" | custom-call | tf_op jit(solution)/shard_map/pallas_call | solution.py:371
  2.2 4.8 %collective-permute-start = (bf16[16,2,64,128]{3,2,1,0:T(8,128)(2,1)}, bf16[16,2,64,128]{3,2,1,0:T(8,128)(2,1)S(1)}, u32[]{:S(2)}, u32[]{:S(2)}) collective-permute-start(bf16[16,2,64,128]{3,2,1,0:T(8,128)(2,1)} %get-tuple-element.11), channel_id=1, source_target_pairs={{0,1},{1,2},{2,3},{3,4},{4,5},{5,6},{6,7},{7,8},{8,9},{9,10},{10,1... | collective-permute-start | bytes 1572872 | tf_op jit(solution)/shard_map/ppermute | solution.py:27
  7.0 1.9 %collective-permute-start.1 = (bf16[16,1,64,128]{3,2,1,0:T(8,128)(2,1)}, bf16[16,1,64,128]{3,2,1,0:T(8,128)(2,1)S(1)}, u32[]{:S(2)}, u32[]{:S(2)}) collective-permute-start(bf16[16,1,64,128]{3,2,1,0:T(8,128)(2,1)} %get-tuple-element.12), channel_id=1, source_target_pairs={{1,0},{2,1},{3,2},{4,3},{5,4},{6,5},{7,6},{8,7},{9,8},{10,9},{11,1... | collective-permute-start | bytes 786440 | tf_op jit(solution)/shard_map/ppermute | solution.py:27
  8.9 0.0 copy-done.4
  8.9 0.1 copy.11
  9.0 0.1 reshape.19.t3_ref
  9.2 1.1 %copy.12.w9_ref = bf16[144,576]{1,0:T(8,128)(2,1)S(1)} copy(bf16[144,576]{0,1:T(8,128)(2,1)} %bitcast.16) | data formatting | bytes 331776 | tf_op jit(solution)/shard_map/reshape | solution.py:175
  10.3 0.0 copy-done.3
  10.3 0.2 copy.15.wd_ref
  10.5 0.1 fusion.2.t3_ref
  10.6 8.0 %collective-permute-done.1.below_ref = bf16[16,1,64,128]{3,2,1,0:T(8,128)(2,1)S(1)} collective-permute-done((bf16[16,1,64,128]{3,2,1,0:T(8,128)(2,1)}, bf16[16,1,64,128]{3,2,1,0:T(8,128)(2,1)S(1)}, u32[]{:S(2)}, u32[]{:S(2)}) %collective-permute-start.1) | collective-permute-done | bytes 262176 | tf_op jit(solution)/shard_map/ppermute | solution.py:27
  18.5 0.0 collective-permute-done.above_ref
  18.5 0.0 copy-done
  18.5 0.8 %shard_map.65.edge_ref = bf16[2,144,1152]{2,1,0:T(8,128)(2,1)S(1)} custom-call(bf16[16,2,64,128]{3,2,1,0:T(8,128)(2,1)S(1)} %collective-permute-done.above_ref, bf16[16,8,64,128]{3,2,1,0:T(8,128)(2,1)S(1)} %copy-done, bf16[16,1,64,128]{3,2,1,0:T(8,128)(2,1)S(1)} %collective-permute-done.1.below_ref, bf16[144,576]{1,0:T(8,128)(2,1)S(1)} %copy.12.w9_ref), custom_call_target="tpu_custom_call" | custom-call | flops 382205952 | bytes 2097152 | tf_op jit(solution)/shard_map/pallas_call | solution.py:192
  19.3 0.1 fusion.4
  19.4 3.1 %collective-permute-start.2 = (bf16[1,144,1152]{2,1,0:T(8,128)(2,1)S(1)}, bf16[1,144,1152]{2,1,0:T(8,128)(2,1)S(1)}, u32[]{:S(2)}, u32[]{:S(2)}) collective-permute-start(bf16[1,144,1152]{2,1,0:T(8,128)(2,1)S(1)} %get-tuple-element.20), channel_id=1, source_target_pairs={{0,16},{16,32},{32,48},{48,64},{64,80},{80,96},{96,112},{1,17},{17... | collective-permute-start | bytes 995336 | tf_op jit(solution)/shard_map/ppermute | solution.py:27
  22.5 4.3 %collective-permute-start.3 = (bf16[1,144,1152]{2,1,0:T(8,128)(2,1)S(1)}, bf16[1,144,1152]{2,1,0:T(8,128)(2,1)S(1)}, u32[]{:S(2)}, u32[]{:S(2)}) collective-permute-start(bf16[1,144,1152]{2,1,0:T(8,128)(2,1)S(1)} %get-tuple-element.19), channel_id=1, source_target_pairs={{16,0},{32,16},{48,32},{64,48},{80,64},{96,80},{112,96},{17,1},{33... | collective-permute-start | bytes 995336 | tf_op jit(solution)/shard_map/ppermute | solution.py:27
  26.8 13.1 %shard_map.66 = (bf16[14,4,64,128]{3,2,1,0:T(8,128)(2,1)S(1)}, bf16[2,144,1152]{2,1,0:T(8,128)(2,1)S(1)}) custom-call(s32[1]{0:T(128)} %bitcast.keep_ref, bf16[16,2,64,128]{3,2,1,0:T(8,128)(2,1)S(1)} %collective-permute-done.above_ref, bf16[16,8,64,128]{3,2,1,0:T(8,128)(2,1)S(1)} %copy-done, bf16[16,1,64,128]{3,2,1,0:T(8,128)(2,1)S(1)} %collective-permute-done.1.below_ref, ...), custom_call_target="tpu_custom_call" | custom-call | flops 5284823040 | bytes 4194304 | tf_op jit(solution)/shard_map/pallas_call | solution.py:202
  39.9 0.0 collective-permute-done.2.before_ref
  39.9 0.0 collective-permute-done.3.after_ref
  39.9 1.3 %shard_map.67 = bf16[2,4,64,128]{3,2,1,0:T(8,128)(2,1)S(1)} custom-call(s32[1]{0:T(128)} %bitcast.keep_ref, bf16[16,2,64,128]{3,2,1,0:T(8,128)(2,1)S(1)} %collective-permute-done.above_ref, bf16[16,8,64,128]{3,2,1,0:T(8,128)(2,1)S(1)} %copy-done, bf16[16,1,64,128]{3,2,1,0:T(8,128)(2,1)S(1)} %collective-permute-done.1.below_ref, ...), custom_call_target="tpu_custom_call" | custom-call | tf_op jit(solution)/shard_map/pallas_call | solution.py:216
  41.2 0.0 copy-start.2
  41.3 0.1 pad_maximum_fusion.xp_ref
  41.4 0.7 fusion.3
  42.1 3.4 %collective-permute-start.4 = (bf16[16,1,64,128]{3,2,1,0:T(8,128)(2,1)}, bf16[16,1,64,128]{3,2,1,0:T(8,128)(2,1)S(1)}, u32[]{:S(2)}, u32[]{:S(2)}) collective-permute-start(bf16[16,1,64,128]{3,2,1,0:T(8,128)(2,1)} %get-tuple-element.18), channel_id=1, source_target_pairs={{0,1},{1,2},{2,3},{3,4},{4,5},{5,6},{6,7},{7,8},{8,9},{9,10},{10,1... | collective-permute-start | bytes 786440 | tf_op jit(solution)/shard_map/ppermute | solution.py:27
  45.5 1.9 %collective-permute-start.5 = (bf16[16,1,64,128]{3,2,1,0:T(8,128)(2,1)S(1)}, bf16[16,1,64,128]{3,2,1,0:T(8,128)(2,1)S(1)}, u32[]{:S(2)}, u32[]{:S(2)}) collective-permute-start(bf16[16,1,64,128]{3,2,1,0:T(8,128)(2,1)S(1)} %get-tuple-element.17), channel_id=1, source_target_pairs={{1,0},{2,1},{3,2},{4,3},{5,4},{6,5},{7,6},{8,7},{9,8},{10,9},{11,1... | collective-permute-start | bytes 786440 | tf_op jit(solution)/shard_map/ppermute | solution.py:27
  47.4 0.0 copy-done.2
  47.4 0.4 copy.16
  47.9 0.0 copy-start.1
  47.9 1.3 %collective-permute-done.4.above_ref = bf16[16,1,64,128]{3,2,1,0:T(8,128)(2,1)S(1)} collective-permute-done((bf16[16,1,64,128]{3,2,1,0:T(8,128)(2,1)}, bf16[16,1,64,128]{3,2,1,0:T(8,128)(2,1)S(1)}, u32[]{:S(2)}, u32[]{:S(2)}) %collective-permute-start.4) | collective-permute-done | bytes 262176 | tf_op jit(solution)/shard_map/ppermute | solution.py:27
  49.1 7.7 %collective-permute-done.5.below_ref = bf16[16,1,64,128]{3,2,1,0:T(8,128)(2,1)S(1)} collective-permute-done((bf16[16,1,64,128]{3,2,1,0:T(8,128)(2,1)S(1)}, bf16[16,1,64,128]{3,2,1,0:T(8,128)(2,1)S(1)}, u32[]{:S(2)}, u32[]{:S(2)}) %collective-permute-start.5) | collective-permute-done | bytes 262176 | tf_op jit(solution)/shard_map/ppermute | solution.py:27
  56.8 0.8 %shard_map.68.edge_ref = bf16[2,256,288]{2,1,0:T(8,128)(2,1)S(1)} custom-call(bf16[16,1,64,128]{3,2,1,0:T(8,128)(2,1)S(1)} %collective-permute-done.4.above_ref, bf16[16,4,64,128]{3,2,1,0:T(8,128)(2,1)S(1)} %pad_maximum_fusion.xp_ref, bf16[16,1,64,128]{3,2,1,0:T(8,128)(2,1)S(1)} %collective-permute-done.5.below_ref, bf16[1152,288]{1,0:T(8,128)(2,1)S(1)} %bitcast.11), custom_call_target="tpu_custom_call" | custom-call | flops 339738624 | bytes 1048576 | tf_op jit(solution)/shard_map/pallas_call | solution.py:324
  57.7 1.9 %collective-permute-start.6 = (bf16[1,256,288]{2,1,0:T(8,128)(2,1)S(1)}, bf16[1,256,288]{2,1,0:T(8,128)(2,1)S(1)}, u32[]{:S(2)}, u32[]{:S(2)}) collective-permute-start(bf16[1,256,288]{2,1,0:T(8,128)(2,1)S(1)} %get-tuple-element.22), channel_id=1, source_target_pairs={{0,16},{16,32},{32,48},{48,64},{64,80},{80,96},{96,112},{1,17},{17... | collective-permute-start | bytes 442376 | tf_op jit(solution)/shard_map/ppermute | solution.py:27
  59.6 5.5 %collective-permute-start.7 = (bf16[1,256,288]{2,1,0:T(8,128)(2,1)S(1)}, bf16[1,256,288]{2,1,0:T(8,128)(2,1)S(1)}, u32[]{:S(2)}, u32[]{:S(2)}) collective-permute-start(bf16[1,256,288]{2,1,0:T(8,128)(2,1)S(1)} %get-tuple-element.21), channel_id=1, source_target_pairs={{16,0},{32,16},{48,32},{64,48},{80,64},{96,80},{112,96},{17,1},{33... | collective-permute-start | bytes 442376 | tf_op jit(solution)/shard_map/ppermute | solution.py:27
  65.1 0.0 copy-done.1
  65.1 8.3 %shard_map.69 = (bf16[14,4,64,128]{3,2,1,0:T(8,128)(2,1)S(1)}, bf16[2,256,288]{2,1,0:T(8,128)(2,1)S(1)}) custom-call(bf16[16,1,64,128]{3,2,1,0:T(8,128)(2,1)S(1)} %collective-permute-done.4.above_ref, bf16[16,4,64,128]{3,2,1,0:T(8,128)(2,1)S(1)} %pad_maximum_fusion.xp_ref, bf16[16,1,64,128]{3,2,1,0:T(8,128)(2,1)S(1)} %collective-permute-done.5.below_ref, ...), custom_call_target="tpu_custom_call" | custom-call | flops 3623878656 | bytes 2097152 | tf_op jit(solution)/shard_map/pallas_call | solution.py:336
  73.4 0.0 collective-permute-done.6.before_ref
  73.4 0.0 collective-permute-done.7.after_ref
  73.4 0.4 shard_map.70
  73.9 1.1 %pad_maximum_fusion.1 = bf16[16,4,64,128]{3,2,1,0:T(8,128)(2,1)} fusion(bf16[1,4,64,128]{3,2,1,0:T(8,128)(2,1)S(1)} %get-tuple-element.24, bf16[14,4,64,128]{3,2,1,0:T(8,128)(2,1)S(1)} %get-tuple-element.16, bf16[1,4,64,128]{3,2,1,0:T(8,128)(2,1)S(1)} %get-tuple-element.23), kind=kLoop, calls=%fused_computation.1 | loop fusion | flops 1048576 | bytes 2097152 | tf_op jit(solution)/shard_map/concatenate | solution.py:359
  (3 shorter events, 0.1 us)
Async XLA Ops:
  0.0 18.5 %copy-start = (bf16[16,8,64,128]{3,2,1,0:T(8,128)(2,1)S(1)}, bf16[16,8,64,128]{3,2,1,0:T(8,128)(2,1)}, u32[]{:S(2)}) copy-start(bf16[16,8,64,128]{3,2,1,0:T(8,128)(2,1)} %xp_ref.5) | copy-start | bytes 6291460
  0.0 8.9 %copy-start.4 = (bf16[3,64,144]{2,1,0:T(8,128)(2,1)S(1)}, bf16[3,64,144]{2,1,0:T(8,128)(2,1)}, u32[]{:S(2)}) copy-start(bf16[3,64,144]{2,1,0:T(8,128)(2,1)} %param.8) | copy-start | bytes 165892
  0.0 10.3 %copy-start.3 = (bf16[3,3,128,64]{2,3,1,0:T(8,128)(2,1)S(1)}, bf16[3,3,128,64]{2,3,1,0:T(8,128)(2,1)}, u32[]{:S(2)}) copy-start(bf16[3,3,128,64]{2,3,1,0:T(8,128)(2,1)} %param.9) | copy-start | bytes 442372
  2.2 16.3 %collective-permute-start = (bf16[16,2,64,128]{3,2,1,0:T(8,128)(2,1)}, bf16[16,2,64,128]{3,2,1,0:T(8,128)(2,1)S(1)}, u32[]{:S(2)}, u32[]{:S(2)}) collective-permute-start(bf16[16,2,64,128]{3,2,1,0:T(8,128)(2,1)} %get-tuple-element.11), channel_id=1, source_target_pairs={{0,1},{1,2},{2,3},{3,4},{4,5},{5,6},{6,7},{7,8},{8,9},{9,10},{10,1... | collective-permute-start | bytes 1572872 | tf_op jit(solution)/shard_map/ppermute | solution.py:27
  7.0 11.5 %collective-permute-start.1 = (bf16[16,1,64,128]{3,2,1,0:T(8,128)(2,1)}, bf16[16,1,64,128]{3,2,1,0:T(8,128)(2,1)S(1)}, u32[]{:S(2)}, u32[]{:S(2)}) collective-permute-start(bf16[16,1,64,128]{3,2,1,0:T(8,128)(2,1)} %get-tuple-element.12), channel_id=1, source_target_pairs={{1,0},{2,1},{3,2},{4,3},{5,4},{6,5},{7,6},{8,7},{9,8},{10,9},{11,1... | collective-permute-start | bytes 786440 | tf_op jit(solution)/shard_map/ppermute | solution.py:27
  19.4 20.5 %collective-permute-start.2 = (bf16[1,144,1152]{2,1,0:T(8,128)(2,1)S(1)}, bf16[1,144,1152]{2,1,0:T(8,128)(2,1)S(1)}, u32[]{:S(2)}, u32[]{:S(2)}) collective-permute-start(bf16[1,144,1152]{2,1,0:T(8,128)(2,1)S(1)} %get-tuple-element.20), channel_id=1, source_target_pairs={{0,16},{16,32},{32,48},{48,64},{64,80},{80,96},{96,112},{1,17},{17... | collective-permute-start | bytes 995336 | tf_op jit(solution)/shard_map/ppermute | solution.py:27
  22.5 17.4 %collective-permute-start.3 = (bf16[1,144,1152]{2,1,0:T(8,128)(2,1)S(1)}, bf16[1,144,1152]{2,1,0:T(8,128)(2,1)S(1)}, u32[]{:S(2)}, u32[]{:S(2)}) collective-permute-start(bf16[1,144,1152]{2,1,0:T(8,128)(2,1)S(1)} %get-tuple-element.19), channel_id=1, source_target_pairs={{16,0},{32,16},{48,32},{64,48},{80,64},{96,80},{112,96},{17,1},{33... | collective-permute-start | bytes 995336 | tf_op jit(solution)/shard_map/ppermute | solution.py:27
  41.2 6.2 %copy-start.2 = (bf16[3,3,288,128]{3,2,1,0:T(8,128)(2,1)S(1)}, bf16[3,3,288,128]{3,2,1,0:T(8,128)(2,1)}, u32[]{:S(2)}) copy-start(bf16[3,3,288,128]{3,2,1,0:T(8,128)(2,1)} %param.10) | copy-start | bytes 1990660
  42.1 7.0 %collective-permute-start.4 = (bf16[16,1,64,128]{3,2,1,0:T(8,128)(2,1)}, bf16[16,1,64,128]{3,2,1,0:T(8,128)(2,1)S(1)}, u32[]{:S(2)}, u32[]{:S(2)}) collective-permute-start(bf16[16,1,64,128]{3,2,1,0:T(8,128)(2,1)} %get-tuple-element.18), channel_id=1, source_target_pairs={{0,1},{1,2},{2,3},{3,4},{4,5},{5,6},{6,7},{7,8},{8,9},{9,10},{10,1... | collective-permute-start | bytes 786440 | tf_op jit(solution)/shard_map/ppermute | solution.py:27
  45.5 11.3 %collective-permute-start.5 = (bf16[16,1,64,128]{3,2,1,0:T(8,128)(2,1)S(1)}, bf16[16,1,64,128]{3,2,1,0:T(8,128)(2,1)S(1)}, u32[]{:S(2)}, u32[]{:S(2)}) collective-permute-start(bf16[16,1,64,128]{3,2,1,0:T(8,128)(2,1)S(1)} %get-tuple-element.17), channel_id=1, source_target_pairs={{1,0},{2,1},{3,2},{4,3},{5,4},{6,5},{7,6},{8,7},{9,8},{10,9},{11,1... | collective-permute-start | bytes 786440 | tf_op jit(solution)/shard_map/ppermute | solution.py:27
  47.9 17.2 %copy-start.1 = (bf16[3,128,288]{1,2,0:T(8,128)(2,1)S(1)}, bf16[3,128,288]{1,2,0:T(8,128)(2,1)}, u32[]{:S(2)}) copy-start(bf16[3,128,288]{1,2,0:T(8,128)(2,1)} %param.11) | copy-start | bytes 663556
  57.7 15.7 %collective-permute-start.6 = (bf16[1,256,288]{2,1,0:T(8,128)(2,1)S(1)}, bf16[1,256,288]{2,1,0:T(8,128)(2,1)S(1)}, u32[]{:S(2)}, u32[]{:S(2)}) collective-permute-start(bf16[1,256,288]{2,1,0:T(8,128)(2,1)S(1)} %get-tuple-element.22), channel_id=1, source_target_pairs={{0,16},{16,32},{32,48},{48,64},{64,80},{80,96},{96,112},{1,17},{17... | collective-permute-start | bytes 442376 | tf_op jit(solution)/shard_map/ppermute | solution.py:27
  59.6 13.8 %collective-permute-start.7 = (bf16[1,256,288]{2,1,0:T(8,128)(2,1)S(1)}, bf16[1,256,288]{2,1,0:T(8,128)(2,1)S(1)}, u32[]{:S(2)}, u32[]{:S(2)}) collective-permute-start(bf16[1,256,288]{2,1,0:T(8,128)(2,1)S(1)} %get-tuple-element.21), channel_id=1, source_target_pairs={{16,0},{32,16},{48,32},{64,48},{80,64},{96,80},{112,96},{17,1},{33... | collective-permute-start | bytes 442376 | tf_op jit(solution)/shard_map/ppermute | solution.py:27

commit v20 on v19

--- a/solution.py
+++ b/solution.py
@@ -145,15 +145,28 @@
 
     channels = t3_ref.shape[0] // 2
 
+    span = mid_ref.shape[-1]
+
+    def run(t, pairs):
+        stacks = [
+            jnp.concatenate([mid_ref[u - 1], mid_ref[u], mid_ref[u + 1], mid_ref[u + 2]], axis=0)
+            for u in [t + 2 * p for p in range(pairs)]
+        ]
+        stacked = stacks[0] if pairs == 1 else jnp.concatenate(stacks, axis=1)
+        s = jnp.dot(t3_ref[...], stacked, preferred_element_type=jnp.float32)
+        for p in range(pairs):
+            u = t + 2 * p
+            part = s[:, p * span : (p + 1) * span]
+            _down(part[:channels], refs, u, wd_ref, keep_ref, out_ref, u - 1)
+            _down(part[channels:], refs, u + 1, wd_ref, keep_ref, out_ref, u)
+
     def section(g, carry):
-        t = 2 * g + 1
-        stacked = jnp.concatenate([mid_ref[t - 1], mid_ref[t], mid_ref[t + 1], mid_ref[t + 2]], axis=0)
-        s = jnp.dot(t3_ref[...], stacked, preferred_element_type=jnp.float32)
-        _down(s[:channels], refs, t, wd_ref, keep_ref, out_ref, t - 1)
-        _down(s[channels:], refs, t + 1, wd_ref, keep_ref, out_ref, t)
+        run(4 * g + 1, 2)
         return carry
 
-    lax.fori_loop(0, (frames - 2) // 2, section, 0)
+    lax.fori_loop(0, (frames - 2) // 4, section, 0)
+    if (frames - 2) % 4:
+        run(frames - 3, 1)
 
 
 def _outer_one_kernel(

time: 75.3 us -> 73.6 us (0.977)
  Pallas kernels: 26.9 us -> 25.2 us
    pallas_call x1, Pallas kernels: 13.1 us -> 11.4 us  [block_one(): pl.pallas_call(_inner_one_kernel, out_shape=(jax.ShapeDtypeStruct((frames...]
  transfers between devices with their start and end apart: 8 -> 8, of which waited for: 3 -> 3; matrix products, arithmetic and copies ran while one was open for 3% -> 3% of each run, Pallas kernels for 28% -> 27%
where the time goes in v20:
time: 73.6 us; the launch traced here: 73.2 us
  starting transfers between devices  26.8 us (36%)
  Pallas kernels  25.2 us (34%)
  waiting for transfers between devices  16.9 us (23%)
  local copies, waits for them, and re-layouts  2.78 us (4%)
  other arithmetic  1.33 us (2%)
    ppermute x8, starting transfers between devices, from_behind(): return lax.ppermute(array, axis, pairs)  26.8 us
    ppermute x8, waiting for transfers between devices, from_behind(): return lax.ppermute(array, axis, pairs)  16.9 us
    pallas_call x1, Pallas kernels, block_one(): pl.pallas_call(_inner_one_kernel, out_shape=(jax.ShapeDtypeStruct((frames...  11.4 us
    pallas_call x1, Pallas kernels, block_two(): pl.pallas_call(_inner_two_kernel, out_shape=(jax.ShapeDtypeStruct((frames...  8.27 us
    pallas_call x1, Pallas kernels, edge_rows(): pl.pallas_call(_copy_kernel, grid=(1,), out_shape=(jax.ShapeDtypeStruct((...  2.17 us
  transfers between devices with their start and end apart: 8, of which 3 were waited for; matrix products, arithmetic and copies ran while one was open for 3% of the time, Pallas kernels for 27%

profile of v20, /device:TPU:57, one launch (start us, length us, event | category | flops | bytes accessed | tf_op | source)
XLA Modules:
  0.0 73.2 jit_solution(6633720343540032420)
XLA Ops:
  0.0 0.0 copy-start
  0.0 0.0 copy-start.4
  0.0 0.0 copy-start.3
  0.0 2.2 %shard_map.64 = (bf16[16,2,64,128]{3,2,1,0:T(8,128)(2,1)}, bf16[16,1,64,128]{3,2,1,0:T(8,128)(2,1)}) custom-call(bf16[16,8,64,128]{3,2,1,0:T(8,128)(2,1)} %xp_ref.5, bf16[16,8,64,128]{3,2,1,0:T(8,128)(2,1)} %xp_ref.5), custom_call_target="tpu_custom_call" | custom-call | tf_op jit(solution)/shard_map/pallas_call | solution.py:384
  2.2 4.8 %collective-permute-start = (bf16[16,2,64,128]{3,2,1,0:T(8,128)(2,1)}, bf16[16,2,64,128]{3,2,1,0:T(8,128)(2,1)S(1)}, u32[]{:S(2)}, u32[]{:S(2)}) collective-permute-start(bf16[16,2,64,128]{3,2,1,0:T(8,128)(2,1)} %get-tuple-element.11), channel_id=1, source_target_pairs={{0,1},{1,2},{2,3},{3,4},{4,5},{5,6},{6,7},{7,8},{8,9},{9,10},{10,1... | collective-permute-start | bytes 1572872 | tf_op jit(solution)/shard_map/ppermute | solution.py:27
  7.0 1.9 %collective-permute-start.1 = (bf16[16,1,64,128]{3,2,1,0:T(8,128)(2,1)}, bf16[16,1,64,128]{3,2,1,0:T(8,128)(2,1)S(1)}, u32[]{:S(2)}, u32[]{:S(2)}) collective-permute-start(bf16[16,1,64,128]{3,2,1,0:T(8,128)(2,1)} %get-tuple-element.12), channel_id=1, source_target_pairs={{1,0},{2,1},{3,2},{4,3},{5,4},{6,5},{7,6},{8,7},{9,8},{10,9},{11,1... | collective-permute-start | bytes 786440 | tf_op jit(solution)/shard_map/ppermute | solution.py:27
  8.9 0.0 copy-done.4
  8.9 0.1 copy.11
  9.0 0.1 reshape.19.t3_ref
  9.2 1.1 %copy.12.w9_ref = bf16[144,576]{1,0:T(8,128)(2,1)S(1)} copy(bf16[144,576]{0,1:T(8,128)(2,1)} %bitcast.16) | data formatting | bytes 331776 | tf_op jit(solution)/shard_map/reshape | solution.py:188
  10.3 0.0 copy-done.3
  10.3 0.2 copy.15.wd_ref
  10.5 0.1 fusion.2.t3_ref
  10.6 8.0 %collective-permute-done.1.below_ref = bf16[16,1,64,128]{3,2,1,0:T(8,128)(2,1)S(1)} collective-permute-done((bf16[16,1,64,128]{3,2,1,0:T(8,128)(2,1)}, bf16[16,1,64,128]{3,2,1,0:T(8,128)(2,1)S(1)}, u32[]{:S(2)}, u32[]{:S(2)}) %collective-permute-start.1) | collective-permute-done | bytes 262176 | tf_op jit(solution)/shard_map/ppermute | solution.py:27
  18.5 0.0 collective-permute-done.above_ref
  18.5 0.0 copy-done
  18.5 0.8 %shard_map.65.edge_ref = bf16[2,144,1152]{2,1,0:T(8,128)(2,1)S(1)} custom-call(bf16[16,2,64,128]{3,2,1,0:T(8,128)(2,1)S(1)} %collective-permute-done.above_ref, bf16[16,8,64,128]{3,2,1,0:T(8,128)(2,1)S(1)} %copy-done, bf16[16,1,64,128]{3,2,1,0:T(8,128)(2,1)S(1)} %collective-permute-done.1.below_ref, bf16[144,576]{1,0:T(8,128)(2,1)S(1)} %copy.12.w9_ref), custom_call_target="tpu_custom_call" | custom-call | flops 382205952 | bytes 2097152 | tf_op jit(solution)/shard_map/pallas_call | solution.py:205
  19.3 0.1 fusion.4
  19.4 3.1 %collective-permute-start.2 = (bf16[1,144,1152]{2,1,0:T(8,128)(2,1)S(1)}, bf16[1,144,1152]{2,1,0:T(8,128)(2,1)S(1)}, u32[]{:S(2)}, u32[]{:S(2)}) collective-permute-start(bf16[1,144,1152]{2,1,0:T(8,128)(2,1)S(1)} %get-tuple-element.20), channel_id=1, source_target_pairs={{0,16},{16,32},{32,48},{48,64},{64,80},{80,96},{96,112},{1,17},{17... | collective-permute-start | bytes 995336 | tf_op jit(solution)/shard_map/ppermute | solution.py:27
  22.5 4.3 %collective-permute-start.3 = (bf16[1,144,1152]{2,1,0:T(8,128)(2,1)S(1)}, bf16[1,144,1152]{2,1,0:T(8,128)(2,1)S(1)}, u32[]{:S(2)}, u32[]{:S(2)}) collective-permute-start(bf16[1,144,1152]{2,1,0:T(8,128)(2,1)S(1)} %get-tuple-element.19), channel_id=1, source_target_pairs={{16,0},{32,16},{48,32},{64,48},{80,64},{96,80},{112,96},{17,1},{33... | collective-permute-start | bytes 995336 | tf_op jit(solution)/shard_map/ppermute | solution.py:27
  26.8 11.4 %shard_map.66 = (bf16[14,4,64,128]{3,2,1,0:T(8,128)(2,1)S(1)}, bf16[2,144,1152]{2,1,0:T(8,128)(2,1)S(1)}) custom-call(s32[1]{0:T(128)} %bitcast.keep_ref, bf16[16,2,64,128]{3,2,1,0:T(8,128)(2,1)S(1)} %collective-permute-done.above_ref, bf16[16,8,64,128]{3,2,1,0:T(8,128)(2,1)S(1)} %copy-done, bf16[16,1,64,128]{3,2,1,0:T(8,128)(2,1)S(1)} %collective-permute-done.1.below_ref, ...), custom_call_target="tpu_custom_call" | custom-call | flops 5284823040 | bytes 4194304 | tf_op jit(solution)/shard_map/pallas_call | solution.py:215
  38.1 0.0 collective-permute-done.2.before_ref
  38.1 0.0 collective-permute-done.3.after_ref
  38.2 1.3 %shard_map.67 = bf16[2,4,64,128]{3,2,1,0:T(8,128)(2,1)S(1)} custom-call(s32[1]{0:T(128)} %bitcast.keep_ref, bf16[16,2,64,128]{3,2,1,0:T(8,128)(2,1)S(1)} %collective-permute-done.above_ref, bf16[16,8,64,128]{3,2,1,0:T(8,128)(2,1)S(1)} %copy-done, bf16[16,1,64,128]{3,2,1,0:T(8,128)(2,1)S(1)} %collective-permute-done.1.below_ref, ...), custom_call_target="tpu_custom_call" | custom-call | tf_op jit(solution)/shard_map/pallas_call | solution.py:229
  39.5 0.0 copy-start.2
  39.5 0.1 pad_maximum_fusion.xp_ref
  39.7 0.7 %fusion.3 = (bf16[16,1,64,128]{3,2,1,0:T(8,128)(2,1)S(1)}, bf16[16,1,64,128]{3,2,1,0:T(8,128)(2,1)}) fusion(bf16[16,4,64,128]{3,2,1,0:T(8,128)(2,1)S(1)} %pad_maximum_fusion.xp_ref), kind=kLoop, calls=%fused_computation.7 | loop fusion | bytes 1048576 | tf_op jit(solution)/shard_map/slice | solution.py:405
  40.4 3.4 %collective-permute-start.4 = (bf16[16,1,64,128]{3,2,1,0:T(8,128)(2,1)}, bf16[16,1,64,128]{3,2,1,0:T(8,128)(2,1)S(1)}, u32[]{:S(2)}, u32[]{:S(2)}) collective-permute-start(bf16[16,1,64,128]{3,2,1,0:T(8,128)(2,1)} %get-tuple-element.18), channel_id=1, source_target_pairs={{0,1},{1,2},{2,3},{3,4},{4,5},{5,6},{6,7},{7,8},{8,9},{9,10},{10,1... | collective-permute-start | bytes 786440 | tf_op jit(solution)/shard_map/ppermute | solution.py:27
  43.8 1.9 %collective-permute-start.5 = (bf16[16,1,64,128]{3,2,1,0:T(8,128)(2,1)S(1)}, bf16[16,1,64,128]{3,2,1,0:T(8,128)(2,1)S(1)}, u32[]{:S(2)}, u32[]{:S(2)}) collective-permute-start(bf16[16,1,64,128]{3,2,1,0:T(8,128)(2,1)S(1)} %get-tuple-element.17), channel_id=1, source_target_pairs={{1,0},{2,1},{3,2},{4,3},{5,4},{6,5},{7,6},{8,7},{9,8},{10,9},{11,1... | collective-permute-start | bytes 786440 | tf_op jit(solution)/shard_map/ppermute | solution.py:27
  45.7 0.0 copy-done.2
  45.7 0.4 copy.16
  46.1 0.0 copy-start.1
  46.1 1.3 %collective-permute-done.4.above_ref = bf16[16,1,64,128]{3,2,1,0:T(8,128)(2,1)S(1)} collective-permute-done((bf16[16,1,64,128]{3,2,1,0:T(8,128)(2,1)}, bf16[16,1,64,128]{3,2,1,0:T(8,128)(2,1)S(1)}, u32[]{:S(2)}, u32[]{:S(2)}) %collective-permute-start.4) | collective-permute-done | bytes 262176 | tf_op jit(solution)/shard_map/ppermute | solution.py:27
  47.4 7.7 %collective-permute-done.5.below_ref = bf16[16,1,64,128]{3,2,1,0:T(8,128)(2,1)S(1)} collective-permute-done((bf16[16,1,64,128]{3,2,1,0:T(8,128)(2,1)S(1)}, bf16[16,1,64,128]{3,2,1,0:T(8,128)(2,1)S(1)}, u32[]{:S(2)}, u32[]{:S(2)}) %collective-permute-start.5) | collective-permute-done | bytes 262176 | tf_op jit(solution)/shard_map/ppermute | solution.py:27
  55.1 0.8 %shard_map.68.edge_ref = bf16[2,256,288]{2,1,0:T(8,128)(2,1)S(1)} custom-call(bf16[16,1,64,128]{3,2,1,0:T(8,128)(2,1)S(1)} %collective-permute-done.4.above_ref, bf16[16,4,64,128]{3,2,1,0:T(8,128)(2,1)S(1)} %pad_maximum_fusion.xp_ref, bf16[16,1,64,128]{3,2,1,0:T(8,128)(2,1)S(1)} %collective-permute-done.5.below_ref, bf16[1152,288]{1,0:T(8,128)(2,1)S(1)} %bitcast.11), custom_call_target="tpu_custom_call" | custom-call | flops 339738624 | bytes 1048576 | tf_op jit(solution)/shard_map/pallas_call | solution.py:337
  55.9 1.9 %collective-permute-start.6 = (bf16[1,256,288]{2,1,0:T(8,128)(2,1)S(1)}, bf16[1,256,288]{2,1,0:T(8,128)(2,1)S(1)}, u32[]{:S(2)}, u32[]{:S(2)}) collective-permute-start(bf16[1,256,288]{2,1,0:T(8,128)(2,1)S(1)} %get-tuple-element.22), channel_id=1, source_target_pairs={{0,16},{16,32},{32,48},{48,64},{64,80},{80,96},{96,112},{1,17},{17... | collective-permute-start | bytes 442376 | tf_op jit(solution)/shard_map/ppermute | solution.py:27
  57.9 5.5 %collective-permute-start.7 = (bf16[1,256,288]{2,1,0:T(8,128)(2,1)S(1)}, bf16[1,256,288]{2,1,0:T(8,128)(2,1)S(1)}, u32[]{:S(2)}, u32[]{:S(2)}) collective-permute-start(bf16[1,256,288]{2,1,0:T(8,128)(2,1)S(1)} %get-tuple-element.21), channel_id=1, source_target_pairs={{16,0},{32,16},{48,32},{64,48},{80,64},{96,80},{112,96},{17,1},{33... | collective-permute-start | bytes 442376 | tf_op jit(solution)/shard_map/ppermute | solution.py:27
  63.4 0.0 copy-done.1
  63.4 8.3 %shard_map.69 = (bf16[14,4,64,128]{3,2,1,0:T(8,128)(2,1)S(1)}, bf16[2,256,288]{2,1,0:T(8,128)(2,1)S(1)}) custom-call(bf16[16,1,64,128]{3,2,1,0:T(8,128)(2,1)S(1)} %collective-permute-done.4.above_ref, bf16[16,4,64,128]{3,2,1,0:T(8,128)(2,1)S(1)} %pad_maximum_fusion.xp_ref, bf16[16,1,64,128]{3,2,1,0:T(8,128)(2,1)S(1)} %collective-permute-done.5.below_ref, ...), custom_call_target="tpu_custom_call" | custom-call | flops 3623878656 | bytes 2097152 | tf_op jit(solution)/shard_map/pallas_call | solution.py:349
  71.6 0.0 collective-permute-done.6.before_ref
  71.7 0.0 collective-permute-done.7.after_ref
  71.7 0.4 shard_map.70
  72.1 1.1 %pad_maximum_fusion.1 = bf16[16,4,64,128]{3,2,1,0:T(8,128)(2,1)} fusion(bf16[1,4,64,128]{3,2,1,0:T(8,128)(2,1)S(1)} %get-tuple-element.24, bf16[14,4,64,128]{3,2,1,0:T(8,128)(2,1)S(1)} %get-tuple-element.16, bf16[1,4,64,128]{3,2,1,0:T(8,128)(2,1)S(1)} %get-tuple-element.23), kind=kLoop, calls=%fused_computation.1 | loop fusion | flops 1048576 | bytes 2097152 | tf_op jit(solution)/shard_map/concatenate | solution.py:372
  (3 shorter events, 0.1 us)
Async XLA Ops:
  0.0 18.5 %copy-start = (bf16[16,8,64,128]{3,2,1,0:T(8,128)(2,1)S(1)}, bf16[16,8,64,128]{3,2,1,0:T(8,128)(2,1)}, u32[]{:S(2)}) copy-start(bf16[16,8,64,128]{3,2,1,0:T(8,128)(2,1)} %xp_ref.5) | copy-start | bytes 6291460
  0.0 8.9 %copy-start.4 = (bf16[3,64,144]{2,1,0:T(8,128)(2,1)S(1)}, bf16[3,64,144]{2,1,0:T(8,128)(2,1)}, u32[]{:S(2)}) copy-start(bf16[3,64,144]{2,1,0:T(8,128)(2,1)} %param.8) | copy-start | bytes 165892
  0.0 10.3 %copy-start.3 = (bf16[3,3,128,64]{2,3,1,0:T(8,128)(2,1)S(1)}, bf16[3,3,128,64]{2,3,1,0:T(8,128)(2,1)}, u32[]{:S(2)}) copy-start(bf16[3,3,128,64]{2,3,1,0:T(8,128)(2,1)} %param.9) | copy-start | bytes 442372
  2.2 16.3 %collective-permute-start = (bf16[16,2,64,128]{3,2,1,0:T(8,128)(2,1)}, bf16[16,2,64,128]{3,2,1,0:T(8,128)(2,1)S(1)}, u32[]{:S(2)}, u32[]{:S(2)}) collective-permute-start(bf16[16,2,64,128]{3,2,1,0:T(8,128)(2,1)} %get-tuple-element.11), channel_id=1, source_target_pairs={{0,1},{1,2},{2,3},{3,4},{4,5},{5,6},{6,7},{7,8},{8,9},{9,10},{10,1... | collective-permute-start | bytes 1572872 | tf_op jit(solution)/shard_map/ppermute | solution.py:27
  7.0 11.5 %collective-permute-start.1 = (bf16[16,1,64,128]{3,2,1,0:T(8,128)(2,1)}, bf16[16,1,64,128]{3,2,1,0:T(8,128)(2,1)S(1)}, u32[]{:S(2)}, u32[]{:S(2)}) collective-permute-start(bf16[16,1,64,128]{3,2,1,0:T(8,128)(2,1)} %get-tuple-element.12), channel_id=1, source_target_pairs={{1,0},{2,1},{3,2},{4,3},{5,4},{6,5},{7,6},{8,7},{9,8},{10,9},{11,1... | collective-permute-start | bytes 786440 | tf_op jit(solution)/shard_map/ppermute | solution.py:27
  19.4 18.8 %collective-permute-start.2 = (bf16[1,144,1152]{2,1,0:T(8,128)(2,1)S(1)}, bf16[1,144,1152]{2,1,0:T(8,128)(2,1)S(1)}, u32[]{:S(2)}, u32[]{:S(2)}) collective-permute-start(bf16[1,144,1152]{2,1,0:T(8,128)(2,1)S(1)} %get-tuple-element.20), channel_id=1, source_target_pairs={{0,16},{16,32},{32,48},{48,64},{64,80},{80,96},{96,112},{1,17},{17... | collective-permute-start | bytes 995336 | tf_op jit(solution)/shard_map/ppermute | solution.py:27
  22.5 15.7 %collective-permute-start.3 = (bf16[1,144,1152]{2,1,0:T(8,128)(2,1)S(1)}, bf16[1,144,1152]{2,1,0:T(8,128)(2,1)S(1)}, u32[]{:S(2)}, u32[]{:S(2)}) collective-permute-start(bf16[1,144,1152]{2,1,0:T(8,128)(2,1)S(1)} %get-tuple-element.19), channel_id=1, source_target_pairs={{16,0},{32,16},{48,32},{64,48},{80,64},{96,80},{112,96},{17,1},{33... | collective-permute-start | bytes 995336 | tf_op jit(solution)/shard_map/ppermute | solution.py:27
  39.5 6.2 %copy-start.2 = (bf16[3,3,288,128]{3,2,1,0:T(8,128)(2,1)S(1)}, bf16[3,3,288,128]{3,2,1,0:T(8,128)(2,1)}, u32[]{:S(2)}) copy-start(bf16[3,3,288,128]{3,2,1,0:T(8,128)(2,1)} %param.10) | copy-start | bytes 1990660
  40.4 7.0 %collective-permute-start.4 = (bf16[16,1,64,128]{3,2,1,0:T(8,128)(2,1)}, bf16[16,1,64,128]{3,2,1,0:T(8,128)(2,1)S(1)}, u32[]{:S(2)}, u32[]{:S(2)}) collective-permute-start(bf16[16,1,64,128]{3,2,1,0:T(8,128)(2,1)} %get-tuple-element.18), channel_id=1, source_target_pairs={{0,1},{1,2},{2,3},{3,4},{4,5},{5,6},{6,7},{7,8},{8,9},{9,10},{10,1... | collective-permute-start | bytes 786440 | tf_op jit(solution)/shard_map/ppermute | solution.py:27
  43.8 11.3 %collective-permute-start.5 = (bf16[16,1,64,128]{3,2,1,0:T(8,128)(2,1)S(1)}, bf16[16,1,64,128]{3,2,1,0:T(8,128)(2,1)S(1)}, u32[]{:S(2)}, u32[]{:S(2)}) collective-permute-start(bf16[16,1,64,128]{3,2,1,0:T(8,128)(2,1)S(1)} %get-tuple-element.17), channel_id=1, source_target_pairs={{1,0},{2,1},{3,2},{4,3},{5,4},{6,5},{7,6},{8,7},{9,8},{10,9},{11,1... | collective-permute-start | bytes 786440 | tf_op jit(solution)/shard_map/ppermute | solution.py:27
  46.1 17.2 %copy-start.1 = (bf16[3,128,288]{1,2,0:T(8,128)(2,1)S(1)}, bf16[3,128,288]{1,2,0:T(8,128)(2,1)}, u32[]{:S(2)}) copy-start(bf16[3,128,288]{1,2,0:T(8,128)(2,1)} %param.11) | copy-start | bytes 663556
  55.9 15.7 %collective-permute-start.6 = (bf16[1,256,288]{2,1,0:T(8,128)(2,1)S(1)}, bf16[1,256,288]{2,1,0:T(8,128)(2,1)S(1)}, u32[]{:S(2)}, u32[]{:S(2)}) collective-permute-start(bf16[1,256,288]{2,1,0:T(8,128)(2,1)S(1)} %get-tuple-element.22), channel_id=1, source_target_pairs={{0,16},{16,32},{32,48},{48,64},{64,80},{80,96},{96,112},{1,17},{17... | collective-permute-start | bytes 442376 | tf_op jit(solution)/shard_map/ppermute | solution.py:27
  57.9 13.8 %collective-permute-start.7 = (bf16[1,256,288]{2,1,0:T(8,128)(2,1)S(1)}, bf16[1,256,288]{2,1,0:T(8,128)(2,1)S(1)}, u32[]{:S(2)}, u32[]{:S(2)}) collective-permute-start(bf16[1,256,288]{2,1,0:T(8,128)(2,1)S(1)} %get-tuple-element.21), channel_id=1, source_target_pairs={{16,0},{32,16},{48,32},{64,48},{80,64},{96,80},{112,96},{17,1},{33... | collective-permute-start | bytes 442376 | tf_op jit(solution)/shard_map/ppermute | solution.py:27

commit v21 on v20

--- a/solution.py
+++ b/solution.py
@@ -87,6 +87,10 @@
 
 
 def _down(s, refs, t, wd_ref, keep_ref, out_ref, slot):
+    _down_many([s], refs, [t], wd_ref, keep_ref, out_ref, [slot])
+
+
+def _down_many(sums, refs, ts, wd_ref, keep_ref, out_ref, slots):
     above_ref, xp_ref, _ = refs
     rows = xp_ref.shape[1] + 1
     width = xp_ref.shape[-1]
@@ -94,27 +98,34 @@
     lane = lax.broadcasted_iota(jnp.int32, (width // 2, width), 1)
     column = lax.broadcasted_iota(jnp.int32, (width // 2, width), 0)
     pick = (lane == 2 * column).astype(jnp.bfloat16)
-    sec = []
-    for h in range(rows):
-        own = above_ref[t, 1] if h == 0 else xp_ref[t, h - 1]
-        v = s[:, h * width : (h + 1) * width] + own.astype(jnp.float32)
-        v = jnp.maximum(v, 0.0)
-        if h == 0:
-            v = v * keep_ref[0].astype(jnp.float32)
-        sec.append(v.astype(jnp.bfloat16).astype(jnp.float32))
-    shifted = [[_lane_shift(r, b - 1).astype(jnp.bfloat16) for b in range(3)] for r in sec]
-    parts = []
-    for a in range(3):
-        for b in range(3):
-            parts.append(jnp.concatenate([shifted[2 * i + a][b] for i in range(reduced_rows)], axis=1))
-    stacked = jnp.concatenate(parts, axis=0)
+    columns = []
+    for s, t in zip(sums, ts):
+        sec = []
+        for h in range(rows):
+            own = above_ref[t, 1] if h == 0 else xp_ref[t, h - 1]
+            v = s[:, h * width : (h + 1) * width] + own.astype(jnp.float32)
+            v = jnp.maximum(v, 0.0)
+            if h == 0:
+                v = v * keep_ref[0].astype(jnp.float32)
+            sec.append(v.astype(jnp.bfloat16).astype(jnp.float32))
+        shifted = [[_lane_shift(r, b - 1).astype(jnp.bfloat16) for b in range(3)] for r in sec]
+        parts = []
+        for a in range(3):
+            for b in range(3):
+                parts.append(jnp.concatenate([shifted[2 * i + a][b] for i in range(reduced_rows)], axis=1))
+        columns.append(jnp.concatenate(parts, axis=0))
+    stacked = columns[0] if len(columns) == 1 else jnp.concatenate(columns, axis=1)
     full = jnp.dot(wd_ref[...], stacked, preferred_element_type=jnp.float32)
     full = jnp.maximum(full, 0.0).astype(jnp.bfloat16)
     outs = full.shape[0]
-    rows_by_d = jnp.concatenate([full[:, i * width : (i + 1) * width] for i in range(reduced_rows)], axis=0)
-    r = lax.dot_general(pick, rows_by_d, (((1,), (1,)), ((), ())), preferred_element_type=jnp.float32)
-    for i in range(reduced_rows):
-        out_ref[slot, i] = r[:, i * outs : (i + 1) * outs].astype(out_ref.dtype)
+    span = reduced_rows * width
+    for n, slot in enumerate(slots):
+        rows_by_d = jnp.concatenate(
+            [full[:, n * span + i * width : n * span + (i + 1) * width] for i in range(reduced_rows)], axis=0
+        )
+        r = lax.dot_general(pick, rows_by_d, (((1,), (1,)), ((), ())), preferred_element_type=jnp.float32)
+        for i in range(reduced_rows):
+            out_ref[slot, i] = r[:, i * outs : (i + 1) * outs].astype(out_ref.dtype)
 
 
 def _edges_one_kernel(above_ref, xp_ref, below_ref, w9_ref, edge_ref):
@@ -154,11 +165,13 @@
         ]
         stacked = stacks[0] if pairs == 1 else jnp.concatenate(stacks, axis=1)
         s = jnp.dot(t3_ref[...], stacked, preferred_element_type=jnp.float32)
+        sums, ts = [], []
         for p in range(pairs):
             u = t + 2 * p
             part = s[:, p * span : (p + 1) * span]
-            _down(part[:channels], refs, u, wd_ref, keep_ref, out_ref, u - 1)
-            _down(part[channels:], refs, u + 1, wd_ref, keep_ref, out_ref, u)
+            sums += [part[:channels], part[channels:]]
+            ts += [u, u + 1]
+        _down_many(sums, refs, ts, wd_ref, keep_ref, out_ref, [u - 1 for u in ts])
 
     def section(g, carry):
         run(4 * g + 1, 2)

time: 73.6 us -> 72.1 us (0.980)
  Pallas kernels: 25.2 us -> 23.7 us
    pallas_call x1, Pallas kernels: 11.4 us -> 9.87 us  [block_one(): pl.pallas_call(_inner_one_kernel, out_shape=(jax.ShapeDtypeStruct((frames...]
  transfers between devices with their start and end apart: 8 -> 8, of which waited for: 3 -> 3; matrix products, arithmetic and copies ran while one was open for 3% -> 3% of each run, Pallas kernels for 27% -> 25%
where the time goes in v21:
time: 72.1 us; the launch traced here: 71.7 us
  starting transfers between devices  26.8 us (37%)
  Pallas kernels  23.7 us (33%)
  waiting for transfers between devices  16.9 us (23%)
  local copies, waits for them, and re-layouts  2.78 us (4%)
  other arithmetic  1.33 us (2%)
    ppermute x8, starting transfers between devices, from_behind(): return lax.ppermute(array, axis, pairs)  26.8 us
    ppermute x8, waiting for transfers between devices, from_behind(): return lax.ppermute(array, axis, pairs)  16.9 us
    pallas_call x1, Pallas kernels, block_one(): pl.pallas_call(_inner_one_kernel, out_shape=(jax.ShapeDtypeStruct((frames...  9.87 us
    pallas_call x1, Pallas kernels, block_two(): pl.pallas_call(_inner_two_kernel, out_shape=(jax.ShapeDtypeStruct((frames...  8.27 us
    pallas_call x1, Pallas kernels, edge_rows(): pl.pallas_call(_copy_kernel, grid=(1,), out_shape=(jax.ShapeDtypeStruct((...  2.17 us
  transfers between devices with their start and end apart: 8, of which 3 were waited for; matrix products, arithmetic and copies ran while one was open for 3% of the time, Pallas kernels for 25%

profile of v21, /device:TPU:57, one launch (start us, length us, event | category | flops | bytes accessed | tf_op | source)
XLA Modules:
  0.0 71.7 jit_solution(5896514501185886996)
XLA Ops:
  0.0 0.0 copy-start
  0.0 0.0 copy-start.4
  0.0 0.0 copy-start.3
  0.0 2.2 %shard_map.64 = (bf16[16,2,64,128]{3,2,1,0:T(8,128)(2,1)}, bf16[16,1,64,128]{3,2,1,0:T(8,128)(2,1)}) custom-call(bf16[16,8,64,128]{3,2,1,0:T(8,128)(2,1)} %xp_ref.5, bf16[16,8,64,128]{3,2,1,0:T(8,128)(2,1)} %xp_ref.5), custom_call_target="tpu_custom_call" | custom-call | tf_op jit(solution)/shard_map/pallas_call | solution.py:397
  2.2 4.8 %collective-permute-start = (bf16[16,2,64,128]{3,2,1,0:T(8,128)(2,1)}, bf16[16,2,64,128]{3,2,1,0:T(8,128)(2,1)S(1)}, u32[]{:S(2)}, u32[]{:S(2)}) collective-permute-start(bf16[16,2,64,128]{3,2,1,0:T(8,128)(2,1)} %get-tuple-element.11), channel_id=1, source_target_pairs={{0,1},{1,2},{2,3},{3,4},{4,5},{5,6},{6,7},{7,8},{8,9},{9,10},{10,1... | collective-permute-start | bytes 1572872 | tf_op jit(solution)/shard_map/ppermute | solution.py:27
  7.0 1.9 %collective-permute-start.1 = (bf16[16,1,64,128]{3,2,1,0:T(8,128)(2,1)}, bf16[16,1,64,128]{3,2,1,0:T(8,128)(2,1)S(1)}, u32[]{:S(2)}, u32[]{:S(2)}) collective-permute-start(bf16[16,1,64,128]{3,2,1,0:T(8,128)(2,1)} %get-tuple-element.12), channel_id=1, source_target_pairs={{1,0},{2,1},{3,2},{4,3},{5,4},{6,5},{7,6},{8,7},{9,8},{10,9},{11,1... | collective-permute-start | bytes 786440 | tf_op jit(solution)/shard_map/ppermute | solution.py:27
  8.9 0.0 copy-done.4
  8.9 0.1 copy.11
  9.0 0.1 reshape.19.t3_ref
  9.2 1.1 %copy.12.w9_ref = bf16[144,576]{1,0:T(8,128)(2,1)S(1)} copy(bf16[144,576]{0,1:T(8,128)(2,1)} %bitcast.16) | data formatting | bytes 331776 | tf_op jit(solution)/shard_map/reshape | solution.py:201
  10.3 0.0 copy-done.3
  10.3 0.2 copy.15.wd_ref
  10.5 0.1 fusion.2.t3_ref
  10.6 8.0 %collective-permute-done.1.below_ref = bf16[16,1,64,128]{3,2,1,0:T(8,128)(2,1)S(1)} collective-permute-done((bf16[16,1,64,128]{3,2,1,0:T(8,128)(2,1)}, bf16[16,1,64,128]{3,2,1,0:T(8,128)(2,1)S(1)}, u32[]{:S(2)}, u32[]{:S(2)}) %collective-permute-start.1) | collective-permute-done | bytes 262176 | tf_op jit(solution)/shard_map/ppermute | solution.py:27
  18.5 0.0 collective-permute-done.above_ref
  18.5 0.0 copy-done
  18.5 0.8 %shard_map.65.edge_ref = bf16[2,144,1152]{2,1,0:T(8,128)(2,1)S(1)} custom-call(bf16[16,2,64,128]{3,2,1,0:T(8,128)(2,1)S(1)} %collective-permute-done.above_ref, bf16[16,8,64,128]{3,2,1,0:T(8,128)(2,1)S(1)} %copy-done, bf16[16,1,64,128]{3,2,1,0:T(8,128)(2,1)S(1)} %collective-permute-done.1.below_ref, bf16[144,576]{1,0:T(8,128)(2,1)S(1)} %copy.12.w9_ref), custom_call_target="tpu_custom_call" | custom-call | flops 382205952 | bytes 2097152 | tf_op jit(solution)/shard_map/pallas_call | solution.py:218
  19.3 0.1 fusion.4
  19.4 3.1 %collective-permute-start.2 = (bf16[1,144,1152]{2,1,0:T(8,128)(2,1)S(1)}, bf16[1,144,1152]{2,1,0:T(8,128)(2,1)S(1)}, u32[]{:S(2)}, u32[]{:S(2)}) collective-permute-start(bf16[1,144,1152]{2,1,0:T(8,128)(2,1)S(1)} %get-tuple-element.20), channel_id=1, source_target_pairs={{0,16},{16,32},{32,48},{48,64},{64,80},{80,96},{96,112},{1,17},{17... | collective-permute-start | bytes 995336 | tf_op jit(solution)/shard_map/ppermute | solution.py:27
  22.5 4.3 %collective-permute-start.3 = (bf16[1,144,1152]{2,1,0:T(8,128)(2,1)S(1)}, bf16[1,144,1152]{2,1,0:T(8,128)(2,1)S(1)}, u32[]{:S(2)}, u32[]{:S(2)}) collective-permute-start(bf16[1,144,1152]{2,1,0:T(8,128)(2,1)S(1)} %get-tuple-element.19), channel_id=1, source_target_pairs={{16,0},{32,16},{48,32},{64,48},{80,64},{96,80},{112,96},{17,1},{33... | collective-permute-start | bytes 995336 | tf_op jit(solution)/shard_map/ppermute | solution.py:27
  26.8 9.9 %shard_map.66 = (bf16[14,4,64,128]{3,2,1,0:T(8,128)(2,1)S(1)}, bf16[2,144,1152]{2,1,0:T(8,128)(2,1)S(1)}) custom-call(s32[1]{0:T(128)} %bitcast.keep_ref, bf16[16,2,64,128]{3,2,1,0:T(8,128)(2,1)S(1)} %collective-permute-done.above_ref, bf16[16,8,64,128]{3,2,1,0:T(8,128)(2,1)S(1)} %copy-done, bf16[16,1,64,128]{3,2,1,0:T(8,128)(2,1)S(1)} %collective-permute-done.1.below_ref, ...), custom_call_target="tpu_custom_call" | custom-call | flops 5284823040 | bytes 4194304 | tf_op jit(solution)/shard_map/pallas_call | solution.py:228
  36.6 0.0 collective-permute-done.2.before_ref
  36.6 0.0 collective-permute-done.3.after_ref
  36.7 1.3 %shard_map.67 = bf16[2,4,64,128]{3,2,1,0:T(8,128)(2,1)S(1)} custom-call(s32[1]{0:T(128)} %bitcast.keep_ref, bf16[16,2,64,128]{3,2,1,0:T(8,128)(2,1)S(1)} %collective-permute-done.above_ref, bf16[16,8,64,128]{3,2,1,0:T(8,128)(2,1)S(1)} %copy-done, bf16[16,1,64,128]{3,2,1,0:T(8,128)(2,1)S(1)} %collective-permute-done.1.below_ref, ...), custom_call_target="tpu_custom_call" | custom-call | tf_op jit(solution)/shard_map/pallas_call | solution.py:242
  38.0 0.0 copy-start.2
  38.0 0.1 pad_maximum_fusion.xp_ref
  38.2 0.7 %fusion.3 = (bf16[16,1,64,128]{3,2,1,0:T(8,128)(2,1)S(1)}, bf16[16,1,64,128]{3,2,1,0:T(8,128)(2,1)}) fusion(bf16[16,4,64,128]{3,2,1,0:T(8,128)(2,1)S(1)} %pad_maximum_fusion.xp_ref), kind=kLoop, calls=%fused_computation.7 | loop fusion | bytes 1048576 | tf_op jit(solution)/shard_map/slice | solution.py:418
  38.9 3.4 %collective-permute-start.4 = (bf16[16,1,64,128]{3,2,1,0:T(8,128)(2,1)}, bf16[16,1,64,128]{3,2,1,0:T(8,128)(2,1)S(1)}, u32[]{:S(2)}, u32[]{:S(2)}) collective-permute-start(bf16[16,1,64,128]{3,2,1,0:T(8,128)(2,1)} %get-tuple-element.18), channel_id=1, source_target_pairs={{0,1},{1,2},{2,3},{3,4},{4,5},{5,6},{6,7},{7,8},{8,9},{9,10},{10,1... | collective-permute-start | bytes 786440 | tf_op jit(solution)/shard_map/ppermute | solution.py:27
  42.3 1.9 %collective-permute-start.5 = (bf16[16,1,64,128]{3,2,1,0:T(8,128)(2,1)S(1)}, bf16[16,1,64,128]{3,2,1,0:T(8,128)(2,1)S(1)}, u32[]{:S(2)}, u32[]{:S(2)}) collective-permute-start(bf16[16,1,64,128]{3,2,1,0:T(8,128)(2,1)S(1)} %get-tuple-element.17), channel_id=1, source_target_pairs={{1,0},{2,1},{3,2},{4,3},{5,4},{6,5},{7,6},{8,7},{9,8},{10,9},{11,1... | collective-permute-start | bytes 786440 | tf_op jit(solution)/shard_map/ppermute | solution.py:27
  44.2 0.0 copy-done.2
  44.2 0.4 copy.16
  44.6 0.0 copy-start.1
  44.6 1.3 %collective-permute-done.4.above_ref = bf16[16,1,64,128]{3,2,1,0:T(8,128)(2,1)S(1)} collective-permute-done((bf16[16,1,64,128]{3,2,1,0:T(8,128)(2,1)}, bf16[16,1,64,128]{3,2,1,0:T(8,128)(2,1)S(1)}, u32[]{:S(2)}, u32[]{:S(2)}) %collective-permute-start.4) | collective-permute-done | bytes 262176 | tf_op jit(solution)/shard_map/ppermute | solution.py:27
  45.9 7.7 %collective-permute-done.5.below_ref = bf16[16,1,64,128]{3,2,1,0:T(8,128)(2,1)S(1)} collective-permute-done((bf16[16,1,64,128]{3,2,1,0:T(8,128)(2,1)S(1)}, bf16[16,1,64,128]{3,2,1,0:T(8,128)(2,1)S(1)}, u32[]{:S(2)}, u32[]{:S(2)}) %collective-permute-start.5) | collective-permute-done | bytes 262176 | tf_op jit(solution)/shard_map/ppermute | solution.py:27
  53.6 0.8 %shard_map.68.edge_ref = bf16[2,256,288]{2,1,0:T(8,128)(2,1)S(1)} custom-call(bf16[16,1,64,128]{3,2,1,0:T(8,128)(2,1)S(1)} %collective-permute-done.4.above_ref, bf16[16,4,64,128]{3,2,1,0:T(8,128)(2,1)S(1)} %pad_maximum_fusion.xp_ref, bf16[16,1,64,128]{3,2,1,0:T(8,128)(2,1)S(1)} %collective-permute-done.5.below_ref, bf16[1152,288]{1,0:T(8,128)(2,1)S(1)} %bitcast.11), custom_call_target="tpu_custom_call" | custom-call | flops 339738624 | bytes 1048576 | tf_op jit(solution)/shard_map/pallas_call | solution.py:350
  54.4 1.9 %collective-permute-start.6 = (bf16[1,256,288]{2,1,0:T(8,128)(2,1)S(1)}, bf16[1,256,288]{2,1,0:T(8,128)(2,1)S(1)}, u32[]{:S(2)}, u32[]{:S(2)}) collective-permute-start(bf16[1,256,288]{2,1,0:T(8,128)(2,1)S(1)} %get-tuple-element.22), channel_id=1, source_target_pairs={{0,16},{16,32},{32,48},{48,64},{64,80},{80,96},{96,112},{1,17},{17... | collective-permute-start | bytes 442376 | tf_op jit(solution)/shard_map/ppermute | solution.py:27
  56.4 5.5 %collective-permute-start.7 = (bf16[1,256,288]{2,1,0:T(8,128)(2,1)S(1)}, bf16[1,256,288]{2,1,0:T(8,128)(2,1)S(1)}, u32[]{:S(2)}, u32[]{:S(2)}) collective-permute-start(bf16[1,256,288]{2,1,0:T(8,128)(2,1)S(1)} %get-tuple-element.21), channel_id=1, source_target_pairs={{16,0},{32,16},{48,32},{64,48},{80,64},{96,80},{112,96},{17,1},{33... | collective-permute-start | bytes 442376 | tf_op jit(solution)/shard_map/ppermute | solution.py:27
  61.9 0.0 copy-done.1
  61.9 8.3 %shard_map.69 = (bf16[14,4,64,128]{3,2,1,0:T(8,128)(2,1)S(1)}, bf16[2,256,288]{2,1,0:T(8,128)(2,1)S(1)}) custom-call(bf16[16,1,64,128]{3,2,1,0:T(8,128)(2,1)S(1)} %collective-permute-done.4.above_ref, bf16[16,4,64,128]{3,2,1,0:T(8,128)(2,1)S(1)} %pad_maximum_fusion.xp_ref, bf16[16,1,64,128]{3,2,1,0:T(8,128)(2,1)S(1)} %collective-permute-done.5.below_ref, ...), custom_call_target="tpu_custom_call" | custom-call | flops 3623878656 | bytes 2097152 | tf_op jit(solution)/shard_map/pallas_call | solution.py:362
  70.1 0.0 collective-permute-done.6.before_ref
  70.2 0.0 collective-permute-done.7.after_ref
  70.2 0.4 shard_map.70
  70.6 1.1 %pad_maximum_fusion.1 = bf16[16,4,64,128]{3,2,1,0:T(8,128)(2,1)} fusion(bf16[1,4,64,128]{3,2,1,0:T(8,128)(2,1)S(1)} %get-tuple-element.24, bf16[14,4,64,128]{3,2,1,0:T(8,128)(2,1)S(1)} %get-tuple-element.16, bf16[1,4,64,128]{3,2,1,0:T(8,128)(2,1)S(1)} %get-tuple-element.23), kind=kLoop, calls=%fused_computation.1 | loop fusion | flops 1048576 | bytes 2097152 | tf_op jit(solution)/shard_map/concatenate | solution.py:385
  (3 shorter events, 0.1 us)
Async XLA Ops:
  0.0 18.5 %copy-start = (bf16[16,8,64,128]{3,2,1,0:T(8,128)(2,1)S(1)}, bf16[16,8,64,128]{3,2,1,0:T(8,128)(2,1)}, u32[]{:S(2)}) copy-start(bf16[16,8,64,128]{3,2,1,0:T(8,128)(2,1)} %xp_ref.5) | copy-start | bytes 6291460
  0.0 8.9 %copy-start.4 = (bf16[3,64,144]{2,1,0:T(8,128)(2,1)S(1)}, bf16[3,64,144]{2,1,0:T(8,128)(2,1)}, u32[]{:S(2)}) copy-start(bf16[3,64,144]{2,1,0:T(8,128)(2,1)} %param.8) | copy-start | bytes 165892
  0.0 10.3 %copy-start.3 = (bf16[3,3,128,64]{2,3,1,0:T(8,128)(2,1)S(1)}, bf16[3,3,128,64]{2,3,1,0:T(8,128)(2,1)}, u32[]{:S(2)}) copy-start(bf16[3,3,128,64]{2,3,1,0:T(8,128)(2,1)} %param.9) | copy-start | bytes 442372
  2.2 16.3 %collective-permute-start = (bf16[16,2,64,128]{3,2,1,0:T(8,128)(2,1)}, bf16[16,2,64,128]{3,2,1,0:T(8,128)(2,1)S(1)}, u32[]{:S(2)}, u32[]{:S(2)}) collective-permute-start(bf16[16,2,64,128]{3,2,1,0:T(8,128)(2,1)} %get-tuple-element.11), channel_id=1, source_target_pairs={{0,1},{1,2},{2,3},{3,4},{4,5},{5,6},{6,7},{7,8},{8,9},{9,10},{10,1... | collective-permute-start | bytes 1572872 | tf_op jit(solution)/shard_map/ppermute | solution.py:27
  7.0 11.5 %collective-permute-start.1 = (bf16[16,1,64,128]{3,2,1,0:T(8,128)(2,1)}, bf16[16,1,64,128]{3,2,1,0:T(8,128)(2,1)S(1)}, u32[]{:S(2)}, u32[]{:S(2)}) collective-permute-start(bf16[16,1,64,128]{3,2,1,0:T(8,128)(2,1)} %get-tuple-element.12), channel_id=1, source_target_pairs={{1,0},{2,1},{3,2},{4,3},{5,4},{6,5},{7,6},{8,7},{9,8},{10,9},{11,1... | collective-permute-start | bytes 786440 | tf_op jit(solution)/shard_map/ppermute | solution.py:27
  19.4 17.3 %collective-permute-start.2 = (bf16[1,144,1152]{2,1,0:T(8,128)(2,1)S(1)}, bf16[1,144,1152]{2,1,0:T(8,128)(2,1)S(1)}, u32[]{:S(2)}, u32[]{:S(2)}) collective-permute-start(bf16[1,144,1152]{2,1,0:T(8,128)(2,1)S(1)} %get-tuple-element.20), channel_id=1, source_target_pairs={{0,16},{16,32},{32,48},{48,64},{64,80},{80,96},{96,112},{1,17},{17... | collective-permute-start | bytes 995336 | tf_op jit(solution)/shard_map/ppermute | solution.py:27
  22.5 14.2 %collective-permute-start.3 = (bf16[1,144,1152]{2,1,0:T(8,128)(2,1)S(1)}, bf16[1,144,1152]{2,1,0:T(8,128)(2,1)S(1)}, u32[]{:S(2)}, u32[]{:S(2)}) collective-permute-start(bf16[1,144,1152]{2,1,0:T(8,128)(2,1)S(1)} %get-tuple-element.19), channel_id=1, source_target_pairs={{16,0},{32,16},{48,32},{64,48},{80,64},{96,80},{112,96},{17,1},{33... | collective-permute-start | bytes 995336 | tf_op jit(solution)/shard_map/ppermute | solution.py:27
  38.0 6.2 %copy-start.2 = (bf16[3,3,288,128]{3,2,1,0:T(8,128)(2,1)S(1)}, bf16[3,3,288,128]{3,2,1,0:T(8,128)(2,1)}, u32[]{:S(2)}) copy-start(bf16[3,3,288,128]{3,2,1,0:T(8,128)(2,1)} %param.10) | copy-start | bytes 1990660
  38.9 7.0 %collective-permute-start.4 = (bf16[16,1,64,128]{3,2,1,0:T(8,128)(2,1)}, bf16[16,1,64,128]{3,2,1,0:T(8,128)(2,1)S(1)}, u32[]{:S(2)}, u32[]{:S(2)}) collective-permute-start(bf16[16,1,64,128]{3,2,1,0:T(8,128)(2,1)} %get-tuple-element.18), channel_id=1, source_target_pairs={{0,1},{1,2},{2,3},{3,4},{4,5},{5,6},{6,7},{7,8},{8,9},{9,10},{10,1... | collective-permute-start | bytes 786440 | tf_op jit(solution)/shard_map/ppermute | solution.py:27
  42.3 11.3 %collective-permute-start.5 = (bf16[16,1,64,128]{3,2,1,0:T(8,128)(2,1)S(1)}, bf16[16,1,64,128]{3,2,1,0:T(8,128)(2,1)S(1)}, u32[]{:S(2)}, u32[]{:S(2)}) collective-permute-start(bf16[16,1,64,128]{3,2,1,0:T(8,128)(2,1)S(1)} %get-tuple-element.17), channel_id=1, source_target_pairs={{1,0},{2,1},{3,2},{4,3},{5,4},{6,5},{7,6},{8,7},{9,8},{10,9},{11,1... | collective-permute-start | bytes 786440 | tf_op jit(solution)/shard_map/ppermute | solution.py:27
  44.6 17.2 %copy-start.1 = (bf16[3,128,288]{1,2,0:T(8,128)(2,1)S(1)}, bf16[3,128,288]{1,2,0:T(8,128)(2,1)}, u32[]{:S(2)}) copy-start(bf16[3,128,288]{1,2,0:T(8,128)(2,1)} %param.11) | copy-start | bytes 663556
  54.4 15.7 %collective-permute-start.6 = (bf16[1,256,288]{2,1,0:T(8,128)(2,1)S(1)}, bf16[1,256,288]{2,1,0:T(8,128)(2,1)S(1)}, u32[]{:S(2)}, u32[]{:S(2)}) collective-permute-start(bf16[1,256,288]{2,1,0:T(8,128)(2,1)S(1)} %get-tuple-element.22), channel_id=1, source_target_pairs={{0,16},{16,32},{32,48},{48,64},{64,80},{80,96},{96,112},{1,17},{17... | collective-permute-start | bytes 442376 | tf_op jit(solution)/shard_map/ppermute | solution.py:27
  56.4 13.8 %collective-permute-start.7 = (bf16[1,256,288]{2,1,0:T(8,128)(2,1)S(1)}, bf16[1,256,288]{2,1,0:T(8,128)(2,1)S(1)}, u32[]{:S(2)}, u32[]{:S(2)}) collective-permute-start(bf16[1,256,288]{2,1,0:T(8,128)(2,1)S(1)} %get-tuple-element.21), channel_id=1, source_target_pairs={{16,0},{32,16},{48,32},{64,48},{80,64},{96,80},{112,96},{17,1},{33... | collective-permute-start | bytes 442376 | tf_op jit(solution)/shard_map/ppermute | solution.py:27

commit v22 on v21

--- a/solution.py
+++ b/solution.py
@@ -187,10 +187,13 @@
 ):
     refs = (above_ref, xp_ref, below_ref)
     frames = xp_ref.shape[0]
-    stacked = jnp.concatenate([before_ref[0], edge_ref[0], side_ref[0]], axis=0)
-    _section_down(stacked, refs, 0, t3_ref, wd_ref, keep_ref, out_ref, 0)
-    stacked = jnp.concatenate([side_ref[1], edge_ref[1], after_ref[0]], axis=0)
-    _section_down(stacked, refs, frames - 1, t3_ref, wd_ref, keep_ref, out_ref, 1)
+    first = jnp.concatenate([before_ref[0], edge_ref[0], side_ref[0]], axis=0)
+    last = jnp.concatenate([side_ref[1], edge_ref[1], after_ref[0]], axis=0)
+    sums = jnp.dot(t3_ref[...], jnp.concatenate([first, last], axis=1), preferred_element_type=jnp.float32)
+    span = first.shape[-1]
+    _down_many(
+        [sums[:, :span], sums[:, span:]], refs, [0, frames - 1], wd_ref, keep_ref, out_ref, [0, 1]
+    )
 
 
 def block_one(above, rowed, below, keep_first, spatial_kernel, temporal_kernel, down_kernel):

time: 72.1 us -> 71.7 us (level)
  no operation moved by 1% of the time
where the time goes in v22:
time: 71.7 us; the launch traced here: 71.3 us
  starting transfers between devices  26.8 us (37%)
  Pallas kernels  23.3 us (32%)
  waiting for transfers between devices  16.9 us (24%)
  local copies, waits for them, and re-layouts  2.78 us (4%)
  other arithmetic  1.33 us (2%)
    ppermute x8, starting transfers between devices, from_behind(): return lax.ppermute(array, axis, pairs)  26.8 us
    ppermute x8, waiting for transfers between devices, from_behind(): return lax.ppermute(array, axis, pairs)  16.9 us
    pallas_call x1, Pallas kernels, block_one(): pl.pallas_call(_inner_one_kernel, out_shape=(jax.ShapeDtypeStruct((frames...  9.87 us
    pallas_call x1, Pallas kernels, block_two(): pl.pallas_call(_inner_two_kernel, out_shape=(jax.ShapeDtypeStruct((frames...  8.27 us
    pallas_call x1, Pallas kernels, edge_rows(): pl.pallas_call(_copy_kernel, grid=(1,), out_shape=(jax.ShapeDtypeStruct((...  2.17 us
  transfers between devices with their start and end apart: 8, of which 3 were waited for; matrix products, arithmetic and copies ran while one was open for 3% of the time, Pallas kernels for 25%

profile of v22, /device:TPU:57, one launch (start us, length us, event | category | flops | bytes accessed | tf_op | source)
XLA Modules:
  0.0 71.3 jit_solution(8546883858087676142)
XLA Ops:
  0.0 0.0 copy-start
  0.0 0.0 copy-start.4
  0.0 0.0 copy-start.3
  0.0 2.2 %shard_map.64 = (bf16[16,2,64,128]{3,2,1,0:T(8,128)(2,1)}, bf16[16,1,64,128]{3,2,1,0:T(8,128)(2,1)}) custom-call(bf16[16,8,64,128]{3,2,1,0:T(8,128)(2,1)} %xp_ref.5, bf16[16,8,64,128]{3,2,1,0:T(8,128)(2,1)} %xp_ref.5), custom_call_target="tpu_custom_call" | custom-call | tf_op jit(solution)/shard_map/pallas_call | solution.py:400
  2.2 4.8 %collective-permute-start = (bf16[16,2,64,128]{3,2,1,0:T(8,128)(2,1)}, bf16[16,2,64,128]{3,2,1,0:T(8,128)(2,1)S(1)}, u32[]{:S(2)}, u32[]{:S(2)}) collective-permute-start(bf16[16,2,64,128]{3,2,1,0:T(8,128)(2,1)} %get-tuple-element.11), channel_id=1, source_target_pairs={{0,1},{1,2},{2,3},{3,4},{4,5},{5,6},{6,7},{7,8},{8,9},{9,10},{10,1... | collective-permute-start | bytes 1572872 | tf_op jit(solution)/shard_map/ppermute | solution.py:27
  7.0 1.9 %collective-permute-start.1 = (bf16[16,1,64,128]{3,2,1,0:T(8,128)(2,1)}, bf16[16,1,64,128]{3,2,1,0:T(8,128)(2,1)S(1)}, u32[]{:S(2)}, u32[]{:S(2)}) collective-permute-start(bf16[16,1,64,128]{3,2,1,0:T(8,128)(2,1)} %get-tuple-element.12), channel_id=1, source_target_pairs={{1,0},{2,1},{3,2},{4,3},{5,4},{6,5},{7,6},{8,7},{9,8},{10,9},{11,1... | collective-permute-start | bytes 786440 | tf_op jit(solution)/shard_map/ppermute | solution.py:27
  8.9 0.0 copy-done.4
  8.9 0.1 copy.11
  9.0 0.1 reshape.19.t3_ref
  9.2 1.1 %copy.12.w9_ref = bf16[144,576]{1,0:T(8,128)(2,1)S(1)} copy(bf16[144,576]{0,1:T(8,128)(2,1)} %bitcast.16) | data formatting | bytes 331776 | tf_op jit(solution)/shard_map/reshape | solution.py:204
  10.3 0.0 copy-done.3
  10.3 0.2 copy.15.wd_ref
  10.5 0.1 fusion.2.t3_ref
  10.6 8.0 %collective-permute-done.1.below_ref = bf16[16,1,64,128]{3,2,1,0:T(8,128)(2,1)S(1)} collective-permute-done((bf16[16,1,64,128]{3,2,1,0:T(8,128)(2,1)}, bf16[16,1,64,128]{3,2,1,0:T(8,128)(2,1)S(1)}, u32[]{:S(2)}, u32[]{:S(2)}) %collective-permute-start.1) | collective-permute-done | bytes 262176 | tf_op jit(solution)/shard_map/ppermute | solution.py:27
  18.5 0.0 collective-permute-done.above_ref
  18.5 0.0 copy-done
  18.5 0.8 %shard_map.65.edge_ref = bf16[2,144,1152]{2,1,0:T(8,128)(2,1)S(1)} custom-call(bf16[16,2,64,128]{3,2,1,0:T(8,128)(2,1)S(1)} %collective-permute-done.above_ref, bf16[16,8,64,128]{3,2,1,0:T(8,128)(2,1)S(1)} %copy-done, bf16[16,1,64,128]{3,2,1,0:T(8,128)(2,1)S(1)} %collective-permute-done.1.below_ref, bf16[144,576]{1,0:T(8,128)(2,1)S(1)} %copy.12.w9_ref), custom_call_target="tpu_custom_call" | custom-call | flops 382205952 | bytes 2097152 | tf_op jit(solution)/shard_map/pallas_call | solution.py:221
  19.3 0.1 fusion.4
  19.4 3.1 %collective-permute-start.2 = (bf16[1,144,1152]{2,1,0:T(8,128)(2,1)S(1)}, bf16[1,144,1152]{2,1,0:T(8,128)(2,1)S(1)}, u32[]{:S(2)}, u32[]{:S(2)}) collective-permute-start(bf16[1,144,1152]{2,1,0:T(8,128)(2,1)S(1)} %get-tuple-element.20), channel_id=1, source_target_pairs={{0,16},{16,32},{32,48},{48,64},{64,80},{80,96},{96,112},{1,17},{17... | collective-permute-start | bytes 995336 | tf_op jit(solution)/shard_map/ppermute | solution.py:27
  22.5 4.3 %collective-permute-start.3 = (bf16[1,144,1152]{2,1,0:T(8,128)(2,1)S(1)}, bf16[1,144,1152]{2,1,0:T(8,128)(2,1)S(1)}, u32[]{:S(2)}, u32[]{:S(2)}) collective-permute-start(bf16[1,144,1152]{2,1,0:T(8,128)(2,1)S(1)} %get-tuple-element.19), channel_id=1, source_target_pairs={{16,0},{32,16},{48,32},{64,48},{80,64},{96,80},{112,96},{17,1},{33... | collective-permute-start | bytes 995336 | tf_op jit(solution)/shard_map/ppermute | solution.py:27
  26.8 9.9 %shard_map.66 = (bf16[14,4,64,128]{3,2,1,0:T(8,128)(2,1)S(1)}, bf16[2,144,1152]{2,1,0:T(8,128)(2,1)S(1)}) custom-call(s32[1]{0:T(128)} %bitcast.keep_ref, bf16[16,2,64,128]{3,2,1,0:T(8,128)(2,1)S(1)} %collective-permute-done.above_ref, bf16[16,8,64,128]{3,2,1,0:T(8,128)(2,1)S(1)} %copy-done, bf16[16,1,64,128]{3,2,1,0:T(8,128)(2,1)S(1)} %collective-permute-done.1.below_ref, ...), custom_call_target="tpu_custom_call" | custom-call | flops 5284823040 | bytes 4194304 | tf_op jit(solution)/shard_map/pallas_call | solution.py:231
  36.6 0.0 collective-permute-done.2.before_ref
  36.6 0.0 collective-permute-done.3.after_ref
  36.7 0.9 %shard_map.67 = bf16[2,4,64,128]{3,2,1,0:T(8,128)(2,1)S(1)} custom-call(s32[1]{0:T(128)} %bitcast.keep_ref, bf16[16,2,64,128]{3,2,1,0:T(8,128)(2,1)S(1)} %collective-permute-done.above_ref, bf16[16,8,64,128]{3,2,1,0:T(8,128)(2,1)S(1)} %copy-done, bf16[16,1,64,128]{3,2,1,0:T(8,128)(2,1)S(1)} %collective-permute-done.1.below_ref, ...), custom_call_target="tpu_custom_call" | custom-call | tf_op jit(solution)/shard_map/pallas_call | solution.py:245
  37.6 0.0 copy-start.2
  37.6 0.1 pad_maximum_fusion.xp_ref
  37.8 0.7 %fusion.3 = (bf16[16,1,64,128]{3,2,1,0:T(8,128)(2,1)S(1)}, bf16[16,1,64,128]{3,2,1,0:T(8,128)(2,1)}) fusion(bf16[16,4,64,128]{3,2,1,0:T(8,128)(2,1)S(1)} %pad_maximum_fusion.xp_ref), kind=kLoop, calls=%fused_computation.7 | loop fusion | bytes 1048576 | tf_op jit(solution)/shard_map/slice | solution.py:421
  38.5 3.4 %collective-permute-start.4 = (bf16[16,1,64,128]{3,2,1,0:T(8,128)(2,1)}, bf16[16,1,64,128]{3,2,1,0:T(8,128)(2,1)S(1)}, u32[]{:S(2)}, u32[]{:S(2)}) collective-permute-start(bf16[16,1,64,128]{3,2,1,0:T(8,128)(2,1)} %get-tuple-element.18), channel_id=1, source_target_pairs={{0,1},{1,2},{2,3},{3,4},{4,5},{5,6},{6,7},{7,8},{8,9},{9,10},{10,1... | collective-permute-start | bytes 786440 | tf_op jit(solution)/shard_map/ppermute | solution.py:27
  41.9 1.9 %collective-permute-start.5 = (bf16[16,1,64,128]{3,2,1,0:T(8,128)(2,1)S(1)}, bf16[16,1,64,128]{3,2,1,0:T(8,128)(2,1)S(1)}, u32[]{:S(2)}, u32[]{:S(2)}) collective-permute-start(bf16[16,1,64,128]{3,2,1,0:T(8,128)(2,1)S(1)} %get-tuple-element.17), channel_id=1, source_target_pairs={{1,0},{2,1},{3,2},{4,3},{5,4},{6,5},{7,6},{8,7},{9,8},{10,9},{11,1... | collective-permute-start | bytes 786440 | tf_op jit(solution)/shard_map/ppermute | solution.py:27
  43.8 0.0 copy-done.2
  43.8 0.4 copy.16
  44.2 0.0 copy-start.1
  44.2 1.3 %collective-permute-done.4.above_ref = bf16[16,1,64,128]{3,2,1,0:T(8,128)(2,1)S(1)} collective-permute-done((bf16[16,1,64,128]{3,2,1,0:T(8,128)(2,1)}, bf16[16,1,64,128]{3,2,1,0:T(8,128)(2,1)S(1)}, u32[]{:S(2)}, u32[]{:S(2)}) %collective-permute-start.4) | collective-permute-done | bytes 262176 | tf_op jit(solution)/shard_map/ppermute | solution.py:27
  45.5 7.7 %collective-permute-done.5.below_ref = bf16[16,1,64,128]{3,2,1,0:T(8,128)(2,1)S(1)} collective-permute-done((bf16[16,1,64,128]{3,2,1,0:T(8,128)(2,1)S(1)}, bf16[16,1,64,128]{3,2,1,0:T(8,128)(2,1)S(1)}, u32[]{:S(2)}, u32[]{:S(2)}) %collective-permute-start.5) | collective-permute-done | bytes 262176 | tf_op jit(solution)/shard_map/ppermute | solution.py:27
  53.2 0.8 %shard_map.68.edge_ref = bf16[2,256,288]{2,1,0:T(8,128)(2,1)S(1)} custom-call(bf16[16,1,64,128]{3,2,1,0:T(8,128)(2,1)S(1)} %collective-permute-done.4.above_ref, bf16[16,4,64,128]{3,2,1,0:T(8,128)(2,1)S(1)} %pad_maximum_fusion.xp_ref, bf16[16,1,64,128]{3,2,1,0:T(8,128)(2,1)S(1)} %collective-permute-done.5.below_ref, bf16[1152,288]{1,0:T(8,128)(2,1)S(1)} %bitcast.11), custom_call_target="tpu_custom_call" | custom-call | flops 339738624 | bytes 1048576 | tf_op jit(solution)/shard_map/pallas_call | solution.py:353
  54.0 1.9 %collective-permute-start.6 = (bf16[1,256,288]{2,1,0:T(8,128)(2,1)S(1)}, bf16[1,256,288]{2,1,0:T(8,128)(2,1)S(1)}, u32[]{:S(2)}, u32[]{:S(2)}) collective-permute-start(bf16[1,256,288]{2,1,0:T(8,128)(2,1)S(1)} %get-tuple-element.22), channel_id=1, source_target_pairs={{0,16},{16,32},{32,48},{48,64},{64,80},{80,96},{96,112},{1,17},{17... | collective-permute-start | bytes 442376 | tf_op jit(solution)/shard_map/ppermute | solution.py:27
  56.0 5.5 %collective-permute-start.7 = (bf16[1,256,288]{2,1,0:T(8,128)(2,1)S(1)}, bf16[1,256,288]{2,1,0:T(8,128)(2,1)S(1)}, u32[]{:S(2)}, u32[]{:S(2)}) collective-permute-start(bf16[1,256,288]{2,1,0:T(8,128)(2,1)S(1)} %get-tuple-element.21), channel_id=1, source_target_pairs={{16,0},{32,16},{48,32},{64,48},{80,64},{96,80},{112,96},{17,1},{33... | collective-permute-start | bytes 442376 | tf_op jit(solution)/shard_map/ppermute | solution.py:27
  61.5 0.0 copy-done.1
  61.5 8.3 %shard_map.69 = (bf16[14,4,64,128]{3,2,1,0:T(8,128)(2,1)S(1)}, bf16[2,256,288]{2,1,0:T(8,128)(2,1)S(1)}) custom-call(bf16[16,1,64,128]{3,2,1,0:T(8,128)(2,1)S(1)} %collective-permute-done.4.above_ref, bf16[16,4,64,128]{3,2,1,0:T(8,128)(2,1)S(1)} %pad_maximum_fusion.xp_ref, bf16[16,1,64,128]{3,2,1,0:T(8,128)(2,1)S(1)} %collective-permute-done.5.below_ref, ...), custom_call_target="tpu_custom_call" | custom-call | flops 3623878656 | bytes 2097152 | tf_op jit(solution)/shard_map/pallas_call | solution.py:365
  69.7 0.0 collective-permute-done.6.before_ref
  69.8 0.0 collective-permute-done.7.after_ref
  69.8 0.4 shard_map.70
  70.2 1.1 %pad_maximum_fusion.1 = bf16[16,4,64,128]{3,2,1,0:T(8,128)(2,1)} fusion(bf16[1,4,64,128]{3,2,1,0:T(8,128)(2,1)S(1)} %get-tuple-element.24, bf16[14,4,64,128]{3,2,1,0:T(8,128)(2,1)S(1)} %get-tuple-element.16, bf16[1,4,64,128]{3,2,1,0:T(8,128)(2,1)S(1)} %get-tuple-element.23), kind=kLoop, calls=%fused_computation.1 | loop fusion | flops 1048576 | bytes 2097152 | tf_op jit(solution)/shard_map/concatenate | solution.py:388
  (3 shorter events, 0.1 us)
Async XLA Ops:
  0.0 18.5 %copy-start = (bf16[16,8,64,128]{3,2,1,0:T(8,128)(2,1)S(1)}, bf16[16,8,64,128]{3,2,1,0:T(8,128)(2,1)}, u32[]{:S(2)}) copy-start(bf16[16,8,64,128]{3,2,1,0:T(8,128)(2,1)} %xp_ref.5) | copy-start | bytes 6291460
  0.0 8.9 %copy-start.4 = (bf16[3,64,144]{2,1,0:T(8,128)(2,1)S(1)}, bf16[3,64,144]{2,1,0:T(8,128)(2,1)}, u32[]{:S(2)}) copy-start(bf16[3,64,144]{2,1,0:T(8,128)(2,1)} %param.8) | copy-start | bytes 165892
  0.0 10.3 %copy-start.3 = (bf16[3,3,128,64]{2,3,1,0:T(8,128)(2,1)S(1)}, bf16[3,3,128,64]{2,3,1,0:T(8,128)(2,1)}, u32[]{:S(2)}) copy-start(bf16[3,3,128,64]{2,3,1,0:T(8,128)(2,1)} %param.9) | copy-start | bytes 442372
  2.2 16.3 %collective-permute-start = (bf16[16,2,64,128]{3,2,1,0:T(8,128)(2,1)}, bf16[16,2,64,128]{3,2,1,0:T(8,128)(2,1)S(1)}, u32[]{:S(2)}, u32[]{:S(2)}) collective-permute-start(bf16[16,2,64,128]{3,2,1,0:T(8,128)(2,1)} %get-tuple-element.11), channel_id=1, source_target_pairs={{0,1},{1,2},{2,3},{3,4},{4,5},{5,6},{6,7},{7,8},{8,9},{9,10},{10,1... | collective-permute-start | bytes 1572872 | tf_op jit(solution)/shard_map/ppermute | solution.py:27
  7.0 11.5 %collective-permute-start.1 = (bf16[16,1,64,128]{3,2,1,0:T(8,128)(2,1)}, bf16[16,1,64,128]{3,2,1,0:T(8,128)(2,1)S(1)}, u32[]{:S(2)}, u32[]{:S(2)}) collective-permute-start(bf16[16,1,64,128]{3,2,1,0:T(8,128)(2,1)} %get-tuple-element.12), channel_id=1, source_target_pairs={{1,0},{2,1},{3,2},{4,3},{5,4},{6,5},{7,6},{8,7},{9,8},{10,9},{11,1... | collective-permute-start | bytes 786440 | tf_op jit(solution)/shard_map/ppermute | solution.py:27
  19.4 17.3 %collective-permute-start.2 = (bf16[1,144,1152]{2,1,0:T(8,128)(2,1)S(1)}, bf16[1,144,1152]{2,1,0:T(8,128)(2,1)S(1)}, u32[]{:S(2)}, u32[]{:S(2)}) collective-permute-start(bf16[1,144,1152]{2,1,0:T(8,128)(2,1)S(1)} %get-tuple-element.20), channel_id=1, source_target_pairs={{0,16},{16,32},{32,48},{48,64},{64,80},{80,96},{96,112},{1,17},{17... | collective-permute-start | bytes 995336 | tf_op jit(solution)/shard_map/ppermute | solution.py:27
  22.5 14.2 %collective-permute-start.3 = (bf16[1,144,1152]{2,1,0:T(8,128)(2,1)S(1)}, bf16[1,144,1152]{2,1,0:T(8,128)(2,1)S(1)}, u32[]{:S(2)}, u32[]{:S(2)}) collective-permute-start(bf16[1,144,1152]{2,1,0:T(8,128)(2,1)S(1)} %get-tuple-element.19), channel_id=1, source_target_pairs={{16,0},{32,16},{48,32},{64,48},{80,64},{96,80},{112,96},{17,1},{33... | collective-permute-start | bytes 995336 | tf_op jit(solution)/shard_map/ppermute | solution.py:27
  37.6 6.2 %copy-start.2 = (bf16[3,3,288,128]{3,2,1,0:T(8,128)(2,1)S(1)}, bf16[3,3,288,128]{3,2,1,0:T(8,128)(2,1)}, u32[]{:S(2)}) copy-start(bf16[3,3,288,128]{3,2,1,0:T(8,128)(2,1)} %param.10) | copy-start | bytes 1990660
  38.5 7.0 %collective-permute-start.4 = (bf16[16,1,64,128]{3,2,1,0:T(8,128)(2,1)}, bf16[16,1,64,128]{3,2,1,0:T(8,128)(2,1)S(1)}, u32[]{:S(2)}, u32[]{:S(2)}) collective-permute-start(bf16[16,1,64,128]{3,2,1,0:T(8,128)(2,1)} %get-tuple-element.18), channel_id=1, source_target_pairs={{0,1},{1,2},{2,3},{3,4},{4,5},{5,6},{6,7},{7,8},{8,9},{9,10},{10,1... | collective-permute-start | bytes 786440 | tf_op jit(solution)/shard_map/ppermute | solution.py:27
  41.9 11.3 %collective-permute-start.5 = (bf16[16,1,64,128]{3,2,1,0:T(8,128)(2,1)S(1)}, bf16[16,1,64,128]{3,2,1,0:T(8,128)(2,1)S(1)}, u32[]{:S(2)}, u32[]{:S(2)}) collective-permute-start(bf16[16,1,64,128]{3,2,1,0:T(8,128)(2,1)S(1)} %get-tuple-element.17), channel_id=1, source_target_pairs={{1,0},{2,1},{3,2},{4,3},{5,4},{6,5},{7,6},{8,7},{9,8},{10,9},{11,1... | collective-permute-start | bytes 786440 | tf_op jit(solution)/shard_map/ppermute | solution.py:27
  44.2 17.2 %copy-start.1 = (bf16[3,128,288]{1,2,0:T(8,128)(2,1)S(1)}, bf16[3,128,288]{1,2,0:T(8,128)(2,1)}, u32[]{:S(2)}) copy-start(bf16[3,128,288]{1,2,0:T(8,128)(2,1)} %param.11) | copy-start | bytes 663556
  54.0 15.7 %collective-permute-start.6 = (bf16[1,256,288]{2,1,0:T(8,128)(2,1)S(1)}, bf16[1,256,288]{2,1,0:T(8,128)(2,1)S(1)}, u32[]{:S(2)}, u32[]{:S(2)}) collective-permute-start(bf16[1,256,288]{2,1,0:T(8,128)(2,1)S(1)} %get-tuple-element.22), channel_id=1, source_target_pairs={{0,16},{16,32},{32,48},{48,64},{64,80},{80,96},{96,112},{1,17},{17... | collective-permute-start | bytes 442376 | tf_op jit(solution)/shard_map/ppermute | solution.py:27
  56.0 13.8 %collective-permute-start.7 = (bf16[1,256,288]{2,1,0:T(8,128)(2,1)S(1)}, bf16[1,256,288]{2,1,0:T(8,128)(2,1)S(1)}, u32[]{:S(2)}, u32[]{:S(2)}) collective-permute-start(bf16[1,256,288]{2,1,0:T(8,128)(2,1)S(1)} %get-tuple-element.21), channel_id=1, source_target_pairs={{16,0},{32,16},{48,32},{64,48},{80,64},{96,80},{112,96},{17,1},{33... | collective-permute-start | bytes 442376 | tf_op jit(solution)/shard_map/ppermute | solution.py:27

commit v23 on v22

--- a/solution.py
+++ b/solution.py
@@ -174,12 +174,13 @@
         _down_many(sums, refs, ts, wd_ref, keep_ref, out_ref, [u - 1 for u in ts])
 
     def section(g, carry):
-        run(4 * g + 1, 2)
+        run(6 * g + 1, 3)
         return carry
 
-    lax.fori_loop(0, (frames - 2) // 4, section, 0)
-    if (frames - 2) % 4:
-        run(frames - 3, 1)
+    lax.fori_loop(0, (frames - 2) // 6, section, 0)
+    left = ((frames - 2) % 6) // 2
+    if left:
+        run(frames - 1 - 2 * left, left)
 
 
 def _outer_one_kernel(

time: 71.7 us -> 71.7 us (level)
  no operation moved by 1% of the time
where the time goes in v23:
time: 71.7 us; the launch traced here: 71.3 us
  starting transfers between devices  26.8 us (37%)
  Pallas kernels  23.3 us (32%)
  waiting for transfers between devices  16.9 us (24%)
  local copies, waits for them, and re-layouts  2.78 us (4%)
  other arithmetic  1.33 us (2%)
    ppermute x8, starting transfers between devices, from_behind(): return lax.ppermute(array, axis, pairs)  26.8 us
    ppermute x8, waiting for transfers between devices, from_behind(): return lax.ppermute(array, axis, pairs)  16.9 us
    pallas_call x1, Pallas kernels, block_one(): pl.pallas_call(_inner_one_kernel, out_shape=(jax.ShapeDtypeStruct((frames...  9.87 us
    pallas_call x1, Pallas kernels, block_two(): pl.pallas_call(_inner_two_kernel, out_shape=(jax.ShapeDtypeStruct((frames...  8.27 us
    pallas_call x1, Pallas kernels, edge_rows(): pl.pallas_call(_copy_kernel, grid=(1,), out_shape=(jax.ShapeDtypeStruct((...  2.17 us
  transfers between devices with their start and end apart: 8, of which 3 were waited for; matrix products, arithmetic and copies ran while one was open for 3% of the time, Pallas kernels for 25%

profile of v23, /device:TPU:57, one launch (start us, length us, event | category | flops | bytes accessed | tf_op | source)
XLA Modules:
  0.0 71.3 jit_solution(18008578012210840952)
XLA Ops:
  0.0 0.0 copy-start
  0.0 0.0 copy-start.4
  0.0 0.0 copy-start.3
  0.0 2.2 %shard_map.64 = (bf16[16,2,64,128]{3,2,1,0:T(8,128)(2,1)}, bf16[16,1,64,128]{3,2,1,0:T(8,128)(2,1)}) custom-call(bf16[16,8,64,128]{3,2,1,0:T(8,128)(2,1)} %xp_ref.5, bf16[16,8,64,128]{3,2,1,0:T(8,128)(2,1)} %xp_ref.5), custom_call_target="tpu_custom_call" | custom-call | tf_op jit(solution)/shard_map/pallas_call | solution.py:401
  2.2 4.8 %collective-permute-start = (bf16[16,2,64,128]{3,2,1,0:T(8,128)(2,1)}, bf16[16,2,64,128]{3,2,1,0:T(8,128)(2,1)S(1)}, u32[]{:S(2)}, u32[]{:S(2)}) collective-permute-start(bf16[16,2,64,128]{3,2,1,0:T(8,128)(2,1)} %get-tuple-element.11), channel_id=1, source_target_pairs={{0,1},{1,2},{2,3},{3,4},{4,5},{5,6},{6,7},{7,8},{8,9},{9,10},{10,1... | collective-permute-start | bytes 1572872 | tf_op jit(solution)/shard_map/ppermute | solution.py:27
  7.0 1.9 %collective-permute-start.1 = (bf16[16,1,64,128]{3,2,1,0:T(8,128)(2,1)}, bf16[16,1,64,128]{3,2,1,0:T(8,128)(2,1)S(1)}, u32[]{:S(2)}, u32[]{:S(2)}) collective-permute-start(bf16[16,1,64,128]{3,2,1,0:T(8,128)(2,1)} %get-tuple-element.12), channel_id=1, source_target_pairs={{1,0},{2,1},{3,2},{4,3},{5,4},{6,5},{7,6},{8,7},{9,8},{10,9},{11,1... | collective-permute-start | bytes 786440 | tf_op jit(solution)/shard_map/ppermute | solution.py:27
  8.9 0.0 copy-done.4
  8.9 0.1 copy.11
  9.0 0.1 reshape.19.t3_ref
  9.2 1.1 %copy.12.w9_ref = bf16[144,576]{1,0:T(8,128)(2,1)S(1)} copy(bf16[144,576]{0,1:T(8,128)(2,1)} %bitcast.16) | data formatting | bytes 331776 | tf_op jit(solution)/shard_map/reshape | solution.py:205
  10.3 0.0 copy-done.3
  10.3 0.2 copy.15.wd_ref
  10.5 0.1 fusion.2.t3_ref
  10.6 8.0 %collective-permute-done.1.below_ref = bf16[16,1,64,128]{3,2,1,0:T(8,128)(2,1)S(1)} collective-permute-done((bf16[16,1,64,128]{3,2,1,0:T(8,128)(2,1)}, bf16[16,1,64,128]{3,2,1,0:T(8,128)(2,1)S(1)}, u32[]{:S(2)}, u32[]{:S(2)}) %collective-permute-start.1) | collective-permute-done | bytes 262176 | tf_op jit(solution)/shard_map/ppermute | solution.py:27
  18.5 0.0 collective-permute-done.above_ref
  18.5 0.0 copy-done
  18.5 0.8 %shard_map.65.edge_ref = bf16[2,144,1152]{2,1,0:T(8,128)(2,1)S(1)} custom-call(bf16[16,2,64,128]{3,2,1,0:T(8,128)(2,1)S(1)} %collective-permute-done.above_ref, bf16[16,8,64,128]{3,2,1,0:T(8,128)(2,1)S(1)} %copy-done, bf16[16,1,64,128]{3,2,1,0:T(8,128)(2,1)S(1)} %collective-permute-done.1.below_ref, bf16[144,576]{1,0:T(8,128)(2,1)S(1)} %copy.12.w9_ref), custom_call_target="tpu_custom_call" | custom-call | flops 382205952 | bytes 2097152 | tf_op jit(solution)/shard_map/pallas_call | solution.py:222
  19.3 0.1 fusion.4
  19.4 3.1 %collective-permute-start.2 = (bf16[1,144,1152]{2,1,0:T(8,128)(2,1)S(1)}, bf16[1,144,1152]{2,1,0:T(8,128)(2,1)S(1)}, u32[]{:S(2)}, u32[]{:S(2)}) collective-permute-start(bf16[1,144,1152]{2,1,0:T(8,128)(2,1)S(1)} %get-tuple-element.20), channel_id=1, source_target_pairs={{0,16},{16,32},{32,48},{48,64},{64,80},{80,96},{96,112},{1,17},{17... | collective-permute-start | bytes 995336 | tf_op jit(solution)/shard_map/ppermute | solution.py:27
  22.5 4.3 %collective-permute-start.3 = (bf16[1,144,1152]{2,1,0:T(8,128)(2,1)S(1)}, bf16[1,144,1152]{2,1,0:T(8,128)(2,1)S(1)}, u32[]{:S(2)}, u32[]{:S(2)}) collective-permute-start(bf16[1,144,1152]{2,1,0:T(8,128)(2,1)S(1)} %get-tuple-element.19), channel_id=1, source_target_pairs={{16,0},{32,16},{48,32},{64,48},{80,64},{96,80},{112,96},{17,1},{33... | collective-permute-start | bytes 995336 | tf_op jit(solution)/shard_map/ppermute | solution.py:27
  26.8 9.9 %shard_map.66 = (bf16[14,4,64,128]{3,2,1,0:T(8,128)(2,1)S(1)}, bf16[2,144,1152]{2,1,0:T(8,128)(2,1)S(1)}) custom-call(s32[1]{0:T(128)} %bitcast.keep_ref, bf16[16,2,64,128]{3,2,1,0:T(8,128)(2,1)S(1)} %collective-permute-done.above_ref, bf16[16,8,64,128]{3,2,1,0:T(8,128)(2,1)S(1)} %copy-done, bf16[16,1,64,128]{3,2,1,0:T(8,128)(2,1)S(1)} %collective-permute-done.1.below_ref, ...), custom_call_target="tpu_custom_call" | custom-call | flops 5284823040 | bytes 4194304 | tf_op jit(solution)/shard_map/pallas_call | solution.py:232
  36.6 0.0 collective-permute-done.2.before_ref
  36.6 0.0 collective-permute-done.3.after_ref
  36.7 0.9 %shard_map.67 = bf16[2,4,64,128]{3,2,1,0:T(8,128)(2,1)S(1)} custom-call(s32[1]{0:T(128)} %bitcast.keep_ref, bf16[16,2,64,128]{3,2,1,0:T(8,128)(2,1)S(1)} %collective-permute-done.above_ref, bf16[16,8,64,128]{3,2,1,0:T(8,128)(2,1)S(1)} %copy-done, bf16[16,1,64,128]{3,2,1,0:T(8,128)(2,1)S(1)} %collective-permute-done.1.below_ref, ...), custom_call_target="tpu_custom_call" | custom-call | tf_op jit(solution)/shard_map/pallas_call | solution.py:246
  37.6 0.0 copy-start.2
  37.6 0.1 pad_maximum_fusion.xp_ref
  37.8 0.7 %fusion.3 = (bf16[16,1,64,128]{3,2,1,0:T(8,128)(2,1)S(1)}, bf16[16,1,64,128]{3,2,1,0:T(8,128)(2,1)}) fusion(bf16[16,4,64,128]{3,2,1,0:T(8,128)(2,1)S(1)} %pad_maximum_fusion.xp_ref), kind=kLoop, calls=%fused_computation.7 | loop fusion | bytes 1048576 | tf_op jit(solution)/shard_map/slice | solution.py:422
  38.5 3.4 %collective-permute-start.4 = (bf16[16,1,64,128]{3,2,1,0:T(8,128)(2,1)}, bf16[16,1,64,128]{3,2,1,0:T(8,128)(2,1)S(1)}, u32[]{:S(2)}, u32[]{:S(2)}) collective-permute-start(bf16[16,1,64,128]{3,2,1,0:T(8,128)(2,1)} %get-tuple-element.18), channel_id=1, source_target_pairs={{0,1},{1,2},{2,3},{3,4},{4,5},{5,6},{6,7},{7,8},{8,9},{9,10},{10,1... | collective-permute-start | bytes 786440 | tf_op jit(solution)/shard_map/ppermute | solution.py:27
  41.9 1.9 %collective-permute-start.5 = (bf16[16,1,64,128]{3,2,1,0:T(8,128)(2,1)S(1)}, bf16[16,1,64,128]{3,2,1,0:T(8,128)(2,1)S(1)}, u32[]{:S(2)}, u32[]{:S(2)}) collective-permute-start(bf16[16,1,64,128]{3,2,1,0:T(8,128)(2,1)S(1)} %get-tuple-element.17), channel_id=1, source_target_pairs={{1,0},{2,1},{3,2},{4,3},{5,4},{6,5},{7,6},{8,7},{9,8},{10,9},{11,1... | collective-permute-start | bytes 786440 | tf_op jit(solution)/shard_map/ppermute | solution.py:27
  43.8 0.0 copy-done.2
  43.8 0.4 copy.16
  44.2 0.0 copy-start.1
  44.2 1.3 %collective-permute-done.4.above_ref = bf16[16,1,64,128]{3,2,1,0:T(8,128)(2,1)S(1)} collective-permute-done((bf16[16,1,64,128]{3,2,1,0:T(8,128)(2,1)}, bf16[16,1,64,128]{3,2,1,0:T(8,128)(2,1)S(1)}, u32[]{:S(2)}, u32[]{:S(2)}) %collective-permute-start.4) | collective-permute-done | bytes 262176 | tf_op jit(solution)/shard_map/ppermute | solution.py:27
  45.5 7.7 %collective-permute-done.5.below_ref = bf16[16,1,64,128]{3,2,1,0:T(8,128)(2,1)S(1)} collective-permute-done((bf16[16,1,64,128]{3,2,1,0:T(8,128)(2,1)S(1)}, bf16[16,1,64,128]{3,2,1,0:T(8,128)(2,1)S(1)}, u32[]{:S(2)}, u32[]{:S(2)}) %collective-permute-start.5) | collective-permute-done | bytes 262176 | tf_op jit(solution)/shard_map/ppermute | solution.py:27
  53.2 0.8 %shard_map.68.edge_ref = bf16[2,256,288]{2,1,0:T(8,128)(2,1)S(1)} custom-call(bf16[16,1,64,128]{3,2,1,0:T(8,128)(2,1)S(1)} %collective-permute-done.4.above_ref, bf16[16,4,64,128]{3,2,1,0:T(8,128)(2,1)S(1)} %pad_maximum_fusion.xp_ref, bf16[16,1,64,128]{3,2,1,0:T(8,128)(2,1)S(1)} %collective-permute-done.5.below_ref, bf16[1152,288]{1,0:T(8,128)(2,1)S(1)} %bitcast.11), custom_call_target="tpu_custom_call" | custom-call | flops 339738624 | bytes 1048576 | tf_op jit(solution)/shard_map/pallas_call | solution.py:354
  54.0 1.9 %collective-permute-start.6 = (bf16[1,256,288]{2,1,0:T(8,128)(2,1)S(1)}, bf16[1,256,288]{2,1,0:T(8,128)(2,1)S(1)}, u32[]{:S(2)}, u32[]{:S(2)}) collective-permute-start(bf16[1,256,288]{2,1,0:T(8,128)(2,1)S(1)} %get-tuple-element.22), channel_id=1, source_target_pairs={{0,16},{16,32},{32,48},{48,64},{64,80},{80,96},{96,112},{1,17},{17... | collective-permute-start | bytes 442376 | tf_op jit(solution)/shard_map/ppermute | solution.py:27
  56.0 5.5 %collective-permute-start.7 = (bf16[1,256,288]{2,1,0:T(8,128)(2,1)S(1)}, bf16[1,256,288]{2,1,0:T(8,128)(2,1)S(1)}, u32[]{:S(2)}, u32[]{:S(2)}) collective-permute-start(bf16[1,256,288]{2,1,0:T(8,128)(2,1)S(1)} %get-tuple-element.21), channel_id=1, source_target_pairs={{16,0},{32,16},{48,32},{64,48},{80,64},{96,80},{112,96},{17,1},{33... | collective-permute-start | bytes 442376 | tf_op jit(solution)/shard_map/ppermute | solution.py:27
  61.5 0.0 copy-done.1
  61.5 8.3 %shard_map.69 = (bf16[14,4,64,128]{3,2,1,0:T(8,128)(2,1)S(1)}, bf16[2,256,288]{2,1,0:T(8,128)(2,1)S(1)}) custom-call(bf16[16,1,64,128]{3,2,1,0:T(8,128)(2,1)S(1)} %collective-permute-done.4.above_ref, bf16[16,4,64,128]{3,2,1,0:T(8,128)(2,1)S(1)} %pad_maximum_fusion.xp_ref, bf16[16,1,64,128]{3,2,1,0:T(8,128)(2,1)S(1)} %collective-permute-done.5.below_ref, ...), custom_call_target="tpu_custom_call" | custom-call | flops 3623878656 | bytes 2097152 | tf_op jit(solution)/shard_map/pallas_call | solution.py:366
  69.7 0.0 collective-permute-done.6.before_ref
  69.8 0.0 collective-permute-done.7.after_ref
  69.8 0.4 shard_map.70
  70.2 1.1 %pad_maximum_fusion.1 = bf16[16,4,64,128]{3,2,1,0:T(8,128)(2,1)} fusion(bf16[1,4,64,128]{3,2,1,0:T(8,128)(2,1)S(1)} %get-tuple-element.24, bf16[14,4,64,128]{3,2,1,0:T(8,128)(2,1)S(1)} %get-tuple-element.16, bf16[1,4,64,128]{3,2,1,0:T(8,128)(2,1)S(1)} %get-tuple-element.23), kind=kLoop, calls=%fused_computation.1 | loop fusion | flops 1048576 | bytes 2097152 | tf_op jit(solution)/shard_map/concatenate | solution.py:389
  (3 shorter events, 0.1 us)
Async XLA Ops:
  0.0 18.5 %copy-start = (bf16[16,8,64,128]{3,2,1,0:T(8,128)(2,1)S(1)}, bf16[16,8,64,128]{3,2,1,0:T(8,128)(2,1)}, u32[]{:S(2)}) copy-start(bf16[16,8,64,128]{3,2,1,0:T(8,128)(2,1)} %xp_ref.5) | copy-start | bytes 6291460
  0.0 8.9 %copy-start.4 = (bf16[3,64,144]{2,1,0:T(8,128)(2,1)S(1)}, bf16[3,64,144]{2,1,0:T(8,128)(2,1)}, u32[]{:S(2)}) copy-start(bf16[3,64,144]{2,1,0:T(8,128)(2,1)} %param.8) | copy-start | bytes 165892
  0.0 10.3 %copy-start.3 = (bf16[3,3,128,64]{2,3,1,0:T(8,128)(2,1)S(1)}, bf16[3,3,128,64]{2,3,1,0:T(8,128)(2,1)}, u32[]{:S(2)}) copy-start(bf16[3,3,128,64]{2,3,1,0:T(8,128)(2,1)} %param.9) | copy-start | bytes 442372
  2.2 16.3 %collective-permute-start = (bf16[16,2,64,128]{3,2,1,0:T(8,128)(2,1)}, bf16[16,2,64,128]{3,2,1,0:T(8,128)(2,1)S(1)}, u32[]{:S(2)}, u32[]{:S(2)}) collective-permute-start(bf16[16,2,64,128]{3,2,1,0:T(8,128)(2,1)} %get-tuple-element.11), channel_id=1, source_target_pairs={{0,1},{1,2},{2,3},{3,4},{4,5},{5,6},{6,7},{7,8},{8,9},{9,10},{10,1... | collective-permute-start | bytes 1572872 | tf_op jit(solution)/shard_map/ppermute | solution.py:27
  7.0 11.5 %collective-permute-start.1 = (bf16[16,1,64,128]{3,2,1,0:T(8,128)(2,1)}, bf16[16,1,64,128]{3,2,1,0:T(8,128)(2,1)S(1)}, u32[]{:S(2)}, u32[]{:S(2)}) collective-permute-start(bf16[16,1,64,128]{3,2,1,0:T(8,128)(2,1)} %get-tuple-element.12), channel_id=1, source_target_pairs={{1,0},{2,1},{3,2},{4,3},{5,4},{6,5},{7,6},{8,7},{9,8},{10,9},{11,1... | collective-permute-start | bytes 786440 | tf_op jit(solution)/shard_map/ppermute | solution.py:27
  19.4 17.3 %collective-permute-start.2 = (bf16[1,144,1152]{2,1,0:T(8,128)(2,1)S(1)}, bf16[1,144,1152]{2,1,0:T(8,128)(2,1)S(1)}, u32[]{:S(2)}, u32[]{:S(2)}) collective-permute-start(bf16[1,144,1152]{2,1,0:T(8,128)(2,1)S(1)} %get-tuple-element.20), channel_id=1, source_target_pairs={{0,16},{16,32},{32,48},{48,64},{64,80},{80,96},{96,112},{1,17},{17... | collective-permute-start | bytes 995336 | tf_op jit(solution)/shard_map/ppermute | solution.py:27
  22.5 14.2 %collective-permute-start.3 = (bf16[1,144,1152]{2,1,0:T(8,128)(2,1)S(1)}, bf16[1,144,1152]{2,1,0:T(8,128)(2,1)S(1)}, u32[]{:S(2)}, u32[]{:S(2)}) collective-permute-start(bf16[1,144,1152]{2,1,0:T(8,128)(2,1)S(1)} %get-tuple-element.19), channel_id=1, source_target_pairs={{16,0},{32,16},{48,32},{64,48},{80,64},{96,80},{112,96},{17,1},{33... | collective-permute-start | bytes 995336 | tf_op jit(solution)/shard_map/ppermute | solution.py:27
  37.6 6.2 %copy-start.2 = (bf16[3,3,288,128]{3,2,1,0:T(8,128)(2,1)S(1)}, bf16[3,3,288,128]{3,2,1,0:T(8,128)(2,1)}, u32[]{:S(2)}) copy-start(bf16[3,3,288,128]{3,2,1,0:T(8,128)(2,1)} %param.10) | copy-start | bytes 1990660
  38.5 7.0 %collective-permute-start.4 = (bf16[16,1,64,128]{3,2,1,0:T(8,128)(2,1)}, bf16[16,1,64,128]{3,2,1,0:T(8,128)(2,1)S(1)}, u32[]{:S(2)}, u32[]{:S(2)}) collective-permute-start(bf16[16,1,64,128]{3,2,1,0:T(8,128)(2,1)} %get-tuple-element.18), channel_id=1, source_target_pairs={{0,1},{1,2},{2,3},{3,4},{4,5},{5,6},{6,7},{7,8},{8,9},{9,10},{10,1... | collective-permute-start | bytes 786440 | tf_op jit(solution)/shard_map/ppermute | solution.py:27
  41.9 11.3 %collective-permute-start.5 = (bf16[16,1,64,128]{3,2,1,0:T(8,128)(2,1)S(1)}, bf16[16,1,64,128]{3,2,1,0:T(8,128)(2,1)S(1)}, u32[]{:S(2)}, u32[]{:S(2)}) collective-permute-start(bf16[16,1,64,128]{3,2,1,0:T(8,128)(2,1)S(1)} %get-tuple-element.17), channel_id=1, source_target_pairs={{1,0},{2,1},{3,2},{4,3},{5,4},{6,5},{7,6},{8,7},{9,8},{10,9},{11,1... | collective-permute-start | bytes 786440 | tf_op jit(solution)/shard_map/ppermute | solution.py:27
  44.2 17.2 %copy-start.1 = (bf16[3,128,288]{1,2,0:T(8,128)(2,1)S(1)}, bf16[3,128,288]{1,2,0:T(8,128)(2,1)}, u32[]{:S(2)}) copy-start(bf16[3,128,288]{1,2,0:T(8,128)(2,1)} %param.11) | copy-start | bytes 663556
  54.0 15.7 %collective-permute-start.6 = (bf16[1,256,288]{2,1,0:T(8,128)(2,1)S(1)}, bf16[1,256,288]{2,1,0:T(8,128)(2,1)S(1)}, u32[]{:S(2)}, u32[]{:S(2)}) collective-permute-start(bf16[1,256,288]{2,1,0:T(8,128)(2,1)S(1)} %get-tuple-element.22), channel_id=1, source_target_pairs={{0,16},{16,32},{32,48},{48,64},{64,80},{80,96},{96,112},{1,17},{17... | collective-permute-start | bytes 442376 | tf_op jit(solution)/shard_map/ppermute | solution.py:27
  56.0 13.8 %collective-permute-start.7 = (bf16[1,256,288]{2,1,0:T(8,128)(2,1)S(1)}, bf16[1,256,288]{2,1,0:T(8,128)(2,1)S(1)}, u32[]{:S(2)}, u32[]{:S(2)}) collective-permute-start(bf16[1,256,288]{2,1,0:T(8,128)(2,1)S(1)} %get-tuple-element.21), channel_id=1, source_target_pairs={{16,0},{32,16},{48,32},{64,48},{80,64},{96,80},{112,96},{17,1},{33... | collective-permute-start | bytes 442376 | tf_op jit(solution)/shard_map/ppermute | solution.py:27
